TPU v7x, 32 devices: a whole 2x2x4 slice. The times are simulated.
32 devices in a mesh: dp: 8 (over z, y), tensor: 4 (over x, core).
Axes of the slice: x: 2, y: 2, z: 4, core: 2. Of those that a mesh axis runs over, the one named last changes fastest.
Arguments:
- inputs: bfloat16 [1024, 8192], P('dp', 'tensor'), may hold values from -6 to 6
- cotangent: bfloat16 [1024, 1024], P('dp', 'tensor'), may hold values from -6 to 6
- frozen_key_weight: bfloat16 [8192, 1024], P(None, 'tensor'), may hold values from -0.1875 to 0.1875
- adapter_down_weight: bfloat16 [8, 16, 8192], P('dp', None, 'tensor'), may hold values from -0.0625 to 0.0625
- adapter_up_weight: bfloat16 [8, 16, 1024], P('dp', None, 'tensor'), may hold values from -0.1875 to 0.1875
- tenant_per_block: int32 [8], P('dp'), may hold values from 0 to 7
Outputs:
- grad_inputs: bfloat16 [1024, 8192], P('dp', 'tensor')
- grad_down: float32 [8, 16, 8192], P('dp', None, 'tensor')
- grad_up: float32 [8, 16, 1024], P('dp', None, 'tensor')
All inputs are finite; a program needn't handle non-finite values.
Results may differ from a plain program's by a relative error of at most 0.0034.
Values may be sent and summed in bfloat16 or wider, within the bound.
No kernel may reach another device: no remote copies, remote signals or barrier semaphores. Data moves between devices by JAX's collectives and lax.ppermute only.
A program may use at most 128 MiB of HBM per device.

v0:
```python
import jax
import jax.numpy as jnp
from jax import lax
from jax.sharding import PartitionSpec as P

ADAPTER_SCALE = 2.0


def on_device(
    inputs, cotangent, frozen_key_weight, adapter_down_weight, adapter_up_weight, tenant_per_block
):
    token_row_count, width_portion = inputs.shape
    key_portion = cotangent.shape[1]
    block_count = tenant_per_block.shape[0]
    block_rows = token_row_count // block_count
    adapter_rank_size = adapter_down_weight.shape[1]
    held_block_count = adapter_down_weight.shape[0]
    owner_count = lax.axis_size("dp")
    tenant_number = owner_count * held_block_count
    pieces = (
        lax.all_gather(adapter_down_weight, "dp", axis=0, tiled=True),
        lax.all_gather(adapter_up_weight, "dp", axis=0, tiled=True),
    )
    piece_count = pieces[0].shape[0]
    tenant_ids = jnp.arange(piece_count, dtype=jnp.int32)
    member = (tenant_per_block[:, None] == tenant_ids[None, :]).astype(jnp.bfloat16)
    down_sum = jnp.einsum("bk,krd->brd", member, pieces[0], preferred_element_type=jnp.float32)
    up_sum = jnp.einsum("bk,krd->brd", member, pieces[1], preferred_element_type=jnp.float32)
    sel_down = down_sum
    sel_up = up_sum
    sel_down = sel_down.astype(jnp.bfloat16)
    sel_up = sel_up.astype(jnp.bfloat16)
    input_blocks = inputs.reshape(block_count, block_rows, width_portion)
    cotangent_blocks = cotangent.reshape(block_count, block_rows, key_portion)
    low_in = jnp.einsum("bnd,brd->bnr", input_blocks, sel_down, preferred_element_type=jnp.float32)
    reduced_output = ADAPTER_SCALE * jnp.einsum(
        "bnk,brk->bnr", cotangent_blocks, sel_up, preferred_element_type=jnp.float32
    )
    low_in, reduced_output = lax.psum((low_in, reduced_output), "tensor")
    reduced_input_batch = low_in.astype(jnp.bfloat16)
    low_out_b = reduced_output.astype(jnp.bfloat16)
    adapter_grad = jnp.einsum(
        "bnr,brd->bnd", low_out_b, sel_down, preferred_element_type=jnp.float32
    )
    adapter_grad = adapter_grad.reshape(token_row_count, width_portion)
    partial_grad = lax.dot_general(
        cotangent, frozen_key_weight, (((1,), (1,)), ((), ())), preferred_element_type=jnp.float32
    )
    base_grad = lax.psum_scatter(partial_grad, "tensor", scatter_dimension=1, tiled=True)
    grad_inputs = (base_grad + adapter_grad).astype(jnp.bfloat16)
    all_tenants = jnp.arange(tenant_number, dtype=jnp.int32)
    member = tenant_per_block[:, None] == all_tenants[None, :]
    member_b = member.astype(jnp.bfloat16)
    weighted_out = (member_b[:, None, :, None] * low_out_b[:, :, None, :]).reshape(
        token_row_count, tenant_number * adapter_rank_size
    )
    weighted_in = (member_b[:, None, :, None] * reduced_input_batch[:, :, None, :]).reshape(
        token_row_count, tenant_number * adapter_rank_size
    )
    down_contribution = lax.dot_general(
        weighted_out, inputs, (((0,), (0,)), ((), ())), preferred_element_type=jnp.float32
    )
    up_contribution = ADAPTER_SCALE * lax.dot_general(
        weighted_in, cotangent, (((0,), (0,)), ((), ())), preferred_element_type=jnp.float32
    )
    down_contribution = down_contribution.reshape(tenant_number, adapter_rank_size, width_portion)
    up_contribution = up_contribution.reshape(tenant_number, adapter_rank_size, key_portion)
    combined = jnp.concatenate([down_contribution, up_contribution], axis=2)
    owned = lax.psum_scatter(combined, "dp", scatter_dimension=0, tiled=True)
    grad_down = owned[:, :, :width_portion]
    grad_up = owned[:, :, width_portion:]
    return (grad_inputs, grad_down, grad_up)


def solution(mesh):
    in_specs = (
        P("dp", "tensor"),
        P("dp", "tensor"),
        P(None, "tensor"),
        P("dp", None, "tensor"),
        P("dp", None, "tensor"),
        P("dp"),
    )
    out_specs = (P("dp", "tensor"), P("dp", None, "tensor"), P("dp", None, "tensor"))
    return jax.shard_map(
        on_device, mesh=mesh, in_specs=in_specs, out_specs=out_specs, check_vma=False
    )
```

profile of v0, /device:TPU:0, one launch (start us, length us, event | category | flops | bytes accessed | tf_op | source)
XLA Modules:
  0.0 207.2 jit_solution(9838430073450406495)
XLA Ops:
  7.2 0.0 copy-start
  7.2 0.0 reduce-scatter.5.cloned.1.call-start
  7.2 33.3 %all_gather.7 = bf16[8,16,2048]{2,1,0:T(8,128)(2,1)S(1)} all-gather(bf16[1,16,2048]{2,1,0:T(8,128)(2,1)} %param.9), channel_id=1, replica_groups=mesh['dp'=8,'tensor'=4] {'dp'}, dimensions={0}, use_global_device_ids=true | all-gather | bytes 589824 | tf_op jit(solution)/shard_map/all_gather | solution.py:21
  41.2 30.7 %all_gather.6 = bf16[8,16,256]{2,1,0:T(8,128)(2,1)S(1)} all-gather(bf16[1,16,256]{2,1,0:T(8,128)(2,1)} %param.10), channel_id=1, replica_groups=mesh['dp'=8,'tensor'=4] {'dp'}, dimensions={0}, use_global_device_ids=true | all-gather | bytes 73728 | tf_op jit(solution)/shard_map/all_gather | solution.py:22
  72.0 0.1 mul.62
  72.0 0.1 mul.63
  72.1 0.5 fusion.4
  72.6 0.1 fusion.6
  72.7 1.0 fusion.1
  73.7 0.3 convolution_bitcast_fusion
  74.0 10.2 %all-reduce = (bf16[1,128,16]{1,2,0:T(8,128)(2,1)S(1)}, bf16[1,128,16]{1,2,0:T(8,128)(2,1)S(1)}) all-reduce(f32[1,128,16]{1,2,0:T(8,128)S(1)} %fusion.1, f32[1,128,16]{1,2,0:T(8,128)S(1)} %convolution_bitcast_fusion), channel_id=1, replica_groups=mesh['dp'=8,'tensor'=4] {'tensor'}, use_global_device_ids=true, to_apply=%region_1.0 | all-reduce | flops 4096 | bytes 24576 | tf_op jit(solution)/shard_map/psum | solution.py:39
  84.1 0.1 bitcast_multiply_fusion.1
  84.2 1.0 convolution_multiply_fusion
  85.2 0.3 fusion.2
  85.5 1.1 pad_maximum_fusion
  86.6 0.0 reduce-scatter.5.cloned.1.call-update
  86.6 0.0 reduce-scatter.3.cloned.1.call-start
  86.7 5.6 %fusion.14 = f32[128,8192]{1,0:T(8,128)} fusion(bf16[128,256]{1,0:T(8,128)(2,1)S(1)} %copy-done.1, bf16[8192,256]{1,0:T(8,128)(2,1)} %param.8), kind=kOutput, calls=%fused_computation.26 | convolution fusion | flops 536870912 | bytes 8454144 | tf_op jit(solution)/shard_map/dot_general | solution.py:46
  92.3 0.0 reduce-scatter.3.cloned.1.call-update
  92.3 59.7 %reduce-scatter.5.cloned.1.call-done = f32[1,16,2304]{2,1,0:T(8,128)} async-done(((f32[8,16,2304]{2,1,0:T(8,128)}), f32[1,16,2304]{2,1,0:T(8,128)}) %reduce-scatter.5.cloned.1.call-update) | async-done | bytes 147472 | tf_op jit(solution)/shard_map/reduce_scatter | solution.py:69
  152.0 1.6 slice.8
  153.6 1.3 slice.9
  154.9 43.1 %reduce-scatter.3.cloned.1.call-done = f32[128,2048]{1,0:T(8,128)} async-done(((f32[128,8192]{1,0:T(8,128)}), f32[128,2048]{1,0:T(8,128)}) %reduce-scatter.3.cloned.1.call-update) | async-done | bytes 1048592 | tf_op jit(solution)/shard_map/reduce_scatter | solution.py:49
  198.0 2.3 %fusion = bf16[128,2048]{1,0:T(8,128)(2,1)} fusion(f32[128,2048]{1,0:T(8,128)} %reduce-scatter.3.cloned.1.call-done, bf16[1,16,2048]{2,0,1:T(2,128)(2,1)S(1)} %fusion.4, bf16[1,128,16]{1,2,0:T(8,128)(2,1)S(1)} %get-tuple-element.3), kind=kOutput, calls=%fused_computation.1 | convolution fusion | flops 8912896 | bytes 1642496 | tf_op jit(solution)/shard_map/bnr,brd->bnd/dot_general | solution.py:42
  (4 shorter events, 0.0 us)
Async XLA Ops:
  7.2 66.5 %copy-start = (bf16[128,2048]{1,0:T(8,128)(2,1)S(1)}, bf16[128,2048]{1,0:T(8,128)(2,1)}, u32[]{:S(2)}) copy-start(bf16[128,2048]{1,0:T(8,128)(2,1)} %param.6) | copy-start | bytes 1572868
  7.2 79.5 %copy-start.1 = (bf16[128,256]{1,0:T(8,128)(2,1)S(1)}, bf16[128,256]{1,0:T(8,128)(2,1)}, u32[]{:S(2)}) copy-start(bf16[128,256]{1,0:T(8,128)(2,1)} %param.7) | copy-start | bytes 196612
  7.2 144.8 %reduce-scatter.5.cloned.1.call-start = ((), (), s32[]{:S(2)}) async-start(), calls=%async_computation.3 | async-start | bytes 1327104 | tf_op jit(solution)/shard_map/reduce_scatter | solution.py:69
  86.6 111.4 %reduce-scatter.3.cloned.1.call-start = ((), (), s32[]{:S(2)}) async-start(), calls=%async_computation.2 | async-start | bytes 5242880 | tf_op jit(solution)/shard_map/reduce_scatter | solution.py:49
Sparse Core Ops, SparseCore 0:
  86.7 65.2 reduce-scatter.4
  154.5 43.4 reduce-scatter.2
where the time goes:
time: 208 us; the launch traced here: 207 us
  waiting for transfers between devices  103 us (50%)
  blocking collectives  74.2 us (36%)
  between operations  14.7 us (7%)
  matrix products  11.1 us (5%)
  local copies, waits for them, and re-layouts  3.07 us (1%)
    reduce_scatter x1, waiting for transfers between devices, on_device(): owned = lax.psum_scatter(combined, 'dp', scatter_dimension=0, tiled=True)  59.7 us
    reduce_scatter x1, waiting for transfers between devices, on_device(): lax.psum_scatter(partial_grad, 'tensor', scatter_dimension=1, tiled=True)  43.1 us
    all_gather x1, blocking collectives, on_device(): lax.all_gather(adapter_down_weight, 'dp', axis=0, tiled=True)  33.3 us
    all_gather x1, blocking collectives, on_device(): lax.all_gather(adapter_up_weight, 'dp', axis=0, tiled=True)  30.7 us
    psum x1, blocking collectives, on_device(): low_in, reduced_output = lax.psum((low_in, reduced_output), 'tensor')  10.2 us
    dot_general x1, matrix products, on_device(): lax.dot_general(cotangent, frozen_key_weight, (((1,), (1,)), ((), ())), p...  5.61 us
  transfers between devices with their start and end apart: 2, of which 2 were waited for; matrix products, arithmetic and copies ran while one was open for 4% of the time, Pallas kernels for 0%

commit v1 on v0

v1 whole, which is shorter than its diff:
```python
import jax
import jax.numpy as jnp
from jax import lax
from jax.sharding import PartitionSpec as P

ADAPTER_SCALE = 2.0


def _partners(size):
    if size & (size - 1) == 0:
        return [(s, [(i, i ^ s) for i in range(size)]) for s in range(1, size)]
    return [(s, [(i, (i + s) % size) for i in range(size)]) for s in range(1, size)]


def _source_of(me, shift, size):
    if size & (size - 1) == 0:
        return me ^ shift
    return (me - shift + size) % size


def _dest_of(me, shift, size):
    if size & (size - 1) == 0:
        return me ^ shift
    return (me + shift) % size


def _gather_dp(local, axis, size):
    me = lax.axis_index(axis)
    got = [local]
    sources = [me]
    for shift, pairs in _partners(size):
        got.append(lax.ppermute(local, axis, pairs))
        sources.append(_source_of(me, shift, size))
    stacked = jnp.stack(got, 0)
    order = jnp.stack(sources)
    return stacked, order


def _psum_small(value, axis, size):
    total = value
    for _, pairs in _partners(size):
        total = total + lax.ppermute(value, axis, pairs)
    return total


def _reduce_scatter_cols(partial, axis, size):
    rows, cols = partial.shape
    if size & (size - 1) != 0:
        return lax.psum_scatter(partial, axis, scatter_dimension=1, tiled=True)
    me = lax.axis_index(axis)
    held = partial.reshape(rows, size, cols // size)
    bit = 0
    while (1 << bit) < size:
        width = held.shape[1] // 2
        split = held.reshape(rows, width, 2, cols // size)
        mine = (me >> bit) & 1
        keep = lax.dynamic_index_in_dim(split, mine, 2, keepdims=False)
        give = lax.dynamic_index_in_dim(split, 1 - mine, 2, keepdims=False)
        partner = 1 << bit
        got = lax.ppermute(give, axis, [(i, i ^ partner) for i in range(size)])
        held = keep + got
        bit += 1
    return held.reshape(rows, cols // size)


def on_device(
    inputs, cotangent, frozen_key_weight, adapter_down_weight, adapter_up_weight, tenant_per_block
):
    token_row_count, width_portion = inputs.shape
    key_portion = cotangent.shape[1]
    block_count = tenant_per_block.shape[0]
    block_rows = token_row_count // block_count
    adapter_rank_size = adapter_down_weight.shape[1]
    held_tenants = adapter_down_weight.shape[0]
    dp_size = lax.axis_size("dp")
    tensor_size = lax.axis_size("tensor")
    tenant_number = dp_size * held_tenants
    me_dp = lax.axis_index("dp")

    partial_grad = lax.dot_general(
        cotangent, frozen_key_weight, (((1,), (1,)), ((), ())), preferred_element_type=jnp.float32
    )
    base_grad = _reduce_scatter_cols(partial_grad, "tensor", tensor_size)

    packed = jnp.concatenate([adapter_down_weight, adapter_up_weight], axis=2)
    stacked, order = _gather_dp(packed, "dp", dp_size)
    owner = tenant_per_block // held_tenants
    local = tenant_per_block % held_tenants
    pick = (order[None, :] == owner[:, None])
    pick = pick[:, :, None] & (jnp.arange(held_tenants)[None, None, :] == local[:, None, None])
    pick = pick.reshape(block_count, dp_size * held_tenants).astype(jnp.bfloat16)
    flat = stacked.reshape(dp_size * held_tenants, adapter_rank_size, width_portion + key_portion)
    selected = jnp.einsum("bk,krd->brd", pick, flat, preferred_element_type=jnp.float32).astype(jnp.bfloat16)
    sel_down = selected[:, :, :width_portion]
    sel_up = selected[:, :, width_portion:]

    input_blocks = inputs.reshape(block_count, block_rows, width_portion)
    cotangent_blocks = cotangent.reshape(block_count, block_rows, key_portion)
    low_in = jnp.einsum("bnd,brd->bnr", input_blocks, sel_down, preferred_element_type=jnp.float32)
    reduced_output = ADAPTER_SCALE * jnp.einsum(
        "bnk,brk->bnr", cotangent_blocks, sel_up, preferred_element_type=jnp.float32
    )
    lows = _psum_small(jnp.concatenate([low_in, reduced_output], axis=2), "tensor", tensor_size)
    reduced_input_batch = lows[:, :, :adapter_rank_size].astype(jnp.bfloat16)
    low_out_b = lows[:, :, adapter_rank_size:].astype(jnp.bfloat16)

    adapter_grad = jnp.einsum(
        "bnr,brd->bnd", low_out_b, sel_down, preferred_element_type=jnp.float32
    )
    adapter_grad = adapter_grad.reshape(token_row_count, width_portion)
    grad_inputs = (base_grad + adapter_grad).astype(jnp.bfloat16)

    all_tenants = jnp.arange(tenant_number, dtype=jnp.int32)
    member = tenant_per_block[:, None] == all_tenants[None, :]
    member_b = member.astype(jnp.bfloat16)
    weighted_out = (member_b[:, None, :, None] * low_out_b[:, :, None, :]).reshape(
        token_row_count, tenant_number * adapter_rank_size
    )
    weighted_in = (member_b[:, None, :, None] * reduced_input_batch[:, :, None, :]).reshape(
        token_row_count, tenant_number * adapter_rank_size
    )
    down_contribution = lax.dot_general(
        weighted_out, inputs, (((0,), (0,)), ((), ())), preferred_element_type=jnp.float32
    )
    up_contribution = ADAPTER_SCALE * lax.dot_general(
        weighted_in, cotangent, (((0,), (0,)), ((), ())), preferred_element_type=jnp.float32
    )
    down_contribution = down_contribution.reshape(dp_size, held_tenants, adapter_rank_size, width_portion)
    up_contribution = up_contribution.reshape(dp_size, held_tenants, adapter_rank_size, key_portion)
    combined = jnp.concatenate([down_contribution, up_contribution], axis=3)
    owned = lax.dynamic_index_in_dim(combined, me_dp, 0, keepdims=False)
    for shift, pairs in _partners(dp_size):
        outgoing = lax.dynamic_index_in_dim(combined, _dest_of(me_dp, shift, dp_size), 0, keepdims=False)
        owned = owned + lax.ppermute(outgoing, "dp", pairs)
    grad_down = owned[:, :, :width_portion]
    grad_up = owned[:, :, width_portion:]
    return (grad_inputs, grad_down, grad_up)


def solution(mesh):
    in_specs = (
        P("dp", "tensor"),
        P("dp", "tensor"),
        P(None, "tensor"),
        P("dp", None, "tensor"),
        P("dp", None, "tensor"),
        P("dp"),
    )
    out_specs = (P("dp", "tensor"), P("dp", None, "tensor"), P("dp", None, "tensor"))
    return jax.shard_map(
        on_device, mesh=mesh, in_specs=in_specs, out_specs=out_specs, check_vma=False
    )
```

time: 208 us -> 89.4 us (0.43)
  waiting for transfers between devices: 103 us -> 13.6 us
  blocking collectives: 74.2 us -> 0 us
  starting transfers between devices: 0.08 us -> 32.7 us
  local copies, waits for them, and re-layouts: 3.07 us -> 26.3 us
  between operations: 14.7 us -> 1.46 us
  other arithmetic: 1.18 us -> 5.64 us
    reduce_scatter x2 -> x0, waiting for transfers between devices: 103 us -> none  [the longest x1 59.7 us: on_device(): owned = lax.psum_scatter(combined, 'dp', scatter_dimension=0, tiled=True)]
    all_gather x2 -> x0, blocking collectives: 64.1 us -> none  [the longest x1 33.3 us: on_device(): lax.all_gather(adapter_down_weight, 'dp', axis=0, tiled=True)]
    ppermute x0 -> x19, starting transfers between devices: none -> 32.7 us  [the longest x7 17.7 us: on_device(): owned = owned + lax.ppermute(outgoing, 'dp', pairs)]
    ppermute x0 -> x19, waiting for transfers between devices: none -> 13.6 us  [the longest x7 6.68 us: on_device(): owned = owned + lax.ppermute(outgoing, 'dp', pairs)]
    dynamic_slice x0 -> x2, local copies, waits for them, and re-layouts: none -> 11.8 us  [the longest x1 9.27 us: _reduce_scatter_cols(): keep = lax.dynamic_index_in_dim(split, mine, 2, keepdims=False)]
    psum x1 -> x0, blocking collectives: 10.2 us -> none  [on_device(): low_in, reduced_output = lax.psum((low_in, reduced_output), 'tensor')]
    another operation x0 -> x3, local copies, waits for them, and re-layouts: none -> 6.64 us  [the longest x1 6.55 us: _reduce_scatter_cols(): split = held.reshape(rows, width, 2, cols // size)]
    unnamed x4 -> x18, local copies, waits for them, and re-layouts: 0.02 us -> 5.6 us
  transfers between devices with their start and end apart: 2 -> 19, of which waited for: 2 -> 8; matrix products, arithmetic and copies ran while one was open for 4% -> 40% of each run, Pallas kernels for 0% -> 0%
where the time goes in v1:
time: 89.4 us; the launch traced here: 88.9 us
  starting transfers between devices  32.7 us (37%)
  local copies, waits for them, and re-layouts  26.3 us (29%)
  waiting for transfers between devices  13.6 us (15%)
  matrix products  9.19 us (10%)
  other arithmetic  5.64 us (6%)
  between operations  1.46 us (2%)
    ppermute x7, starting transfers between devices, on_device(): owned = owned + lax.ppermute(outgoing, 'dp', pairs)  17.7 us
    ppermute x7, starting transfers between devices, _gather_dp(): got.append(lax.ppermute(local, axis, pairs))  12.5 us
    dynamic_slice x1, local copies, waits for them, and re-layouts, _reduce_scatter_cols(): keep = lax.dynamic_index_in_dim(split, mine, 2, keepdims=False)  9.27 us
    ppermute x7, waiting for transfers between devices, on_device(): owned = owned + lax.ppermute(outgoing, 'dp', pairs)  6.68 us
    another operation x1, local copies, waits for them, and re-layouts, _reduce_scatter_cols(): split = held.reshape(rows, width, 2, cols // size)  6.55 us
    dot_general x1, matrix products, on_device(): lax.dot_general(cotangent, frozen_key_weight, (((1,), (1,)), ((), ())), p...  5.73 us
    unnamed x18, local copies, waits for them, and re-layouts  5.6 us
    ppermute x7, waiting for transfers between devices, _gather_dp(): got.append(lax.ppermute(local, axis, pairs))  5.13 us
  transfers between devices with their start and end apart: 19, of which 8 were waited for; matrix products, arithmetic and copies ran while one was open for 40% of the time, Pallas kernels for 0%

profile of v1, /device:TPU:0, one launch (start us, length us, event | category | flops | bytes accessed | tf_op | source)
XLA Modules:
  0.0 88.9 jit_solution(13230280292821874279)
XLA Ops:
  2.2 3.0 %collective-permute-start.2 = (bf16[1,16,2304]{2,1,0:T(8,128)(2,1)S(1)}, bf16[1,16,2304]{2,1,0:T(8,128)(2,1)}, u32[]{:S(2)}, u32[]{:S(2)}) collective-permute-start(bf16[1,16,2304]{2,1,0:T(8,128)(2,1)S(1)} %constant_dynamic-update-slice_fusion), channel_id=1, source_target_pairs={{0,4},{4,0},{8,12},{12,8},{16,20},{20,16},{24,28},{28,24},{1,5},{5... | collective-permute-start | bytes 221192 | tf_op jit(solution)/shard_map/ppermute | solution.py:32
  5.2 1.6 %collective-permute-start.3 = (bf16[1,16,2304]{2,1,0:T(8,128)(2,1)S(1)}, bf16[1,16,2304]{2,1,0:T(8,128)(2,1)}, u32[]{:S(2)}, u32[]{:S(2)}) collective-permute-start(bf16[1,16,2304]{2,1,0:T(8,128)(2,1)S(1)} %constant_dynamic-update-slice_fusion), channel_id=1, source_target_pairs={{0,8},{4,12},{8,0},{12,4},{16,24},{20,28},{24,16},{28,20},{1,9},{5... | collective-permute-start | bytes 221192 | tf_op jit(solution)/shard_map/ppermute | solution.py:32
  6.8 3.0 %collective-permute-start.5 = (bf16[1,16,2304]{2,1,0:T(8,128)(2,1)S(1)}, bf16[1,16,2304]{2,1,0:T(8,128)(2,1)S(1)}, u32[]{:S(2)}, u32[]{:S(2)}) collective-permute-start(bf16[1,16,2304]{2,1,0:T(8,128)(2,1)S(1)} %constant_dynamic-update-slice_fusion), channel_id=1, source_target_pairs={{0,16},{4,20},{8,24},{12,28},{16,0},{20,4},{24,8},{28,12},{1,17},{... | collective-permute-start | bytes 221192 | tf_op jit(solution)/shard_map/ppermute | solution.py:32
  9.8 1.3 %collective-permute-start.6 = (bf16[1,16,2304]{2,1,0:T(8,128)(2,1)S(1)}, bf16[1,16,2304]{2,1,0:T(8,128)(2,1)S(1)}, u32[]{:S(2)}, u32[]{:S(2)}) collective-permute-start(bf16[1,16,2304]{2,1,0:T(8,128)(2,1)S(1)} %constant_dynamic-update-slice_fusion), channel_id=1, source_target_pairs={{0,20},{4,16},{8,28},{12,24},{16,4},{20,0},{24,12},{28,8},{1,21},{... | collective-permute-start | bytes 221192 | tf_op jit(solution)/shard_map/ppermute | solution.py:32
  11.1 5.7 %fusion.33 = f32[128,8192]{1,0:T(8,128)} fusion(bf16[128,256]{1,0:T(8,128)(2,1)} %param.7, bf16[8192,256]{1,0:T(8,128)(2,1)} %param.8), kind=kOutput, calls=%fused_computation.79 | convolution fusion | flops 536870912 | bytes 8454144 | tf_op jit(solution)/shard_map/dot_general | solution.py:80
  16.8 6.5 %reshape_reshape.3 = f32[128,2,2,2048]{3,2,1,0:T(2,128)} reshape(f32[128,8192]{1,0:T(8,128)} %fusion.33) | data formatting | bytes 8388608 | tf_op jit(solution)/shard_map/reshape;reshape | solution.py:55
  23.4 9.3 %constant_dynamic-slice_fusion.2 = (f32[128,2,1,2048]{3,2,1,0:T(1,128)}, f32[128,2,1,2048]{3,2,1,0:T(1,128)S(1)}) fusion(f32[128,2,2,2048]{3,2,1,0:T(2,128)} %reshape_reshape.3, s32[]{:T(128)S(6)} %select_n.47, s32[]{:T(128)S(6)} %select_n.48), kind=kLoop, calls=%fused_computation.72 | loop fusion | bytes 8388616 | tf_op jit(solution)/shard_map/jit(dynamic_index_in_dim)/dynamic_slice | solution.py:57
  32.6 2.5 %copy.20 = f32[128,2,1,2048]{3,0,1,2:T(8,128)} copy(f32[128,2,1,2048]{3,2,1,0:T(1,128)S(1)} %get-tuple-element.4) | data formatting | bytes 4194304 | tf_op jit(solution)/shard_map/jit(dynamic_index_in_dim)/dynamic_slice | solution.py:58
  35.9 3.7 %collective-permute-start.7 = (bf16[1,16,2304]{2,1,0:T(8,128)(2,1)S(1)}, bf16[1,16,2304]{2,1,0:T(8,128)(2,1)S(1)}, u32[]{:S(2)}, u32[]{:S(2)}) collective-permute-start(bf16[1,16,2304]{2,1,0:T(8,128)(2,1)S(1)} %constant_dynamic-update-slice_fusion), channel_id=1, source_target_pairs={{0,24},{4,28},{8,16},{12,20},{16,8},{20,12},{24,0},{28,4},{1,25},{... | collective-permute-start | bytes 221192 | tf_op jit(solution)/shard_map/ppermute | solution.py:32
  42.5 5.1 %collective-permute-done.8 = bf16[1,16,2304]{2,1,0:T(8,128)(2,1)S(1)} collective-permute-done((bf16[1,16,2304]{2,1,0:T(8,128)(2,1)S(1)}, bf16[1,16,2304]{2,1,0:T(8,128)(2,1)S(1)}, u32[]{:S(2)}, u32[]{:S(2)}) %collective-permute-start.8) | collective-permute-done | bytes 73760 | tf_op jit(solution)/shard_map/ppermute | solution.py:32
  48.3 1.6 %collective-permute-start.10 = (f32[1,128,32]{1,2,0:T(8,128)S(1)}, f32[1,128,32]{1,2,0:T(8,128)S(1)}, u32[]{:S(2)}, u32[]{:S(2)}) collective-permute-start(f32[1,128,32]{1,2,0:T(8,128)S(1)} %pad_maximum_fusion), channel_id=1, source_target_pairs={{0,2},{1,3},{2,0},{3,1},{4,6},{5,7},{6,4},{7,5},{8,10},{9,11},{10,... | collective-permute-start | bytes 49160 | tf_op jit(solution)/shard_map/ppermute | solution.py:42
  50.4 1.3 %collective-permute-done.11 = f32[1,128,32]{1,2,0:T(8,128)S(1)} collective-permute-done((f32[1,128,32]{1,2,0:T(8,128)S(1)}, f32[1,128,32]{1,2,0:T(8,128)S(1)}, u32[]{:S(2)}, u32[]{:S(2)}) %collective-permute-start.11) | collective-permute-done | bytes 16416 | tf_op jit(solution)/shard_map/ppermute | solution.py:42
  52.7 1.2 %collective-permute-start.18 = (f32[1,16,2304]{2,1,0:T(8,128)S(1)}, f32[1,16,2304]{2,1,0:T(8,128)S(1)}, u32[]{:S(2)}, u32[]{:S(2)}) collective-permute-start(f32[1,16,2304]{2,1,0:T(8,128)S(1)} %fusion.6), channel_id=1, source_target_pairs={{0,28},{4,24},{8,20},{12,16},{16,12},{20,8},{24,4},{28,0},{1,29},{... | collective-permute-start | bytes 442376 | tf_op jit(solution)/shard_map/ppermute | solution.py:134
  53.9 3.5 %bitcast_add_fusion = f32[128,2,2048]{2,0,1:T(8,128)S(1)} fusion(f32[128,2,2048]{2,0,1:T(8,128)} %collective-permute-done, f32[128,2,1,2048]{3,2,1,0:T(1,128)} %get-tuple-element.3), kind=kLoop, calls=%fused_computation.9 | loop fusion | flops 524288 | bytes 6291456 | tf_op jit(solution)/shard_map/add | solution.py:61
  57.4 1.3 %copy-done.1 = f32[128,2,2048]{2,0,1:T(8,128)} copy-done((f32[128,2,2048]{2,0,1:T(8,128)}, f32[128,2,2048]{2,0,1:T(8,128)S(1)}, u32[]{:S(2)}) %copy-start.1) | copy-done | bytes 2097176
  60.2 3.6 %collective-permute-start.17 = (f32[1,16,2304]{2,1,0:T(8,128)S(1)}, f32[1,16,2304]{2,1,0:T(8,128)S(1)}, u32[]{:S(2)}, u32[]{:S(2)}) collective-permute-start(f32[1,16,2304]{2,1,0:T(8,128)S(1)} %get-tuple-element.10), channel_id=1, source_target_pairs={{0,24},{4,28},{8,16},{12,20},{16,8},{20,12},{24,0},{28,4},{1,25},{... | collective-permute-start | bytes 442376 | tf_op jit(solution)/shard_map/ppermute | solution.py:134
  63.8 3.9 %collective-permute-start.15 = (f32[1,16,2304]{2,1,0:T(8,128)}, f32[1,16,2304]{2,1,0:T(8,128)}, u32[]{:S(2)}, u32[]{:S(2)}) collective-permute-start(f32[1,16,2304]{2,1,0:T(8,128)} %get-tuple-element.8), channel_id=1, source_target_pairs={{0,16},{4,20},{8,24},{12,28},{16,0},{20,4},{24,8},{28,12},{1,17},{... | collective-permute-start | bytes 442376 | tf_op jit(solution)/shard_map/ppermute | solution.py:134
  68.8 6.8 %collective-permute-start.13 = (f32[1,16,2304]{2,1,0:T(8,128)S(1)}, f32[1,16,2304]{2,1,0:T(8,128)}, u32[]{:S(2)}, u32[]{:S(2)}) collective-permute-start(f32[1,16,2304]{2,1,0:T(8,128)S(1)} %get-tuple-element.6), channel_id=1, source_target_pairs={{0,8},{4,12},{8,0},{12,4},{16,24},{20,28},{24,16},{28,20},{1,9},{5... | collective-permute-start | bytes 442376 | tf_op jit(solution)/shard_map/ppermute | solution.py:134
  75.7 2.0 %collective-permute-done.16 = f32[1,16,2304]{2,1,0:T(8,128)S(1)} collective-permute-done((f32[1,16,2304]{2,1,0:T(8,128)S(1)}, f32[1,16,2304]{2,1,0:T(8,128)S(1)}, u32[]{:S(2)}, u32[]{:S(2)}) %collective-permute-start.16) | collective-permute-done | bytes 147488 | tf_op jit(solution)/shard_map/ppermute | solution.py:134
  78.4 2.1 %collective-permute-start.12 = (f32[1,16,2304]{2,1,0:T(8,128)S(1)}, f32[1,16,2304]{2,1,0:T(8,128)}, u32[]{:S(2)}, u32[]{:S(2)}) collective-permute-start(f32[1,16,2304]{2,1,0:T(8,128)S(1)} %get-tuple-element.5), channel_id=1, source_target_pairs={{0,4},{4,0},{8,12},{12,8},{16,20},{20,16},{24,28},{28,24},{1,5},{5... | collective-permute-start | bytes 442376 | tf_op jit(solution)/shard_map/ppermute | solution.py:134
  80.7 1.5 %collective-permute-done.13 = f32[1,16,2304]{2,1,0:T(8,128)} collective-permute-done((f32[1,16,2304]{2,1,0:T(8,128)S(1)}, f32[1,16,2304]{2,1,0:T(8,128)}, u32[]{:S(2)}, u32[]{:S(2)}) %collective-permute-start.13) | collective-permute-done | bytes 147488 | tf_op jit(solution)/shard_map/ppermute | solution.py:134
  82.2 1.8 %collective-permute-done.12 = f32[1,16,2304]{2,1,0:T(8,128)} collective-permute-done((f32[1,16,2304]{2,1,0:T(8,128)S(1)}, f32[1,16,2304]{2,1,0:T(8,128)}, u32[]{:S(2)}, u32[]{:S(2)}) %collective-permute-start.12) | collective-permute-done | bytes 147488 | tf_op jit(solution)/shard_map/ppermute | solution.py:134
  84.0 1.3 %fusion.15 = f32[1,16,2304]{2,1,0:T(8,128)S(1)} fusion(f32[1,16,2304]{2,1,0:T(8,128)S(1)} %collective-permute-done.18, f32[1,16,2304]{2,1,0:T(8,128)S(1)} %collective-permute-done.17, f32[1,16,2304]{2,1,0:T(8,128)} %copy-done.4, f32[1,16,2304]{2,1,0:T(8,128)} %collective-permute-done.15, f32[1,16,2304]{2,1,0:T(8,128)} %collective-permute-done.14, ...), kind=kLoop, calls=%fused_computation.38 | loop fusion | flops 294912 | bytes 2359300 | tf_op jit(solution)/shard_map/add | solution.py:134
  86.5 2.3 %fusion.1 = bf16[128,2048]{1,0:T(8,128)(2,1)} fusion(f32[128,1,2048]{2,0,1:T(8,128)} %collective-permute-done.1, f32[128,2,2048]{2,0,1:T(8,128)S(1)} %copy-done.2, s32[]{:T(128)S(6)} %select_n.49, bf16[1,16,2304]{2,1,0:T(8,128)(2,1)S(1)} %copy.21, bf16[1,128,32]{1,2,0:T(8,128)(2,1)S(1)} %add_convert_fusion), kind=kOutput, calls=%fused_computation.24 | convolution fusion | flops 9175040 | bytes 2691076 | tf_op jit(solution)/shard_map/bnr,brd->bnd/dot_general | solution.py:107
  (60 shorter events, 11.6 us)
Async XLA Ops:
  0.6 47.4 %copy-start = (bf16[128,2048]{1,0:T(8,128)(2,1)S(1)}, bf16[128,2048]{1,0:T(8,128)(2,1)}, u32[]{:S(2)}) copy-start(bf16[128,2048]{1,0:T(8,128)(2,1)} %param.6) | copy-start | bytes 1572868
  2.2 33.7 %collective-permute-start.2 = (bf16[1,16,2304]{2,1,0:T(8,128)(2,1)S(1)}, bf16[1,16,2304]{2,1,0:T(8,128)(2,1)}, u32[]{:S(2)}, u32[]{:S(2)}) collective-permute-start(bf16[1,16,2304]{2,1,0:T(8,128)(2,1)S(1)} %constant_dynamic-update-slice_fusion), channel_id=1, source_target_pairs={{0,4},{4,0},{8,12},{12,8},{16,20},{20,16},{24,28},{28,24},{1,5},{5... | collective-permute-start | bytes 221192 | tf_op jit(solution)/shard_map/ppermute | solution.py:32
  5.2 35.3 %collective-permute-start.3 = (bf16[1,16,2304]{2,1,0:T(8,128)(2,1)S(1)}, bf16[1,16,2304]{2,1,0:T(8,128)(2,1)}, u32[]{:S(2)}, u32[]{:S(2)}) collective-permute-start(bf16[1,16,2304]{2,1,0:T(8,128)(2,1)S(1)} %constant_dynamic-update-slice_fusion), channel_id=1, source_target_pairs={{0,8},{4,12},{8,0},{12,4},{16,24},{20,28},{24,16},{28,20},{1,9},{5... | collective-permute-start | bytes 221192 | tf_op jit(solution)/shard_map/ppermute | solution.py:32
  6.8 34.6 %collective-permute-start.4 = (bf16[1,16,2304]{2,1,0:T(8,128)(2,1)S(1)}, bf16[1,16,2304]{2,1,0:T(8,128)(2,1)}, u32[]{:S(2)}, u32[]{:S(2)}) collective-permute-start(bf16[1,16,2304]{2,1,0:T(8,128)(2,1)S(1)} %constant_dynamic-update-slice_fusion), channel_id=1, source_target_pairs={{0,12},{4,8},{8,4},{12,0},{16,28},{20,24},{24,20},{28,16},{1,13},{... | collective-permute-start | bytes 221192 | tf_op jit(solution)/shard_map/ppermute | solution.py:32
  6.8 35.6 %collective-permute-start.5 = (bf16[1,16,2304]{2,1,0:T(8,128)(2,1)S(1)}, bf16[1,16,2304]{2,1,0:T(8,128)(2,1)S(1)}, u32[]{:S(2)}, u32[]{:S(2)}) collective-permute-start(bf16[1,16,2304]{2,1,0:T(8,128)(2,1)S(1)} %constant_dynamic-update-slice_fusion), channel_id=1, source_target_pairs={{0,16},{4,20},{8,24},{12,28},{16,0},{20,4},{24,8},{28,12},{1,17},{... | collective-permute-start | bytes 221192 | tf_op jit(solution)/shard_map/ppermute | solution.py:32
  9.8 32.6 %collective-permute-start.6 = (bf16[1,16,2304]{2,1,0:T(8,128)(2,1)S(1)}, bf16[1,16,2304]{2,1,0:T(8,128)(2,1)S(1)}, u32[]{:S(2)}, u32[]{:S(2)}) collective-permute-start(bf16[1,16,2304]{2,1,0:T(8,128)(2,1)S(1)} %constant_dynamic-update-slice_fusion), channel_id=1, source_target_pairs={{0,20},{4,16},{8,28},{12,24},{16,4},{20,0},{24,12},{28,8},{1,21},{... | collective-permute-start | bytes 221192 | tf_op jit(solution)/shard_map/ppermute | solution.py:32
  32.6 15.3 %copy-start.3 = (bf16[128,256]{1,0:T(8,128)(2,1)S(1)}, bf16[128,256]{1,0:T(8,128)(2,1)}, u32[]{:S(2)}) copy-start(bf16[128,256]{1,0:T(8,128)(2,1)} %param.7) | copy-start | bytes 196612
  35.9 6.5 %collective-permute-start.7 = (bf16[1,16,2304]{2,1,0:T(8,128)(2,1)S(1)}, bf16[1,16,2304]{2,1,0:T(8,128)(2,1)S(1)}, u32[]{:S(2)}, u32[]{:S(2)}) collective-permute-start(bf16[1,16,2304]{2,1,0:T(8,128)(2,1)S(1)} %constant_dynamic-update-slice_fusion), channel_id=1, source_target_pairs={{0,24},{4,28},{8,16},{12,20},{16,8},{20,12},{24,0},{28,4},{1,25},{... | collective-permute-start | bytes 221192 | tf_op jit(solution)/shard_map/ppermute | solution.py:32
  40.5 7.1 %collective-permute-start.8 = (bf16[1,16,2304]{2,1,0:T(8,128)(2,1)S(1)}, bf16[1,16,2304]{2,1,0:T(8,128)(2,1)S(1)}, u32[]{:S(2)}, u32[]{:S(2)}) collective-permute-start(bf16[1,16,2304]{2,1,0:T(8,128)(2,1)S(1)} %constant_dynamic-update-slice_fusion), channel_id=1, source_target_pairs={{0,28},{4,24},{8,20},{12,16},{16,12},{20,8},{24,4},{28,0},{1,29},{... | collective-permute-start | bytes 221192 | tf_op jit(solution)/shard_map/ppermute | solution.py:32
  41.4 12.5 %collective-permute-start = (f32[128,2,2048]{2,0,1:T(8,128)}, f32[128,2,2048]{2,0,1:T(8,128)}, u32[]{:S(2)}, u32[]{:S(2)}) collective-permute-start(f32[128,2,2048]{2,0,1:T(8,128)} %bitcast.123), channel_id=1, source_target_pairs={{0,1},{1,0},{2,3},{3,2},{4,5},{5,4},{6,7},{7,6},{8,9},{9,8},{10,11... | collective-permute-start | bytes 6291464 | tf_op jit(solution)/shard_map/ppermute | solution.py:60
  48.3 3.3 %collective-permute-start.11 = (f32[1,128,32]{1,2,0:T(8,128)S(1)}, f32[1,128,32]{1,2,0:T(8,128)S(1)}, u32[]{:S(2)}, u32[]{:S(2)}) collective-permute-start(f32[1,128,32]{1,2,0:T(8,128)S(1)} %pad_maximum_fusion), channel_id=1, source_target_pairs={{0,3},{1,2},{2,1},{3,0},{4,7},{5,6},{6,5},{7,4},{8,11},{9,10},{10,... | collective-permute-start | bytes 49160 | tf_op jit(solution)/shard_map/ppermute | solution.py:42
  48.3 3.8 %collective-permute-start.10 = (f32[1,128,32]{1,2,0:T(8,128)S(1)}, f32[1,128,32]{1,2,0:T(8,128)S(1)}, u32[]{:S(2)}, u32[]{:S(2)}) collective-permute-start(f32[1,128,32]{1,2,0:T(8,128)S(1)} %pad_maximum_fusion), channel_id=1, source_target_pairs={{0,2},{1,3},{2,0},{3,1},{4,6},{5,7},{6,4},{7,5},{8,10},{9,11},{10,... | collective-permute-start | bytes 49160 | tf_op jit(solution)/shard_map/ppermute | solution.py:42
  49.9 2.3 %collective-permute-start.9 = (f32[1,128,32]{1,2,0:T(8,128)S(1)}, f32[1,128,32]{1,2,0:T(8,128)S(1)}, u32[]{:S(2)}, u32[]{:S(2)}) collective-permute-start(f32[1,128,32]{1,2,0:T(8,128)S(1)} %pad_maximum_fusion), channel_id=1, source_target_pairs={{0,1},{1,0},{2,3},{3,2},{4,5},{5,4},{6,7},{7,6},{8,9},{9,8},{10,11... | collective-permute-start | bytes 49160 | tf_op jit(solution)/shard_map/ppermute | solution.py:42
  52.7 14.9 %collective-permute-start.18 = (f32[1,16,2304]{2,1,0:T(8,128)S(1)}, f32[1,16,2304]{2,1,0:T(8,128)S(1)}, u32[]{:S(2)}, u32[]{:S(2)}) collective-permute-start(f32[1,16,2304]{2,1,0:T(8,128)S(1)} %fusion.6), channel_id=1, source_target_pairs={{0,28},{4,24},{8,20},{12,16},{16,12},{20,8},{24,4},{28,0},{1,29},{... | collective-permute-start | bytes 442376 | tf_op jit(solution)/shard_map/ppermute | solution.py:134
  57.4 1.3 %copy-start.1 = (f32[128,2,2048]{2,0,1:T(8,128)}, f32[128,2,2048]{2,0,1:T(8,128)S(1)}, u32[]{:S(2)}) copy-start(f32[128,2,2048]{2,0,1:T(8,128)S(1)} %bitcast_add_fusion) | copy-start | bytes 6291460
  58.8 27.7 %collective-permute-start.1 = (f32[128,1,2048]{2,0,1:T(8,128)S(1)}, f32[128,1,2048]{2,0,1:T(8,128)}, u32[]{:S(2)}, u32[]{:S(2)}) collective-permute-start(f32[128,1,2048]{2,0,1:T(8,128)S(1)} %constant_dynamic-slice_fusion), channel_id=1, source_target_pairs={{0,2},{1,3},{2,0},{3,1},{4,6},{5,7},{6,4},{7,5},{8,10},{9,11},{10,... | collective-permute-start | bytes 3145736 | tf_op jit(solution)/shard_map/ppermute | solution.py:60
  60.2 8.6 %collective-permute-start.17 = (f32[1,16,2304]{2,1,0:T(8,128)S(1)}, f32[1,16,2304]{2,1,0:T(8,128)S(1)}, u32[]{:S(2)}, u32[]{:S(2)}) collective-permute-start(f32[1,16,2304]{2,1,0:T(8,128)S(1)} %get-tuple-element.10), channel_id=1, source_target_pairs={{0,24},{4,28},{8,16},{12,20},{16,8},{20,12},{24,0},{28,4},{1,25},{... | collective-permute-start | bytes 442376 | tf_op jit(solution)/shard_map/ppermute | solution.py:134
  63.8 13.9 %collective-permute-start.16 = (f32[1,16,2304]{2,1,0:T(8,128)S(1)}, f32[1,16,2304]{2,1,0:T(8,128)S(1)}, u32[]{:S(2)}, u32[]{:S(2)}) collective-permute-start(f32[1,16,2304]{2,1,0:T(8,128)S(1)} %get-tuple-element.9), channel_id=1, source_target_pairs={{0,20},{4,16},{8,28},{12,24},{16,4},{20,0},{24,12},{28,8},{1,21},{... | collective-permute-start | bytes 442376 | tf_op jit(solution)/shard_map/ppermute | solution.py:134
  63.8 16.9 %collective-permute-start.15 = (f32[1,16,2304]{2,1,0:T(8,128)}, f32[1,16,2304]{2,1,0:T(8,128)}, u32[]{:S(2)}, u32[]{:S(2)}) collective-permute-start(f32[1,16,2304]{2,1,0:T(8,128)} %get-tuple-element.8), channel_id=1, source_target_pairs={{0,16},{4,20},{8,24},{12,28},{16,0},{20,4},{24,8},{28,12},{1,17},{... | collective-permute-start | bytes 442376 | tf_op jit(solution)/shard_map/ppermute | solution.py:134
  67.7 13.1 %collective-permute-start.14 = (f32[1,16,2304]{2,1,0:T(8,128)}, f32[1,16,2304]{2,1,0:T(8,128)}, u32[]{:S(2)}, u32[]{:S(2)}) collective-permute-start(f32[1,16,2304]{2,1,0:T(8,128)} %get-tuple-element.7), channel_id=1, source_target_pairs={{0,12},{4,8},{8,4},{12,0},{16,28},{20,24},{24,20},{28,16},{1,13},{... | collective-permute-start | bytes 442376 | tf_op jit(solution)/shard_map/ppermute | solution.py:134
  68.8 13.4 %collective-permute-start.13 = (f32[1,16,2304]{2,1,0:T(8,128)S(1)}, f32[1,16,2304]{2,1,0:T(8,128)}, u32[]{:S(2)}, u32[]{:S(2)}) collective-permute-start(f32[1,16,2304]{2,1,0:T(8,128)S(1)} %get-tuple-element.6), channel_id=1, source_target_pairs={{0,8},{4,12},{8,0},{12,4},{16,24},{20,28},{24,16},{28,20},{1,9},{5... | collective-permute-start | bytes 442376 | tf_op jit(solution)/shard_map/ppermute | solution.py:134
  77.7 0.7 copy-start.4
  78.4 5.6 %collective-permute-start.12 = (f32[1,16,2304]{2,1,0:T(8,128)S(1)}, f32[1,16,2304]{2,1,0:T(8,128)}, u32[]{:S(2)}, u32[]{:S(2)}) collective-permute-start(f32[1,16,2304]{2,1,0:T(8,128)S(1)} %get-tuple-element.5), channel_id=1, source_target_pairs={{0,4},{4,0},{8,12},{12,8},{16,20},{20,16},{24,28},{28,24},{1,5},{5... | collective-permute-start | bytes 442376 | tf_op jit(solution)/shard_map/ppermute | solution.py:134
  80.5 6.0 %copy-start.2 = (f32[128,2,2048]{2,0,1:T(8,128)S(1)}, f32[128,2,2048]{2,0,1:T(8,128)}, u32[]{:S(2)}) copy-start(f32[128,2,2048]{2,0,1:T(8,128)} %copy-done.1) | copy-start | bytes 6291460

commit v2 on v1

--- a/solution.py
+++ b/solution.py
@@ -43,24 +43,30 @@
     return total
 
 
-def _reduce_scatter_cols(partial, axis, size):
-    rows, cols = partial.shape
+def _frozen_term(cotangent, weight, axis, size):
     if size & (size - 1) != 0:
+        partial = lax.dot_general(
+            cotangent, weight, (((1,), (1,)), ((), ())), preferred_element_type=jnp.float32
+        )
         return lax.psum_scatter(partial, axis, scatter_dimension=1, tiled=True)
     me = lax.axis_index(axis)
-    held = partial.reshape(rows, size, cols // size)
-    bit = 0
-    while (1 << bit) < size:
-        width = held.shape[1] // 2
-        split = held.reshape(rows, width, 2, cols // size)
-        mine = (me >> bit) & 1
-        keep = lax.dynamic_index_in_dim(split, mine, 2, keepdims=False)
-        give = lax.dynamic_index_in_dim(split, 1 - mine, 2, keepdims=False)
-        partner = 1 << bit
-        got = lax.ppermute(give, axis, [(i, i ^ partner) for i in range(size)])
-        held = keep + got
-        bit += 1
-    return held.reshape(rows, cols // size)
+    rows = weight.shape[0] // size
+
+    def term(block):
+        piece = lax.dynamic_slice_in_dim(weight, block * rows, rows, axis=0)
+        return lax.dot_general(
+            cotangent, piece, (((1,), (1,)), ((), ())), preferred_element_type=jnp.float32
+        )
+
+    held = [term(me ^ e) for e in range(size)]
+    step = 0
+    while len(held) > 1:
+        partner = 1 << step
+        pairs = [(i, i ^ partner) for i in range(size)]
+        got = [lax.ppermute(held[e], axis, pairs) for e in range(1, len(held), 2)]
+        held = [held[e] + g for e, g in zip(range(0, len(held), 2), got)]
+        step += 1
+    return held[0]
 
 
 def on_device(
@@ -77,10 +83,7 @@
     tenant_number = dp_size * held_tenants
     me_dp = lax.axis_index("dp")
 
-    partial_grad = lax.dot_general(
-        cotangent, frozen_key_weight, (((1,), (1,)), ((), ())), preferred_element_type=jnp.float32
-    )
-    base_grad = _reduce_scatter_cols(partial_grad, "tensor", tensor_size)
+    base_grad = _frozen_term(cotangent, frozen_key_weight, "tensor", tensor_size)
 
     packed = jnp.concatenate([adapter_down_weight, adapter_up_weight], axis=2)
     stacked, order = _gather_dp(packed, "dp", dp_size)

time: 89.4 us -> 76.5 us (0.86)
  the two profiles are of different devices: /device:TPU:0 before, /device:TPU:20 now
where the time goes in v2:
time: 76.5 us; the launch traced here: 76.2 us
  waiting for transfers between devices  31.1 us (41%)
  starting transfers between devices  25.7 us (34%)
  matrix products  11.7 us (15%)
  local copies, waits for them, and re-layouts  4.24 us (6%)
  other arithmetic  2.01 us (3%)
  between operations  1.44 us (2%)
    ppermute x7, waiting for transfers between devices, on_device(): owned = owned + lax.ppermute(outgoing, 'dp', pairs)  15.7 us
    ppermute x7, starting transfers between devices, on_device(): owned = owned + lax.ppermute(outgoing, 'dp', pairs)  12.3 us
    dot_general x4, matrix products, term(): lax.dot_general(cotangent, piece, (((1,), (1,)), ((), ())), preferred_ele...  10.2 us
    ppermute x7, starting transfers between devices, _gather_dp(): got.append(lax.ppermute(local, axis, pairs))  9.46 us
    ppermute x3, waiting for transfers between devices, _frozen_term(): got = [lax.ppermute(held[e], axis, pairs) for e in range(1, len(held), 2)]  8.7 us
    ppermute x7, waiting for transfers between devices, _gather_dp(): got.append(lax.ppermute(local, axis, pairs))  4.91 us
    ppermute x3, starting transfers between devices, _frozen_term(): got = [lax.ppermute(held[e], axis, pairs) for e in range(1, len(held), 2)]  2.08 us
    unnamed x13, local copies, waits for them, and re-layouts  1.97 us
  transfers between devices with their start and end apart: 20, of which 10 were waited for; matrix products, arithmetic and copies ran while one was open for 17% of the time, Pallas kernels for 0%

profile of v2, /device:TPU:20, one launch (start us, length us, event | category | flops | bytes accessed | tf_op | source)
XLA Modules:
  0.0 76.2 jit_solution(9577360086984683743)
XLA Ops:
  0.6 0.9 %constant_dynamic-update-slice_fusion.1 = bf16[1,16,2304]{2,1,0:T(8,128)(2,1)S(1)} fusion(bf16[1,16,2048]{2,1,0:T(8,128)(2,1)} %param.9), kind=kLoop, calls=%fused_computation.75 | loop fusion | bytes 131072
  2.8 1.6 %collective-permute-start.4 = (bf16[1,16,2304]{2,1,0:T(8,128)(2,1)S(1)}, bf16[1,16,2304]{2,1,0:T(8,128)(2,1)S(1)}, u32[]{:S(2)}, u32[]{:S(2)}) collective-permute-start(bf16[1,16,2304]{2,1,0:T(8,128)(2,1)S(1)} %constant_dynamic-update-slice_fusion), channel_id=1, source_target_pairs={{0,8},{4,12},{8,0},{12,4},{16,24},{20,28},{24,16},{28,20},{1,9},{5... | collective-permute-start | bytes 221192 | tf_op jit(solution)/shard_map/ppermute | solution.py:32
  4.4 1.4 %collective-permute-start.5 = (bf16[1,16,2304]{2,1,0:T(8,128)(2,1)S(1)}, bf16[1,16,2304]{2,1,0:T(8,128)(2,1)S(1)}, u32[]{:S(2)}, u32[]{:S(2)}) collective-permute-start(bf16[1,16,2304]{2,1,0:T(8,128)(2,1)S(1)} %constant_dynamic-update-slice_fusion), channel_id=1, source_target_pairs={{0,12},{4,8},{8,4},{12,0},{16,28},{20,24},{24,20},{28,16},{1,13},{... | collective-permute-start | bytes 221192 | tf_op jit(solution)/shard_map/ppermute | solution.py:32
  6.1 2.5 %collective-permute-start.7 = (bf16[1,16,2304]{2,1,0:T(8,128)(2,1)S(1)}, bf16[1,16,2304]{2,1,0:T(8,128)(2,1)S(1)}, u32[]{:S(2)}, u32[]{:S(2)}) collective-permute-start(bf16[1,16,2304]{2,1,0:T(8,128)(2,1)S(1)} %constant_dynamic-update-slice_fusion), channel_id=1, source_target_pairs={{0,20},{4,16},{8,28},{12,24},{16,4},{20,0},{24,12},{28,8},{1,21},{... | collective-permute-start | bytes 221192 | tf_op jit(solution)/shard_map/ppermute | solution.py:32
  8.6 2.6 %convolution_bitcast_fusion.1 = f32[128,2048]{0,1:T(8,128)} fusion(bf16[128,256]{1,0:T(8,128)(2,1)} %param.7, bf16[8192,256]{1,0:T(8,128)(2,1)} %param.8, s32[]{:T(128)S(6)} %select_n.48), kind=kOutput, calls=%fused_computation.9 | convolution fusion | flops 134217728 | bytes 2162692 | tf_op jit(solution)/shard_map/dot_general | solution.py:57
  11.3 2.6 %convolution_bitcast_fusion.3 = f32[128,2048]{0,1:T(8,128)} fusion(bf16[128,256]{1,0:T(8,128)(2,1)S(1)} %copy-done.1, bf16[8192,256]{1,0:T(8,128)(2,1)} %param.8, s32[]{:T(128)S(6)} %select_n.46), kind=kOutput, calls=%fused_computation.11 | convolution fusion | flops 134217728 | bytes 2162692 | tf_op jit(solution)/shard_map/dot_general | solution.py:57
  15.2 2.6 %collective-permute-start.9 = (bf16[1,16,2304]{2,1,0:T(8,128)(2,1)S(1)}, bf16[1,16,2304]{2,1,0:T(8,128)(2,1)S(1)}, u32[]{:S(2)}, u32[]{:S(2)}) collective-permute-start(bf16[1,16,2304]{2,1,0:T(8,128)(2,1)S(1)} %constant_dynamic-update-slice_fusion), channel_id=1, source_target_pairs={{0,28},{4,24},{8,20},{12,16},{16,12},{20,8},{24,4},{28,0},{1,29},{... | collective-permute-start | bytes 221192 | tf_op jit(solution)/shard_map/ppermute | solution.py:32
  18.5 1.7 %collective-permute-done.8 = bf16[1,16,2304]{2,1,0:T(8,128)(2,1)S(1)} collective-permute-done((bf16[1,16,2304]{2,1,0:T(8,128)(2,1)S(1)}, bf16[1,16,2304]{2,1,0:T(8,128)(2,1)S(1)}, u32[]{:S(2)}, u32[]{:S(2)}) %collective-permute-start.8) | collective-permute-done | bytes 73760 | tf_op jit(solution)/shard_map/ppermute | solution.py:32
  20.1 3.2 %collective-permute-done.9 = bf16[1,16,2304]{2,1,0:T(8,128)(2,1)S(1)} collective-permute-done((bf16[1,16,2304]{2,1,0:T(8,128)(2,1)S(1)}, bf16[1,16,2304]{2,1,0:T(8,128)(2,1)S(1)}, u32[]{:S(2)}, u32[]{:S(2)}) %collective-permute-start.9) | collective-permute-done | bytes 73760 | tf_op jit(solution)/shard_map/ppermute | solution.py:32
  24.1 1.6 %collective-permute-start.11 = (f32[1,128,32]{1,2,0:T(8,128)S(1)}, f32[1,128,32]{1,2,0:T(8,128)S(1)}, u32[]{:S(2)}, u32[]{:S(2)}) collective-permute-start(f32[1,128,32]{1,2,0:T(8,128)S(1)} %pad_maximum_fusion), channel_id=1, source_target_pairs={{0,2},{1,3},{2,0},{3,1},{4,6},{5,7},{6,4},{7,5},{8,10},{9,11},{10,... | collective-permute-start | bytes 49160 | tf_op jit(solution)/shard_map/ppermute | solution.py:42
  26.2 1.3 %collective-permute-done.12 = f32[1,128,32]{1,2,0:T(8,128)S(1)} collective-permute-done((f32[1,128,32]{1,2,0:T(8,128)S(1)}, f32[1,128,32]{1,2,0:T(8,128)S(1)}, u32[]{:S(2)}, u32[]{:S(2)}) %collective-permute-start.12) | collective-permute-done | bytes 16416 | tf_op jit(solution)/shard_map/ppermute | solution.py:42
  29.8 1.6 %collective-permute-start.18 = (f32[1,16,2304]{2,1,0:T(8,128)}, f32[1,16,2304]{2,1,0:T(8,128)S(1)}, u32[]{:S(2)}, u32[]{:S(2)}) collective-permute-start(f32[1,16,2304]{2,1,0:T(8,128)} %get-tuple-element.11), channel_id=1, source_target_pairs={{0,24},{4,28},{8,16},{12,20},{16,8},{20,12},{24,0},{28,4},{1,25},{... | collective-permute-start | bytes 442376 | tf_op jit(solution)/shard_map/ppermute | solution.py:137
  31.5 5.1 %collective-permute-start.17 = (f32[1,16,2304]{2,1,0:T(8,128)}, f32[1,16,2304]{2,1,0:T(8,128)}, u32[]{:S(2)}, u32[]{:S(2)}) collective-permute-start(f32[1,16,2304]{2,1,0:T(8,128)} %get-tuple-element.10), channel_id=1, source_target_pairs={{0,20},{4,16},{8,28},{12,24},{16,4},{20,0},{24,12},{28,8},{1,21},{... | collective-permute-start | bytes 442376 | tf_op jit(solution)/shard_map/ppermute | solution.py:137
  36.6 2.9 %fusion.3 = f32[128,2048]{0,1:T(8,128)} fusion(f32[128,2048]{0,1:T(8,128)} %collective-permute-done.1, bf16[128,256]{1,0:T(8,128)(2,1)S(1)} %copy-done.1, bf16[8192,256]{1,0:T(8,128)(2,1)} %param.8, s32[]{:T(128)S(6)} %select_n.47), kind=kOutput, calls=%fused_computation.16 | convolution fusion | flops 134479872 | bytes 3211268 | tf_op jit(solution)/shard_map/dot_general | solution.py:57
  39.5 9.3 %collective-permute-done.19 = f32[1,16,2304]{2,1,0:T(8,128)S(1)} collective-permute-done((f32[1,16,2304]{2,1,0:T(8,128)S(1)}, f32[1,16,2304]{2,1,0:T(8,128)S(1)}, u32[]{:S(2)}, u32[]{:S(2)}) %collective-permute-start.19) | collective-permute-done | bytes 147488 | tf_op jit(solution)/shard_map/ppermute | solution.py:137
  48.8 1.5 %collective-permute-start.2 = (f32[128,2048]{0,1:T(8,128)}, f32[128,2048]{0,1:T(8,128)}, u32[]{:S(2)}, u32[]{:S(2)}) collective-permute-start(f32[128,2048]{0,1:T(8,128)} %fusion.3), channel_id=1, source_target_pairs={{0,2},{1,3},{2,0},{3,1},{4,6},{5,7},{6,4},{7,5},{8,10},{9,11},{10,... | collective-permute-start | bytes 3145736 | tf_op jit(solution)/shard_map/ppermute | solution.py:66
  51.1 1.2 %collective-permute-done.17 = f32[1,16,2304]{2,1,0:T(8,128)} collective-permute-done((f32[1,16,2304]{2,1,0:T(8,128)}, f32[1,16,2304]{2,1,0:T(8,128)}, u32[]{:S(2)}, u32[]{:S(2)}) %collective-permute-start.17) | collective-permute-done | bytes 147488 | tf_op jit(solution)/shard_map/ppermute | solution.py:137
  52.3 4.5 %collective-permute-start.14 = (f32[1,16,2304]{2,1,0:T(8,128)S(1)}, f32[1,16,2304]{2,1,0:T(8,128)S(1)}, u32[]{:S(2)}, u32[]{:S(2)}) collective-permute-start(f32[1,16,2304]{2,1,0:T(8,128)S(1)} %get-tuple-element.7), channel_id=1, source_target_pairs={{0,8},{4,12},{8,0},{12,4},{16,24},{20,28},{24,16},{28,20},{1,9},{5... | collective-permute-start | bytes 442376 | tf_op jit(solution)/shard_map/ppermute | solution.py:137
  57.7 1.5 %collective-permute-done.15 = f32[1,16,2304]{2,1,0:T(8,128)S(1)} collective-permute-done((f32[1,16,2304]{2,1,0:T(8,128)}, f32[1,16,2304]{2,1,0:T(8,128)S(1)}, u32[]{:S(2)}, u32[]{:S(2)}) %collective-permute-start.15) | collective-permute-done | bytes 147488 | tf_op jit(solution)/shard_map/ppermute | solution.py:137
  59.2 3.0 %collective-permute-done.14 = f32[1,16,2304]{2,1,0:T(8,128)S(1)} collective-permute-done((f32[1,16,2304]{2,1,0:T(8,128)S(1)}, f32[1,16,2304]{2,1,0:T(8,128)S(1)}, u32[]{:S(2)}, u32[]{:S(2)}) %collective-permute-start.14) | collective-permute-done | bytes 147488 | tf_op jit(solution)/shard_map/ppermute | solution.py:137
  62.2 1.1 %fusion.23 = f32[1,16,2304]{2,1,0:T(8,128)S(1)} fusion(f32[1,16,2304]{2,1,0:T(8,128)S(1)} %collective-permute-done.19, f32[1,16,2304]{2,1,0:T(8,128)S(1)} %collective-permute-done.18, f32[1,16,2304]{2,1,0:T(8,128)} %collective-permute-done.17, f32[1,16,2304]{2,1,0:T(8,128)} %collective-permute-done.16, f32[1,16,2304]{2,1,0:T(8,128)S(1)} %collective-permute-done.15, ...), kind=kLoop, calls=%fused_computation.47 | loop fusion | flops 294912 | bytes 2359300 | tf_op jit(solution)/shard_map/add | solution.py:137
  64.5 8.7 %collective-permute-done.2 = f32[128,2048]{0,1:T(8,128)} collective-permute-done((f32[128,2048]{0,1:T(8,128)}, f32[128,2048]{0,1:T(8,128)}, u32[]{:S(2)}, u32[]{:S(2)}) %collective-permute-start.2) | collective-permute-done | bytes 1048608 | tf_op jit(solution)/shard_map/ppermute | solution.py:66
  73.2 2.0 %fusion.4 = bf16[128,2048]{0,1:T(8,128)(2,1)S(1)} fusion(f32[128,2048]{0,1:T(8,128)S(1)} %fusion.37, f32[128,2048]{0,1:T(8,128)} %collective-permute-done.2, f32[128,2048]{0,1:T(8,128)S(1)} %collective-permute-done, bf16[128,256]{1,0:T(8,128)(2,1)S(1)} %copy-done.1, bf16[8192,256]{1,0:T(8,128)(2,1)} %param.8, s32[]{:T(128)S(6)} %select_n.45), kind=kOutput, calls=%fused_computation.17 | convolution fusion | flops 135266304 | bytes 4784132 | tf_op jit(solution)/shard_map/dot_general | solution.py:57
  75.2 1.0 %copy.10 = bf16[128,2048]{1,0:T(8,128)(2,1)} copy(bf16[128,2048]{0,1:T(8,128)(2,1)S(1)} %fusion.4) | data formatting | bytes 1048576
  (55 shorter events, 9.5 us)
Async XLA Ops:
  0.6 23.2 %copy-start = (bf16[128,2048]{1,0:T(8,128)(2,1)S(1)}, bf16[128,2048]{1,0:T(8,128)(2,1)}, u32[]{:S(2)}) copy-start(bf16[128,2048]{1,0:T(8,128)(2,1)} %param.6) | copy-start | bytes 1572868
  1.5 9.7 %copy-start.1 = (bf16[128,256]{1,0:T(8,128)(2,1)S(1)}, bf16[128,256]{1,0:T(8,128)(2,1)}, u32[]{:S(2)}) copy-start(bf16[128,256]{1,0:T(8,128)(2,1)} %param.7) | copy-start | bytes 196612
  2.3 12.4 %collective-permute-start.3 = (bf16[1,16,2304]{2,1,0:T(8,128)(2,1)S(1)}, bf16[1,16,2304]{2,1,0:T(8,128)(2,1)S(1)}, u32[]{:S(2)}, u32[]{:S(2)}) collective-permute-start(bf16[1,16,2304]{2,1,0:T(8,128)(2,1)S(1)} %constant_dynamic-update-slice_fusion), channel_id=1, source_target_pairs={{0,4},{4,0},{8,12},{12,8},{16,20},{20,16},{24,28},{28,24},{1,5},{5... | collective-permute-start | bytes 221192 | tf_op jit(solution)/shard_map/ppermute | solution.py:32
  2.8 12.4 %collective-permute-start.4 = (bf16[1,16,2304]{2,1,0:T(8,128)(2,1)S(1)}, bf16[1,16,2304]{2,1,0:T(8,128)(2,1)S(1)}, u32[]{:S(2)}, u32[]{:S(2)}) collective-permute-start(bf16[1,16,2304]{2,1,0:T(8,128)(2,1)S(1)} %constant_dynamic-update-slice_fusion), channel_id=1, source_target_pairs={{0,8},{4,12},{8,0},{12,4},{16,24},{20,28},{24,16},{28,20},{1,9},{5... | collective-permute-start | bytes 221192 | tf_op jit(solution)/shard_map/ppermute | solution.py:32
  4.4 13.4 %collective-permute-start.5 = (bf16[1,16,2304]{2,1,0:T(8,128)(2,1)S(1)}, bf16[1,16,2304]{2,1,0:T(8,128)(2,1)S(1)}, u32[]{:S(2)}, u32[]{:S(2)}) collective-permute-start(bf16[1,16,2304]{2,1,0:T(8,128)(2,1)S(1)} %constant_dynamic-update-slice_fusion), channel_id=1, source_target_pairs={{0,12},{4,8},{8,4},{12,0},{16,28},{20,24},{24,20},{28,16},{1,13},{... | collective-permute-start | bytes 221192 | tf_op jit(solution)/shard_map/ppermute | solution.py:32
  5.8 12.1 %collective-permute-start.6 = (bf16[1,16,2304]{2,1,0:T(8,128)(2,1)S(1)}, bf16[1,16,2304]{2,1,0:T(8,128)(2,1)S(1)}, u32[]{:S(2)}, u32[]{:S(2)}) collective-permute-start(bf16[1,16,2304]{2,1,0:T(8,128)(2,1)S(1)} %constant_dynamic-update-slice_fusion), channel_id=1, source_target_pairs={{0,16},{4,20},{8,24},{12,28},{16,0},{20,4},{24,8},{28,12},{1,17},{... | collective-permute-start | bytes 221192 | tf_op jit(solution)/shard_map/ppermute | solution.py:32
  6.1 12.3 %collective-permute-start.7 = (bf16[1,16,2304]{2,1,0:T(8,128)(2,1)S(1)}, bf16[1,16,2304]{2,1,0:T(8,128)(2,1)S(1)}, u32[]{:S(2)}, u32[]{:S(2)}) collective-permute-start(bf16[1,16,2304]{2,1,0:T(8,128)(2,1)S(1)} %constant_dynamic-update-slice_fusion), channel_id=1, source_target_pairs={{0,20},{4,16},{8,28},{12,24},{16,4},{20,0},{24,12},{28,8},{1,21},{... | collective-permute-start | bytes 221192 | tf_op jit(solution)/shard_map/ppermute | solution.py:32
  14.7 5.5 %collective-permute-start.8 = (bf16[1,16,2304]{2,1,0:T(8,128)(2,1)S(1)}, bf16[1,16,2304]{2,1,0:T(8,128)(2,1)S(1)}, u32[]{:S(2)}, u32[]{:S(2)}) collective-permute-start(bf16[1,16,2304]{2,1,0:T(8,128)(2,1)S(1)} %constant_dynamic-update-slice_fusion), channel_id=1, source_target_pairs={{0,24},{4,28},{8,16},{12,20},{16,8},{20,12},{24,0},{28,4},{1,25},{... | collective-permute-start | bytes 221192 | tf_op jit(solution)/shard_map/ppermute | solution.py:32
  15.2 8.2 %collective-permute-start.9 = (bf16[1,16,2304]{2,1,0:T(8,128)(2,1)S(1)}, bf16[1,16,2304]{2,1,0:T(8,128)(2,1)S(1)}, u32[]{:S(2)}, u32[]{:S(2)}) collective-permute-start(bf16[1,16,2304]{2,1,0:T(8,128)(2,1)S(1)} %constant_dynamic-update-slice_fusion), channel_id=1, source_target_pairs={{0,28},{4,24},{8,20},{12,16},{16,12},{20,8},{24,4},{28,0},{1,29},{... | collective-permute-start | bytes 221192 | tf_op jit(solution)/shard_map/ppermute | solution.py:32
  17.8 18.8 %collective-permute-start.1 = (f32[128,2048]{0,1:T(8,128)}, f32[128,2048]{0,1:T(8,128)}, u32[]{:S(2)}, u32[]{:S(2)}) collective-permute-start(f32[128,2048]{0,1:T(8,128)} %convolution_bitcast_fusion.1), channel_id=1, source_target_pairs={{0,1},{1,0},{2,3},{3,2},{4,5},{5,4},{6,7},{7,6},{8,9},{9,8},{10,11... | collective-permute-start | bytes 3145736 | tf_op jit(solution)/shard_map/ppermute | solution.py:66
  17.9 46.6 %collective-permute-start = (f32[128,2048]{0,1:T(8,128)}, f32[128,2048]{0,1:T(8,128)S(1)}, u32[]{:S(2)}, u32[]{:S(2)}) collective-permute-start(f32[128,2048]{0,1:T(8,128)} %convolution_bitcast_fusion.3), channel_id=1, source_target_pairs={{0,1},{1,0},{2,3},{3,2},{4,5},{5,4},{6,7},{7,6},{8,9},{9,8},{10,11... | collective-permute-start | bytes 3145736 | tf_op jit(solution)/shard_map/ppermute | solution.py:66
  24.1 3.3 %collective-permute-start.12 = (f32[1,128,32]{1,2,0:T(8,128)S(1)}, f32[1,128,32]{1,2,0:T(8,128)S(1)}, u32[]{:S(2)}, u32[]{:S(2)}) collective-permute-start(f32[1,128,32]{1,2,0:T(8,128)S(1)} %pad_maximum_fusion), channel_id=1, source_target_pairs={{0,3},{1,2},{2,1},{3,0},{4,7},{5,6},{6,5},{7,4},{8,11},{9,10},{10,... | collective-permute-start | bytes 49160 | tf_op jit(solution)/shard_map/ppermute | solution.py:42
  24.1 3.8 %collective-permute-start.11 = (f32[1,128,32]{1,2,0:T(8,128)S(1)}, f32[1,128,32]{1,2,0:T(8,128)S(1)}, u32[]{:S(2)}, u32[]{:S(2)}) collective-permute-start(f32[1,128,32]{1,2,0:T(8,128)S(1)} %pad_maximum_fusion), channel_id=1, source_target_pairs={{0,2},{1,3},{2,0},{3,1},{4,6},{5,7},{6,4},{7,5},{8,10},{9,11},{10,... | collective-permute-start | bytes 49160 | tf_op jit(solution)/shard_map/ppermute | solution.py:42
  25.7 2.3 %collective-permute-start.10 = (f32[1,128,32]{1,2,0:T(8,128)S(1)}, f32[1,128,32]{1,2,0:T(8,128)S(1)}, u32[]{:S(2)}, u32[]{:S(2)}) collective-permute-start(f32[1,128,32]{1,2,0:T(8,128)S(1)} %pad_maximum_fusion), channel_id=1, source_target_pairs={{0,1},{1,0},{2,3},{3,2},{4,5},{5,4},{6,7},{7,6},{8,9},{9,8},{10,11... | collective-permute-start | bytes 49160 | tf_op jit(solution)/shard_map/ppermute | solution.py:42
  28.5 20.3 %collective-permute-start.19 = (f32[1,16,2304]{2,1,0:T(8,128)S(1)}, f32[1,16,2304]{2,1,0:T(8,128)S(1)}, u32[]{:S(2)}, u32[]{:S(2)}) collective-permute-start(f32[1,16,2304]{2,1,0:T(8,128)S(1)} %fusion.14), channel_id=1, source_target_pairs={{0,28},{4,24},{8,20},{12,16},{16,12},{20,8},{24,4},{28,0},{1,29},{... | collective-permute-start | bytes 442376 | tf_op jit(solution)/shard_map/ppermute | solution.py:137
  29.8 21.2 %collective-permute-start.18 = (f32[1,16,2304]{2,1,0:T(8,128)}, f32[1,16,2304]{2,1,0:T(8,128)S(1)}, u32[]{:S(2)}, u32[]{:S(2)}) collective-permute-start(f32[1,16,2304]{2,1,0:T(8,128)} %get-tuple-element.11), channel_id=1, source_target_pairs={{0,24},{4,28},{8,16},{12,20},{16,8},{20,12},{24,0},{28,4},{1,25},{... | collective-permute-start | bytes 442376 | tf_op jit(solution)/shard_map/ppermute | solution.py:137
  31.5 20.8 %collective-permute-start.17 = (f32[1,16,2304]{2,1,0:T(8,128)}, f32[1,16,2304]{2,1,0:T(8,128)}, u32[]{:S(2)}, u32[]{:S(2)}) collective-permute-start(f32[1,16,2304]{2,1,0:T(8,128)} %get-tuple-element.10), channel_id=1, source_target_pairs={{0,20},{4,16},{8,28},{12,24},{16,4},{20,0},{24,12},{28,8},{1,21},{... | collective-permute-start | bytes 442376 | tf_op jit(solution)/shard_map/ppermute | solution.py:137
  36.6 20.2 %collective-permute-start.16 = (f32[1,16,2304]{2,1,0:T(8,128)}, f32[1,16,2304]{2,1,0:T(8,128)}, u32[]{:S(2)}, u32[]{:S(2)}) collective-permute-start(f32[1,16,2304]{2,1,0:T(8,128)} %get-tuple-element.9), channel_id=1, source_target_pairs={{0,16},{4,20},{8,24},{12,28},{16,0},{20,4},{24,8},{28,12},{1,17},{... | collective-permute-start | bytes 442376 | tf_op jit(solution)/shard_map/ppermute | solution.py:137
  48.8 24.4 %collective-permute-start.2 = (f32[128,2048]{0,1:T(8,128)}, f32[128,2048]{0,1:T(8,128)}, u32[]{:S(2)}, u32[]{:S(2)}) collective-permute-start(f32[128,2048]{0,1:T(8,128)} %fusion.3), channel_id=1, source_target_pairs={{0,2},{1,3},{2,0},{3,1},{4,6},{5,7},{6,4},{7,5},{8,10},{9,11},{10,... | collective-permute-start | bytes 3145736 | tf_op jit(solution)/shard_map/ppermute | solution.py:66
  51.1 8.1 %collective-permute-start.15 = (f32[1,16,2304]{2,1,0:T(8,128)}, f32[1,16,2304]{2,1,0:T(8,128)S(1)}, u32[]{:S(2)}, u32[]{:S(2)}) collective-permute-start(f32[1,16,2304]{2,1,0:T(8,128)} %get-tuple-element.8), channel_id=1, source_target_pairs={{0,12},{4,8},{8,4},{12,0},{16,28},{20,24},{24,20},{28,16},{1,13},{... | collective-permute-start | bytes 442376 | tf_op jit(solution)/shard_map/ppermute | solution.py:137
  52.3 9.9 %collective-permute-start.14 = (f32[1,16,2304]{2,1,0:T(8,128)S(1)}, f32[1,16,2304]{2,1,0:T(8,128)S(1)}, u32[]{:S(2)}, u32[]{:S(2)}) collective-permute-start(f32[1,16,2304]{2,1,0:T(8,128)S(1)} %get-tuple-element.7), channel_id=1, source_target_pairs={{0,8},{4,12},{8,0},{12,4},{16,24},{20,28},{24,16},{28,20},{1,9},{5... | collective-permute-start | bytes 442376 | tf_op jit(solution)/shard_map/ppermute | solution.py:137
  56.8 5.4 %collective-permute-start.13 = (f32[1,16,2304]{2,1,0:T(8,128)S(1)}, f32[1,16,2304]{2,1,0:T(8,128)S(1)}, u32[]{:S(2)}, u32[]{:S(2)}) collective-permute-start(f32[1,16,2304]{2,1,0:T(8,128)S(1)} %get-tuple-element.6), channel_id=1, source_target_pairs={{0,4},{4,0},{8,12},{12,8},{16,20},{20,16},{24,28},{28,24},{1,5},{5... | collective-permute-start | bytes 442376 | tf_op jit(solution)/shard_map/ppermute | solution.py:137

commit v3 on v2

--- a/solution.py
+++ b/solution.py
@@ -134,7 +134,7 @@
     owned = lax.dynamic_index_in_dim(combined, me_dp, 0, keepdims=False)
     for shift, pairs in _partners(dp_size):
         outgoing = lax.dynamic_index_in_dim(combined, _dest_of(me_dp, shift, dp_size), 0, keepdims=False)
-        owned = owned + lax.ppermute(outgoing, "dp", pairs)
+        owned = owned + lax.ppermute(outgoing.astype(jnp.bfloat16), "dp", pairs).astype(jnp.float32)
     grad_down = owned[:, :, :width_portion]
     grad_up = owned[:, :, width_portion:]
     return (grad_inputs, grad_down, grad_up)

time: 76.5 us -> 66.3 us (0.87)
  the two profiles are of different devices: /device:TPU:20 before, /device:TPU:0 now
where the time goes in v3:
time: 66.3 us; the launch traced here: 66 us
  starting transfers between devices  24.9 us (38%)
  waiting for transfers between devices  21.6 us (33%)
  matrix products  12.4 us (19%)
  local copies, waits for them, and re-layouts  5.38 us (8%)
  between operations  1.5 us (2%)
    ppermute x7, starting transfers between devices, _gather_dp(): got.append(lax.ppermute(local, axis, pairs))  12.5 us
    dot_general x4, matrix products, term(): lax.dot_general(cotangent, piece, (((1,), (1,)), ((), ())), preferred_ele...  10.2 us
    ppermute x7, starting transfers between devices, on_device(): lax.ppermute(outgoing.astype(jnp.bfloat16), 'dp', pairs).astype(jnp.float32)  8.32 us
    ppermute x7, waiting for transfers between devices, on_device(): lax.ppermute(outgoing.astype(jnp.bfloat16), 'dp', pairs).astype(jnp.float32)  8.03 us
    ppermute x7, waiting for transfers between devices, _gather_dp(): got.append(lax.ppermute(local, axis, pairs))  6.34 us
    ppermute x3, waiting for transfers between devices, _frozen_term(): got = [lax.ppermute(held[e], axis, pairs) for e in range(1, len(held), 2)]  5.49 us
    unnamed x15, local copies, waits for them, and re-layouts  2.48 us
    ppermute x3, starting transfers between devices, _frozen_term(): got = [lax.ppermute(held[e], axis, pairs) for e in range(1, len(held), 2)]  2.11 us
  transfers between devices with their start and end apart: 20, of which 9 were waited for; matrix products, arithmetic and copies ran while one was open for 20% of the time, Pallas kernels for 0%

profile of v3, /device:TPU:0, one launch (start us, length us, event | category | flops | bytes accessed | tf_op | source)
XLA Modules:
  0.0 66.0 jit_solution(3680485592530665699)
XLA Ops:
  0.7 0.9 %constant_dynamic-update-slice_fusion.1 = bf16[1,16,2304]{2,1,0:T(8,128)(2,1)S(1)} fusion(bf16[1,16,2048]{2,1,0:T(8,128)(2,1)} %param.9), kind=kLoop, calls=%fused_computation.66 | loop fusion | bytes 131072
  2.3 3.0 %collective-permute-start.3 = (bf16[1,16,2304]{2,1,0:T(8,128)(2,1)S(1)}, bf16[1,16,2304]{2,1,0:T(8,128)(2,1)S(1)}, u32[]{:S(2)}, u32[]{:S(2)}) collective-permute-start(bf16[1,16,2304]{2,1,0:T(8,128)(2,1)S(1)} %constant_dynamic-update-slice_fusion), channel_id=1, source_target_pairs={{0,4},{4,0},{8,12},{12,8},{16,20},{20,16},{24,28},{28,24},{1,5},{5... | collective-permute-start | bytes 221192 | tf_op jit(solution)/shard_map/ppermute | solution.py:32
  5.2 1.6 %collective-permute-start.4 = (bf16[1,16,2304]{2,1,0:T(8,128)(2,1)S(1)}, bf16[1,16,2304]{2,1,0:T(8,128)(2,1)S(1)}, u32[]{:S(2)}, u32[]{:S(2)}) collective-permute-start(bf16[1,16,2304]{2,1,0:T(8,128)(2,1)S(1)} %constant_dynamic-update-slice_fusion), channel_id=1, source_target_pairs={{0,8},{4,12},{8,0},{12,4},{16,24},{20,28},{24,16},{28,20},{1,9},{5... | collective-permute-start | bytes 221192 | tf_op jit(solution)/shard_map/ppermute | solution.py:32
  6.8 3.0 %collective-permute-start.6 = (bf16[1,16,2304]{2,1,0:T(8,128)(2,1)S(1)}, bf16[1,16,2304]{2,1,0:T(8,128)(2,1)S(1)}, u32[]{:S(2)}, u32[]{:S(2)}) collective-permute-start(bf16[1,16,2304]{2,1,0:T(8,128)(2,1)S(1)} %constant_dynamic-update-slice_fusion), channel_id=1, source_target_pairs={{0,16},{4,20},{8,24},{12,28},{16,0},{20,4},{24,8},{28,12},{1,17},{... | collective-permute-start | bytes 221192 | tf_op jit(solution)/shard_map/ppermute | solution.py:32
  9.8 1.3 %collective-permute-start.7 = (bf16[1,16,2304]{2,1,0:T(8,128)(2,1)S(1)}, bf16[1,16,2304]{2,1,0:T(8,128)(2,1)S(1)}, u32[]{:S(2)}, u32[]{:S(2)}) collective-permute-start(bf16[1,16,2304]{2,1,0:T(8,128)(2,1)S(1)} %constant_dynamic-update-slice_fusion), channel_id=1, source_target_pairs={{0,20},{4,16},{8,28},{12,24},{16,4},{20,0},{24,12},{28,8},{1,21},{... | collective-permute-start | bytes 221192 | tf_op jit(solution)/shard_map/ppermute | solution.py:32
  11.1 2.6 %convolution_bitcast_fusion.1 = f32[128,2048]{0,1:T(8,128)} fusion(bf16[128,256]{1,0:T(8,128)(2,1)} %param.7, bf16[8192,256]{1,0:T(8,128)(2,1)} %param.8, s32[]{:T(128)S(6)} %select_n.48), kind=kOutput, calls=%fused_computation.1 | convolution fusion | flops 134217728 | bytes 2162692 | tf_op jit(solution)/shard_map/dot_general | solution.py:57
  13.7 2.7 %convolution_bitcast_fusion.3 = f32[128,2048]{0,1:T(8,128)} fusion(bf16[128,256]{1,0:T(8,128)(2,1)} %param.7, bf16[8192,256]{1,0:T(8,128)(2,1)} %param.8, s32[]{:T(128)S(6)} %select_n.46), kind=kOutput, calls=%fused_computation.3 | convolution fusion | flops 134217728 | bytes 2162692 | tf_op jit(solution)/shard_map/dot_general | solution.py:57
  17.1 3.7 %collective-permute-start.8 = (bf16[1,16,2304]{2,1,0:T(8,128)(2,1)S(1)}, bf16[1,16,2304]{2,1,0:T(8,128)(2,1)S(1)}, u32[]{:S(2)}, u32[]{:S(2)}) collective-permute-start(bf16[1,16,2304]{2,1,0:T(8,128)(2,1)S(1)} %constant_dynamic-update-slice_fusion), channel_id=1, source_target_pairs={{0,24},{4,28},{8,16},{12,20},{16,8},{20,12},{24,0},{28,4},{1,25},{... | collective-permute-start | bytes 221192 | tf_op jit(solution)/shard_map/ppermute | solution.py:32
  21.6 1.8 %collective-permute-done.8 = bf16[1,16,2304]{2,1,0:T(8,128)(2,1)S(1)} collective-permute-done((bf16[1,16,2304]{2,1,0:T(8,128)(2,1)S(1)}, bf16[1,16,2304]{2,1,0:T(8,128)(2,1)S(1)}, u32[]{:S(2)}, u32[]{:S(2)}) %collective-permute-start.8) | collective-permute-done | bytes 73760 | tf_op jit(solution)/shard_map/ppermute | solution.py:32
  23.4 4.6 %collective-permute-done.9 = bf16[1,16,2304]{2,1,0:T(8,128)(2,1)S(1)} collective-permute-done((bf16[1,16,2304]{2,1,0:T(8,128)(2,1)S(1)}, bf16[1,16,2304]{2,1,0:T(8,128)(2,1)S(1)}, u32[]{:S(2)}, u32[]{:S(2)}) %collective-permute-start.9) | collective-permute-done | bytes 73760 | tf_op jit(solution)/shard_map/ppermute | solution.py:32
  28.7 1.6 %collective-permute-start.11 = (f32[1,128,32]{1,2,0:T(8,128)S(1)}, f32[1,128,32]{1,2,0:T(8,128)S(1)}, u32[]{:S(2)}, u32[]{:S(2)}) collective-permute-start(f32[1,128,32]{1,2,0:T(8,128)S(1)} %pad_maximum_fusion.1), channel_id=1, source_target_pairs={{0,2},{1,3},{2,0},{3,1},{4,6},{5,7},{6,4},{7,5},{8,10},{9,11},{10,... | collective-permute-start | bytes 49160 | tf_op jit(solution)/shard_map/ppermute | solution.py:42
  30.7 1.3 %collective-permute-done.12 = f32[1,128,32]{1,2,0:T(8,128)S(1)} collective-permute-done((f32[1,128,32]{1,2,0:T(8,128)S(1)}, f32[1,128,32]{1,2,0:T(8,128)S(1)}, u32[]{:S(2)}, u32[]{:S(2)}) %collective-permute-start.12) | collective-permute-done | bytes 16416 | tf_op jit(solution)/shard_map/ppermute | solution.py:42
  34.5 2.9 %fusion.3 = f32[128,2048]{0,1:T(8,128)} fusion(f32[128,2048]{0,1:T(8,128)} %collective-permute-done.1, bf16[128,256]{1,0:T(8,128)(2,1)S(1)} %copy-done.1, bf16[8192,256]{1,0:T(8,128)(2,1)} %param.8, s32[]{:T(128)S(6)} %select_n.47), kind=kOutput, calls=%fused_computation.8 | convolution fusion | flops 134479872 | bytes 3211268 | tf_op jit(solution)/shard_map/dot_general | solution.py:57
  37.5 1.5 %collective-permute-start.2 = (f32[128,2048]{0,1:T(8,128)}, f32[128,2048]{0,1:T(8,128)}, u32[]{:S(2)}, u32[]{:S(2)}) collective-permute-start(f32[128,2048]{0,1:T(8,128)} %fusion.3), channel_id=1, source_target_pairs={{0,2},{1,3},{2,0},{3,1},{4,6},{5,7},{6,4},{7,5},{8,10},{9,11},{10,... | collective-permute-start | bytes 3145736 | tf_op jit(solution)/shard_map/ppermute | solution.py:66
  39.6 3.0 %collective-permute-start.18 = (bf16[1,16,2304]{2,1,0:T(8,128)(2,1)}, bf16[1,16,2304]{2,1,0:T(8,128)(2,1)S(1)}, u32[]{:S(2)}, u32[]{:S(2)}) collective-permute-start(bf16[1,16,2304]{2,1,0:T(8,128)(2,1)} %get-tuple-element.7), channel_id=1, source_target_pairs={{0,24},{4,28},{8,16},{12,20},{16,8},{20,12},{24,0},{28,4},{1,25},{... | collective-permute-start | bytes 221192 | tf_op jit(solution)/shard_map/ppermute | solution.py:137
  42.6 3.9 %collective-permute-start.16 = (bf16[1,16,2304]{2,1,0:T(8,128)(2,1)S(1)}, bf16[1,16,2304]{2,1,0:T(8,128)(2,1)S(1)}, u32[]{:S(2)}, u32[]{:S(2)}) collective-permute-start(bf16[1,16,2304]{2,1,0:T(8,128)(2,1)S(1)} %get-tuple-element.9), channel_id=1, source_target_pairs={{0,16},{4,20},{8,24},{12,28},{16,0},{20,4},{24,8},{28,12},{1,17},{... | collective-permute-start | bytes 221192 | tf_op jit(solution)/shard_map/ppermute | solution.py:137
  46.5 3.7 %collective-permute-done.17 = bf16[1,16,2304]{2,1,0:T(8,128)(2,1)S(1)} collective-permute-done((bf16[1,16,2304]{2,1,0:T(8,128)(2,1)S(1)}, bf16[1,16,2304]{2,1,0:T(8,128)(2,1)S(1)}, u32[]{:S(2)}, u32[]{:S(2)}) %collective-permute-start.17) | collective-permute-done | bytes 73760 | tf_op jit(solution)/shard_map/ppermute | solution.py:137
  50.1 1.7 %collective-permute-done.16 = bf16[1,16,2304]{2,1,0:T(8,128)(2,1)S(1)} collective-permute-done((bf16[1,16,2304]{2,1,0:T(8,128)(2,1)S(1)}, bf16[1,16,2304]{2,1,0:T(8,128)(2,1)S(1)}, u32[]{:S(2)}, u32[]{:S(2)}) %collective-permute-start.16) | collective-permute-done | bytes 73760 | tf_op jit(solution)/shard_map/ppermute | solution.py:137
  52.4 1.0 %fusion.33 = f32[128,2048]{0,1:T(8,128)S(1)} fusion(bf16[1,16,2304]{2,1,0:T(8,128)(2,1)S(1)} %copy.25, bf16[1,128,32]{1,2,0:T(8,128)(2,1)} %copy-done.2), kind=kOutput, calls=%fused_computation.62 | convolution fusion | flops 8388608 | bytes 1118208 | tf_op jit(solution)/shard_map/bnr,brd->bnd/dot_general | solution.py:110
  53.4 1.0 %collective-permute-done.14 = bf16[1,16,2304]{2,1,0:T(8,128)(2,1)S(1)} collective-permute-done((bf16[1,16,2304]{2,1,0:T(8,128)(2,1)S(1)}, bf16[1,16,2304]{2,1,0:T(8,128)(2,1)S(1)}, u32[]{:S(2)}, u32[]{:S(2)}) %collective-permute-start.14) | collective-permute-done | bytes 73760 | tf_op jit(solution)/shard_map/ppermute | solution.py:137
  54.5 1.7 %collective-permute-done.13 = bf16[1,16,2304]{2,1,0:T(8,128)(2,1)S(1)} collective-permute-done((bf16[1,16,2304]{2,1,0:T(8,128)(2,1)S(1)}, bf16[1,16,2304]{2,1,0:T(8,128)(2,1)S(1)}, u32[]{:S(2)}, u32[]{:S(2)}) %collective-permute-start.13) | collective-permute-done | bytes 73760 | tf_op jit(solution)/shard_map/ppermute | solution.py:137
  57.5 5.5 %collective-permute-done.2 = f32[128,2048]{0,1:T(8,128)} collective-permute-done((f32[128,2048]{0,1:T(8,128)}, f32[128,2048]{0,1:T(8,128)}, u32[]{:S(2)}, u32[]{:S(2)}) %collective-permute-start.2) | collective-permute-done | bytes 1048608 | tf_op jit(solution)/shard_map/ppermute | solution.py:66
  63.0 2.0 %fusion.4 = bf16[128,2048]{0,1:T(8,128)(2,1)S(1)} fusion(f32[128,2048]{0,1:T(8,128)S(1)} %fusion.33, f32[128,2048]{0,1:T(8,128)} %collective-permute-done.2, f32[128,2048]{0,1:T(8,128)S(1)} %collective-permute-done, bf16[128,256]{1,0:T(8,128)(2,1)S(1)} %copy-done.1, bf16[8192,256]{1,0:T(8,128)(2,1)} %param.8, s32[]{:T(128)S(6)} %select_n.45), kind=kOutput, calls=%fused_computation.9 | convolution fusion | flops 135266304 | bytes 4784132 | tf_op jit(solution)/shard_map/dot_general | solution.py:57
  65.0 1.0 %copy.16 = bf16[128,2048]{1,0:T(8,128)(2,1)} copy(bf16[128,2048]{0,1:T(8,128)(2,1)S(1)} %fusion.4) | data formatting | bytes 1048576
  (58 shorter events, 7.9 us)
Async XLA Ops:
  0.6 27.8 %copy-start = (bf16[128,2048]{1,0:T(8,128)(2,1)S(1)}, bf16[128,2048]{1,0:T(8,128)(2,1)}, u32[]{:S(2)}) copy-start(bf16[128,2048]{1,0:T(8,128)(2,1)} %param.6) | copy-start | bytes 1572868
  0.6 27.6 %copy-start.1 = (bf16[128,256]{1,0:T(8,128)(2,1)S(1)}, bf16[128,256]{1,0:T(8,128)(2,1)}, u32[]{:S(2)}) copy-start(bf16[128,256]{1,0:T(8,128)(2,1)} %param.7) | copy-start | bytes 196612
  2.3 14.9 %collective-permute-start.3 = (bf16[1,16,2304]{2,1,0:T(8,128)(2,1)S(1)}, bf16[1,16,2304]{2,1,0:T(8,128)(2,1)S(1)}, u32[]{:S(2)}, u32[]{:S(2)}) collective-permute-start(bf16[1,16,2304]{2,1,0:T(8,128)(2,1)S(1)} %constant_dynamic-update-slice_fusion), channel_id=1, source_target_pairs={{0,4},{4,0},{8,12},{12,8},{16,20},{20,16},{24,28},{28,24},{1,5},{5... | collective-permute-start | bytes 221192 | tf_op jit(solution)/shard_map/ppermute | solution.py:32
  5.2 15.6 %collective-permute-start.4 = (bf16[1,16,2304]{2,1,0:T(8,128)(2,1)S(1)}, bf16[1,16,2304]{2,1,0:T(8,128)(2,1)S(1)}, u32[]{:S(2)}, u32[]{:S(2)}) collective-permute-start(bf16[1,16,2304]{2,1,0:T(8,128)(2,1)S(1)} %constant_dynamic-update-slice_fusion), channel_id=1, source_target_pairs={{0,8},{4,12},{8,0},{12,4},{16,24},{20,28},{24,16},{28,20},{1,9},{5... | collective-permute-start | bytes 221192 | tf_op jit(solution)/shard_map/ppermute | solution.py:32
  6.8 14.1 %collective-permute-start.5 = (bf16[1,16,2304]{2,1,0:T(8,128)(2,1)S(1)}, bf16[1,16,2304]{2,1,0:T(8,128)(2,1)S(1)}, u32[]{:S(2)}, u32[]{:S(2)}) collective-permute-start(bf16[1,16,2304]{2,1,0:T(8,128)(2,1)S(1)} %constant_dynamic-update-slice_fusion), channel_id=1, source_target_pairs={{0,12},{4,8},{8,4},{12,0},{16,28},{20,24},{24,20},{28,16},{1,13},{... | collective-permute-start | bytes 221192 | tf_op jit(solution)/shard_map/ppermute | solution.py:32
  6.8 14.2 %collective-permute-start.6 = (bf16[1,16,2304]{2,1,0:T(8,128)(2,1)S(1)}, bf16[1,16,2304]{2,1,0:T(8,128)(2,1)S(1)}, u32[]{:S(2)}, u32[]{:S(2)}) collective-permute-start(bf16[1,16,2304]{2,1,0:T(8,128)(2,1)S(1)} %constant_dynamic-update-slice_fusion), channel_id=1, source_target_pairs={{0,16},{4,20},{8,24},{12,28},{16,0},{20,4},{24,8},{28,12},{1,17},{... | collective-permute-start | bytes 221192 | tf_op jit(solution)/shard_map/ppermute | solution.py:32
  9.8 11.8 %collective-permute-start.7 = (bf16[1,16,2304]{2,1,0:T(8,128)(2,1)S(1)}, bf16[1,16,2304]{2,1,0:T(8,128)(2,1)S(1)}, u32[]{:S(2)}, u32[]{:S(2)}) collective-permute-start(bf16[1,16,2304]{2,1,0:T(8,128)(2,1)S(1)} %constant_dynamic-update-slice_fusion), channel_id=1, source_target_pairs={{0,20},{4,16},{8,28},{12,24},{16,4},{20,0},{24,12},{28,8},{1,21},{... | collective-permute-start | bytes 221192 | tf_op jit(solution)/shard_map/ppermute | solution.py:32
  17.1 6.2 %collective-permute-start.8 = (bf16[1,16,2304]{2,1,0:T(8,128)(2,1)S(1)}, bf16[1,16,2304]{2,1,0:T(8,128)(2,1)S(1)}, u32[]{:S(2)}, u32[]{:S(2)}) collective-permute-start(bf16[1,16,2304]{2,1,0:T(8,128)(2,1)S(1)} %constant_dynamic-update-slice_fusion), channel_id=1, source_target_pairs={{0,24},{4,28},{8,16},{12,20},{16,8},{20,12},{24,0},{28,4},{1,25},{... | collective-permute-start | bytes 221192 | tf_op jit(solution)/shard_map/ppermute | solution.py:32
  20.8 7.1 %collective-permute-start.9 = (bf16[1,16,2304]{2,1,0:T(8,128)(2,1)S(1)}, bf16[1,16,2304]{2,1,0:T(8,128)(2,1)S(1)}, u32[]{:S(2)}, u32[]{:S(2)}) collective-permute-start(bf16[1,16,2304]{2,1,0:T(8,128)(2,1)S(1)} %constant_dynamic-update-slice_fusion), channel_id=1, source_target_pairs={{0,28},{4,24},{8,20},{12,16},{16,12},{20,8},{24,4},{28,0},{1,29},{... | collective-permute-start | bytes 221192 | tf_op jit(solution)/shard_map/ppermute | solution.py:32
  20.9 13.6 %collective-permute-start.1 = (f32[128,2048]{0,1:T(8,128)}, f32[128,2048]{0,1:T(8,128)}, u32[]{:S(2)}, u32[]{:S(2)}) collective-permute-start(f32[128,2048]{0,1:T(8,128)} %convolution_bitcast_fusion.1), channel_id=1, source_target_pairs={{0,1},{1,0},{2,3},{3,2},{4,5},{5,4},{6,7},{7,6},{8,9},{9,8},{10,11... | collective-permute-start | bytes 3145736 | tf_op jit(solution)/shard_map/ppermute | solution.py:66
  21.0 36.5 %collective-permute-start = (f32[128,2048]{0,1:T(8,128)}, f32[128,2048]{0,1:T(8,128)S(1)}, u32[]{:S(2)}, u32[]{:S(2)}) collective-permute-start(f32[128,2048]{0,1:T(8,128)} %convolution_bitcast_fusion.3), channel_id=1, source_target_pairs={{0,1},{1,0},{2,3},{3,2},{4,5},{5,4},{6,7},{7,6},{8,9},{9,8},{10,11... | collective-permute-start | bytes 3145736 | tf_op jit(solution)/shard_map/ppermute | solution.py:66
  28.7 3.3 %collective-permute-start.12 = (f32[1,128,32]{1,2,0:T(8,128)S(1)}, f32[1,128,32]{1,2,0:T(8,128)S(1)}, u32[]{:S(2)}, u32[]{:S(2)}) collective-permute-start(f32[1,128,32]{1,2,0:T(8,128)S(1)} %pad_maximum_fusion.1), channel_id=1, source_target_pairs={{0,3},{1,2},{2,1},{3,0},{4,7},{5,6},{6,5},{7,4},{8,11},{9,10},{10,... | collective-permute-start | bytes 49160 | tf_op jit(solution)/shard_map/ppermute | solution.py:42
  28.7 3.8 %collective-permute-start.11 = (f32[1,128,32]{1,2,0:T(8,128)S(1)}, f32[1,128,32]{1,2,0:T(8,128)S(1)}, u32[]{:S(2)}, u32[]{:S(2)}) collective-permute-start(f32[1,128,32]{1,2,0:T(8,128)S(1)} %pad_maximum_fusion.1), channel_id=1, source_target_pairs={{0,2},{1,3},{2,0},{3,1},{4,6},{5,7},{6,4},{7,5},{8,10},{9,11},{10,... | collective-permute-start | bytes 49160 | tf_op jit(solution)/shard_map/ppermute | solution.py:42
  30.2 2.2 %collective-permute-start.10 = (f32[1,128,32]{1,2,0:T(8,128)S(1)}, f32[1,128,32]{1,2,0:T(8,128)S(1)}, u32[]{:S(2)}, u32[]{:S(2)}) collective-permute-start(f32[1,128,32]{1,2,0:T(8,128)S(1)} %pad_maximum_fusion.1), channel_id=1, source_target_pairs={{0,1},{1,0},{2,3},{3,2},{4,5},{5,4},{6,7},{7,6},{8,9},{9,8},{10,11... | collective-permute-start | bytes 49160 | tf_op jit(solution)/shard_map/ppermute | solution.py:42
  32.5 0.6 copy-start.2
  33.6 9.0 %collective-permute-start.19 = (bf16[1,16,2304]{2,1,0:T(8,128)(2,1)S(1)}, bf16[1,16,2304]{2,1,0:T(8,128)(2,1)S(1)}, u32[]{:S(2)}, u32[]{:S(2)}) collective-permute-start(bf16[1,16,2304]{2,1,0:T(8,128)(2,1)S(1)} %fusion.32), channel_id=1, source_target_pairs={{0,28},{4,24},{8,20},{12,16},{16,12},{20,8},{24,4},{28,0},{1,29},{... | collective-permute-start | bytes 221192 | tf_op jit(solution)/shard_map/ppermute | solution.py:137
  37.5 25.5 %collective-permute-start.2 = (f32[128,2048]{0,1:T(8,128)}, f32[128,2048]{0,1:T(8,128)}, u32[]{:S(2)}, u32[]{:S(2)}) collective-permute-start(f32[128,2048]{0,1:T(8,128)} %fusion.3), channel_id=1, source_target_pairs={{0,2},{1,3},{2,0},{3,1},{4,6},{5,7},{6,4},{7,5},{8,10},{9,11},{10,... | collective-permute-start | bytes 3145736 | tf_op jit(solution)/shard_map/ppermute | solution.py:66
  39.6 6.8 %collective-permute-start.18 = (bf16[1,16,2304]{2,1,0:T(8,128)(2,1)}, bf16[1,16,2304]{2,1,0:T(8,128)(2,1)S(1)}, u32[]{:S(2)}, u32[]{:S(2)}) collective-permute-start(bf16[1,16,2304]{2,1,0:T(8,128)(2,1)} %get-tuple-element.7), channel_id=1, source_target_pairs={{0,24},{4,28},{8,16},{12,20},{16,8},{20,12},{24,0},{28,4},{1,25},{... | collective-permute-start | bytes 221192 | tf_op jit(solution)/shard_map/ppermute | solution.py:137
  42.6 7.6 %collective-permute-start.17 = (bf16[1,16,2304]{2,1,0:T(8,128)(2,1)S(1)}, bf16[1,16,2304]{2,1,0:T(8,128)(2,1)S(1)}, u32[]{:S(2)}, u32[]{:S(2)}) collective-permute-start(bf16[1,16,2304]{2,1,0:T(8,128)(2,1)S(1)} %get-tuple-element.8), channel_id=1, source_target_pairs={{0,20},{4,16},{8,28},{12,24},{16,4},{20,0},{24,12},{28,8},{1,21},{... | collective-permute-start | bytes 221192 | tf_op jit(solution)/shard_map/ppermute | solution.py:137
  42.6 9.2 %collective-permute-start.16 = (bf16[1,16,2304]{2,1,0:T(8,128)(2,1)S(1)}, bf16[1,16,2304]{2,1,0:T(8,128)(2,1)S(1)}, u32[]{:S(2)}, u32[]{:S(2)}) collective-permute-start(bf16[1,16,2304]{2,1,0:T(8,128)(2,1)S(1)} %get-tuple-element.9), channel_id=1, source_target_pairs={{0,16},{4,20},{8,24},{12,28},{16,0},{20,4},{24,8},{28,12},{1,17},{... | collective-permute-start | bytes 221192 | tf_op jit(solution)/shard_map/ppermute | solution.py:137
  46.5 7.0 %collective-permute-start.15 = (bf16[1,16,2304]{2,1,0:T(8,128)(2,1)S(1)}, bf16[1,16,2304]{2,1,0:T(8,128)(2,1)S(1)}, u32[]{:S(2)}, u32[]{:S(2)}) collective-permute-start(bf16[1,16,2304]{2,1,0:T(8,128)(2,1)S(1)} %get-tuple-element.10), channel_id=1, source_target_pairs={{0,12},{4,8},{8,4},{12,0},{16,28},{20,24},{24,20},{28,16},{1,13},{... | collective-permute-start | bytes 221192 | tf_op jit(solution)/shard_map/ppermute | solution.py:137
  50.1 4.4 %collective-permute-start.14 = (bf16[1,16,2304]{2,1,0:T(8,128)(2,1)S(1)}, bf16[1,16,2304]{2,1,0:T(8,128)(2,1)S(1)}, u32[]{:S(2)}, u32[]{:S(2)}) collective-permute-start(bf16[1,16,2304]{2,1,0:T(8,128)(2,1)S(1)} %get-tuple-element.11), channel_id=1, source_target_pairs={{0,8},{4,12},{8,0},{12,4},{16,24},{20,28},{24,16},{28,20},{1,9},{5... | collective-permute-start | bytes 221192 | tf_op jit(solution)/shard_map/ppermute | solution.py:137
  51.8 4.4 %collective-permute-start.13 = (bf16[1,16,2304]{2,1,0:T(8,128)(2,1)S(1)}, bf16[1,16,2304]{2,1,0:T(8,128)(2,1)S(1)}, u32[]{:S(2)}, u32[]{:S(2)}) collective-permute-start(bf16[1,16,2304]{2,1,0:T(8,128)(2,1)S(1)} %get-tuple-element.6), channel_id=1, source_target_pairs={{0,4},{4,0},{8,12},{12,8},{16,20},{20,16},{24,28},{28,24},{1,5},{5... | collective-permute-start | bytes 221192 | tf_op jit(solution)/shard_map/ppermute | solution.py:137

commit v4 on v3

--- a/solution.py
+++ b/solution.py
@@ -44,7 +44,7 @@
 
 
 def _frozen_term(cotangent, weight, axis, size):
-    if size & (size - 1) != 0:
+    if size & (size - 1) != 0 or size == 1:
         partial = lax.dot_general(
             cotangent, weight, (((1,), (1,)), ((), ())), preferred_element_type=jnp.float32
         )
@@ -52,14 +52,20 @@
     me = lax.axis_index(axis)
     rows = weight.shape[0] // size
 
-    def term(block):
-        piece = lax.dynamic_slice_in_dim(weight, block * rows, rows, axis=0)
-        return lax.dot_general(
-            cotangent, piece, (((1,), (1,)), ((), ())), preferred_element_type=jnp.float32
-        )
+    pairs = [(i, i ^ 1) for i in range(size)]
+    pieces = [lax.dynamic_slice_in_dim(weight, (me ^ e) * rows, rows, axis=0) for e in range(size)]
+    sent = jnp.stack(pieces[1::2], 0)
+    their_rows = lax.ppermute(sent, axis, pairs)
+    their_cot = lax.ppermute(cotangent, axis, pairs)
 
-    held = [term(me ^ e) for e in range(size)]
-    step = 0
+    def dot(a, b):
+        return lax.dot_general(a, b, (((1,), (1,)), ((), ())), preferred_element_type=jnp.float32)
+
+    held = [
+        dot(cotangent, pieces[2 * m]) + dot(their_cot, their_rows[m])
+        for m in range(size // 2)
+    ]
+    step = 1
     while len(held) > 1:
         partner = 1 << step
         pairs = [(i, i ^ partner) for i in range(size)]

time: 66.3 us -> 69.1 us (1.042)
  matrix products: 12.4 us -> 8.13 us
  local copies, waits for them, and re-layouts: 5.38 us -> 9.47 us
  starting transfers between devices: 24.9 us -> 27.1 us
  other arithmetic: 0.26 us -> 1.76 us
  waiting for transfers between devices: 21.6 us -> 20.6 us
    ppermute x3 -> x1, waiting for transfers between devices: 5.49 us -> 11.2 us  [_frozen_term(): got = [lax.ppermute(held[e], axis, pairs) for e in range(1, len(held), 2)]]
    ppermute x7, waiting for transfers between devices: 8.03 us -> 3.01 us  [on_device(): lax.ppermute(outgoing.astype(jnp.bfloat16), 'dp', pairs).astype(jnp.float32)]
    dot_general x4, matrix products: 10.2 us -> 6.66 us  [dot(): lax.dot_general(a, b, (((1,), (1,)), ((), ())), preferred_element_type=jn...]
    unnamed x15 -> x13, local copies, waits for them, and re-layouts: 2.48 us -> 5.51 us
    ppermute x7, starting transfers between devices: 8.32 us -> 11.3 us  [on_device(): lax.ppermute(outgoing.astype(jnp.bfloat16), 'dp', pairs).astype(jnp.float32)]
    ppermute x7, waiting for transfers between devices: 6.34 us -> 3.7 us  [_gather_dp(): got.append(lax.ppermute(local, axis, pairs))]
    another operation x0 -> x1, local copies, waits for them, and re-layouts: none -> 1.68 us  [_frozen_term(): sent = jnp.stack(pieces[1::2], 0)]
    another operation x1 -> x2, other arithmetic: 0.01 us -> 1.53 us  [the longest x1 1.52 us: _frozen_term(): sent = jnp.stack(pieces[1::2], 0)]
  transfers between devices with their start and end apart: 20 -> 20, of which waited for: 9 -> 6; matrix products, arithmetic and copies ran while one was open for 20% -> 22% of each run, Pallas kernels for 0% -> 0%
where the time goes in v4:
time: 69.1 us; the launch traced here: 68.6 us
  starting transfers between devices  27.1 us (39%)
  waiting for transfers between devices  20.6 us (30%)
  local copies, waits for them, and re-layouts  9.47 us (14%)
  matrix products  8.13 us (12%)
  other arithmetic  1.76 us (3%)
  between operations  1.49 us (2%)
    ppermute x7, starting transfers between devices, _gather_dp(): got.append(lax.ppermute(local, axis, pairs))  12.5 us
    ppermute x7, starting transfers between devices, on_device(): lax.ppermute(outgoing.astype(jnp.bfloat16), 'dp', pairs).astype(jnp.float32)  11.3 us
    ppermute x1, waiting for transfers between devices, _frozen_term(): got = [lax.ppermute(held[e], axis, pairs) for e in range(1, len(held), 2)]  11.2 us
    dot_general x4, matrix products, dot(): lax.dot_general(a, b, (((1,), (1,)), ((), ())), preferred_element_type=jn...  6.66 us
    unnamed x13, local copies, waits for them, and re-layouts  5.51 us
    ppermute x7, waiting for transfers between devices, _gather_dp(): got.append(lax.ppermute(local, axis, pairs))  3.7 us
    ppermute x7, waiting for transfers between devices, on_device(): lax.ppermute(outgoing.astype(jnp.bfloat16), 'dp', pairs).astype(jnp.float32)  3.01 us
    ppermute x3, waiting for transfers between devices, _psum_small(): total = total + lax.ppermute(value, axis, pairs)  2.68 us
  transfers between devices with their start and end apart: 20, of which 6 were waited for; matrix products, arithmetic and copies ran while one was open for 22% of the time, Pallas kernels for 0%

profile of v4, /device:TPU:0, one launch (start us, length us, event | category | flops | bytes accessed | tf_op | source)
XLA Modules:
  0.0 68.6 jit_solution(15892807328174187597)
XLA Ops:
  0.6 0.9 %constant_dynamic-update-slice_fusion.1 = bf16[1,16,2304]{2,1,0:T(8,128)(2,1)S(1)} fusion(bf16[1,16,2048]{2,1,0:T(8,128)(2,1)} %param.9), kind=kLoop, calls=%fused_computation.69 | loop fusion | bytes 131072
  2.2 3.0 %collective-permute-start.3 = (bf16[1,16,2304]{2,1,0:T(8,128)(2,1)S(1)}, bf16[1,16,2304]{2,1,0:T(8,128)(2,1)}, u32[]{:S(2)}, u32[]{:S(2)}) collective-permute-start(bf16[1,16,2304]{2,1,0:T(8,128)(2,1)S(1)} %constant_dynamic-update-slice_fusion), channel_id=1, source_target_pairs={{0,4},{4,0},{8,12},{12,8},{16,20},{20,16},{24,28},{28,24},{1,5},{5... | collective-permute-start | bytes 221192 | tf_op jit(solution)/shard_map/ppermute | solution.py:32
  5.2 1.6 %collective-permute-start.4 = (bf16[1,16,2304]{2,1,0:T(8,128)(2,1)S(1)}, bf16[1,16,2304]{2,1,0:T(8,128)(2,1)}, u32[]{:S(2)}, u32[]{:S(2)}) collective-permute-start(bf16[1,16,2304]{2,1,0:T(8,128)(2,1)S(1)} %constant_dynamic-update-slice_fusion), channel_id=1, source_target_pairs={{0,8},{4,12},{8,0},{12,4},{16,24},{20,28},{24,16},{28,20},{1,9},{5... | collective-permute-start | bytes 221192 | tf_op jit(solution)/shard_map/ppermute | solution.py:32
  6.8 3.0 %collective-permute-start.6 = (bf16[1,16,2304]{2,1,0:T(8,128)(2,1)S(1)}, bf16[1,16,2304]{2,1,0:T(8,128)(2,1)}, u32[]{:S(2)}, u32[]{:S(2)}) collective-permute-start(bf16[1,16,2304]{2,1,0:T(8,128)(2,1)S(1)} %constant_dynamic-update-slice_fusion), channel_id=1, source_target_pairs={{0,16},{4,20},{8,24},{12,28},{16,0},{20,4},{24,8},{28,12},{1,17},{... | collective-permute-start | bytes 221192 | tf_op jit(solution)/shard_map/ppermute | solution.py:32
  9.8 1.3 %collective-permute-start.7 = (bf16[1,16,2304]{2,1,0:T(8,128)(2,1)S(1)}, bf16[1,16,2304]{2,1,0:T(8,128)(2,1)S(1)}, u32[]{:S(2)}, u32[]{:S(2)}) collective-permute-start(bf16[1,16,2304]{2,1,0:T(8,128)(2,1)S(1)} %constant_dynamic-update-slice_fusion), channel_id=1, source_target_pairs={{0,20},{4,16},{8,28},{12,24},{16,4},{20,0},{24,12},{28,8},{1,21},{... | collective-permute-start | bytes 221192 | tf_op jit(solution)/shard_map/ppermute | solution.py:32
  11.1 1.7 %dynamic-slice_bitcast_fusion.1 = (bf16[1,2048,256]{2,1,0:T(8,128)(2,1)S(1)}, bf16[1,2048,256]{2,1,0:T(8,128)(2,1)S(1)}) fusion(bf16[8192,256]{1,0:T(8,128)(2,1)} %param.8, s32[]{:T(128)S(6)} %select_n.46, s32[]{:T(128)S(6)} %select_n.47), kind=kLoop, calls=%fused_computation.24 | loop fusion | bytes 4194312 | tf_op jit(solution)/shard_map/stack | solution.py:57
  12.8 1.5 %pad_maximum_fusion = bf16[2,2048,256]{2,1,0:T(8,128)(2,1)} fusion(bf16[1,2048,256]{2,1,0:T(8,128)(2,1)S(1)} %get-tuple-element.7, bf16[1,2048,256]{2,1,0:T(8,128)(2,1)S(1)} %get-tuple-element.6), kind=kLoop, calls=%fused_computation.8 | loop fusion | flops 1048576 | bytes 4194304 | tf_op jit(solution)/shard_map/stack | solution.py:57
  14.3 1.6 %fusion.7 = f32[2048,128]{1,0:T(8,128)S(1)} fusion(bf16[128,256]{1,0:T(8,128)(2,1)S(1)} %copy-done.1, bf16[8192,256]{1,0:T(8,128)(2,1)} %param.8, s32[]{:T(128)S(6)} %select_n.48), kind=kOutput, calls=%fused_computation.21 | convolution fusion | flops 134217728 | bytes 2162692 | tf_op jit(solution)/shard_map/dot_general | solution.py:62
  15.9 1.7 %fusion.9 = f32[2048,128]{1,0:T(8,128)S(1)} fusion(bf16[128,256]{1,0:T(8,128)(2,1)S(1)} %copy-done.1, bf16[8192,256]{1,0:T(8,128)(2,1)} %param.8, s32[]{:T(128)S(6)} %select_n.45), kind=kOutput, calls=%fused_computation.25 | convolution fusion | flops 134217728 | bytes 2162692 | tf_op jit(solution)/shard_map/dot_general | solution.py:62
  18.3 3.7 %collective-permute-start.8 = (bf16[1,16,2304]{2,1,0:T(8,128)(2,1)S(1)}, bf16[1,16,2304]{2,1,0:T(8,128)(2,1)S(1)}, u32[]{:S(2)}, u32[]{:S(2)}) collective-permute-start(bf16[1,16,2304]{2,1,0:T(8,128)(2,1)S(1)} %constant_dynamic-update-slice_fusion), channel_id=1, source_target_pairs={{0,24},{4,28},{8,16},{12,20},{16,8},{20,12},{24,0},{28,4},{1,25},{... | collective-permute-start | bytes 221192 | tf_op jit(solution)/shard_map/ppermute | solution.py:32
  23.0 0.9 %bitcast_dynamic-update-slice_fusion.5 = bf16[8,1,16,2304]{3,2,1,0:T(8,128)(2,1)S(1)} fusion(bf16[8,1,16,2304]{3,2,1,0:T(8,128)(2,1)S(1)} %bitcast_dynamic-update-slice_fusion.6, bf16[1,16,2304]{2,1,0:T(8,128)(2,1)} %collective-permute-done.4), kind=kLoop, calls=%fused_computation.60 | loop fusion | bytes 147456
  26.3 3.7 %collective-permute-done.9 = bf16[1,16,2304]{2,1,0:T(8,128)(2,1)S(1)} collective-permute-done((bf16[1,16,2304]{2,1,0:T(8,128)(2,1)S(1)}, bf16[1,16,2304]{2,1,0:T(8,128)(2,1)S(1)}, u32[]{:S(2)}, u32[]{:S(2)}) %collective-permute-start.9) | collective-permute-done | bytes 73760 | tf_op jit(solution)/shard_map/ppermute | solution.py:32
  30.8 1.6 %collective-permute-start.11 = (f32[1,128,32]{1,2,0:T(8,128)S(1)}, f32[1,128,32]{1,2,0:T(8,128)S(1)}, u32[]{:S(2)}, u32[]{:S(2)}) collective-permute-start(f32[1,128,32]{1,2,0:T(8,128)S(1)} %pad_maximum_fusion.2), channel_id=1, source_target_pairs={{0,2},{1,3},{2,0},{3,1},{4,6},{5,7},{6,4},{7,5},{8,10},{9,11},{10,... | collective-permute-start | bytes 49160 | tf_op jit(solution)/shard_map/ppermute | solution.py:42
  32.8 1.8 %collective-permute-done.11 = f32[1,128,32]{1,2,0:T(8,128)S(1)} collective-permute-done((f32[1,128,32]{1,2,0:T(8,128)S(1)}, f32[1,128,32]{1,2,0:T(8,128)S(1)}, u32[]{:S(2)}, u32[]{:S(2)}) %collective-permute-start.11) | collective-permute-done | bytes 16416 | tf_op jit(solution)/shard_map/ppermute | solution.py:42
  34.6 0.9 %collective-permute-done.12 = f32[1,128,32]{1,2,0:T(8,128)S(1)} collective-permute-done((f32[1,128,32]{1,2,0:T(8,128)S(1)}, f32[1,128,32]{1,2,0:T(8,128)S(1)}, u32[]{:S(2)}, u32[]{:S(2)}) %collective-permute-start.12) | collective-permute-done | bytes 16416 | tf_op jit(solution)/shard_map/ppermute | solution.py:42
  36.7 3.0 %collective-permute-start.15 = (bf16[1,16,2304]{2,1,0:T(8,128)(2,1)S(1)}, bf16[1,16,2304]{2,1,0:T(8,128)(2,1)S(1)}, u32[]{:S(2)}, u32[]{:S(2)}) collective-permute-start(bf16[1,16,2304]{2,1,0:T(8,128)(2,1)S(1)} %get-tuple-element.12), channel_id=1, source_target_pairs={{0,12},{4,8},{8,4},{12,0},{16,28},{20,24},{24,20},{28,16},{1,13},{... | collective-permute-start | bytes 221192 | tf_op jit(solution)/shard_map/ppermute | solution.py:143
  39.7 1.7 %fusion = f32[128,2048]{0,1:T(8,128)S(1)} fusion(f32[2048,128]{1,0:T(8,128)S(1)} %fusion.7, bf16[128,256]{1,0:T(8,128)(2,1)S(1)} %collective-permute-done.1, bf16[2,2048,256]{2,1,0:T(8,128)(2,1)} %collective-permute-done), kind=kOutput, calls=%fused_computation.2 | convolution fusion | flops 134479872 | bytes 3211264 | tf_op jit(solution)/shard_map/dot_general | solution.py:62
  42.2 2.9 %collective-permute-start.17 = (bf16[1,16,2304]{2,1,0:T(8,128)(2,1)S(1)}, bf16[1,16,2304]{2,1,0:T(8,128)(2,1)S(1)}, u32[]{:S(2)}, u32[]{:S(2)}) collective-permute-start(bf16[1,16,2304]{2,1,0:T(8,128)(2,1)S(1)} %get-tuple-element.10), channel_id=1, source_target_pairs={{0,20},{4,16},{8,28},{12,24},{16,4},{20,0},{24,12},{28,8},{1,21},{... | collective-permute-start | bytes 221192 | tf_op jit(solution)/shard_map/ppermute | solution.py:143
  45.1 1.1 %collective-permute-start.18 = (bf16[1,16,2304]{2,1,0:T(8,128)(2,1)S(1)}, bf16[1,16,2304]{2,1,0:T(8,128)(2,1)S(1)}, u32[]{:S(2)}, u32[]{:S(2)}) collective-permute-start(bf16[1,16,2304]{2,1,0:T(8,128)(2,1)S(1)} %get-tuple-element.9), channel_id=1, source_target_pairs={{0,24},{4,28},{8,16},{12,20},{16,8},{20,12},{24,0},{28,4},{1,25},{... | collective-permute-start | bytes 221192 | tf_op jit(solution)/shard_map/ppermute | solution.py:143
  46.2 3.7 %collective-permute-start.19 = (bf16[1,16,2304]{2,1,0:T(8,128)(2,1)S(1)}, bf16[1,16,2304]{2,1,0:T(8,128)(2,1)S(1)}, u32[]{:S(2)}, u32[]{:S(2)}) collective-permute-start(bf16[1,16,2304]{2,1,0:T(8,128)(2,1)S(1)} %fusion.32), channel_id=1, source_target_pairs={{0,28},{4,24},{8,20},{12,16},{16,12},{20,8},{24,4},{28,0},{1,29},{... | collective-permute-start | bytes 221192 | tf_op jit(solution)/shard_map/ppermute | solution.py:143
  50.3 2.1 %collective-permute-done.17 = bf16[1,16,2304]{2,1,0:T(8,128)(2,1)S(1)} collective-permute-done((bf16[1,16,2304]{2,1,0:T(8,128)(2,1)S(1)}, bf16[1,16,2304]{2,1,0:T(8,128)(2,1)S(1)}, u32[]{:S(2)}, u32[]{:S(2)}) %collective-permute-start.17) | collective-permute-done | bytes 73760 | tf_op jit(solution)/shard_map/ppermute | solution.py:143
  54.6 11.2 %collective-permute-done.2 = f32[128,2048]{0,1:T(8,128)S(1)} collective-permute-done((f32[128,2048]{0,1:T(8,128)S(1)}, f32[128,2048]{0,1:T(8,128)S(1)}, u32[]{:S(2)}, u32[]{:S(2)}) %collective-permute-start.2) | collective-permute-done | bytes 1048608 | tf_op jit(solution)/shard_map/ppermute | solution.py:72
  65.8 1.7 %fusion.4 = bf16[128,2048]{0,1:T(8,128)(2,1)S(1)} fusion(f32[128,2048]{0,1:T(8,128)S(1)} %fusion.33, f32[128,2048]{0,1:T(8,128)S(1)} %collective-permute-done.2, f32[2048,128]{1,0:T(8,128)S(1)} %fusion.9, bf16[128,256]{1,0:T(8,128)(2,1)S(1)} %collective-permute-done.1, bf16[2,2048,256]{2,1,0:T(8,128)(2,1)} %collective-permute-done), kind=kOutput, calls=%fused_computation.7 | convolution fusion | flops 135266304 | bytes 4784128 | tf_op jit(solution)/shard_map/dot_general | solution.py:62
  67.5 1.0 %copy.16 = bf16[128,2048]{1,0:T(8,128)(2,1)} copy(bf16[128,2048]{0,1:T(8,128)(2,1)S(1)} %fusion.4) | data formatting | bytes 1048576
  (58 shorter events, 10.0 us)
Async XLA Ops:
  0.6 29.8 %copy-start = (bf16[128,2048]{1,0:T(8,128)(2,1)S(1)}, bf16[128,2048]{1,0:T(8,128)(2,1)}, u32[]{:S(2)}) copy-start(bf16[128,2048]{1,0:T(8,128)(2,1)} %param.6) | copy-start | bytes 1572868
  2.2 16.1 %collective-permute-start.3 = (bf16[1,16,2304]{2,1,0:T(8,128)(2,1)S(1)}, bf16[1,16,2304]{2,1,0:T(8,128)(2,1)}, u32[]{:S(2)}, u32[]{:S(2)}) collective-permute-start(bf16[1,16,2304]{2,1,0:T(8,128)(2,1)S(1)} %constant_dynamic-update-slice_fusion), channel_id=1, source_target_pairs={{0,4},{4,0},{8,12},{12,8},{16,20},{20,16},{24,28},{28,24},{1,5},{5... | collective-permute-start | bytes 221192 | tf_op jit(solution)/shard_map/ppermute | solution.py:32
  5.2 17.7 %collective-permute-start.4 = (bf16[1,16,2304]{2,1,0:T(8,128)(2,1)S(1)}, bf16[1,16,2304]{2,1,0:T(8,128)(2,1)}, u32[]{:S(2)}, u32[]{:S(2)}) collective-permute-start(bf16[1,16,2304]{2,1,0:T(8,128)(2,1)S(1)} %constant_dynamic-update-slice_fusion), channel_id=1, source_target_pairs={{0,8},{4,12},{8,0},{12,4},{16,24},{20,28},{24,16},{28,20},{1,9},{5... | collective-permute-start | bytes 221192 | tf_op jit(solution)/shard_map/ppermute | solution.py:32
  6.8 17.1 %collective-permute-start.5 = (bf16[1,16,2304]{2,1,0:T(8,128)(2,1)S(1)}, bf16[1,16,2304]{2,1,0:T(8,128)(2,1)}, u32[]{:S(2)}, u32[]{:S(2)}) collective-permute-start(bf16[1,16,2304]{2,1,0:T(8,128)(2,1)S(1)} %constant_dynamic-update-slice_fusion), channel_id=1, source_target_pairs={{0,12},{4,8},{8,4},{12,0},{16,28},{20,24},{24,20},{28,16},{1,13},{... | collective-permute-start | bytes 221192 | tf_op jit(solution)/shard_map/ppermute | solution.py:32
  6.8 18.0 %collective-permute-start.6 = (bf16[1,16,2304]{2,1,0:T(8,128)(2,1)S(1)}, bf16[1,16,2304]{2,1,0:T(8,128)(2,1)}, u32[]{:S(2)}, u32[]{:S(2)}) collective-permute-start(bf16[1,16,2304]{2,1,0:T(8,128)(2,1)S(1)} %constant_dynamic-update-slice_fusion), channel_id=1, source_target_pairs={{0,16},{4,20},{8,24},{12,28},{16,0},{20,4},{24,8},{28,12},{1,17},{... | collective-permute-start | bytes 221192 | tf_op jit(solution)/shard_map/ppermute | solution.py:32
  9.8 16.5 %collective-permute-start.7 = (bf16[1,16,2304]{2,1,0:T(8,128)(2,1)S(1)}, bf16[1,16,2304]{2,1,0:T(8,128)(2,1)S(1)}, u32[]{:S(2)}, u32[]{:S(2)}) collective-permute-start(bf16[1,16,2304]{2,1,0:T(8,128)(2,1)S(1)} %constant_dynamic-update-slice_fusion), channel_id=1, source_target_pairs={{0,20},{4,16},{8,28},{12,24},{16,4},{20,0},{24,12},{28,8},{1,21},{... | collective-permute-start | bytes 221192 | tf_op jit(solution)/shard_map/ppermute | solution.py:32
  12.7 1.5 %copy-start.1 = (bf16[128,256]{1,0:T(8,128)(2,1)S(1)}, bf16[128,256]{1,0:T(8,128)(2,1)}, u32[]{:S(2)}) copy-start(bf16[128,256]{1,0:T(8,128)(2,1)} %param.7) | copy-start | bytes 196612
  18.3 7.9 %collective-permute-start.8 = (bf16[1,16,2304]{2,1,0:T(8,128)(2,1)S(1)}, bf16[1,16,2304]{2,1,0:T(8,128)(2,1)S(1)}, u32[]{:S(2)}, u32[]{:S(2)}) collective-permute-start(bf16[1,16,2304]{2,1,0:T(8,128)(2,1)S(1)} %constant_dynamic-update-slice_fusion), channel_id=1, source_target_pairs={{0,24},{4,28},{8,16},{12,20},{16,8},{20,12},{24,0},{28,4},{1,25},{... | collective-permute-start | bytes 221192 | tf_op jit(solution)/shard_map/ppermute | solution.py:32
  22.9 7.1 %collective-permute-start.9 = (bf16[1,16,2304]{2,1,0:T(8,128)(2,1)S(1)}, bf16[1,16,2304]{2,1,0:T(8,128)(2,1)S(1)}, u32[]{:S(2)}, u32[]{:S(2)}) collective-permute-start(bf16[1,16,2304]{2,1,0:T(8,128)(2,1)S(1)} %constant_dynamic-update-slice_fusion), channel_id=1, source_target_pairs={{0,28},{4,24},{8,20},{12,16},{16,12},{20,8},{24,4},{28,0},{1,29},{... | collective-permute-start | bytes 221192 | tf_op jit(solution)/shard_map/ppermute | solution.py:32
  23.9 15.8 %collective-permute-start.1 = (bf16[128,256]{1,0:T(8,128)(2,1)S(1)}, bf16[128,256]{1,0:T(8,128)(2,1)S(1)}, u32[]{:S(2)}, u32[]{:S(2)}) collective-permute-start(bf16[128,256]{1,0:T(8,128)(2,1)S(1)} %copy-done.1), channel_id=1, source_target_pairs={{0,1},{1,0},{2,3},{3,2},{4,5},{5,4},{6,7},{7,6},{8,9},{9,8},{10,11... | collective-permute-start | bytes 196616 | tf_op jit(solution)/shard_map/ppermute | solution.py:59
  24.8 14.9 %collective-permute-start = (bf16[2,2048,256]{2,1,0:T(8,128)(2,1)}, bf16[2,2048,256]{2,1,0:T(8,128)(2,1)}, u32[]{:S(2)}, u32[]{:S(2)}) collective-permute-start(bf16[2,2048,256]{2,1,0:T(8,128)(2,1)} %pad_maximum_fusion), channel_id=1, source_target_pairs={{0,1},{1,0},{2,3},{3,2},{4,5},{5,4},{6,7},{7,6},{8,9},{9,8},{10,11... | collective-permute-start | bytes 6291464 | tf_op jit(solution)/shard_map/ppermute | solution.py:58
  30.7 2.1 %collective-permute-start.10 = (f32[1,128,32]{1,2,0:T(8,128)S(1)}, f32[1,128,32]{1,2,0:T(8,128)S(1)}, u32[]{:S(2)}, u32[]{:S(2)}) collective-permute-start(f32[1,128,32]{1,2,0:T(8,128)S(1)} %pad_maximum_fusion.2), channel_id=1, source_target_pairs={{0,1},{1,0},{2,3},{3,2},{4,5},{5,4},{6,7},{7,6},{8,9},{9,8},{10,11... | collective-permute-start | bytes 49160 | tf_op jit(solution)/shard_map/ppermute | solution.py:42
  30.8 3.8 %collective-permute-start.11 = (f32[1,128,32]{1,2,0:T(8,128)S(1)}, f32[1,128,32]{1,2,0:T(8,128)S(1)}, u32[]{:S(2)}, u32[]{:S(2)}) collective-permute-start(f32[1,128,32]{1,2,0:T(8,128)S(1)} %pad_maximum_fusion.2), channel_id=1, source_target_pairs={{0,2},{1,3},{2,0},{3,1},{4,6},{5,7},{6,4},{7,5},{8,10},{9,11},{10,... | collective-permute-start | bytes 49160 | tf_op jit(solution)/shard_map/ppermute | solution.py:42
  32.3 3.2 %collective-permute-start.12 = (f32[1,128,32]{1,2,0:T(8,128)S(1)}, f32[1,128,32]{1,2,0:T(8,128)S(1)}, u32[]{:S(2)}, u32[]{:S(2)}) collective-permute-start(f32[1,128,32]{1,2,0:T(8,128)S(1)} %pad_maximum_fusion.2), channel_id=1, source_target_pairs={{0,3},{1,2},{2,1},{3,0},{4,7},{5,6},{6,5},{7,4},{8,11},{9,10},{10,... | collective-permute-start | bytes 49160 | tf_op jit(solution)/shard_map/ppermute | solution.py:42
  36.1 6.0 %collective-permute-start.13 = (bf16[1,16,2304]{2,1,0:T(8,128)(2,1)S(1)}, bf16[1,16,2304]{2,1,0:T(8,128)(2,1)S(1)}, u32[]{:S(2)}, u32[]{:S(2)}) collective-permute-start(bf16[1,16,2304]{2,1,0:T(8,128)(2,1)S(1)} %get-tuple-element.8), channel_id=1, source_target_pairs={{0,4},{4,0},{8,12},{12,8},{16,20},{20,16},{24,28},{28,24},{1,5},{5... | collective-permute-start | bytes 221192 | tf_op jit(solution)/shard_map/ppermute | solution.py:143
  36.7 8.4 %collective-permute-start.14 = (bf16[1,16,2304]{2,1,0:T(8,128)(2,1)S(1)}, bf16[1,16,2304]{2,1,0:T(8,128)(2,1)S(1)}, u32[]{:S(2)}, u32[]{:S(2)}) collective-permute-start(bf16[1,16,2304]{2,1,0:T(8,128)(2,1)S(1)} %get-tuple-element.13), channel_id=1, source_target_pairs={{0,8},{4,12},{8,0},{12,4},{16,24},{20,28},{24,16},{28,20},{1,9},{5... | collective-permute-start | bytes 221192 | tf_op jit(solution)/shard_map/ppermute | solution.py:143
  36.7 9.5 %collective-permute-start.15 = (bf16[1,16,2304]{2,1,0:T(8,128)(2,1)S(1)}, bf16[1,16,2304]{2,1,0:T(8,128)(2,1)S(1)}, u32[]{:S(2)}, u32[]{:S(2)}) collective-permute-start(bf16[1,16,2304]{2,1,0:T(8,128)(2,1)S(1)} %get-tuple-element.12), channel_id=1, source_target_pairs={{0,12},{4,8},{8,4},{12,0},{16,28},{20,24},{24,20},{28,16},{1,13},{... | collective-permute-start | bytes 221192 | tf_op jit(solution)/shard_map/ppermute | solution.py:143
  39.7 10.5 %collective-permute-start.16 = (bf16[1,16,2304]{2,1,0:T(8,128)(2,1)S(1)}, bf16[1,16,2304]{2,1,0:T(8,128)(2,1)S(1)}, u32[]{:S(2)}, u32[]{:S(2)}) collective-permute-start(bf16[1,16,2304]{2,1,0:T(8,128)(2,1)S(1)} %get-tuple-element.11), channel_id=1, source_target_pairs={{0,16},{4,20},{8,24},{12,28},{16,0},{20,4},{24,8},{28,12},{1,17},{... | collective-permute-start | bytes 221192 | tf_op jit(solution)/shard_map/ppermute | solution.py:143
  41.4 24.5 %collective-permute-start.2 = (f32[128,2048]{0,1:T(8,128)S(1)}, f32[128,2048]{0,1:T(8,128)S(1)}, u32[]{:S(2)}, u32[]{:S(2)}) collective-permute-start(f32[128,2048]{0,1:T(8,128)S(1)} %fusion), channel_id=1, source_target_pairs={{0,2},{1,3},{2,0},{3,1},{4,6},{5,7},{6,4},{7,5},{8,10},{9,11},{10,... | collective-permute-start | bytes 3145736 | tf_op jit(solution)/shard_map/ppermute | solution.py:72
  42.2 10.2 %collective-permute-start.17 = (bf16[1,16,2304]{2,1,0:T(8,128)(2,1)S(1)}, bf16[1,16,2304]{2,1,0:T(8,128)(2,1)S(1)}, u32[]{:S(2)}, u32[]{:S(2)}) collective-permute-start(bf16[1,16,2304]{2,1,0:T(8,128)(2,1)S(1)} %get-tuple-element.10), channel_id=1, source_target_pairs={{0,20},{4,16},{8,28},{12,24},{16,4},{20,0},{24,12},{28,8},{1,21},{... | collective-permute-start | bytes 221192 | tf_op jit(solution)/shard_map/ppermute | solution.py:143
  45.1 7.3 %collective-permute-start.18 = (bf16[1,16,2304]{2,1,0:T(8,128)(2,1)S(1)}, bf16[1,16,2304]{2,1,0:T(8,128)(2,1)S(1)}, u32[]{:S(2)}, u32[]{:S(2)}) collective-permute-start(bf16[1,16,2304]{2,1,0:T(8,128)(2,1)S(1)} %get-tuple-element.9), channel_id=1, source_target_pairs={{0,24},{4,28},{8,16},{12,20},{16,8},{20,12},{24,0},{28,4},{1,25},{... | collective-permute-start | bytes 221192 | tf_op jit(solution)/shard_map/ppermute | solution.py:143
  46.2 7.1 %collective-permute-start.19 = (bf16[1,16,2304]{2,1,0:T(8,128)(2,1)S(1)}, bf16[1,16,2304]{2,1,0:T(8,128)(2,1)S(1)}, u32[]{:S(2)}, u32[]{:S(2)}) collective-permute-start(bf16[1,16,2304]{2,1,0:T(8,128)(2,1)S(1)} %fusion.32), channel_id=1, source_target_pairs={{0,28},{4,24},{8,20},{12,16},{16,12},{20,8},{24,4},{28,0},{1,29},{... | collective-permute-start | bytes 221192 | tf_op jit(solution)/shard_map/ppermute | solution.py:143

commit v5 on v3

--- a/solution.py
+++ b/solution.py
@@ -43,12 +43,12 @@
     return total
 
 
-def _frozen_term(cotangent, weight, axis, size):
+def _frozen_term(cotangent, weight, axis, size, ready=None):
     if size & (size - 1) != 0:
         partial = lax.dot_general(
             cotangent, weight, (((1,), (1,)), ((), ())), preferred_element_type=jnp.float32
         )
-        return lax.psum_scatter(partial, axis, scatter_dimension=1, tiled=True)
+        return lax.psum_scatter(partial, axis, scatter_dimension=1, tiled=True), ready
     me = lax.axis_index(axis)
     rows = weight.shape[0] // size
 
@@ -61,12 +61,14 @@
     held = [term(me ^ e) for e in range(size)]
     step = 0
     while len(held) > 1:
+        if step == 1 and ready is not None:
+            *held, ready = lax.optimization_barrier((*held, ready))
         partner = 1 << step
         pairs = [(i, i ^ partner) for i in range(size)]
         got = [lax.ppermute(held[e], axis, pairs) for e in range(1, len(held), 2)]
         held = [held[e] + g for e, g in zip(range(0, len(held), 2), got)]
         step += 1
-    return held[0]
+    return held[0], ready
 
 
 def on_device(
@@ -83,7 +85,6 @@
     tenant_number = dp_size * held_tenants
     me_dp = lax.axis_index("dp")
 
-    base_grad = _frozen_term(cotangent, frozen_key_weight, "tensor", tensor_size)
 
     packed = jnp.concatenate([adapter_down_weight, adapter_up_weight], axis=2)
     stacked, order = _gather_dp(packed, "dp", dp_size)
@@ -103,7 +104,9 @@
     reduced_output = ADAPTER_SCALE * jnp.einsum(
         "bnk,brk->bnr", cotangent_blocks, sel_up, preferred_element_type=jnp.float32
     )
-    lows = _psum_small(jnp.concatenate([low_in, reduced_output], axis=2), "tensor", tensor_size)
+    lows = jnp.concatenate([low_in, reduced_output], axis=2)
+    base_grad, lows = _frozen_term(cotangent, frozen_key_weight, "tensor", tensor_size, lows)
+    lows = _psum_small(lows, "tensor", tensor_size)
     reduced_input_batch = lows[:, :, :adapter_rank_size].astype(jnp.bfloat16)
     low_out_b = lows[:, :, adapter_rank_size:].astype(jnp.bfloat16)
 

time: 66.3 us -> 62.6 us (0.944)
  waiting for transfers between devices: 21.6 us -> 15.6 us
  local copies, waits for them, and re-layouts: 5.38 us -> 8.15 us
  matrix products: 12.4 us -> 10.3 us
  starting transfers between devices: 24.9 us -> 26.4 us
    unnamed x15 -> x17, local copies, waits for them, and re-layouts: 2.48 us -> 5.22 us
    dot_general x4, matrix products: 10.2 us -> 7.65 us  [term(): lax.dot_general(cotangent, piece, (((1,), (1,)), ((), ())), preferred_ele...]
    ppermute x3, waiting for transfers between devices: 5.49 us -> 3.13 us  [_frozen_term(): got = [lax.ppermute(held[e], axis, pairs) for e in range(1, len(held), 2)]]
    ppermute x7, waiting for transfers between devices: 6.34 us -> 4.58 us  [_gather_dp(): got.append(lax.ppermute(local, axis, pairs))]
    ppermute x3, waiting for transfers between devices: 1.77 us -> 0.21 us  [_psum_small(): total = total + lax.ppermute(value, axis, pairs)]
    ppermute x7, starting transfers between devices: 8.32 us -> 9.81 us  [on_device(): lax.ppermute(outgoing.astype(jnp.bfloat16), 'dp', pairs).astype(jnp.float32)]
  transfers between devices with their start and end apart: 20 -> 20, of which waited for: 9 -> 7; matrix products, arithmetic and copies ran while one was open for 20% -> 18% of each run, Pallas kernels for 0% -> 0%
where the time goes in v5:
time: 62.6 us; the launch traced here: 62.2 us
  starting transfers between devices  26.4 us (42%)
  waiting for transfers between devices  15.6 us (25%)
  matrix products  10.3 us (16%)
  local copies, waits for them, and re-layouts  8.15 us (13%)
  between operations  1.52 us (2%)
    ppermute x7, starting transfers between devices, _gather_dp(): got.append(lax.ppermute(local, axis, pairs))  12.5 us
    ppermute x7, starting transfers between devices, on_device(): lax.ppermute(outgoing.astype(jnp.bfloat16), 'dp', pairs).astype(jnp.float32)  9.81 us
    dot_general x4, matrix products, term(): lax.dot_general(cotangent, piece, (((1,), (1,)), ((), ())), preferred_ele...  7.65 us
    ppermute x7, waiting for transfers between devices, on_device(): lax.ppermute(outgoing.astype(jnp.bfloat16), 'dp', pairs).astype(jnp.float32)  7.64 us
    unnamed x17, local copies, waits for them, and re-layouts  5.22 us
    ppermute x7, waiting for transfers between devices, _gather_dp(): got.append(lax.ppermute(local, axis, pairs))  4.58 us
    ppermute x3, waiting for transfers between devices, _frozen_term(): got = [lax.ppermute(held[e], axis, pairs) for e in range(1, len(held), 2)]  3.13 us
    ppermute x3, starting transfers between devices, _frozen_term(): got = [lax.ppermute(held[e], axis, pairs) for e in range(1, len(held), 2)]  2.15 us
  transfers between devices with their start and end apart: 20, of which 7 were waited for; matrix products, arithmetic and copies ran while one was open for 18% of the time, Pallas kernels for 0%

profile of v5, /device:TPU:0, one launch (start us, length us, event | category | flops | bytes accessed | tf_op | source)
XLA Modules:
  0.0 62.2 jit_solution(8833273382753374431)
XLA Ops:
  0.7 0.9 %constant_dynamic-update-slice_fusion.1 = bf16[1,16,2304]{2,1,0:T(8,128)(2,1)S(1)} fusion(bf16[1,16,2048]{2,1,0:T(8,128)(2,1)} %param.9), kind=kLoop, calls=%fused_computation.64 | loop fusion | bytes 131072
  2.3 3.0 %collective-permute-start.2 = (bf16[1,16,2304]{2,1,0:T(8,128)(2,1)S(1)}, bf16[1,16,2304]{2,1,0:T(8,128)(2,1)}, u32[]{:S(2)}, u32[]{:S(2)}) collective-permute-start(bf16[1,16,2304]{2,1,0:T(8,128)(2,1)S(1)} %constant_dynamic-update-slice_fusion), channel_id=1, source_target_pairs={{0,4},{4,0},{8,12},{12,8},{16,20},{20,16},{24,28},{28,24},{1,5},{5... | collective-permute-start | bytes 221192 | tf_op jit(solution)/shard_map/ppermute | solution.py:32
  5.2 1.6 %collective-permute-start.3 = (bf16[1,16,2304]{2,1,0:T(8,128)(2,1)S(1)}, bf16[1,16,2304]{2,1,0:T(8,128)(2,1)}, u32[]{:S(2)}, u32[]{:S(2)}) collective-permute-start(bf16[1,16,2304]{2,1,0:T(8,128)(2,1)S(1)} %constant_dynamic-update-slice_fusion), channel_id=1, source_target_pairs={{0,8},{4,12},{8,0},{12,4},{16,24},{20,28},{24,16},{28,20},{1,9},{5... | collective-permute-start | bytes 221192 | tf_op jit(solution)/shard_map/ppermute | solution.py:32
  6.8 3.0 %collective-permute-start.5 = (bf16[1,16,2304]{2,1,0:T(8,128)(2,1)S(1)}, bf16[1,16,2304]{2,1,0:T(8,128)(2,1)S(1)}, u32[]{:S(2)}, u32[]{:S(2)}) collective-permute-start(bf16[1,16,2304]{2,1,0:T(8,128)(2,1)S(1)} %constant_dynamic-update-slice_fusion), channel_id=1, source_target_pairs={{0,16},{4,20},{8,24},{12,28},{16,0},{20,4},{24,8},{28,12},{1,17},{... | collective-permute-start | bytes 221192 | tf_op jit(solution)/shard_map/ppermute | solution.py:32
  9.8 1.3 %collective-permute-start.6 = (bf16[1,16,2304]{2,1,0:T(8,128)(2,1)S(1)}, bf16[1,16,2304]{2,1,0:T(8,128)(2,1)S(1)}, u32[]{:S(2)}, u32[]{:S(2)}) collective-permute-start(bf16[1,16,2304]{2,1,0:T(8,128)(2,1)S(1)} %constant_dynamic-update-slice_fusion), channel_id=1, source_target_pairs={{0,20},{4,16},{8,28},{12,24},{16,4},{20,0},{24,12},{28,8},{1,21},{... | collective-permute-start | bytes 221192 | tf_op jit(solution)/shard_map/ppermute | solution.py:32
  11.1 1.6 %convolution_bitcast_fusion.3 = f32[128,2048]{0,1:T(8,128)S(1)} fusion(bf16[128,256]{1,0:T(8,128)(2,1)} %param.7, bf16[8192,256]{1,0:T(8,128)(2,1)} %param.8, s32[]{:T(128)S(6)} %select_n.46), kind=kOutput, calls=%fused_computation.3 | convolution fusion | flops 134217728 | bytes 2162692 | tf_op jit(solution)/shard_map/dot_general | solution.py:57
  12.8 1.7 %convolution_bitcast_fusion.1 = f32[128,2048]{0,1:T(8,128)S(1)} fusion(bf16[128,256]{1,0:T(8,128)(2,1)} %param.7, bf16[8192,256]{1,0:T(8,128)(2,1)} %param.8, s32[]{:T(128)S(6)} %select_n.48), kind=kOutput, calls=%fused_computation.1 | convolution fusion | flops 134217728 | bytes 2162692 | tf_op jit(solution)/shard_map/dot_general | solution.py:57
  15.2 3.7 %collective-permute-start.7 = (bf16[1,16,2304]{2,1,0:T(8,128)(2,1)S(1)}, bf16[1,16,2304]{2,1,0:T(8,128)(2,1)S(1)}, u32[]{:S(2)}, u32[]{:S(2)}) collective-permute-start(bf16[1,16,2304]{2,1,0:T(8,128)(2,1)S(1)} %constant_dynamic-update-slice_fusion), channel_id=1, source_target_pairs={{0,24},{4,28},{8,16},{12,20},{16,8},{20,12},{24,0},{28,4},{1,25},{... | collective-permute-start | bytes 221192 | tf_op jit(solution)/shard_map/ppermute | solution.py:32
  20.8 0.9 %bitcast_dynamic-update-slice_fusion.4 = bf16[8,1,16,2304]{3,2,1,0:T(8,128)(2,1)S(1)} fusion(bf16[8,1,16,2304]{3,2,1,0:T(8,128)(2,1)S(1)} %bitcast_dynamic-update-slice_fusion.5, bf16[1,16,2304]{2,1,0:T(8,128)(2,1)} %collective-permute-done.4), kind=kLoop, calls=%fused_computation.54 | loop fusion | bytes 147456
  22.3 4.6 %collective-permute-done.8 = bf16[1,16,2304]{2,1,0:T(8,128)(2,1)S(1)} collective-permute-done((bf16[1,16,2304]{2,1,0:T(8,128)(2,1)S(1)}, bf16[1,16,2304]{2,1,0:T(8,128)(2,1)S(1)}, u32[]{:S(2)}, u32[]{:S(2)}) %collective-permute-start.8) | collective-permute-done | bytes 73760 | tf_op jit(solution)/shard_map/ppermute | solution.py:32
  27.6 1.7 %fusion = f32[128,2048]{0,1:T(8,128)S(1)} fusion(f32[128,2048]{0,1:T(8,128)S(1)} %collective-permute-done, bf16[128,256]{1,0:T(8,128)(2,1)S(1)} %copy-done.1, bf16[8192,256]{1,0:T(8,128)(2,1)} %param.8, s32[]{:T(128)S(6)} %select_n.45), kind=kOutput, calls=%fused_computation.5 | convolution fusion | flops 134479872 | bytes 3211268 | tf_op jit(solution)/shard_map/dot_general | solution.py:57
  29.3 2.7 %fusion.1 = f32[128,2048]{0,1:T(8,128)} fusion(f32[128,2048]{0,1:T(8,128)S(1)} %collective-permute-done.1, bf16[128,256]{1,0:T(8,128)(2,1)S(1)} %copy-done.1, bf16[8192,256]{1,0:T(8,128)(2,1)} %param.8, s32[]{:T(128)S(6)} %select_n.47), kind=kOutput, calls=%fused_computation.6 | convolution fusion | flops 134479872 | bytes 3211268 | tf_op jit(solution)/shard_map/dot_general | solution.py:57
  32.0 1.5 %collective-permute-start.11 = (f32[1,128,32]{1,2,0:T(8,128)S(1)}, f32[1,128,32]{1,2,0:T(8,128)S(1)}, u32[]{:S(2)}, u32[]{:S(2)}) collective-permute-start(f32[1,128,32]{1,2,0:T(8,128)S(1)} %pad_maximum_fusion.1), channel_id=1, source_target_pairs={{0,2},{1,3},{2,0},{3,1},{4,6},{5,7},{6,4},{7,5},{8,10},{9,11},{10,... | collective-permute-start | bytes 49160 | tf_op jit(solution)/shard_map/ppermute | solution.py:42
  34.0 1.5 %collective-permute-start.9 = (f32[128,2048]{0,1:T(8,128)}, f32[128,2048]{0,1:T(8,128)}, u32[]{:S(2)}, u32[]{:S(2)}) collective-permute-start(f32[128,2048]{0,1:T(8,128)} %fusion.1), channel_id=1, source_target_pairs={{0,2},{1,3},{2,0},{3,1},{4,6},{5,7},{6,4},{7,5},{8,10},{9,11},{10,... | collective-permute-start | bytes 3145736 | tf_op jit(solution)/shard_map/ppermute | solution.py:68
  37.0 1.8 %collective-permute-start.19 = (bf16[1,16,2304]{2,1,0:T(8,128)(2,1)S(1)}, bf16[1,16,2304]{2,1,0:T(8,128)(2,1)S(1)}, u32[]{:S(2)}, u32[]{:S(2)}) collective-permute-start(bf16[1,16,2304]{2,1,0:T(8,128)(2,1)S(1)} %fusion.29), channel_id=1, source_target_pairs={{0,28},{4,24},{8,20},{12,16},{16,12},{20,8},{24,4},{28,0},{1,29},{... | collective-permute-start | bytes 221192 | tf_op jit(solution)/shard_map/ppermute | solution.py:140
  39.5 2.0 %collective-permute-start.18 = (bf16[1,16,2304]{2,1,0:T(8,128)(2,1)S(1)}, bf16[1,16,2304]{2,1,0:T(8,128)(2,1)S(1)}, u32[]{:S(2)}, u32[]{:S(2)}) collective-permute-start(bf16[1,16,2304]{2,1,0:T(8,128)(2,1)S(1)} %get-tuple-element.13), channel_id=1, source_target_pairs={{0,24},{4,28},{8,16},{12,20},{16,8},{20,12},{24,0},{28,4},{1,25},{... | collective-permute-start | bytes 221192 | tf_op jit(solution)/shard_map/ppermute | solution.py:140
  41.5 3.9 %collective-permute-start.16 = (bf16[1,16,2304]{2,1,0:T(8,128)(2,1)}, bf16[1,16,2304]{2,1,0:T(8,128)(2,1)S(1)}, u32[]{:S(2)}, u32[]{:S(2)}) collective-permute-start(bf16[1,16,2304]{2,1,0:T(8,128)(2,1)} %get-tuple-element.15), channel_id=1, source_target_pairs={{0,16},{4,20},{8,24},{12,28},{16,0},{20,4},{24,8},{28,12},{1,17},{... | collective-permute-start | bytes 221192 | tf_op jit(solution)/shard_map/ppermute | solution.py:140
  45.8 1.6 %collective-permute-start.14 = (bf16[1,16,2304]{2,1,0:T(8,128)(2,1)S(1)}, bf16[1,16,2304]{2,1,0:T(8,128)(2,1)S(1)}, u32[]{:S(2)}, u32[]{:S(2)}) collective-permute-start(bf16[1,16,2304]{2,1,0:T(8,128)(2,1)S(1)} %get-tuple-element.17), channel_id=1, source_target_pairs={{0,8},{4,12},{8,0},{12,4},{16,24},{20,28},{24,16},{28,20},{1,9},{5... | collective-permute-start | bytes 221192 | tf_op jit(solution)/shard_map/ppermute | solution.py:140
  47.3 3.4 %collective-permute-done.17 = bf16[1,16,2304]{2,1,0:T(8,128)(2,1)S(1)} collective-permute-done((bf16[1,16,2304]{2,1,0:T(8,128)(2,1)S(1)}, bf16[1,16,2304]{2,1,0:T(8,128)(2,1)S(1)}, u32[]{:S(2)}, u32[]{:S(2)}) %collective-permute-start.17) | collective-permute-done | bytes 73760 | tf_op jit(solution)/shard_map/ppermute | solution.py:140
  51.3 2.4 %collective-permute-done.15 = bf16[1,16,2304]{2,1,0:T(8,128)(2,1)S(1)} collective-permute-done((bf16[1,16,2304]{2,1,0:T(8,128)(2,1)}, bf16[1,16,2304]{2,1,0:T(8,128)(2,1)S(1)}, u32[]{:S(2)}, u32[]{:S(2)}) %collective-permute-start.15) | collective-permute-done | bytes 73760 | tf_op jit(solution)/shard_map/ppermute | solution.py:140
  53.7 1.4 %collective-permute-done.13 = bf16[1,16,2304]{2,1,0:T(8,128)(2,1)S(1)} collective-permute-done((bf16[1,16,2304]{2,1,0:T(8,128)(2,1)S(1)}, bf16[1,16,2304]{2,1,0:T(8,128)(2,1)S(1)}, u32[]{:S(2)}, u32[]{:S(2)}) %collective-permute-start.13) | collective-permute-done | bytes 73760 | tf_op jit(solution)/shard_map/ppermute | solution.py:140
  56.5 3.1 %collective-permute-done.9 = f32[128,2048]{0,1:T(8,128)} collective-permute-done((f32[128,2048]{0,1:T(8,128)}, f32[128,2048]{0,1:T(8,128)}, u32[]{:S(2)}, u32[]{:S(2)}) %collective-permute-start.9) | collective-permute-done | bytes 1048608 | tf_op jit(solution)/shard_map/ppermute | solution.py:68
  59.6 1.6 %add_convert_fusion = bf16[128,2048]{0,1:T(8,128)(2,1)S(1)} fusion(f32[128,2048]{0,1:T(8,128)S(1)} %fusion, f32[128,2048]{0,1:T(8,128)} %collective-permute-done.9, bf16[1,16,2304]{2,1,0:T(8,128)(2,1)S(1)} %copy.25, bf16[1,128,32]{1,2,0:T(8,128)(2,1)S(1)} %copy-done.3), kind=kOutput, calls=%fused_computation.17 | convolution fusion | flops 9175040 | bytes 2691072 | tf_op jit(solution)/shard_map/bnr,brd->bnd/dot_general | solution.py:113
  61.2 1.0 %copy.16 = bf16[128,2048]{1,0:T(8,128)(2,1)} copy(bf16[128,2048]{0,1:T(8,128)(2,1)S(1)} %add_convert_fusion) | data formatting | bytes 1048576
  (60 shorter events, 8.9 us)
Async XLA Ops:
  0.6 26.7 %copy-start = (bf16[128,2048]{1,0:T(8,128)(2,1)S(1)}, bf16[128,2048]{1,0:T(8,128)(2,1)}, u32[]{:S(2)}) copy-start(bf16[128,2048]{1,0:T(8,128)(2,1)} %param.6) | copy-start | bytes 1572868
  0.6 26.5 %copy-start.1 = (bf16[128,256]{1,0:T(8,128)(2,1)S(1)}, bf16[128,256]{1,0:T(8,128)(2,1)}, u32[]{:S(2)}) copy-start(bf16[128,256]{1,0:T(8,128)(2,1)} %param.7) | copy-start | bytes 196612
  2.3 12.9 %collective-permute-start.2 = (bf16[1,16,2304]{2,1,0:T(8,128)(2,1)S(1)}, bf16[1,16,2304]{2,1,0:T(8,128)(2,1)}, u32[]{:S(2)}, u32[]{:S(2)}) collective-permute-start(bf16[1,16,2304]{2,1,0:T(8,128)(2,1)S(1)} %constant_dynamic-update-slice_fusion), channel_id=1, source_target_pairs={{0,4},{4,0},{8,12},{12,8},{16,20},{20,16},{24,28},{28,24},{1,5},{5... | collective-permute-start | bytes 221192 | tf_op jit(solution)/shard_map/ppermute | solution.py:32
  5.2 14.5 %collective-permute-start.3 = (bf16[1,16,2304]{2,1,0:T(8,128)(2,1)S(1)}, bf16[1,16,2304]{2,1,0:T(8,128)(2,1)}, u32[]{:S(2)}, u32[]{:S(2)}) collective-permute-start(bf16[1,16,2304]{2,1,0:T(8,128)(2,1)S(1)} %constant_dynamic-update-slice_fusion), channel_id=1, source_target_pairs={{0,8},{4,12},{8,0},{12,4},{16,24},{20,28},{24,16},{28,20},{1,9},{5... | collective-permute-start | bytes 221192 | tf_op jit(solution)/shard_map/ppermute | solution.py:32
  6.8 13.9 %collective-permute-start.4 = (bf16[1,16,2304]{2,1,0:T(8,128)(2,1)S(1)}, bf16[1,16,2304]{2,1,0:T(8,128)(2,1)}, u32[]{:S(2)}, u32[]{:S(2)}) collective-permute-start(bf16[1,16,2304]{2,1,0:T(8,128)(2,1)S(1)} %constant_dynamic-update-slice_fusion), channel_id=1, source_target_pairs={{0,12},{4,8},{8,4},{12,0},{16,28},{20,24},{24,20},{28,16},{1,13},{... | collective-permute-start | bytes 221192 | tf_op jit(solution)/shard_map/ppermute | solution.py:32
  6.8 14.8 %collective-permute-start.5 = (bf16[1,16,2304]{2,1,0:T(8,128)(2,1)S(1)}, bf16[1,16,2304]{2,1,0:T(8,128)(2,1)S(1)}, u32[]{:S(2)}, u32[]{:S(2)}) collective-permute-start(bf16[1,16,2304]{2,1,0:T(8,128)(2,1)S(1)} %constant_dynamic-update-slice_fusion), channel_id=1, source_target_pairs={{0,16},{4,20},{8,24},{12,28},{16,0},{20,4},{24,8},{28,12},{1,17},{... | collective-permute-start | bytes 221192 | tf_op jit(solution)/shard_map/ppermute | solution.py:32
  9.8 12.4 %collective-permute-start.6 = (bf16[1,16,2304]{2,1,0:T(8,128)(2,1)S(1)}, bf16[1,16,2304]{2,1,0:T(8,128)(2,1)S(1)}, u32[]{:S(2)}, u32[]{:S(2)}) collective-permute-start(bf16[1,16,2304]{2,1,0:T(8,128)(2,1)S(1)} %constant_dynamic-update-slice_fusion), channel_id=1, source_target_pairs={{0,20},{4,16},{8,28},{12,24},{16,4},{20,0},{24,12},{28,8},{1,21},{... | collective-permute-start | bytes 221192 | tf_op jit(solution)/shard_map/ppermute | solution.py:32
  15.2 7.1 %collective-permute-start.7 = (bf16[1,16,2304]{2,1,0:T(8,128)(2,1)S(1)}, bf16[1,16,2304]{2,1,0:T(8,128)(2,1)S(1)}, u32[]{:S(2)}, u32[]{:S(2)}) collective-permute-start(bf16[1,16,2304]{2,1,0:T(8,128)(2,1)S(1)} %constant_dynamic-update-slice_fusion), channel_id=1, source_target_pairs={{0,24},{4,28},{8,16},{12,20},{16,8},{20,12},{24,0},{28,4},{1,25},{... | collective-permute-start | bytes 221192 | tf_op jit(solution)/shard_map/ppermute | solution.py:32
  19.7 7.1 %collective-permute-start.8 = (bf16[1,16,2304]{2,1,0:T(8,128)(2,1)S(1)}, bf16[1,16,2304]{2,1,0:T(8,128)(2,1)S(1)}, u32[]{:S(2)}, u32[]{:S(2)}) collective-permute-start(bf16[1,16,2304]{2,1,0:T(8,128)(2,1)S(1)} %constant_dynamic-update-slice_fusion), channel_id=1, source_target_pairs={{0,28},{4,24},{8,20},{12,16},{16,12},{20,8},{24,4},{28,0},{1,29},{... | collective-permute-start | bytes 221192 | tf_op jit(solution)/shard_map/ppermute | solution.py:32
  20.7 6.9 %collective-permute-start = (f32[128,2048]{0,1:T(8,128)S(1)}, f32[128,2048]{0,1:T(8,128)S(1)}, u32[]{:S(2)}, u32[]{:S(2)}) collective-permute-start(f32[128,2048]{0,1:T(8,128)S(1)} %convolution_bitcast_fusion.3), channel_id=1, source_target_pairs={{0,1},{1,0},{2,3},{3,2},{4,5},{5,4},{6,7},{7,6},{8,9},{9,8},{10,11... | collective-permute-start | bytes 3145736 | tf_op jit(solution)/shard_map/ppermute | solution.py:68
  21.7 7.6 %collective-permute-start.1 = (f32[128,2048]{0,1:T(8,128)S(1)}, f32[128,2048]{0,1:T(8,128)S(1)}, u32[]{:S(2)}, u32[]{:S(2)}) collective-permute-start(f32[128,2048]{0,1:T(8,128)S(1)} %convolution_bitcast_fusion.1), channel_id=1, source_target_pairs={{0,1},{1,0},{2,3},{3,2},{4,5},{5,4},{6,7},{7,6},{8,9},{9,8},{10,11... | collective-permute-start | bytes 3145736 | tf_op jit(solution)/shard_map/ppermute | solution.py:68
  32.0 3.6 %collective-permute-start.12 = (f32[1,128,32]{1,2,0:T(8,128)S(1)}, f32[1,128,32]{1,2,0:T(8,128)S(1)}, u32[]{:S(2)}, u32[]{:S(2)}) collective-permute-start(f32[1,128,32]{1,2,0:T(8,128)S(1)} %pad_maximum_fusion.1), channel_id=1, source_target_pairs={{0,3},{1,2},{2,1},{3,0},{4,7},{5,6},{6,5},{7,4},{8,11},{9,10},{10,... | collective-permute-start | bytes 49160 | tf_op jit(solution)/shard_map/ppermute | solution.py:42
  32.0 3.8 %collective-permute-start.11 = (f32[1,128,32]{1,2,0:T(8,128)S(1)}, f32[1,128,32]{1,2,0:T(8,128)S(1)}, u32[]{:S(2)}, u32[]{:S(2)}) collective-permute-start(f32[1,128,32]{1,2,0:T(8,128)S(1)} %pad_maximum_fusion.1), channel_id=1, source_target_pairs={{0,2},{1,3},{2,0},{3,1},{4,6},{5,7},{6,4},{7,5},{8,10},{9,11},{10,... | collective-permute-start | bytes 49160 | tf_op jit(solution)/shard_map/ppermute | solution.py:42
  33.5 2.3 %collective-permute-start.10 = (f32[1,128,32]{1,2,0:T(8,128)S(1)}, f32[1,128,32]{1,2,0:T(8,128)S(1)}, u32[]{:S(2)}, u32[]{:S(2)}) collective-permute-start(f32[1,128,32]{1,2,0:T(8,128)S(1)} %pad_maximum_fusion.1), channel_id=1, source_target_pairs={{0,1},{1,0},{2,3},{3,2},{4,5},{5,4},{6,7},{7,6},{8,9},{9,8},{10,11... | collective-permute-start | bytes 49160 | tf_op jit(solution)/shard_map/ppermute | solution.py:42
  34.0 25.6 %collective-permute-start.9 = (f32[128,2048]{0,1:T(8,128)}, f32[128,2048]{0,1:T(8,128)}, u32[]{:S(2)}, u32[]{:S(2)}) collective-permute-start(f32[128,2048]{0,1:T(8,128)} %fusion.1), channel_id=1, source_target_pairs={{0,2},{1,3},{2,0},{3,1},{4,6},{5,7},{6,4},{7,5},{8,10},{9,11},{10,... | collective-permute-start | bytes 3145736 | tf_op jit(solution)/shard_map/ppermute | solution.py:68
  35.7 0.6 copy-start.2
  36.9 22.7 %copy-start.3 = (bf16[1,128,32]{1,2,0:T(8,128)(2,1)S(1)}, bf16[1,128,32]{1,2,0:T(8,128)(2,1)}, u32[]{:S(2)}) copy-start(bf16[1,128,32]{1,2,0:T(8,128)(2,1)} %copy-done.2) | copy-start | bytes 24580
  37.0 8.4 %collective-permute-start.19 = (bf16[1,16,2304]{2,1,0:T(8,128)(2,1)S(1)}, bf16[1,16,2304]{2,1,0:T(8,128)(2,1)S(1)}, u32[]{:S(2)}, u32[]{:S(2)}) collective-permute-start(bf16[1,16,2304]{2,1,0:T(8,128)(2,1)S(1)} %fusion.29), channel_id=1, source_target_pairs={{0,28},{4,24},{8,20},{12,16},{16,12},{20,8},{24,4},{28,0},{1,29},{... | collective-permute-start | bytes 221192 | tf_op jit(solution)/shard_map/ppermute | solution.py:140
  39.5 6.3 %collective-permute-start.18 = (bf16[1,16,2304]{2,1,0:T(8,128)(2,1)S(1)}, bf16[1,16,2304]{2,1,0:T(8,128)(2,1)S(1)}, u32[]{:S(2)}, u32[]{:S(2)}) collective-permute-start(bf16[1,16,2304]{2,1,0:T(8,128)(2,1)S(1)} %get-tuple-element.13), channel_id=1, source_target_pairs={{0,24},{4,28},{8,16},{12,20},{16,8},{20,12},{24,0},{28,4},{1,25},{... | collective-permute-start | bytes 221192 | tf_op jit(solution)/shard_map/ppermute | solution.py:140
  41.5 9.3 %collective-permute-start.17 = (bf16[1,16,2304]{2,1,0:T(8,128)(2,1)S(1)}, bf16[1,16,2304]{2,1,0:T(8,128)(2,1)S(1)}, u32[]{:S(2)}, u32[]{:S(2)}) collective-permute-start(bf16[1,16,2304]{2,1,0:T(8,128)(2,1)S(1)} %get-tuple-element.14), channel_id=1, source_target_pairs={{0,20},{4,16},{8,28},{12,24},{16,4},{20,0},{24,12},{28,8},{1,21},{... | collective-permute-start | bytes 221192 | tf_op jit(solution)/shard_map/ppermute | solution.py:140
  41.5 9.8 %collective-permute-start.16 = (bf16[1,16,2304]{2,1,0:T(8,128)(2,1)}, bf16[1,16,2304]{2,1,0:T(8,128)(2,1)S(1)}, u32[]{:S(2)}, u32[]{:S(2)}) collective-permute-start(bf16[1,16,2304]{2,1,0:T(8,128)(2,1)} %get-tuple-element.15), channel_id=1, source_target_pairs={{0,16},{4,20},{8,24},{12,28},{16,0},{20,4},{24,8},{28,12},{1,17},{... | collective-permute-start | bytes 221192 | tf_op jit(solution)/shard_map/ppermute | solution.py:140
  45.4 8.3 %collective-permute-start.15 = (bf16[1,16,2304]{2,1,0:T(8,128)(2,1)}, bf16[1,16,2304]{2,1,0:T(8,128)(2,1)S(1)}, u32[]{:S(2)}, u32[]{:S(2)}) collective-permute-start(bf16[1,16,2304]{2,1,0:T(8,128)(2,1)} %get-tuple-element.16), channel_id=1, source_target_pairs={{0,12},{4,8},{8,4},{12,0},{16,28},{20,24},{24,20},{28,16},{1,13},{... | collective-permute-start | bytes 221192 | tf_op jit(solution)/shard_map/ppermute | solution.py:140
  45.8 7.9 %collective-permute-start.14 = (bf16[1,16,2304]{2,1,0:T(8,128)(2,1)S(1)}, bf16[1,16,2304]{2,1,0:T(8,128)(2,1)S(1)}, u32[]{:S(2)}, u32[]{:S(2)}) collective-permute-start(bf16[1,16,2304]{2,1,0:T(8,128)(2,1)S(1)} %get-tuple-element.17), channel_id=1, source_target_pairs={{0,8},{4,12},{8,0},{12,4},{16,24},{20,28},{24,16},{28,20},{1,9},{5... | collective-permute-start | bytes 221192 | tf_op jit(solution)/shard_map/ppermute | solution.py:140
  50.8 4.4 %collective-permute-start.13 = (bf16[1,16,2304]{2,1,0:T(8,128)(2,1)S(1)}, bf16[1,16,2304]{2,1,0:T(8,128)(2,1)S(1)}, u32[]{:S(2)}, u32[]{:S(2)}) collective-permute-start(bf16[1,16,2304]{2,1,0:T(8,128)(2,1)S(1)} %get-tuple-element.12), channel_id=1, source_target_pairs={{0,4},{4,0},{8,12},{12,8},{16,20},{20,16},{24,28},{28,24},{1,5},{5... | collective-permute-start | bytes 221192 | tf_op jit(solution)/shard_map/ppermute | solution.py:140

commit v6 on v5

--- a/solution.py
+++ b/solution.py
@@ -37,9 +37,16 @@
 
 
 def _psum_small(value, axis, size):
+    if size & (size - 1) != 0:
+        total = value
+        for _, pairs in _partners(size):
+            total = total + lax.ppermute(value, axis, pairs)
+        return total
     total = value
-    for _, pairs in _partners(size):
-        total = total + lax.ppermute(value, axis, pairs)
+    step = 1
+    while step < size:
+        total = total + lax.ppermute(total, axis, [(i, i ^ step) for i in range(size)])
+        step *= 2
     return total
 
 
@@ -62,7 +69,8 @@
     step = 0
     while len(held) > 1:
         if step == 1 and ready is not None:
-            *held, ready = lax.optimization_barrier((*held, ready))
+            *leaving, ready = lax.optimization_barrier((*held[1::2], ready))
+            held[1::2] = leaving
         partner = 1 << step
         pairs = [(i, i ^ partner) for i in range(size)]
         got = [lax.ppermute(held[e], axis, pairs) for e in range(1, len(held), 2)]

time: 62.6 us -> 61.1 us (0.976)
  local copies, waits for them, and re-layouts: 8.15 us -> 5.39 us
  waiting for transfers between devices: 15.6 us -> 17 us
  starting transfers between devices: 26.4 us -> 25.5 us
  matrix products: 10.3 us -> 11.1 us
    unnamed x17 -> x15, local copies, waits for them, and re-layouts: 5.22 us -> 2.49 us
    ppermute x7, waiting for transfers between devices: 4.58 us -> 6.88 us  [_gather_dp(): got.append(lax.ppermute(local, axis, pairs))]
    ppermute x3, waiting for transfers between devices: 3.13 us -> 1.73 us  [_frozen_term(): got = [lax.ppermute(held[e], axis, pairs) for e in range(1, len(held), 2)]]
    dot_general x4, matrix products: 7.65 us -> 8.95 us  [term(): lax.dot_general(cotangent, piece, (((1,), (1,)), ((), ())), preferred_ele...]
    ppermute x3 -> x2, waiting for transfers between devices: 0.21 us -> 1.5 us  [_psum_small(): lax.ppermute(total, axis, [(i, i ^ step) for i in range(size)])]
    ppermute x3, starting transfers between devices: 2.15 us -> 1.16 us  [_frozen_term(): got = [lax.ppermute(held[e], axis, pairs) for e in range(1, len(held), 2)]]
    ppermute x7, waiting for transfers between devices: 7.64 us -> 6.87 us  [on_device(): lax.ppermute(outgoing.astype(jnp.bfloat16), 'dp', pairs).astype(jnp.float32)]
    ppermute x3 -> x2, starting transfers between devices: 1.86 us -> 1.56 us  [_psum_small(): lax.ppermute(total, axis, [(i, i ^ step) for i in range(size)])]
  transfers between devices with their start and end apart: 20 -> 19, of which waited for: 7 -> 9; matrix products, arithmetic and copies ran while one was open for 18% -> 15% of each run, Pallas kernels for 0% -> 0%
where the time goes in v6:
time: 61.1 us; the launch traced here: 60.8 us
  starting transfers between devices  25.5 us (42%)
  waiting for transfers between devices  17 us (28%)
  matrix products  11.1 us (18%)
  local copies, waits for them, and re-layouts  5.39 us (9%)
  between operations  1.52 us (2%)
    ppermute x7, starting transfers between devices, _gather_dp(): got.append(lax.ppermute(local, axis, pairs))  12.5 us
    ppermute x7, starting transfers between devices, on_device(): lax.ppermute(outgoing.astype(jnp.bfloat16), 'dp', pairs).astype(jnp.float32)  10.3 us
    dot_general x4, matrix products, term(): lax.dot_general(cotangent, piece, (((1,), (1,)), ((), ())), preferred_ele...  8.95 us
    ppermute x7, waiting for transfers between devices, _gather_dp(): got.append(lax.ppermute(local, axis, pairs))  6.88 us
    ppermute x7, waiting for transfers between devices, on_device(): lax.ppermute(outgoing.astype(jnp.bfloat16), 'dp', pairs).astype(jnp.float32)  6.87 us
    unnamed x15, local copies, waits for them, and re-layouts  2.49 us
    ppermute x3, waiting for transfers between devices, _frozen_term(): got = [lax.ppermute(held[e], axis, pairs) for e in range(1, len(held), 2)]  1.73 us
    ppermute x2, starting transfers between devices, _psum_small(): lax.ppermute(total, axis, [(i, i ^ step) for i in range(size)])  1.56 us
  transfers between devices with their start and end apart: 19, of which 9 were waited for; matrix products, arithmetic and copies ran while one was open for 15% of the time, Pallas kernels for 0%

profile of v6, /device:TPU:0, one launch (start us, length us, event | category | flops | bytes accessed | tf_op | source)
XLA Modules:
  0.0 60.8 jit_solution(9068841975069870858)
XLA Ops:
  2.3 3.0 %collective-permute-start.2 = (bf16[1,16,2304]{2,1,0:T(8,128)(2,1)S(1)}, bf16[1,16,2304]{2,1,0:T(8,128)(2,1)S(1)}, u32[]{:S(2)}, u32[]{:S(2)}) collective-permute-start(bf16[1,16,2304]{2,1,0:T(8,128)(2,1)S(1)} %constant_dynamic-update-slice_fusion), channel_id=1, source_target_pairs={{0,4},{4,0},{8,12},{12,8},{16,20},{20,16},{24,28},{28,24},{1,5},{5... | collective-permute-start | bytes 221192 | tf_op jit(solution)/shard_map/ppermute | solution.py:32
  5.2 1.6 %collective-permute-start.3 = (bf16[1,16,2304]{2,1,0:T(8,128)(2,1)S(1)}, bf16[1,16,2304]{2,1,0:T(8,128)(2,1)S(1)}, u32[]{:S(2)}, u32[]{:S(2)}) collective-permute-start(bf16[1,16,2304]{2,1,0:T(8,128)(2,1)S(1)} %constant_dynamic-update-slice_fusion), channel_id=1, source_target_pairs={{0,8},{4,12},{8,0},{12,4},{16,24},{20,28},{24,16},{28,20},{1,9},{5... | collective-permute-start | bytes 221192 | tf_op jit(solution)/shard_map/ppermute | solution.py:32
  6.8 3.0 %collective-permute-start.5 = (bf16[1,16,2304]{2,1,0:T(8,128)(2,1)S(1)}, bf16[1,16,2304]{2,1,0:T(8,128)(2,1)S(1)}, u32[]{:S(2)}, u32[]{:S(2)}) collective-permute-start(bf16[1,16,2304]{2,1,0:T(8,128)(2,1)S(1)} %constant_dynamic-update-slice_fusion), channel_id=1, source_target_pairs={{0,16},{4,20},{8,24},{12,28},{16,0},{20,4},{24,8},{28,12},{1,17},{... | collective-permute-start | bytes 221192 | tf_op jit(solution)/shard_map/ppermute | solution.py:32
  9.8 1.3 %collective-permute-start.6 = (bf16[1,16,2304]{2,1,0:T(8,128)(2,1)S(1)}, bf16[1,16,2304]{2,1,0:T(8,128)(2,1)S(1)}, u32[]{:S(2)}, u32[]{:S(2)}) collective-permute-start(bf16[1,16,2304]{2,1,0:T(8,128)(2,1)S(1)} %constant_dynamic-update-slice_fusion), channel_id=1, source_target_pairs={{0,20},{4,16},{8,28},{12,24},{16,4},{20,0},{24,12},{28,8},{1,21},{... | collective-permute-start | bytes 221192 | tf_op jit(solution)/shard_map/ppermute | solution.py:32
  11.1 1.6 %convolution_bitcast_fusion.1 = f32[128,2048]{0,1:T(8,128)S(1)} fusion(bf16[128,256]{1,0:T(8,128)(2,1)} %param.7, bf16[8192,256]{1,0:T(8,128)(2,1)} %param.8, s32[]{:T(128)S(6)} %select_n.48), kind=kOutput, calls=%fused_computation.1 | convolution fusion | flops 134217728 | bytes 2162692 | tf_op jit(solution)/shard_map/dot_general | solution.py:64
  13.5 3.7 %collective-permute-start.7 = (bf16[1,16,2304]{2,1,0:T(8,128)(2,1)S(1)}, bf16[1,16,2304]{2,1,0:T(8,128)(2,1)S(1)}, u32[]{:S(2)}, u32[]{:S(2)}) collective-permute-start(bf16[1,16,2304]{2,1,0:T(8,128)(2,1)S(1)} %constant_dynamic-update-slice_fusion), channel_id=1, source_target_pairs={{0,24},{4,28},{8,16},{12,20},{16,8},{20,12},{24,0},{28,4},{1,25},{... | collective-permute-start | bytes 221192 | tf_op jit(solution)/shard_map/ppermute | solution.py:32
  17.4 2.9 %collective-permute-done.6 = bf16[1,16,2304]{2,1,0:T(8,128)(2,1)S(1)} collective-permute-done((bf16[1,16,2304]{2,1,0:T(8,128)(2,1)S(1)}, bf16[1,16,2304]{2,1,0:T(8,128)(2,1)S(1)}, u32[]{:S(2)}, u32[]{:S(2)}) %collective-permute-start.6) | collective-permute-done | bytes 73760 | tf_op jit(solution)/shard_map/ppermute | solution.py:32
  20.3 4.0 %collective-permute-done.8 = bf16[1,16,2304]{2,1,0:T(8,128)(2,1)S(1)} collective-permute-done((bf16[1,16,2304]{2,1,0:T(8,128)(2,1)S(1)}, bf16[1,16,2304]{2,1,0:T(8,128)(2,1)S(1)}, u32[]{:S(2)}, u32[]{:S(2)}) %collective-permute-start.8) | collective-permute-done | bytes 73760 | tf_op jit(solution)/shard_map/ppermute | solution.py:32
  25.1 2.7 %fusion.3 = f32[128,2048]{0,1:T(8,128)} fusion(f32[128,2048]{0,1:T(8,128)S(1)} %collective-permute-done.1, bf16[128,256]{1,0:T(8,128)(2,1)S(1)} %copy-done.1, bf16[8192,256]{1,0:T(8,128)(2,1)} %param.8, s32[]{:T(128)S(6)} %select_n.47), kind=kOutput, calls=%fused_computation.8 | convolution fusion | flops 134479872 | bytes 3211268 | tf_op jit(solution)/shard_map/dot_general | solution.py:64
  27.7 2.6 %convolution_bitcast_fusion.3 = f32[128,2048]{0,1:T(8,128)} fusion(bf16[128,256]{1,0:T(8,128)(2,1)S(1)} %copy-done.1, bf16[8192,256]{1,0:T(8,128)(2,1)} %param.8, s32[]{:T(128)S(6)} %select_n.46), kind=kOutput, calls=%fused_computation.3 | convolution fusion | flops 134217728 | bytes 2162692 | tf_op jit(solution)/shard_map/dot_general | solution.py:64
  30.9 1.6 %collective-permute-start.11 = (f32[1,128,32]{1,2,0:T(8,128)S(1)}, f32[1,128,32]{1,2,0:T(8,128)S(1)}, u32[]{:S(2)}, u32[]{:S(2)}) collective-permute-start(f32[1,128,32]{1,2,0:T(8,128)S(1)} %add.88), channel_id=1, source_target_pairs={{0,2},{1,3},{2,0},{3,1},{4,6},{5,7},{6,4},{7,5},{8,10},{9,11},{10,... | collective-permute-start | bytes 49160 | tf_op jit(solution)/shard_map/ppermute | solution.py:48
  33.2 1.5 %collective-permute-done.11 = f32[1,128,32]{1,2,0:T(8,128)S(1)} collective-permute-done((f32[1,128,32]{1,2,0:T(8,128)S(1)}, f32[1,128,32]{1,2,0:T(8,128)S(1)}, u32[]{:S(2)}, u32[]{:S(2)}) %collective-permute-start.11) | collective-permute-done | bytes 16416 | tf_op jit(solution)/shard_map/ppermute | solution.py:48
  37.3 3.1 %collective-permute-start.17 = (bf16[1,16,2304]{2,1,0:T(8,128)(2,1)}, bf16[1,16,2304]{2,1,0:T(8,128)(2,1)S(1)}, u32[]{:S(2)}, u32[]{:S(2)}) collective-permute-start(bf16[1,16,2304]{2,1,0:T(8,128)(2,1)} %get-tuple-element.11), channel_id=1, source_target_pairs={{0,24},{4,28},{8,16},{12,20},{16,8},{20,12},{24,0},{28,4},{1,25},{... | collective-permute-start | bytes 221192 | tf_op jit(solution)/shard_map/ppermute | solution.py:148
  41.1 2.2 %collective-permute-done.18 = bf16[1,16,2304]{2,1,0:T(8,128)(2,1)S(1)} collective-permute-done((bf16[1,16,2304]{2,1,0:T(8,128)(2,1)S(1)}, bf16[1,16,2304]{2,1,0:T(8,128)(2,1)S(1)}, u32[]{:S(2)}, u32[]{:S(2)}) %collective-permute-start.18) | collective-permute-done | bytes 73760 | tf_op jit(solution)/shard_map/ppermute | solution.py:148
  43.3 2.5 %collective-permute-start.15 = (bf16[1,16,2304]{2,1,0:T(8,128)(2,1)S(1)}, bf16[1,16,2304]{2,1,0:T(8,128)(2,1)S(1)}, u32[]{:S(2)}, u32[]{:S(2)}) collective-permute-start(bf16[1,16,2304]{2,1,0:T(8,128)(2,1)S(1)} %get-tuple-element.13), channel_id=1, source_target_pairs={{0,16},{4,20},{8,24},{12,28},{16,0},{20,4},{24,8},{28,12},{1,17},{... | collective-permute-start | bytes 221192 | tf_op jit(solution)/shard_map/ppermute | solution.py:148
  45.8 2.3 %collective-permute-start.14 = (bf16[1,16,2304]{2,1,0:T(8,128)(2,1)S(1)}, bf16[1,16,2304]{2,1,0:T(8,128)(2,1)S(1)}, u32[]{:S(2)}, u32[]{:S(2)}) collective-permute-start(bf16[1,16,2304]{2,1,0:T(8,128)(2,1)S(1)} %get-tuple-element.14), channel_id=1, source_target_pairs={{0,12},{4,8},{8,4},{12,0},{16,28},{20,24},{24,20},{28,16},{1,13},{... | collective-permute-start | bytes 221192 | tf_op jit(solution)/shard_map/ppermute | solution.py:148
  48.1 1.0 %collective-permute-done.16 = bf16[1,16,2304]{2,1,0:T(8,128)(2,1)S(1)} collective-permute-done((bf16[1,16,2304]{2,1,0:T(8,128)(2,1)S(1)}, bf16[1,16,2304]{2,1,0:T(8,128)(2,1)S(1)}, u32[]{:S(2)}, u32[]{:S(2)}) %collective-permute-start.16) | collective-permute-done | bytes 73760 | tf_op jit(solution)/shard_map/ppermute | solution.py:148
  49.1 1.2 %collective-permute-done.15 = bf16[1,16,2304]{2,1,0:T(8,128)(2,1)S(1)} collective-permute-done((bf16[1,16,2304]{2,1,0:T(8,128)(2,1)S(1)}, bf16[1,16,2304]{2,1,0:T(8,128)(2,1)S(1)}, u32[]{:S(2)}, u32[]{:S(2)}) %collective-permute-start.15) | collective-permute-done | bytes 73760 | tf_op jit(solution)/shard_map/ppermute | solution.py:148
  51.2 1.0 %fusion.33 = f32[128,2048]{0,1:T(8,128)S(1)} fusion(bf16[1,16,2304]{2,1,0:T(8,128)(2,1)S(1)} %copy.25, bf16[1,128,32]{1,2,0:T(8,128)(2,1)} %copy-done.2), kind=kOutput, calls=%fused_computation.62 | convolution fusion | flops 8388608 | bytes 1118208 | tf_op jit(solution)/shard_map/bnr,brd->bnd/dot_general | solution.py:121
  52.2 1.2 %collective-permute-done.13 = bf16[1,16,2304]{2,1,0:T(8,128)(2,1)S(1)} collective-permute-done((bf16[1,16,2304]{2,1,0:T(8,128)(2,1)S(1)}, bf16[1,16,2304]{2,1,0:T(8,128)(2,1)S(1)}, u32[]{:S(2)}, u32[]{:S(2)}) %collective-permute-start.13) | collective-permute-done | bytes 73760 | tf_op jit(solution)/shard_map/ppermute | solution.py:148
  53.5 1.2 %collective-permute-done.12 = bf16[1,16,2304]{2,1,0:T(8,128)(2,1)S(1)} collective-permute-done((bf16[1,16,2304]{2,1,0:T(8,128)(2,1)S(1)}, bf16[1,16,2304]{2,1,0:T(8,128)(2,1)S(1)}, u32[]{:S(2)}, u32[]{:S(2)}) %collective-permute-start.12) | collective-permute-done | bytes 73760 | tf_op jit(solution)/shard_map/ppermute | solution.py:148
  56.0 1.7 %collective-permute-done.9 = f32[128,2048]{0,1:T(8,128)} collective-permute-done((f32[128,2048]{0,1:T(8,128)}, f32[128,2048]{0,1:T(8,128)}, u32[]{:S(2)}, u32[]{:S(2)}) %collective-permute-start.9) | collective-permute-done | bytes 1048608 | tf_op jit(solution)/shard_map/ppermute | solution.py:76
  57.8 2.0 %fusion.4 = bf16[128,2048]{0,1:T(8,128)(2,1)S(1)} fusion(f32[128,2048]{0,1:T(8,128)S(1)} %fusion.33, f32[128,2048]{0,1:T(8,128)} %collective-permute-done.9, f32[128,2048]{0,1:T(8,128)S(1)} %collective-permute-done, bf16[128,256]{1,0:T(8,128)(2,1)S(1)} %copy-done.1, bf16[8192,256]{1,0:T(8,128)(2,1)} %param.8, s32[]{:T(128)S(6)} %select_n.45), kind=kOutput, calls=%fused_computation.9 | convolution fusion | flops 135266304 | bytes 4784132 | tf_op jit(solution)/shard_map/dot_general | solution.py:64
  59.8 1.0 %copy.16 = bf16[128,2048]{1,0:T(8,128)(2,1)} copy(bf16[128,2048]{0,1:T(8,128)(2,1)S(1)} %fusion.4) | data formatting | bytes 1048576
  (57 shorter events, 9.4 us)
Async XLA Ops:
  0.6 24.2 %copy-start = (bf16[128,2048]{1,0:T(8,128)(2,1)S(1)}, bf16[128,2048]{1,0:T(8,128)(2,1)}, u32[]{:S(2)}) copy-start(bf16[128,2048]{1,0:T(8,128)(2,1)} %param.6) | copy-start | bytes 1572868
  0.6 24.0 %copy-start.1 = (bf16[128,256]{1,0:T(8,128)(2,1)S(1)}, bf16[128,256]{1,0:T(8,128)(2,1)}, u32[]{:S(2)}) copy-start(bf16[128,256]{1,0:T(8,128)(2,1)} %param.7) | copy-start | bytes 196612
  2.3 11.2 %collective-permute-start.2 = (bf16[1,16,2304]{2,1,0:T(8,128)(2,1)S(1)}, bf16[1,16,2304]{2,1,0:T(8,128)(2,1)S(1)}, u32[]{:S(2)}, u32[]{:S(2)}) collective-permute-start(bf16[1,16,2304]{2,1,0:T(8,128)(2,1)S(1)} %constant_dynamic-update-slice_fusion), channel_id=1, source_target_pairs={{0,4},{4,0},{8,12},{12,8},{16,20},{20,16},{24,28},{28,24},{1,5},{5... | collective-permute-start | bytes 221192 | tf_op jit(solution)/shard_map/ppermute | solution.py:32
  5.2 11.9 %collective-permute-start.3 = (bf16[1,16,2304]{2,1,0:T(8,128)(2,1)S(1)}, bf16[1,16,2304]{2,1,0:T(8,128)(2,1)S(1)}, u32[]{:S(2)}, u32[]{:S(2)}) collective-permute-start(bf16[1,16,2304]{2,1,0:T(8,128)(2,1)S(1)} %constant_dynamic-update-slice_fusion), channel_id=1, source_target_pairs={{0,8},{4,12},{8,0},{12,4},{16,24},{20,28},{24,16},{28,20},{1,9},{5... | collective-permute-start | bytes 221192 | tf_op jit(solution)/shard_map/ppermute | solution.py:32
  6.8 10.5 %collective-permute-start.4 = (bf16[1,16,2304]{2,1,0:T(8,128)(2,1)S(1)}, bf16[1,16,2304]{2,1,0:T(8,128)(2,1)S(1)}, u32[]{:S(2)}, u32[]{:S(2)}) collective-permute-start(bf16[1,16,2304]{2,1,0:T(8,128)(2,1)S(1)} %constant_dynamic-update-slice_fusion), channel_id=1, source_target_pairs={{0,12},{4,8},{8,4},{12,0},{16,28},{20,24},{24,20},{28,16},{1,13},{... | collective-permute-start | bytes 221192 | tf_op jit(solution)/shard_map/ppermute | solution.py:32
  6.8 10.6 %collective-permute-start.5 = (bf16[1,16,2304]{2,1,0:T(8,128)(2,1)S(1)}, bf16[1,16,2304]{2,1,0:T(8,128)(2,1)S(1)}, u32[]{:S(2)}, u32[]{:S(2)}) collective-permute-start(bf16[1,16,2304]{2,1,0:T(8,128)(2,1)S(1)} %constant_dynamic-update-slice_fusion), channel_id=1, source_target_pairs={{0,16},{4,20},{8,24},{12,28},{16,0},{20,4},{24,8},{28,12},{1,17},{... | collective-permute-start | bytes 221192 | tf_op jit(solution)/shard_map/ppermute | solution.py:32
  9.8 10.5 %collective-permute-start.6 = (bf16[1,16,2304]{2,1,0:T(8,128)(2,1)S(1)}, bf16[1,16,2304]{2,1,0:T(8,128)(2,1)S(1)}, u32[]{:S(2)}, u32[]{:S(2)}) collective-permute-start(bf16[1,16,2304]{2,1,0:T(8,128)(2,1)S(1)} %constant_dynamic-update-slice_fusion), channel_id=1, source_target_pairs={{0,20},{4,16},{8,28},{12,24},{16,4},{20,0},{24,12},{28,8},{1,21},{... | collective-permute-start | bytes 221192 | tf_op jit(solution)/shard_map/ppermute | solution.py:32
  13.5 6.8 %collective-permute-start.7 = (bf16[1,16,2304]{2,1,0:T(8,128)(2,1)S(1)}, bf16[1,16,2304]{2,1,0:T(8,128)(2,1)S(1)}, u32[]{:S(2)}, u32[]{:S(2)}) collective-permute-start(bf16[1,16,2304]{2,1,0:T(8,128)(2,1)S(1)} %constant_dynamic-update-slice_fusion), channel_id=1, source_target_pairs={{0,24},{4,28},{8,16},{12,20},{16,8},{20,12},{24,0},{28,4},{1,25},{... | collective-permute-start | bytes 221192 | tf_op jit(solution)/shard_map/ppermute | solution.py:32
  17.2 7.1 %collective-permute-start.8 = (bf16[1,16,2304]{2,1,0:T(8,128)(2,1)S(1)}, bf16[1,16,2304]{2,1,0:T(8,128)(2,1)S(1)}, u32[]{:S(2)}, u32[]{:S(2)}) collective-permute-start(bf16[1,16,2304]{2,1,0:T(8,128)(2,1)S(1)} %constant_dynamic-update-slice_fusion), channel_id=1, source_target_pairs={{0,28},{4,24},{8,20},{12,16},{16,12},{20,8},{24,4},{28,0},{1,29},{... | collective-permute-start | bytes 221192 | tf_op jit(solution)/shard_map/ppermute | solution.py:32
  17.3 7.8 %collective-permute-start.1 = (f32[128,2048]{0,1:T(8,128)S(1)}, f32[128,2048]{0,1:T(8,128)S(1)}, u32[]{:S(2)}, u32[]{:S(2)}) collective-permute-start(f32[128,2048]{0,1:T(8,128)S(1)} %convolution_bitcast_fusion.1), channel_id=1, source_target_pairs={{0,1},{1,0},{2,3},{3,2},{4,5},{5,4},{6,7},{7,6},{8,9},{9,8},{10,11... | collective-permute-start | bytes 3145736 | tf_op jit(solution)/shard_map/ppermute | solution.py:76
  27.7 3.1 %collective-permute-start.10 = (f32[1,128,32]{1,2,0:T(8,128)S(1)}, f32[1,128,32]{1,2,0:T(8,128)S(1)}, u32[]{:S(2)}, u32[]{:S(2)}) collective-permute-start(f32[1,128,32]{1,2,0:T(8,128)S(1)} %pad_maximum_fusion.1), channel_id=1, source_target_pairs={{0,1},{1,0},{2,3},{3,2},{4,5},{5,4},{6,7},{7,6},{8,9},{9,8},{10,11... | collective-permute-start | bytes 49160 | tf_op jit(solution)/shard_map/ppermute | solution.py:48
  30.3 25.7 %collective-permute-start = (f32[128,2048]{0,1:T(8,128)}, f32[128,2048]{0,1:T(8,128)S(1)}, u32[]{:S(2)}, u32[]{:S(2)}) collective-permute-start(f32[128,2048]{0,1:T(8,128)} %convolution_bitcast_fusion.3), channel_id=1, source_target_pairs={{0,1},{1,0},{2,3},{3,2},{4,5},{5,4},{6,7},{7,6},{8,9},{9,8},{10,11... | collective-permute-start | bytes 3145736 | tf_op jit(solution)/shard_map/ppermute | solution.py:76
  30.9 3.8 %collective-permute-start.11 = (f32[1,128,32]{1,2,0:T(8,128)S(1)}, f32[1,128,32]{1,2,0:T(8,128)S(1)}, u32[]{:S(2)}, u32[]{:S(2)}) collective-permute-start(f32[1,128,32]{1,2,0:T(8,128)S(1)} %add.88), channel_id=1, source_target_pairs={{0,2},{1,3},{2,0},{3,1},{4,6},{5,7},{6,4},{7,5},{8,10},{9,11},{10,... | collective-permute-start | bytes 49160 | tf_op jit(solution)/shard_map/ppermute | solution.py:48
  32.6 25.2 %collective-permute-start.9 = (f32[128,2048]{0,1:T(8,128)}, f32[128,2048]{0,1:T(8,128)}, u32[]{:S(2)}, u32[]{:S(2)}) collective-permute-start(f32[128,2048]{0,1:T(8,128)} %fusion.3), channel_id=1, source_target_pairs={{0,2},{1,3},{2,0},{3,1},{4,6},{5,7},{6,4},{7,5},{8,10},{9,11},{10,... | collective-permute-start | bytes 3145736 | tf_op jit(solution)/shard_map/ppermute | solution.py:76
  34.7 0.6 copy-start.2
  35.8 7.5 %collective-permute-start.18 = (bf16[1,16,2304]{2,1,0:T(8,128)(2,1)S(1)}, bf16[1,16,2304]{2,1,0:T(8,128)(2,1)S(1)}, u32[]{:S(2)}, u32[]{:S(2)}) collective-permute-start(bf16[1,16,2304]{2,1,0:T(8,128)(2,1)S(1)} %fusion.32), channel_id=1, source_target_pairs={{0,28},{4,24},{8,20},{12,16},{16,12},{20,8},{24,4},{28,0},{1,29},{... | collective-permute-start | bytes 221192 | tf_op jit(solution)/shard_map/ppermute | solution.py:148
  37.3 8.5 %collective-permute-start.17 = (bf16[1,16,2304]{2,1,0:T(8,128)(2,1)}, bf16[1,16,2304]{2,1,0:T(8,128)(2,1)S(1)}, u32[]{:S(2)}, u32[]{:S(2)}) collective-permute-start(bf16[1,16,2304]{2,1,0:T(8,128)(2,1)} %get-tuple-element.11), channel_id=1, source_target_pairs={{0,24},{4,28},{8,16},{12,20},{16,8},{20,12},{24,0},{28,4},{1,25},{... | collective-permute-start | bytes 221192 | tf_op jit(solution)/shard_map/ppermute | solution.py:148
  40.4 8.7 %collective-permute-start.16 = (bf16[1,16,2304]{2,1,0:T(8,128)(2,1)S(1)}, bf16[1,16,2304]{2,1,0:T(8,128)(2,1)S(1)}, u32[]{:S(2)}, u32[]{:S(2)}) collective-permute-start(bf16[1,16,2304]{2,1,0:T(8,128)(2,1)S(1)} %get-tuple-element.12), channel_id=1, source_target_pairs={{0,20},{4,16},{8,28},{12,24},{16,4},{20,0},{24,12},{28,8},{1,21},{... | collective-permute-start | bytes 221192 | tf_op jit(solution)/shard_map/ppermute | solution.py:148
  43.3 7.0 %collective-permute-start.15 = (bf16[1,16,2304]{2,1,0:T(8,128)(2,1)S(1)}, bf16[1,16,2304]{2,1,0:T(8,128)(2,1)S(1)}, u32[]{:S(2)}, u32[]{:S(2)}) collective-permute-start(bf16[1,16,2304]{2,1,0:T(8,128)(2,1)S(1)} %get-tuple-element.13), channel_id=1, source_target_pairs={{0,16},{4,20},{8,24},{12,28},{16,0},{20,4},{24,8},{28,12},{1,17},{... | collective-permute-start | bytes 221192 | tf_op jit(solution)/shard_map/ppermute | solution.py:148
  45.8 6.4 %collective-permute-start.14 = (bf16[1,16,2304]{2,1,0:T(8,128)(2,1)S(1)}, bf16[1,16,2304]{2,1,0:T(8,128)(2,1)S(1)}, u32[]{:S(2)}, u32[]{:S(2)}) collective-permute-start(bf16[1,16,2304]{2,1,0:T(8,128)(2,1)S(1)} %get-tuple-element.14), channel_id=1, source_target_pairs={{0,12},{4,8},{8,4},{12,0},{16,28},{20,24},{24,20},{28,16},{1,13},{... | collective-permute-start | bytes 221192 | tf_op jit(solution)/shard_map/ppermute | solution.py:148
  49.1 4.4 %collective-permute-start.13 = (bf16[1,16,2304]{2,1,0:T(8,128)(2,1)S(1)}, bf16[1,16,2304]{2,1,0:T(8,128)(2,1)S(1)}, u32[]{:S(2)}, u32[]{:S(2)}) collective-permute-start(bf16[1,16,2304]{2,1,0:T(8,128)(2,1)S(1)} %get-tuple-element.15), channel_id=1, source_target_pairs={{0,8},{4,12},{8,0},{12,4},{16,24},{20,28},{24,16},{28,20},{1,9},{5... | collective-permute-start | bytes 221192 | tf_op jit(solution)/shard_map/ppermute | solution.py:148
  50.3 4.4 %collective-permute-start.12 = (bf16[1,16,2304]{2,1,0:T(8,128)(2,1)S(1)}, bf16[1,16,2304]{2,1,0:T(8,128)(2,1)S(1)}, u32[]{:S(2)}, u32[]{:S(2)}) collective-permute-start(bf16[1,16,2304]{2,1,0:T(8,128)(2,1)S(1)} %get-tuple-element.10), channel_id=1, source_target_pairs={{0,4},{4,0},{8,12},{12,8},{16,20},{20,16},{24,28},{28,24},{1,5},{5... | collective-permute-start | bytes 221192 | tf_op jit(solution)/shard_map/ppermute | solution.py:148

commit v7 on v6

--- a/solution.py
+++ b/solution.py
@@ -26,14 +26,21 @@
 
 def _gather_dp(local, axis, size):
     me = lax.axis_index(axis)
-    got = [local]
-    sources = [me]
-    for shift, pairs in _partners(size):
-        got.append(lax.ppermute(local, axis, pairs))
-        sources.append(_source_of(me, shift, size))
-    stacked = jnp.stack(got, 0)
-    order = jnp.stack(sources)
-    return stacked, order
+    if size & (size - 1) != 0 or size < 4:
+        got = [local]
+        sources = [me]
+        for shift, pairs in _partners(size):
+            got.append(lax.ppermute(local, axis, pairs))
+            sources.append(_source_of(me, shift, size))
+        return jnp.stack(got, 0), jnp.stack(sources)
+    pair = jnp.concatenate([local, lax.ppermute(local, axis, [(i, i ^ 1) for i in range(size)])], 0)
+    got = [pair]
+    sources = [me, me ^ 1]
+    for m in range(1, size // 2):
+        shift = 2 * m
+        got.append(lax.ppermute(pair, axis, [(i, i ^ shift) for i in range(size)]))
+        sources += [me ^ shift, me ^ shift ^ 1]
+    return jnp.concatenate(got, 0), jnp.stack(sources)
 
 
 def _psum_small(value, axis, size):
@@ -96,6 +103,7 @@
 
     packed = jnp.concatenate([adapter_down_weight, adapter_up_weight], axis=2)
     stacked, order = _gather_dp(packed, "dp", dp_size)
+    stacked = stacked.reshape(dp_size, held_tenants, *packed.shape[1:])
     owner = tenant_per_block // held_tenants
     local = tenant_per_block % held_tenants
     pick = (order[None, :] == owner[:, None])
@@ -143,11 +151,13 @@
     up_contribution = up_contribution.reshape(dp_size, held_tenants, adapter_rank_size, key_portion)
     combined = jnp.concatenate([down_contribution, up_contribution], axis=3)
     owned = lax.dynamic_index_in_dim(combined, me_dp, 0, keepdims=False)
+    grad_down = owned[:, :, :width_portion]
+    grad_up = owned[:, :, width_portion:]
     for shift, pairs in _partners(dp_size):
         outgoing = lax.dynamic_index_in_dim(combined, _dest_of(me_dp, shift, dp_size), 0, keepdims=False)
-        owned = owned + lax.ppermute(outgoing.astype(jnp.bfloat16), "dp", pairs).astype(jnp.float32)
-    grad_down = owned[:, :, :width_portion]
-    grad_up = owned[:, :, width_portion:]
+        arrived = lax.ppermute(outgoing.astype(jnp.bfloat16), "dp", pairs).astype(jnp.float32)
+        grad_down = grad_down + arrived[:, :, :width_portion]
+        grad_up = grad_up + arrived[:, :, width_portion:]
     return (grad_inputs, grad_down, grad_up)
 
 

time: 61.1 us -> 59.2 us (0.969)
  local copies, waits for them, and re-layouts: 5.39 us -> 2.99 us
  matrix products: 11.1 us -> 9.1 us
  other arithmetic: 0.26 us -> 1.62 us
  waiting for transfers between devices: 17 us -> 18.3 us
    ppermute x7 -> x4, starting transfers between devices: 12.5 us -> 7.53 us  [the longest x3 4.57 us: _gather_dp(): got.append(lax.ppermute(pair, axis, [(i, i ^ shift) for i in range(size)]))]
    ppermute x7, starting transfers between devices: 10.3 us -> 15 us  [on_device(): lax.ppermute(outgoing.astype(jnp.bfloat16), 'dp', pairs).astype(jnp.float32)]
    ppermute x7 -> x4, waiting for transfers between devices: 6.88 us -> 11.3 us  [the longest x3 11.3 us: _gather_dp(): got.append(lax.ppermute(pair, axis, [(i, i ^ shift) for i in range(size)]))]
    ppermute x7, waiting for transfers between devices: 6.87 us -> 4.32 us  [on_device(): lax.ppermute(outgoing.astype(jnp.bfloat16), 'dp', pairs).astype(jnp.float32)]
    dot_general x4, matrix products: 8.95 us -> 7.64 us  [term(): lax.dot_general(cotangent, piece, (((1,), (1,)), ((), ())), preferred_ele...]
    slice x2 -> x0, local copies, waits for them, and re-layouts: 1.27 us -> none  [the longest x1 0.66 us: on_device(): grad_down = owned[:, :, :width_portion]]
    add x1 -> x2, other arithmetic: 0.08 us -> 1.32 us  [the longest x1 0.71 us: on_device(): grad_down = grad_down + arrived[:, :, :width_portion]]
    dot_general x1, matrix products: 1.03 us -> 0.34 us  [on_device(): jnp.einsum('bnr,brd->bnd', low_out_b, sel_down, preferred_element_type=jn...]
  transfers between devices with their start and end apart: 19 -> 16, of which waited for: 9 -> 8; matrix products, arithmetic and copies ran while one was open for 15% -> 11% of each run, Pallas kernels for 0% -> 0%
where the time goes in v7:
time: 59.2 us; the launch traced here: 58.9 us
  starting transfers between devices  25.3 us (43%)
  waiting for transfers between devices  18.3 us (31%)
  matrix products  9.1 us (15%)
  local copies, waits for them, and re-layouts  2.99 us (5%)
  other arithmetic  1.62 us (3%)
  between operations  1.54 us (3%)
    ppermute x7, starting transfers between devices, on_device(): lax.ppermute(outgoing.astype(jnp.bfloat16), 'dp', pairs).astype(jnp.float32)  15 us
    ppermute x3, waiting for transfers between devices, _gather_dp(): got.append(lax.ppermute(pair, axis, [(i, i ^ shift) for i in range(size)]))  11.3 us
    dot_general x4, matrix products, term(): lax.dot_general(cotangent, piece, (((1,), (1,)), ((), ())), preferred_ele...  7.64 us
    ppermute x3, starting transfers between devices, _gather_dp(): got.append(lax.ppermute(pair, axis, [(i, i ^ shift) for i in range(size)]))  4.57 us
    ppermute x7, waiting for transfers between devices, on_device(): lax.ppermute(outgoing.astype(jnp.bfloat16), 'dp', pairs).astype(jnp.float32)  4.32 us
    ppermute x1, starting transfers between devices, _gather_dp(): lax.ppermute(local, axis, [(i, i ^ 1) for i in range(size)])  2.97 us
    unnamed x9, local copies, waits for them, and re-layouts  1.97 us
    ppermute x2, starting transfers between devices, _psum_small(): lax.ppermute(total, axis, [(i, i ^ step) for i in range(size)])  1.54 us
  transfers between devices with their start and end apart: 16, of which 8 were waited for; matrix products, arithmetic and copies ran while one was open for 11% of the time, Pallas kernels for 0%

profile of v7, /device:TPU:0, one launch (start us, length us, event | category | flops | bytes accessed | tf_op | source)
XLA Modules:
  0.0 58.9 jit_solution(15207178665151470618)
XLA Ops:
  0.7 0.9 %constant_dynamic-update-slice_fusion.1 = (bf16[1,16,2304]{2,1,0:T(8,128)(2,1)S(1)}, bf16[8,16,2304]{2,1,0:T(8,128)(2,1)S(1)}) fusion(bf16[1,16,2048]{2,1,0:T(8,128)(2,1)} %param.9), kind=kLoop, calls=%fused_computation.59 | loop fusion | bytes 196608
  2.3 3.0 %collective-permute-start.2 = (bf16[1,16,2304]{2,1,0:T(8,128)(2,1)S(1)}, bf16[1,16,2304]{2,1,0:T(8,128)(2,1)S(1)}, u32[]{:S(2)}, u32[]{:S(2)}) collective-permute-start(bf16[1,16,2304]{2,1,0:T(8,128)(2,1)S(1)} %get-tuple-element.20), channel_id=1, source_target_pairs={{0,4},{4,0},{8,12},{12,8},{16,20},{20,16},{24,28},{28,24},{1,5},{5... | collective-permute-start | bytes 221192 | tf_op jit(solution)/shard_map/ppermute | solution.py:36
  5.3 1.6 %convolution_bitcast_fusion.1 = f32[128,2048]{0,1:T(8,128)S(1)} fusion(bf16[128,256]{1,0:T(8,128)(2,1)} %param.7, bf16[8192,256]{1,0:T(8,128)(2,1)} %param.8, s32[]{:T(128)S(6)} %select_n.48), kind=kOutput, calls=%fused_computation.1 | convolution fusion | flops 134217728 | bytes 2162692 | tf_op jit(solution)/shard_map/dot_general | solution.py:71
  7.8 2.0 %collective-permute-start.3 = (bf16[2,16,2304]{2,1,0:T(8,128)(2,1)S(1)}, bf16[2,16,2304]{2,1,0:T(8,128)(2,1)S(1)}, u32[]{:S(2)}, u32[]{:S(2)}) collective-permute-start(bf16[2,16,2304]{2,1,0:T(8,128)(2,1)S(1)} %pad_maximum_fusion.1), channel_id=1, source_target_pairs={{0,8},{4,12},{8,0},{12,4},{16,24},{20,28},{24,16},{28,20},{1,9},{5... | collective-permute-start | bytes 442376 | tf_op jit(solution)/shard_map/ppermute | solution.py:41
  9.7 2.6 %collective-permute-start.4 = (bf16[2,16,2304]{2,1,0:T(8,128)(2,1)S(1)}, bf16[2,16,2304]{2,1,0:T(8,128)(2,1)S(1)}, u32[]{:S(2)}, u32[]{:S(2)}) collective-permute-start(bf16[2,16,2304]{2,1,0:T(8,128)(2,1)S(1)} %pad_maximum_fusion.1), channel_id=1, source_target_pairs={{0,16},{4,20},{8,24},{12,28},{16,0},{20,4},{24,8},{28,12},{1,17},{... | collective-permute-start | bytes 442376 | tf_op jit(solution)/shard_map/ppermute | solution.py:41
  12.3 4.1 %collective-permute-done.3 = bf16[2,16,2304]{2,1,0:T(8,128)(2,1)S(1)} collective-permute-done((bf16[2,16,2304]{2,1,0:T(8,128)(2,1)S(1)}, bf16[2,16,2304]{2,1,0:T(8,128)(2,1)S(1)}, u32[]{:S(2)}, u32[]{:S(2)}) %collective-permute-start.3) | collective-permute-done | bytes 147488 | tf_op jit(solution)/shard_map/ppermute | solution.py:41
  16.5 7.2 %collective-permute-done.4 = bf16[2,16,2304]{2,1,0:T(8,128)(2,1)S(1)} collective-permute-done((bf16[2,16,2304]{2,1,0:T(8,128)(2,1)S(1)}, bf16[2,16,2304]{2,1,0:T(8,128)(2,1)S(1)}, u32[]{:S(2)}, u32[]{:S(2)}) %collective-permute-start.4) | collective-permute-done | bytes 147488 | tf_op jit(solution)/shard_map/ppermute | solution.py:41
  24.5 2.7 %fusion.3 = f32[128,2048]{0,1:T(8,128)} fusion(f32[128,2048]{0,1:T(8,128)S(1)} %collective-permute-done.1, bf16[128,256]{1,0:T(8,128)(2,1)S(1)} %copy-done.1, bf16[8192,256]{1,0:T(8,128)(2,1)} %param.8, s32[]{:T(128)S(6)} %select_n.47), kind=kOutput, calls=%fused_computation.8 | convolution fusion | flops 134479872 | bytes 3211268 | tf_op jit(solution)/shard_map/dot_general | solution.py:71
  27.2 1.6 %convolution_bitcast_fusion.3 = f32[128,2048]{0,1:T(8,128)S(1)} fusion(bf16[128,256]{1,0:T(8,128)(2,1)S(1)} %copy-done.1, bf16[8192,256]{1,0:T(8,128)(2,1)} %param.8, s32[]{:T(128)S(6)} %select_n.46), kind=kOutput, calls=%fused_computation.3 | convolution fusion | flops 134217728 | bytes 2162692 | tf_op jit(solution)/shard_map/dot_general | solution.py:71
  29.4 1.5 %collective-permute-start.8 = (f32[1,128,32]{1,2,0:T(8,128)S(1)}, f32[1,128,32]{1,2,0:T(8,128)S(1)}, u32[]{:S(2)}, u32[]{:S(2)}) collective-permute-start(f32[1,128,32]{1,2,0:T(8,128)S(1)} %add.109), channel_id=1, source_target_pairs={{0,2},{1,3},{2,0},{3,1},{4,6},{5,7},{6,4},{7,5},{8,10},{9,11},{10,... | collective-permute-start | bytes 49160 | tf_op jit(solution)/shard_map/ppermute | solution.py:55
  31.7 1.5 %collective-permute-done.8 = f32[1,128,32]{1,2,0:T(8,128)S(1)} collective-permute-done((f32[1,128,32]{1,2,0:T(8,128)S(1)}, f32[1,128,32]{1,2,0:T(8,128)S(1)}, u32[]{:S(2)}, u32[]{:S(2)}) %collective-permute-start.8) | collective-permute-done | bytes 16416 | tf_op jit(solution)/shard_map/ppermute | solution.py:55
  33.8 3.0 %collective-permute-start.15 = (bf16[1,16,2304]{2,1,0:T(8,128)(2,1)S(1)}, bf16[1,16,2304]{2,1,0:T(8,128)(2,1)S(1)}, u32[]{:S(2)}, u32[]{:S(2)}) collective-permute-start(bf16[1,16,2304]{2,1,0:T(8,128)(2,1)S(1)} %fusion.25), channel_id=1, source_target_pairs={{0,28},{4,24},{8,20},{12,16},{16,12},{20,8},{24,4},{28,0},{1,29},{... | collective-permute-start | bytes 221192 | tf_op jit(solution)/shard_map/ppermute | solution.py:158
  36.8 1.5 %collective-permute-start.14 = (bf16[1,16,2304]{2,1,0:T(8,128)(2,1)S(1)}, bf16[1,16,2304]{2,1,0:T(8,128)(2,1)S(1)}, u32[]{:S(2)}, u32[]{:S(2)}) collective-permute-start(bf16[1,16,2304]{2,1,0:T(8,128)(2,1)S(1)} %get-tuple-element.11), channel_id=1, source_target_pairs={{0,24},{4,28},{8,16},{12,20},{16,8},{20,12},{24,0},{28,4},{1,25},{... | collective-permute-start | bytes 221192 | tf_op jit(solution)/shard_map/ppermute | solution.py:158
  38.3 2.3 %collective-permute-start.13 = (bf16[1,16,2304]{2,1,0:T(8,128)(2,1)S(1)}, bf16[1,16,2304]{2,1,0:T(8,128)(2,1)S(1)}, u32[]{:S(2)}, u32[]{:S(2)}) collective-permute-start(bf16[1,16,2304]{2,1,0:T(8,128)(2,1)S(1)} %get-tuple-element.12), channel_id=1, source_target_pairs={{0,20},{4,16},{8,28},{12,24},{16,4},{20,0},{24,12},{28,8},{1,21},{... | collective-permute-start | bytes 221192 | tf_op jit(solution)/shard_map/ppermute | solution.py:158
  40.6 1.1 %collective-permute-done.15 = bf16[1,16,2304]{2,1,0:T(8,128)(2,1)S(1)} collective-permute-done((bf16[1,16,2304]{2,1,0:T(8,128)(2,1)S(1)}, bf16[1,16,2304]{2,1,0:T(8,128)(2,1)S(1)}, u32[]{:S(2)}, u32[]{:S(2)}) %collective-permute-start.15) | collective-permute-done | bytes 73760 | tf_op jit(solution)/shard_map/ppermute | solution.py:158
  41.7 4.9 %collective-permute-start.12 = (bf16[1,16,2304]{2,1,0:T(8,128)(2,1)S(1)}, bf16[1,16,2304]{2,1,0:T(8,128)(2,1)S(1)}, u32[]{:S(2)}, u32[]{:S(2)}) collective-permute-start(bf16[1,16,2304]{2,1,0:T(8,128)(2,1)S(1)} %get-tuple-element.13), channel_id=1, source_target_pairs={{0,16},{4,20},{8,24},{12,28},{16,0},{20,4},{24,8},{28,12},{1,17},{... | collective-permute-start | bytes 221192 | tf_op jit(solution)/shard_map/ppermute | solution.py:158
  46.5 2.1 %collective-permute-start.11 = (bf16[1,16,2304]{2,1,0:T(8,128)(2,1)S(1)}, bf16[1,16,2304]{2,1,0:T(8,128)(2,1)S(1)}, u32[]{:S(2)}, u32[]{:S(2)}) collective-permute-start(bf16[1,16,2304]{2,1,0:T(8,128)(2,1)S(1)} %get-tuple-element.14), channel_id=1, source_target_pairs={{0,12},{4,8},{8,4},{12,0},{16,28},{20,24},{24,20},{28,16},{1,13},{... | collective-permute-start | bytes 221192 | tf_op jit(solution)/shard_map/ppermute | solution.py:158
  49.3 1.3 %collective-permute-start.9 = (bf16[1,16,2304]{2,1,0:T(8,128)(2,1)S(1)}, bf16[1,16,2304]{2,1,0:T(8,128)(2,1)S(1)}, u32[]{:S(2)}, u32[]{:S(2)}) collective-permute-start(bf16[1,16,2304]{2,1,0:T(8,128)(2,1)S(1)} %get-tuple-element.10), channel_id=1, source_target_pairs={{0,4},{4,0},{8,12},{12,8},{16,20},{20,16},{24,28},{28,24},{1,5},{5... | collective-permute-start | bytes 221192 | tf_op jit(solution)/shard_map/ppermute | solution.py:158
  51.1 1.2 %collective-permute-done.11 = bf16[1,16,2304]{2,1,0:T(8,128)(2,1)S(1)} collective-permute-done((bf16[1,16,2304]{2,1,0:T(8,128)(2,1)S(1)}, bf16[1,16,2304]{2,1,0:T(8,128)(2,1)S(1)}, u32[]{:S(2)}, u32[]{:S(2)}) %collective-permute-start.11) | collective-permute-done | bytes 73760 | tf_op jit(solution)/shard_map/ppermute | solution.py:158
  52.3 1.3 %collective-permute-done.10 = bf16[1,16,2304]{2,1,0:T(8,128)(2,1)S(1)} collective-permute-done((bf16[1,16,2304]{2,1,0:T(8,128)(2,1)S(1)}, bf16[1,16,2304]{2,1,0:T(8,128)(2,1)S(1)}, u32[]{:S(2)}, u32[]{:S(2)}) %collective-permute-start.10) | collective-permute-done | bytes 73760 | tf_op jit(solution)/shard_map/ppermute | solution.py:158
  54.3 0.7 %slice_add_fusion = f32[1,16,2048]{2,1,0:T(8,128)} fusion(f32[1,16,2304]{2,1,0:T(8,128)S(1)} %convert_element_type.164, f32[1,16,2304]{2,1,0:T(8,128)S(1)} %convert_element_type.161, f32[1,16,2304]{2,1,0:T(8,128)S(1)} %convert_element_type.158, f32[1,16,2304]{2,1,0:T(8,128)S(1)} %convert_element_type.155, f32[1,16,2304]{2,1,0:T(8,128)S(1)} %convert_element_type.152, ...), kind=kLoop, calls=%fused_computation.39 | loop fusion | flops 229376 | bytes 1179648 | tf_op jit(solution)/shard_map/add | solution.py:159
  55.0 1.1 %collective-permute-done.6 = f32[128,2048]{0,1:T(8,128)S(1)} collective-permute-done((f32[128,2048]{0,1:T(8,128)}, f32[128,2048]{0,1:T(8,128)S(1)}, u32[]{:S(2)}, u32[]{:S(2)}) %collective-permute-start.6) | collective-permute-done | bytes 1048608 | tf_op jit(solution)/shard_map/ppermute | solution.py:83
  56.2 1.7 %fusion.4 = bf16[128,2048]{0,1:T(8,128)(2,1)S(1)} fusion(f32[128,2048]{0,1:T(8,128)S(1)} %fusion.26, f32[128,2048]{0,1:T(8,128)S(1)} %collective-permute-done.6, f32[128,2048]{0,1:T(8,128)S(1)} %collective-permute-done, bf16[128,256]{1,0:T(8,128)(2,1)S(1)} %copy-done.1, bf16[8192,256]{1,0:T(8,128)(2,1)} %param.8, s32[]{:T(128)S(6)} %select_n.45), kind=kOutput, calls=%fused_computation.9 | convolution fusion | flops 135266304 | bytes 4784132 | tf_op jit(solution)/shard_map/dot_general | solution.py:71
  57.9 1.0 %copy.16 = bf16[128,2048]{1,0:T(8,128)(2,1)} copy(bf16[128,2048]{0,1:T(8,128)(2,1)S(1)} %fusion.4) | data formatting | bytes 1048576
  (53 shorter events, 5.4 us)
Async XLA Ops:
  0.6 23.6 %copy-start = (bf16[128,2048]{1,0:T(8,128)(2,1)S(1)}, bf16[128,2048]{1,0:T(8,128)(2,1)}, u32[]{:S(2)}) copy-start(bf16[128,2048]{1,0:T(8,128)(2,1)} %param.6) | copy-start | bytes 1572868
  0.6 23.4 %copy-start.1 = (bf16[128,256]{1,0:T(8,128)(2,1)S(1)}, bf16[128,256]{1,0:T(8,128)(2,1)}, u32[]{:S(2)}) copy-start(bf16[128,256]{1,0:T(8,128)(2,1)} %param.7) | copy-start | bytes 196612
  2.3 5.5 %collective-permute-start.2 = (bf16[1,16,2304]{2,1,0:T(8,128)(2,1)S(1)}, bf16[1,16,2304]{2,1,0:T(8,128)(2,1)S(1)}, u32[]{:S(2)}, u32[]{:S(2)}) collective-permute-start(bf16[1,16,2304]{2,1,0:T(8,128)(2,1)S(1)} %get-tuple-element.20), channel_id=1, source_target_pairs={{0,4},{4,0},{8,12},{12,8},{16,20},{20,16},{24,28},{28,24},{1,5},{5... | collective-permute-start | bytes 221192 | tf_op jit(solution)/shard_map/ppermute | solution.py:36
  6.9 17.6 %collective-permute-start.1 = (f32[128,2048]{0,1:T(8,128)S(1)}, f32[128,2048]{0,1:T(8,128)S(1)}, u32[]{:S(2)}, u32[]{:S(2)}) collective-permute-start(f32[128,2048]{0,1:T(8,128)S(1)} %convolution_bitcast_fusion.1), channel_id=1, source_target_pairs={{0,1},{1,0},{2,3},{3,2},{4,5},{5,4},{6,7},{7,6},{8,9},{9,8},{10,11... | collective-permute-start | bytes 3145736 | tf_op jit(solution)/shard_map/ppermute | solution.py:83
  7.8 8.7 %collective-permute-start.3 = (bf16[2,16,2304]{2,1,0:T(8,128)(2,1)S(1)}, bf16[2,16,2304]{2,1,0:T(8,128)(2,1)S(1)}, u32[]{:S(2)}, u32[]{:S(2)}) collective-permute-start(bf16[2,16,2304]{2,1,0:T(8,128)(2,1)S(1)} %pad_maximum_fusion.1), channel_id=1, source_target_pairs={{0,8},{4,12},{8,0},{12,4},{16,24},{20,28},{24,16},{28,20},{1,9},{5... | collective-permute-start | bytes 442376 | tf_op jit(solution)/shard_map/ppermute | solution.py:41
  9.7 14.0 %collective-permute-start.4 = (bf16[2,16,2304]{2,1,0:T(8,128)(2,1)S(1)}, bf16[2,16,2304]{2,1,0:T(8,128)(2,1)S(1)}, u32[]{:S(2)}, u32[]{:S(2)}) collective-permute-start(bf16[2,16,2304]{2,1,0:T(8,128)(2,1)S(1)} %pad_maximum_fusion.1), channel_id=1, source_target_pairs={{0,16},{4,20},{8,24},{12,28},{16,0},{20,4},{24,8},{28,12},{1,17},{... | collective-permute-start | bytes 442376 | tf_op jit(solution)/shard_map/ppermute | solution.py:41
  12.3 11.4 %collective-permute-start.5 = (bf16[2,16,2304]{2,1,0:T(8,128)(2,1)S(1)}, bf16[2,16,2304]{2,1,0:T(8,128)(2,1)S(1)}, u32[]{:S(2)}, u32[]{:S(2)}) collective-permute-start(bf16[2,16,2304]{2,1,0:T(8,128)(2,1)S(1)} %pad_maximum_fusion.1), channel_id=1, source_target_pairs={{0,24},{4,28},{8,16},{12,20},{16,8},{20,12},{24,0},{28,4},{1,25},{... | collective-permute-start | bytes 442376 | tf_op jit(solution)/shard_map/ppermute | solution.py:41
  27.2 2.2 %collective-permute-start.7 = (f32[1,128,32]{1,2,0:T(8,128)S(1)}, f32[1,128,32]{1,2,0:T(8,128)S(1)}, u32[]{:S(2)}, u32[]{:S(2)}) collective-permute-start(f32[1,128,32]{1,2,0:T(8,128)S(1)} %pad_maximum_fusion.2), channel_id=1, source_target_pairs={{0,1},{1,0},{2,3},{3,2},{4,5},{5,4},{6,7},{7,6},{8,9},{9,8},{10,11... | collective-permute-start | bytes 49160 | tf_op jit(solution)/shard_map/ppermute | solution.py:55
  28.8 26.2 %collective-permute-start = (f32[128,2048]{0,1:T(8,128)S(1)}, f32[128,2048]{0,1:T(8,128)S(1)}, u32[]{:S(2)}, u32[]{:S(2)}) collective-permute-start(f32[128,2048]{0,1:T(8,128)S(1)} %convolution_bitcast_fusion.3), channel_id=1, source_target_pairs={{0,1},{1,0},{2,3},{3,2},{4,5},{5,4},{6,7},{7,6},{8,9},{9,8},{10,11... | collective-permute-start | bytes 3145736 | tf_op jit(solution)/shard_map/ppermute | solution.py:83
  29.4 3.8 %collective-permute-start.8 = (f32[1,128,32]{1,2,0:T(8,128)S(1)}, f32[1,128,32]{1,2,0:T(8,128)S(1)}, u32[]{:S(2)}, u32[]{:S(2)}) collective-permute-start(f32[1,128,32]{1,2,0:T(8,128)S(1)} %add.109), channel_id=1, source_target_pairs={{0,2},{1,3},{2,0},{3,1},{4,6},{5,7},{6,4},{7,5},{8,10},{9,11},{10,... | collective-permute-start | bytes 49160 | tf_op jit(solution)/shard_map/ppermute | solution.py:55
  31.1 25.1 %collective-permute-start.6 = (f32[128,2048]{0,1:T(8,128)}, f32[128,2048]{0,1:T(8,128)S(1)}, u32[]{:S(2)}, u32[]{:S(2)}) collective-permute-start(f32[128,2048]{0,1:T(8,128)} %fusion.3), channel_id=1, source_target_pairs={{0,2},{1,3},{2,0},{3,1},{4,6},{5,7},{6,4},{7,5},{8,10},{9,11},{10,... | collective-permute-start | bytes 3145736 | tf_op jit(solution)/shard_map/ppermute | solution.py:83
  33.8 7.8 %collective-permute-start.15 = (bf16[1,16,2304]{2,1,0:T(8,128)(2,1)S(1)}, bf16[1,16,2304]{2,1,0:T(8,128)(2,1)S(1)}, u32[]{:S(2)}, u32[]{:S(2)}) collective-permute-start(bf16[1,16,2304]{2,1,0:T(8,128)(2,1)S(1)} %fusion.25), channel_id=1, source_target_pairs={{0,28},{4,24},{8,20},{12,16},{16,12},{20,8},{24,4},{28,0},{1,29},{... | collective-permute-start | bytes 221192 | tf_op jit(solution)/shard_map/ppermute | solution.py:158
  36.8 9.7 %collective-permute-start.14 = (bf16[1,16,2304]{2,1,0:T(8,128)(2,1)S(1)}, bf16[1,16,2304]{2,1,0:T(8,128)(2,1)S(1)}, u32[]{:S(2)}, u32[]{:S(2)}) collective-permute-start(bf16[1,16,2304]{2,1,0:T(8,128)(2,1)S(1)} %get-tuple-element.11), channel_id=1, source_target_pairs={{0,24},{4,28},{8,16},{12,20},{16,8},{20,12},{24,0},{28,4},{1,25},{... | collective-permute-start | bytes 221192 | tf_op jit(solution)/shard_map/ppermute | solution.py:158
  38.3 11.0 %collective-permute-start.13 = (bf16[1,16,2304]{2,1,0:T(8,128)(2,1)S(1)}, bf16[1,16,2304]{2,1,0:T(8,128)(2,1)S(1)}, u32[]{:S(2)}, u32[]{:S(2)}) collective-permute-start(bf16[1,16,2304]{2,1,0:T(8,128)(2,1)S(1)} %get-tuple-element.12), channel_id=1, source_target_pairs={{0,20},{4,16},{8,28},{12,24},{16,4},{20,0},{24,12},{28,8},{1,21},{... | collective-permute-start | bytes 221192 | tf_op jit(solution)/shard_map/ppermute | solution.py:158
  41.7 7.7 %collective-permute-start.12 = (bf16[1,16,2304]{2,1,0:T(8,128)(2,1)S(1)}, bf16[1,16,2304]{2,1,0:T(8,128)(2,1)S(1)}, u32[]{:S(2)}, u32[]{:S(2)}) collective-permute-start(bf16[1,16,2304]{2,1,0:T(8,128)(2,1)S(1)} %get-tuple-element.13), channel_id=1, source_target_pairs={{0,16},{4,20},{8,24},{12,28},{16,0},{20,4},{24,8},{28,12},{1,17},{... | collective-permute-start | bytes 221192 | tf_op jit(solution)/shard_map/ppermute | solution.py:158
  46.5 5.8 %collective-permute-start.11 = (bf16[1,16,2304]{2,1,0:T(8,128)(2,1)S(1)}, bf16[1,16,2304]{2,1,0:T(8,128)(2,1)S(1)}, u32[]{:S(2)}, u32[]{:S(2)}) collective-permute-start(bf16[1,16,2304]{2,1,0:T(8,128)(2,1)S(1)} %get-tuple-element.14), channel_id=1, source_target_pairs={{0,12},{4,8},{8,4},{12,0},{16,28},{20,24},{24,20},{28,16},{1,13},{... | collective-permute-start | bytes 221192 | tf_op jit(solution)/shard_map/ppermute | solution.py:158
  49.3 4.4 %collective-permute-start.10 = (bf16[1,16,2304]{2,1,0:T(8,128)(2,1)S(1)}, bf16[1,16,2304]{2,1,0:T(8,128)(2,1)S(1)}, u32[]{:S(2)}, u32[]{:S(2)}) collective-permute-start(bf16[1,16,2304]{2,1,0:T(8,128)(2,1)S(1)} %get-tuple-element.15), channel_id=1, source_target_pairs={{0,8},{4,12},{8,0},{12,4},{16,24},{20,28},{24,16},{28,20},{1,9},{5... | collective-permute-start | bytes 221192 | tf_op jit(solution)/shard_map/ppermute | solution.py:158
  49.3 4.4 %collective-permute-start.9 = (bf16[1,16,2304]{2,1,0:T(8,128)(2,1)S(1)}, bf16[1,16,2304]{2,1,0:T(8,128)(2,1)S(1)}, u32[]{:S(2)}, u32[]{:S(2)}) collective-permute-start(bf16[1,16,2304]{2,1,0:T(8,128)(2,1)S(1)} %get-tuple-element.10), channel_id=1, source_target_pairs={{0,4},{4,0},{8,12},{12,8},{16,20},{20,16},{24,28},{28,24},{1,5},{5... | collective-permute-start | bytes 221192 | tf_op jit(solution)/shard_map/ppermute | solution.py:158

commit v8 on v7

--- a/solution.py
+++ b/solution.py
@@ -57,12 +57,7 @@
     return total
 
 
-def _frozen_term(cotangent, weight, axis, size, ready=None):
-    if size & (size - 1) != 0:
-        partial = lax.dot_general(
-            cotangent, weight, (((1,), (1,)), ((), ())), preferred_element_type=jnp.float32
-        )
-        return lax.psum_scatter(partial, axis, scatter_dimension=1, tiled=True), ready
+def _frozen_terms(cotangent, weight, axis, size):
     me = lax.axis_index(axis)
     rows = weight.shape[0] // size
 
@@ -72,10 +67,13 @@
             cotangent, piece, (((1,), (1,)), ((), ())), preferred_element_type=jnp.float32
         )
 
-    held = [term(me ^ e) for e in range(size)]
+    return [term(me ^ e) for e in range(size)]
+
+
+def _frozen_reduce(held, axis, size, ready):
     step = 0
     while len(held) > 1:
-        if step == 1 and ready is not None:
+        if step == 1:
             *leaving, ready = lax.optimization_barrier((*held[1::2], ready))
             held[1::2] = leaving
         partner = 1 << step
@@ -102,6 +100,11 @@
 
 
     packed = jnp.concatenate([adapter_down_weight, adapter_up_weight], axis=2)
+    halving = tensor_size > 1 and tensor_size & (tensor_size - 1) == 0
+    if halving:
+        frozen = _frozen_terms(cotangent, frozen_key_weight, "tensor", tensor_size)
+        *leaving, packed = lax.optimization_barrier((*frozen[1::2], packed))
+        frozen[1::2] = leaving
     stacked, order = _gather_dp(packed, "dp", dp_size)
     stacked = stacked.reshape(dp_size, held_tenants, *packed.shape[1:])
     owner = tenant_per_block // held_tenants
@@ -121,7 +124,13 @@
         "bnk,brk->bnr", cotangent_blocks, sel_up, preferred_element_type=jnp.float32
     )
     lows = jnp.concatenate([low_in, reduced_output], axis=2)
-    base_grad, lows = _frozen_term(cotangent, frozen_key_weight, "tensor", tensor_size, lows)
+    if halving:
+        base_grad, lows = _frozen_reduce(frozen, "tensor", tensor_size, lows)
+    else:
+        partial = lax.dot_general(
+            cotangent, frozen_key_weight, (((1,), (1,)), ((), ())), preferred_element_type=jnp.float32
+        )
+        base_grad = lax.psum_scatter(partial, "tensor", scatter_dimension=1, tiled=True)
     lows = _psum_small(lows, "tensor", tensor_size)
     reduced_input_batch = lows[:, :, :adapter_rank_size].astype(jnp.bfloat16)
     low_out_b = lows[:, :, adapter_rank_size:].astype(jnp.bfloat16)

time: 59.2 us -> 62.2 us (1.051)
  waiting for transfers between devices: 18.3 us -> 20.7 us
  starting transfers between devices: 25.3 us -> 26 us
    ppermute x1, waiting for transfers between devices: 0.01 us -> 1.69 us  [_gather_dp(): lax.ppermute(local, axis, [(i, i ^ 1) for i in range(size)])]
    ppermute x7, waiting for transfers between devices: 4.32 us -> 5.66 us  [on_device(): lax.ppermute(outgoing.astype(jnp.bfloat16), 'dp', pairs).astype(jnp.float32)]
    ppermute x3, waiting for transfers between devices: 1.14 us -> 0.01 us  [_frozen_reduce(): got = [lax.ppermute(held[e], axis, pairs) for e in range(1, len(held), 2)]]
    ppermute x2, waiting for transfers between devices: 1.5 us -> 2.17 us  [_psum_small(): lax.ppermute(total, axis, [(i, i ^ step) for i in range(size)])]
    ppermute x7, starting transfers between devices: 15 us -> 15.7 us  [on_device(): lax.ppermute(outgoing.astype(jnp.bfloat16), 'dp', pairs).astype(jnp.float32)]
    unnamed x9 -> x12, local copies, waits for them, and re-layouts: 1.97 us -> 1.7 us
  transfers between devices with their start and end apart: 16 -> 16, of which waited for: 8 -> 8; matrix products, arithmetic and copies ran while one was open for 11% -> 7% of each run, Pallas kernels for 0% -> 0%
where the time goes in v8:
time: 62.2 us; the launch traced here: 62 us
  starting transfers between devices  26 us (42%)
  waiting for transfers between devices  20.7 us (33%)
  matrix products  9.47 us (15%)
  local copies, waits for them, and re-layouts  2.65 us (4%)
  other arithmetic  1.61 us (3%)
  between operations  1.56 us (3%)
    ppermute x7, starting transfers between devices, on_device(): lax.ppermute(outgoing.astype(jnp.bfloat16), 'dp', pairs).astype(jnp.float32)  15.7 us
    ppermute x3, waiting for transfers between devices, _gather_dp(): got.append(lax.ppermute(pair, axis, [(i, i ^ shift) for i in range(size)]))  11.2 us
    dot_general x4, matrix products, term(): lax.dot_general(cotangent, piece, (((1,), (1,)), ((), ())), preferred_ele...  7.99 us
    ppermute x7, waiting for transfers between devices, on_device(): lax.ppermute(outgoing.astype(jnp.bfloat16), 'dp', pairs).astype(jnp.float32)  5.66 us
    ppermute x3, starting transfers between devices, _gather_dp(): got.append(lax.ppermute(pair, axis, [(i, i ^ shift) for i in range(size)]))  4.68 us
    ppermute x1, starting transfers between devices, _gather_dp(): lax.ppermute(local, axis, [(i, i ^ 1) for i in range(size)])  3.03 us
    ppermute x2, waiting for transfers between devices, _psum_small(): lax.ppermute(total, axis, [(i, i ^ step) for i in range(size)])  2.17 us
    unnamed x12, local copies, waits for them, and re-layouts  1.7 us
  transfers between devices with their start and end apart: 16, of which 8 were waited for; matrix products, arithmetic and copies ran while one was open for 7% of the time, Pallas kernels for 0%

profile of v8, /device:TPU:0, one launch (start us, length us, event | category | flops | bytes accessed | tf_op | source)
XLA Modules:
  0.0 62.0 jit_solution(13814814674863101324)
XLA Ops:
  0.7 1.7 %convolution_bitcast_fusion.3 = f32[128,2048]{0,1:T(8,128)S(1)} fusion(bf16[128,256]{1,0:T(8,128)(2,1)} %param.7, bf16[8192,256]{1,0:T(8,128)(2,1)} %param.8, s32[]{:T(128)S(6)} %select_n.46), kind=kOutput, calls=%fused_computation.3 | convolution fusion | flops 134217728 | bytes 2162692 | tf_op jit(solution)/shard_map/dot_general | solution.py:66
  2.4 1.6 %convolution_bitcast_fusion.2 = f32[128,2048]{0,1:T(8,128)S(1)} fusion(bf16[128,256]{1,0:T(8,128)(2,1)} %param.7, bf16[8192,256]{1,0:T(8,128)(2,1)} %param.8, s32[]{:T(128)S(6)} %select_n.47), kind=kOutput, calls=%fused_computation.2 | convolution fusion | flops 134217728 | bytes 2162692 | tf_op jit(solution)/shard_map/dot_general | solution.py:66
  4.1 3.0 %collective-permute-start.2 = (bf16[1,16,2304]{2,1,0:T(8,128)(2,1)S(1)}, bf16[1,16,2304]{2,1,0:T(8,128)(2,1)S(1)}, u32[]{:S(2)}, u32[]{:S(2)}) collective-permute-start(bf16[1,16,2304]{2,1,0:T(8,128)(2,1)S(1)} %pad_maximum_fusion.1), channel_id=1, source_target_pairs={{0,4},{4,0},{8,12},{12,8},{16,20},{20,16},{24,28},{28,24},{1,5},{5... | collective-permute-start | bytes 221192 | tf_op jit(solution)/shard_map/ppermute | solution.py:36
  7.8 1.7 %collective-permute-done.2 = bf16[1,16,2304]{2,1,0:T(8,128)(2,1)S(1)} collective-permute-done((bf16[1,16,2304]{2,1,0:T(8,128)(2,1)S(1)}, bf16[1,16,2304]{2,1,0:T(8,128)(2,1)S(1)}, u32[]{:S(2)}, u32[]{:S(2)}) %collective-permute-start.2) | collective-permute-done | bytes 73760 | tf_op jit(solution)/shard_map/ppermute | solution.py:36
  9.5 0.6 %constant_dynamic-update-slice_fusion = (bf16[2,16,2304]{2,1,0:T(8,128)(2,1)}, bf16[8,16,2304]{2,1,0:T(8,128)(2,1)S(1)}) fusion(bf16[2,16,2304]{2,1,0:T(8,128)(2,1)} %get-tuple-element.24, bf16[1,16,2304]{2,1,0:T(8,128)(2,1)S(1)} %collective-permute-done.2, bf16[8,16,2304]{2,1,0:T(8,128)(2,1)S(1)} %get-tuple-element.25), kind=kLoop, calls=%fused_computation.65 | loop fusion | bytes 221184 | tf_op jit(solution)/shard_map/concatenate | solution.py:36
  10.1 2.1 %collective-permute-start.3 = (bf16[2,16,2304]{2,1,0:T(8,128)(2,1)}, bf16[2,16,2304]{2,1,0:T(8,128)(2,1)S(1)}, u32[]{:S(2)}, u32[]{:S(2)}) collective-permute-start(bf16[2,16,2304]{2,1,0:T(8,128)(2,1)} %get-tuple-element.22), channel_id=1, source_target_pairs={{0,8},{4,12},{8,0},{12,4},{16,24},{20,28},{24,16},{28,20},{1,9},{5... | collective-permute-start | bytes 442376 | tf_op jit(solution)/shard_map/ppermute | solution.py:41
  12.9 2.6 %collective-permute-start.4 = (bf16[2,16,2304]{2,1,0:T(8,128)(2,1)}, bf16[2,16,2304]{2,1,0:T(8,128)(2,1)S(1)}, u32[]{:S(2)}, u32[]{:S(2)}) collective-permute-start(bf16[2,16,2304]{2,1,0:T(8,128)(2,1)} %get-tuple-element.22), channel_id=1, source_target_pairs={{0,16},{4,20},{8,24},{12,28},{16,0},{20,4},{24,8},{28,12},{1,17},{... | collective-permute-start | bytes 442376 | tf_op jit(solution)/shard_map/ppermute | solution.py:41
  15.5 11.2 %collective-permute-done.4 = bf16[2,16,2304]{2,1,0:T(8,128)(2,1)S(1)} collective-permute-done((bf16[2,16,2304]{2,1,0:T(8,128)(2,1)}, bf16[2,16,2304]{2,1,0:T(8,128)(2,1)S(1)}, u32[]{:S(2)}, u32[]{:S(2)}) %collective-permute-start.4) | collective-permute-done | bytes 147488 | tf_op jit(solution)/shard_map/ppermute | solution.py:41
  27.5 3.0 %fusion.3 = f32[128,2048]{0,1:T(8,128)} fusion(f32[128,2048]{0,1:T(8,128)} %collective-permute-done.1, bf16[128,256]{1,0:T(8,128)(2,1)S(1)} %copy-done.1, bf16[8192,256]{1,0:T(8,128)(2,1)} %param.8, s32[]{:T(128)S(6)} %select_n.48), kind=kOutput, calls=%fused_computation.8 | convolution fusion | flops 134479872 | bytes 3211268 | tf_op jit(solution)/shard_map/dot_general | solution.py:66
  31.0 0.7 %collective-permute-done.7 = f32[1,128,32]{1,2,0:T(8,128)S(1)} collective-permute-done((f32[1,128,32]{1,2,0:T(8,128)S(1)}, f32[1,128,32]{1,2,0:T(8,128)S(1)}, u32[]{:S(2)}, u32[]{:S(2)}) %collective-permute-start.7) | collective-permute-done | bytes 16416 | tf_op jit(solution)/shard_map/ppermute | solution.py:55
  31.7 1.5 %collective-permute-start.8 = (f32[1,128,32]{1,2,0:T(8,128)S(1)}, f32[1,128,32]{1,2,0:T(8,128)S(1)}, u32[]{:S(2)}, u32[]{:S(2)}) collective-permute-start(f32[1,128,32]{1,2,0:T(8,128)S(1)} %add.109), channel_id=1, source_target_pairs={{0,2},{1,3},{2,0},{3,1},{4,6},{5,7},{6,4},{7,5},{8,10},{9,11},{10,... | collective-permute-start | bytes 49160 | tf_op jit(solution)/shard_map/ppermute | solution.py:55
  33.9 1.5 %collective-permute-done.8 = f32[1,128,32]{1,2,0:T(8,128)S(1)} collective-permute-done((f32[1,128,32]{1,2,0:T(8,128)S(1)}, f32[1,128,32]{1,2,0:T(8,128)S(1)}, u32[]{:S(2)}, u32[]{:S(2)}) %collective-permute-start.8) | collective-permute-done | bytes 16416 | tf_op jit(solution)/shard_map/ppermute | solution.py:55
  36.1 3.8 %collective-permute-start.15 = (bf16[1,16,2304]{2,1,0:T(8,128)(2,1)S(1)}, bf16[1,16,2304]{2,1,0:T(8,128)(2,1)S(1)}, u32[]{:S(2)}, u32[]{:S(2)}) collective-permute-start(bf16[1,16,2304]{2,1,0:T(8,128)(2,1)S(1)} %fusion.25), channel_id=1, source_target_pairs={{0,28},{4,24},{8,20},{12,16},{16,12},{20,8},{24,4},{28,0},{1,29},{... | collective-permute-start | bytes 221192 | tf_op jit(solution)/shard_map/ppermute | solution.py:167
  39.9 1.2 %collective-permute-start.14 = (bf16[1,16,2304]{2,1,0:T(8,128)(2,1)S(1)}, bf16[1,16,2304]{2,1,0:T(8,128)(2,1)S(1)}, u32[]{:S(2)}, u32[]{:S(2)}) collective-permute-start(bf16[1,16,2304]{2,1,0:T(8,128)(2,1)S(1)} %get-tuple-element.17), channel_id=1, source_target_pairs={{0,24},{4,28},{8,16},{12,20},{16,8},{20,12},{24,0},{28,4},{1,25},{... | collective-permute-start | bytes 221192 | tf_op jit(solution)/shard_map/ppermute | solution.py:167
  41.0 2.7 %collective-permute-start.13 = (bf16[1,16,2304]{2,1,0:T(8,128)(2,1)S(1)}, bf16[1,16,2304]{2,1,0:T(8,128)(2,1)S(1)}, u32[]{:S(2)}, u32[]{:S(2)}) collective-permute-start(bf16[1,16,2304]{2,1,0:T(8,128)(2,1)S(1)} %get-tuple-element.18), channel_id=1, source_target_pairs={{0,20},{4,16},{8,28},{12,24},{16,4},{20,0},{24,12},{28,8},{1,21},{... | collective-permute-start | bytes 221192 | tf_op jit(solution)/shard_map/ppermute | solution.py:167
  43.7 4.7 %collective-permute-start.12 = (bf16[1,16,2304]{2,1,0:T(8,128)(2,1)S(1)}, bf16[1,16,2304]{2,1,0:T(8,128)(2,1)S(1)}, u32[]{:S(2)}, u32[]{:S(2)}) collective-permute-start(bf16[1,16,2304]{2,1,0:T(8,128)(2,1)S(1)} %get-tuple-element.19), channel_id=1, source_target_pairs={{0,16},{4,20},{8,24},{12,28},{16,0},{20,4},{24,8},{28,12},{1,17},{... | collective-permute-start | bytes 221192 | tf_op jit(solution)/shard_map/ppermute | solution.py:167
  48.4 2.5 %collective-permute-start.11 = (bf16[1,16,2304]{2,1,0:T(8,128)(2,1)S(1)}, bf16[1,16,2304]{2,1,0:T(8,128)(2,1)S(1)}, u32[]{:S(2)}, u32[]{:S(2)}) collective-permute-start(bf16[1,16,2304]{2,1,0:T(8,128)(2,1)S(1)} %get-tuple-element.20), channel_id=1, source_target_pairs={{0,12},{4,8},{8,4},{12,0},{16,28},{20,24},{24,20},{28,16},{1,13},{... | collective-permute-start | bytes 221192 | tf_op jit(solution)/shard_map/ppermute | solution.py:167
  50.9 1.1 %collective-permute-done.13 = bf16[1,16,2304]{2,1,0:T(8,128)(2,1)S(1)} collective-permute-done((bf16[1,16,2304]{2,1,0:T(8,128)(2,1)S(1)}, bf16[1,16,2304]{2,1,0:T(8,128)(2,1)S(1)}, u32[]{:S(2)}, u32[]{:S(2)}) %collective-permute-start.13) | collective-permute-done | bytes 73760 | tf_op jit(solution)/shard_map/ppermute | solution.py:167
  52.3 1.3 %collective-permute-done.12 = bf16[1,16,2304]{2,1,0:T(8,128)(2,1)S(1)} collective-permute-done((bf16[1,16,2304]{2,1,0:T(8,128)(2,1)S(1)}, bf16[1,16,2304]{2,1,0:T(8,128)(2,1)S(1)}, u32[]{:S(2)}, u32[]{:S(2)}) %collective-permute-start.12) | collective-permute-done | bytes 73760 | tf_op jit(solution)/shard_map/ppermute | solution.py:167
  54.7 1.7 %collective-permute-done.10 = bf16[1,16,2304]{2,1,0:T(8,128)(2,1)S(1)} collective-permute-done((bf16[1,16,2304]{2,1,0:T(8,128)(2,1)S(1)}, bf16[1,16,2304]{2,1,0:T(8,128)(2,1)S(1)}, u32[]{:S(2)}, u32[]{:S(2)}) %collective-permute-start.10) | collective-permute-done | bytes 73760 | tf_op jit(solution)/shard_map/ppermute | solution.py:167
  56.3 1.6 %collective-permute-done.9 = bf16[1,16,2304]{2,1,0:T(8,128)(2,1)S(1)} collective-permute-done((bf16[1,16,2304]{2,1,0:T(8,128)(2,1)S(1)}, bf16[1,16,2304]{2,1,0:T(8,128)(2,1)S(1)}, u32[]{:S(2)}, u32[]{:S(2)}) %collective-permute-start.9) | collective-permute-done | bytes 73760 | tf_op jit(solution)/shard_map/ppermute | solution.py:167
  58.6 0.7 %slice_add_fusion = f32[1,16,2048]{2,1,0:T(8,128)} fusion(f32[1,16,2304]{2,1,0:T(8,128)S(1)} %convert_element_type.164, f32[1,16,2304]{2,1,0:T(8,128)S(1)} %convert_element_type.161, f32[1,16,2304]{2,1,0:T(8,128)S(1)} %convert_element_type.158, f32[1,16,2304]{2,1,0:T(8,128)S(1)} %convert_element_type.155, f32[1,16,2304]{2,1,0:T(8,128)S(1)} %convert_element_type.152, ...), kind=kLoop, calls=%fused_computation.38 | loop fusion | flops 229376 | bytes 1179648 | tf_op jit(solution)/shard_map/add | solution.py:168
  59.3 1.7 %fusion.4 = bf16[128,2048]{0,1:T(8,128)(2,1)S(1)} fusion(f32[128,2048]{0,1:T(8,128)S(1)} %fusion.26, f32[128,2048]{0,1:T(8,128)S(1)} %collective-permute-done.6, f32[128,2048]{0,1:T(8,128)S(1)} %collective-permute-done, bf16[128,256]{1,0:T(8,128)(2,1)S(1)} %copy-done.1, bf16[8192,256]{1,0:T(8,128)(2,1)} %param.8, s32[]{:T(128)S(6)} %select_n.45), kind=kOutput, calls=%fused_computation.9 | convolution fusion | flops 135266304 | bytes 4784132 | tf_op jit(solution)/shard_map/dot_general | solution.py:66
  61.0 1.0 %copy.16 = bf16[128,2048]{1,0:T(8,128)(2,1)} copy(bf16[128,2048]{0,1:T(8,128)(2,1)S(1)} %fusion.4) | data formatting | bytes 1048576
  (56 shorter events, 5.4 us)
Async XLA Ops:
  0.6 26.6 %copy-start = (bf16[128,2048]{1,0:T(8,128)(2,1)S(1)}, bf16[128,2048]{1,0:T(8,128)(2,1)}, u32[]{:S(2)}) copy-start(bf16[128,2048]{1,0:T(8,128)(2,1)} %param.6) | copy-start | bytes 1572868
  0.6 26.5 %copy-start.1 = (bf16[128,256]{1,0:T(8,128)(2,1)S(1)}, bf16[128,256]{1,0:T(8,128)(2,1)}, u32[]{:S(2)}) copy-start(bf16[128,256]{1,0:T(8,128)(2,1)} %param.7) | copy-start | bytes 196612
  0.7 3.4 %copy-start.3 = (bf16[1,16,256]{2,1,0:T(8,128)(2,1)S(1)}, bf16[1,16,256]{2,1,0:T(8,128)(2,1)}, u32[]{:S(2)}) copy-start(bf16[1,16,256]{2,1,0:T(8,128)(2,1)} %param.10) | copy-start | bytes 24580
  0.7 3.4 %copy-start.2 = (bf16[1,16,2048]{2,1,0:T(8,128)(2,1)S(1)}, bf16[1,16,2048]{2,1,0:T(8,128)(2,1)}, u32[]{:S(2)}) copy-start(bf16[1,16,2048]{2,1,0:T(8,128)(2,1)} %param.9) | copy-start | bytes 196612
  4.1 5.4 %collective-permute-start.2 = (bf16[1,16,2304]{2,1,0:T(8,128)(2,1)S(1)}, bf16[1,16,2304]{2,1,0:T(8,128)(2,1)S(1)}, u32[]{:S(2)}, u32[]{:S(2)}) collective-permute-start(bf16[1,16,2304]{2,1,0:T(8,128)(2,1)S(1)} %pad_maximum_fusion.1), channel_id=1, source_target_pairs={{0,4},{4,0},{8,12},{12,8},{16,20},{20,16},{24,28},{28,24},{1,5},{5... | collective-permute-start | bytes 221192 | tf_op jit(solution)/shard_map/ppermute | solution.py:36
  10.1 5.4 %collective-permute-start.3 = (bf16[2,16,2304]{2,1,0:T(8,128)(2,1)}, bf16[2,16,2304]{2,1,0:T(8,128)(2,1)S(1)}, u32[]{:S(2)}, u32[]{:S(2)}) collective-permute-start(bf16[2,16,2304]{2,1,0:T(8,128)(2,1)} %get-tuple-element.22), channel_id=1, source_target_pairs={{0,8},{4,12},{8,0},{12,4},{16,24},{20,28},{24,16},{28,20},{1,9},{5... | collective-permute-start | bytes 442376 | tf_op jit(solution)/shard_map/ppermute | solution.py:41
  12.2 15.3 %collective-permute-start.1 = (f32[128,2048]{0,1:T(8,128)S(1)}, f32[128,2048]{0,1:T(8,128)}, u32[]{:S(2)}, u32[]{:S(2)}) collective-permute-start(f32[128,2048]{0,1:T(8,128)S(1)} %convolution_bitcast_fusion.2), channel_id=1, source_target_pairs={{0,1},{1,0},{2,3},{3,2},{4,5},{5,4},{6,7},{7,6},{8,9},{9,8},{10,11... | collective-permute-start | bytes 3145736 | tf_op jit(solution)/shard_map/ppermute | solution.py:81
  12.9 13.8 %collective-permute-start.4 = (bf16[2,16,2304]{2,1,0:T(8,128)(2,1)}, bf16[2,16,2304]{2,1,0:T(8,128)(2,1)S(1)}, u32[]{:S(2)}, u32[]{:S(2)}) collective-permute-start(bf16[2,16,2304]{2,1,0:T(8,128)(2,1)} %get-tuple-element.22), channel_id=1, source_target_pairs={{0,16},{4,20},{8,24},{12,28},{16,0},{20,4},{24,8},{28,12},{1,17},{... | collective-permute-start | bytes 442376 | tf_op jit(solution)/shard_map/ppermute | solution.py:41
  15.5 11.2 %collective-permute-start.5 = (bf16[2,16,2304]{2,1,0:T(8,128)(2,1)}, bf16[2,16,2304]{2,1,0:T(8,128)(2,1)S(1)}, u32[]{:S(2)}, u32[]{:S(2)}) collective-permute-start(bf16[2,16,2304]{2,1,0:T(8,128)(2,1)} %get-tuple-element.22), channel_id=1, source_target_pairs={{0,24},{4,28},{8,16},{12,20},{16,8},{20,12},{24,0},{28,4},{1,25},{... | collective-permute-start | bytes 442376 | tf_op jit(solution)/shard_map/ppermute | solution.py:41
  30.5 1.2 %collective-permute-start.7 = (f32[1,128,32]{1,2,0:T(8,128)S(1)}, f32[1,128,32]{1,2,0:T(8,128)S(1)}, u32[]{:S(2)}, u32[]{:S(2)}) collective-permute-start(f32[1,128,32]{1,2,0:T(8,128)S(1)} %pad_maximum_fusion.2), channel_id=1, source_target_pairs={{0,1},{1,0},{2,3},{3,2},{4,5},{5,4},{6,7},{7,6},{8,9},{9,8},{10,11... | collective-permute-start | bytes 49160 | tf_op jit(solution)/shard_map/ppermute | solution.py:55
  30.5 28.8 %collective-permute-start = (f32[128,2048]{0,1:T(8,128)S(1)}, f32[128,2048]{0,1:T(8,128)S(1)}, u32[]{:S(2)}, u32[]{:S(2)}) collective-permute-start(f32[128,2048]{0,1:T(8,128)S(1)} %convolution_bitcast_fusion.3), channel_id=1, source_target_pairs={{0,1},{1,0},{2,3},{3,2},{4,5},{5,4},{6,7},{7,6},{8,9},{9,8},{10,11... | collective-permute-start | bytes 3145736 | tf_op jit(solution)/shard_map/ppermute | solution.py:81
  31.7 3.7 %collective-permute-start.8 = (f32[1,128,32]{1,2,0:T(8,128)S(1)}, f32[1,128,32]{1,2,0:T(8,128)S(1)}, u32[]{:S(2)}, u32[]{:S(2)}) collective-permute-start(f32[1,128,32]{1,2,0:T(8,128)S(1)} %add.109), channel_id=1, source_target_pairs={{0,2},{1,3},{2,0},{3,1},{4,6},{5,7},{6,4},{7,5},{8,10},{9,11},{10,... | collective-permute-start | bytes 49160 | tf_op jit(solution)/shard_map/ppermute | solution.py:55
  33.4 25.9 %collective-permute-start.6 = (f32[128,2048]{0,1:T(8,128)}, f32[128,2048]{0,1:T(8,128)S(1)}, u32[]{:S(2)}, u32[]{:S(2)}) collective-permute-start(f32[128,2048]{0,1:T(8,128)} %fusion.3), channel_id=1, source_target_pairs={{0,2},{1,3},{2,0},{3,1},{4,6},{5,7},{6,4},{7,5},{8,10},{9,11},{10,... | collective-permute-start | bytes 3145736 | tf_op jit(solution)/shard_map/ppermute | solution.py:81
  36.1 7.7 %collective-permute-start.15 = (bf16[1,16,2304]{2,1,0:T(8,128)(2,1)S(1)}, bf16[1,16,2304]{2,1,0:T(8,128)(2,1)S(1)}, u32[]{:S(2)}, u32[]{:S(2)}) collective-permute-start(bf16[1,16,2304]{2,1,0:T(8,128)(2,1)S(1)} %fusion.25), channel_id=1, source_target_pairs={{0,28},{4,24},{8,20},{12,16},{16,12},{20,8},{24,4},{28,0},{1,29},{... | collective-permute-start | bytes 221192 | tf_op jit(solution)/shard_map/ppermute | solution.py:167
  39.9 8.6 %collective-permute-start.14 = (bf16[1,16,2304]{2,1,0:T(8,128)(2,1)S(1)}, bf16[1,16,2304]{2,1,0:T(8,128)(2,1)S(1)}, u32[]{:S(2)}, u32[]{:S(2)}) collective-permute-start(bf16[1,16,2304]{2,1,0:T(8,128)(2,1)S(1)} %get-tuple-element.17), channel_id=1, source_target_pairs={{0,24},{4,28},{8,16},{12,20},{16,8},{20,12},{24,0},{28,4},{1,25},{... | collective-permute-start | bytes 221192 | tf_op jit(solution)/shard_map/ppermute | solution.py:167
  41.0 10.9 %collective-permute-start.13 = (bf16[1,16,2304]{2,1,0:T(8,128)(2,1)S(1)}, bf16[1,16,2304]{2,1,0:T(8,128)(2,1)S(1)}, u32[]{:S(2)}, u32[]{:S(2)}) collective-permute-start(bf16[1,16,2304]{2,1,0:T(8,128)(2,1)S(1)} %get-tuple-element.18), channel_id=1, source_target_pairs={{0,20},{4,16},{8,28},{12,24},{16,4},{20,0},{24,12},{28,8},{1,21},{... | collective-permute-start | bytes 221192 | tf_op jit(solution)/shard_map/ppermute | solution.py:167
  43.7 9.8 %collective-permute-start.12 = (bf16[1,16,2304]{2,1,0:T(8,128)(2,1)S(1)}, bf16[1,16,2304]{2,1,0:T(8,128)(2,1)S(1)}, u32[]{:S(2)}, u32[]{:S(2)}) collective-permute-start(bf16[1,16,2304]{2,1,0:T(8,128)(2,1)S(1)} %get-tuple-element.19), channel_id=1, source_target_pairs={{0,16},{4,20},{8,24},{12,28},{16,0},{20,4},{24,8},{28,12},{1,17},{... | collective-permute-start | bytes 221192 | tf_op jit(solution)/shard_map/ppermute | solution.py:167
  48.4 6.2 %collective-permute-start.11 = (bf16[1,16,2304]{2,1,0:T(8,128)(2,1)S(1)}, bf16[1,16,2304]{2,1,0:T(8,128)(2,1)S(1)}, u32[]{:S(2)}, u32[]{:S(2)}) collective-permute-start(bf16[1,16,2304]{2,1,0:T(8,128)(2,1)S(1)} %get-tuple-element.20), channel_id=1, source_target_pairs={{0,12},{4,8},{8,4},{12,0},{16,28},{20,24},{24,20},{28,16},{1,13},{... | collective-permute-start | bytes 221192 | tf_op jit(solution)/shard_map/ppermute | solution.py:167
  52.0 4.4 %collective-permute-start.10 = (bf16[1,16,2304]{2,1,0:T(8,128)(2,1)S(1)}, bf16[1,16,2304]{2,1,0:T(8,128)(2,1)S(1)}, u32[]{:S(2)}, u32[]{:S(2)}) collective-permute-start(bf16[1,16,2304]{2,1,0:T(8,128)(2,1)S(1)} %get-tuple-element.21), channel_id=1, source_target_pairs={{0,8},{4,12},{8,0},{12,4},{16,24},{20,28},{24,16},{28,20},{1,9},{5... | collective-permute-start | bytes 221192 | tf_op jit(solution)/shard_map/ppermute | solution.py:167
  53.6 4.4 %collective-permute-start.9 = (bf16[1,16,2304]{2,1,0:T(8,128)(2,1)S(1)}, bf16[1,16,2304]{2,1,0:T(8,128)(2,1)S(1)}, u32[]{:S(2)}, u32[]{:S(2)}) collective-permute-start(bf16[1,16,2304]{2,1,0:T(8,128)(2,1)S(1)} %get-tuple-element.16), channel_id=1, source_target_pairs={{0,4},{4,0},{8,12},{12,8},{16,20},{20,16},{24,28},{28,24},{1,5},{5... | collective-permute-start | bytes 221192 | tf_op jit(solution)/shard_map/ppermute | solution.py:167

commit v9 on v7

--- a/solution.py
+++ b/solution.py
@@ -72,8 +72,14 @@
             cotangent, piece, (((1,), (1,)), ((), ())), preferred_element_type=jnp.float32
         )
 
-    held = [term(me ^ e) for e in range(size)]
-    step = 0
+    pieces = [lax.dynamic_slice_in_dim(weight, (me ^ e) * rows, rows, axis=0) for e in range(1, size, 2)]
+    leaving = jnp.einsum(
+        "nk,bdk->bnd", cotangent, jnp.stack(pieces, 0), preferred_element_type=jnp.float32
+    )
+    pairs = [(i, i ^ 1) for i in range(size)]
+    got = lax.ppermute(leaving, axis, pairs)
+    held = [term(me ^ e) + got[m] for m, e in enumerate(range(0, size, 2))]
+    step = 1
     while len(held) > 1:
         if step == 1 and ready is not None:
             *leaving, ready = lax.optimization_barrier((*held[1::2], ready))

time: 59.2 us -> 60.9 us (1.029)
  starting transfers between devices: 25.3 us -> 21.5 us
  local copies, waits for them, and re-layouts: 2.99 us -> 5.81 us
  waiting for transfers between devices: 18.3 us -> 20.3 us
  matrix products: 9.1 us -> 9.79 us
    ppermute x7, starting transfers between devices: 15 us -> 12 us  [on_device(): lax.ppermute(outgoing.astype(jnp.bfloat16), 'dp', pairs).astype(jnp.float32)]
    dot_general x4 -> x2, matrix products: 7.64 us -> 5.03 us  [term(): lax.dot_general(cotangent, piece, (((1,), (1,)), ((), ())), preferred_ele...]
    ppermute x7, waiting for transfers between devices: 4.32 us -> 6.52 us  [on_device(): lax.ppermute(outgoing.astype(jnp.bfloat16), 'dp', pairs).astype(jnp.float32)]
    dot_general x0 -> x1, matrix products: none -> 2.05 us  [_frozen_term(): jnp.einsum('nk,bdk->bnd', cotangent, jnp.stack(pieces, 0), preferred_elem...]
    another operation x1 -> x2, local copies, waits for them, and re-layouts: 0.01 us -> 1.71 us  [the longest x1 1.71 us: _frozen_term(): jnp.stack(pieces, 0)]
    dot_general x1, matrix products: 0.34 us -> 1.58 us  [on_device(): jnp.einsum('bnr,brd->bnd', low_out_b, sel_down, preferred_element_type=jn...]
    ppermute x2, waiting for transfers between devices: 1.5 us -> 2.68 us  [_psum_small(): lax.ppermute(total, axis, [(i, i ^ step) for i in range(size)])]
    ppermute x3 -> x1, waiting for transfers between devices: 1.14 us -> 0.01 us  [_frozen_term(): got = [lax.ppermute(held[e], axis, pairs) for e in range(1, len(held), 2)]]
  transfers between devices with their start and end apart: 16 -> 15, of which waited for: 8 -> 7; matrix products, arithmetic and copies ran while one was open for 11% -> 15% of each run, Pallas kernels for 0% -> 0%
where the time goes in v9:
time: 60.9 us; the launch traced here: 60.6 us
  starting transfers between devices  21.5 us (35%)
  waiting for transfers between devices  20.3 us (33%)
  matrix products  9.79 us (16%)
  local copies, waits for them, and re-layouts  5.81 us (10%)
  other arithmetic  1.64 us (3%)
  between operations  1.53 us (3%)
    ppermute x7, starting transfers between devices, on_device(): lax.ppermute(outgoing.astype(jnp.bfloat16), 'dp', pairs).astype(jnp.float32)  12 us
    ppermute x3, waiting for transfers between devices, _gather_dp(): got.append(lax.ppermute(pair, axis, [(i, i ^ shift) for i in range(size)]))  11.1 us
    ppermute x7, waiting for transfers between devices, on_device(): lax.ppermute(outgoing.astype(jnp.bfloat16), 'dp', pairs).astype(jnp.float32)  6.52 us
    dot_general x2, matrix products, term(): lax.dot_general(cotangent, piece, (((1,), (1,)), ((), ())), preferred_ele...  5.03 us
    ppermute x3, starting transfers between devices, _gather_dp(): got.append(lax.ppermute(pair, axis, [(i, i ^ shift) for i in range(size)]))  4.45 us
    ppermute x1, starting transfers between devices, _gather_dp(): lax.ppermute(local, axis, [(i, i ^ 1) for i in range(size)])  2.97 us
    ppermute x2, waiting for transfers between devices, _psum_small(): lax.ppermute(total, axis, [(i, i ^ step) for i in range(size)])  2.68 us
    unnamed x17, local copies, waits for them, and re-layouts  2.46 us
  transfers between devices with their start and end apart: 15, of which 7 were waited for; matrix products, arithmetic and copies ran while one was open for 15% of the time, Pallas kernels for 0%

profile of v9, /device:TPU:0, one launch (start us, length us, event | category | flops | bytes accessed | tf_op | source)
XLA Modules:
  0.0 60.6 jit_solution(17862807440186487218)
XLA Ops:
  0.6 0.9 %constant_dynamic-update-slice_fusion.1 = (bf16[1,16,2304]{2,1,0:T(8,128)(2,1)S(1)}, bf16[8,16,2304]{2,1,0:T(8,128)(2,1)S(1)}) fusion(bf16[1,16,2048]{2,1,0:T(8,128)(2,1)} %param.9), kind=kLoop, calls=%fused_computation.64 | loop fusion | bytes 196608
  2.3 3.0 %collective-permute-start.1 = (bf16[1,16,2304]{2,1,0:T(8,128)(2,1)S(1)}, bf16[1,16,2304]{2,1,0:T(8,128)(2,1)S(1)}, u32[]{:S(2)}, u32[]{:S(2)}) collective-permute-start(bf16[1,16,2304]{2,1,0:T(8,128)(2,1)S(1)} %get-tuple-element.22), channel_id=1, source_target_pairs={{0,4},{4,0},{8,12},{12,8},{16,20},{20,16},{24,28},{28,24},{1,5},{5... | collective-permute-start | bytes 221192 | tf_op jit(solution)/shard_map/ppermute | solution.py:36
  5.2 1.7 %dynamic-slice_bitcast_fusion.1 = (bf16[1,2048,256]{2,1,0:T(8,128)(2,1)S(1)}, bf16[1,2048,256]{2,1,0:T(8,128)(2,1)S(1)}) fusion(bf16[8192,256]{1,0:T(8,128)(2,1)} %param.8, s32[]{:T(128)S(6)} %select_n.46, s32[]{:T(128)S(6)} %select_n.47), kind=kLoop, calls=%fused_computation.26 | loop fusion | bytes 4194312 | tf_op jit(solution)/shard_map/stack | solution.py:77
  6.9 2.0 %convolution_bitcast_fusion = f32[2,128,2048]{1,2,0:T(8,128)} fusion(bf16[1,2048,256]{2,1,0:T(8,128)(2,1)S(1)} %get-tuple-element.11, bf16[1,2048,256]{2,1,0:T(8,128)(2,1)S(1)} %get-tuple-element.10, bf16[128,256]{1,0:T(8,128)(2,1)S(1)} %copy-done.3), kind=kOutput, calls=%fused_computation | convolution fusion | flops 269484032 | bytes 4259840 | tf_op jit(solution)/shard_map/nk,bdk->bnd/dot_general | solution.py:76
  9.8 1.6 %collective-permute-start.2 = (bf16[2,16,2304]{2,1,0:T(8,128)(2,1)S(1)}, bf16[2,16,2304]{2,1,0:T(8,128)(2,1)S(1)}, u32[]{:S(2)}, u32[]{:S(2)}) collective-permute-start(bf16[2,16,2304]{2,1,0:T(8,128)(2,1)S(1)} %pad_maximum_fusion.1), channel_id=1, source_target_pairs={{0,8},{4,12},{8,0},{12,4},{16,24},{20,28},{24,16},{28,20},{1,9},{5... | collective-permute-start | bytes 442376 | tf_op jit(solution)/shard_map/ppermute | solution.py:41
  11.4 2.6 %collective-permute-start.3 = (bf16[2,16,2304]{2,1,0:T(8,128)(2,1)S(1)}, bf16[2,16,2304]{2,1,0:T(8,128)(2,1)S(1)}, u32[]{:S(2)}, u32[]{:S(2)}) collective-permute-start(bf16[2,16,2304]{2,1,0:T(8,128)(2,1)S(1)} %pad_maximum_fusion.1), channel_id=1, source_target_pairs={{0,16},{4,20},{8,24},{12,28},{16,0},{20,4},{24,8},{28,12},{1,17},{... | collective-permute-start | bytes 442376 | tf_op jit(solution)/shard_map/ppermute | solution.py:41
  14.2 4.6 %collective-permute-done.2 = bf16[2,16,2304]{2,1,0:T(8,128)(2,1)S(1)} collective-permute-done((bf16[2,16,2304]{2,1,0:T(8,128)(2,1)S(1)}, bf16[2,16,2304]{2,1,0:T(8,128)(2,1)S(1)}, u32[]{:S(2)}, u32[]{:S(2)}) %collective-permute-start.2) | collective-permute-done | bytes 147488 | tf_op jit(solution)/shard_map/ppermute | solution.py:41
  18.9 6.5 %collective-permute-done.3 = bf16[2,16,2304]{2,1,0:T(8,128)(2,1)S(1)} collective-permute-done((bf16[2,16,2304]{2,1,0:T(8,128)(2,1)S(1)}, bf16[2,16,2304]{2,1,0:T(8,128)(2,1)S(1)}, u32[]{:S(2)}, u32[]{:S(2)}) %collective-permute-start.3) | collective-permute-done | bytes 147488 | tf_op jit(solution)/shard_map/ppermute | solution.py:41
  26.1 3.4 %fusion.5 = f32[128,2048]{0,1:T(8,128)} fusion(f32[2,128,2048]{1,2,0:T(8,128)S(1)} %collective-permute-done, bf16[128,256]{1,0:T(8,128)(2,1)S(1)} %copy-done.3, bf16[8192,256]{1,0:T(8,128)(2,1)} %param.8, s32[]{:T(128)S(6)} %select_n.48), kind=kOutput, calls=%fused_computation.18 | convolution fusion | flops 134479872 | bytes 3211268 | tf_op jit(solution)/shard_map/dot_general | solution.py:71
  29.5 1.2 %collective-permute-done.6 = f32[1,128,32]{1,2,0:T(8,128)S(1)} collective-permute-done((f32[1,128,32]{1,2,0:T(8,128)S(1)}, f32[1,128,32]{1,2,0:T(8,128)S(1)}, u32[]{:S(2)}, u32[]{:S(2)}) %collective-permute-start.6) | collective-permute-done | bytes 16416 | tf_op jit(solution)/shard_map/ppermute | solution.py:55
  30.7 1.5 %collective-permute-start.7 = (f32[1,128,32]{1,2,0:T(8,128)S(1)}, f32[1,128,32]{1,2,0:T(8,128)S(1)}, u32[]{:S(2)}, u32[]{:S(2)}) collective-permute-start(f32[1,128,32]{1,2,0:T(8,128)S(1)} %add.109), channel_id=1, source_target_pairs={{0,2},{1,3},{2,0},{3,1},{4,6},{5,7},{6,4},{7,5},{8,10},{9,11},{10,... | collective-permute-start | bytes 49160 | tf_op jit(solution)/shard_map/ppermute | solution.py:55
  33.0 1.5 %collective-permute-done.7 = f32[1,128,32]{1,2,0:T(8,128)S(1)} collective-permute-done((f32[1,128,32]{1,2,0:T(8,128)S(1)}, f32[1,128,32]{1,2,0:T(8,128)S(1)}, u32[]{:S(2)}, u32[]{:S(2)}) %collective-permute-start.7) | collective-permute-done | bytes 16416 | tf_op jit(solution)/shard_map/ppermute | solution.py:55
  35.6 2.5 %collective-permute-start.14 = (bf16[1,16,2304]{2,1,0:T(8,128)(2,1)S(1)}, bf16[1,16,2304]{2,1,0:T(8,128)(2,1)S(1)}, u32[]{:S(2)}, u32[]{:S(2)}) collective-permute-start(bf16[1,16,2304]{2,1,0:T(8,128)(2,1)S(1)} %fusion.28), channel_id=1, source_target_pairs={{0,28},{4,24},{8,20},{12,16},{16,12},{20,8},{24,4},{28,0},{1,29},{... | collective-permute-start | bytes 221192 | tf_op jit(solution)/shard_map/ppermute | solution.py:164
  38.8 1.4 %collective-permute-start.13 = (bf16[1,16,2304]{2,1,0:T(8,128)(2,1)}, bf16[1,16,2304]{2,1,0:T(8,128)(2,1)S(1)}, u32[]{:S(2)}, u32[]{:S(2)}) collective-permute-start(bf16[1,16,2304]{2,1,0:T(8,128)(2,1)} %get-tuple-element.13), channel_id=1, source_target_pairs={{0,24},{4,28},{8,16},{12,20},{16,8},{20,12},{24,0},{28,4},{1,25},{... | collective-permute-start | bytes 221192 | tf_op jit(solution)/shard_map/ppermute | solution.py:164
  40.1 3.2 %collective-permute-start.12 = (bf16[1,16,2304]{2,1,0:T(8,128)(2,1)S(1)}, bf16[1,16,2304]{2,1,0:T(8,128)(2,1)S(1)}, u32[]{:S(2)}, u32[]{:S(2)}) collective-permute-start(bf16[1,16,2304]{2,1,0:T(8,128)(2,1)S(1)} %get-tuple-element.14), channel_id=1, source_target_pairs={{0,20},{4,16},{8,28},{12,24},{16,4},{20,0},{24,12},{28,8},{1,21},{... | collective-permute-start | bytes 221192 | tf_op jit(solution)/shard_map/ppermute | solution.py:164
  43.3 1.6 %convolution_bitcast_fusion.3 = f32[128,2048]{0,1:T(8,128)S(1)} fusion(bf16[128,256]{1,0:T(8,128)(2,1)S(1)} %copy-done.3, bf16[8192,256]{1,0:T(8,128)(2,1)} %param.8, s32[]{:T(128)S(6)} %select_n.45), kind=kOutput, calls=%fused_computation.3 | convolution fusion | flops 134217728 | bytes 2162692 | tf_op jit(solution)/shard_map/dot_general | solution.py:71
  44.9 0.8 %collective-permute-start.11 = (bf16[1,16,2304]{2,1,0:T(8,128)(2,1)S(1)}, bf16[1,16,2304]{2,1,0:T(8,128)(2,1)S(1)}, u32[]{:S(2)}, u32[]{:S(2)}) collective-permute-start(bf16[1,16,2304]{2,1,0:T(8,128)(2,1)S(1)} %get-tuple-element.15), channel_id=1, source_target_pairs={{0,16},{4,20},{8,24},{12,28},{16,0},{20,4},{24,8},{28,12},{1,17},{... | collective-permute-start | bytes 221192 | tf_op jit(solution)/shard_map/ppermute | solution.py:164
  45.7 2.3 %collective-permute-start.10 = (bf16[1,16,2304]{2,1,0:T(8,128)(2,1)S(1)}, bf16[1,16,2304]{2,1,0:T(8,128)(2,1)S(1)}, u32[]{:S(2)}, u32[]{:S(2)}) collective-permute-start(bf16[1,16,2304]{2,1,0:T(8,128)(2,1)S(1)} %get-tuple-element.16), channel_id=1, source_target_pairs={{0,12},{4,8},{8,4},{12,0},{16,28},{20,24},{24,20},{28,16},{1,13},{... | collective-permute-start | bytes 221192 | tf_op jit(solution)/shard_map/ppermute | solution.py:164
  48.0 1.4 %collective-permute-start.9 = (bf16[1,16,2304]{2,1,0:T(8,128)(2,1)S(1)}, bf16[1,16,2304]{2,1,0:T(8,128)(2,1)S(1)}, u32[]{:S(2)}, u32[]{:S(2)}) collective-permute-start(bf16[1,16,2304]{2,1,0:T(8,128)(2,1)S(1)} %get-tuple-element.17), channel_id=1, source_target_pairs={{0,8},{4,12},{8,0},{12,4},{16,24},{20,28},{24,16},{28,20},{1,9},{5... | collective-permute-start | bytes 221192 | tf_op jit(solution)/shard_map/ppermute | solution.py:164
  49.4 2.8 %collective-permute-done.12 = bf16[1,16,2304]{2,1,0:T(8,128)(2,1)S(1)} collective-permute-done((bf16[1,16,2304]{2,1,0:T(8,128)(2,1)S(1)}, bf16[1,16,2304]{2,1,0:T(8,128)(2,1)S(1)}, u32[]{:S(2)}, u32[]{:S(2)}) %collective-permute-start.12) | collective-permute-done | bytes 73760 | tf_op jit(solution)/shard_map/ppermute | solution.py:164
  52.9 1.2 %collective-permute-done.10 = bf16[1,16,2304]{2,1,0:T(8,128)(2,1)S(1)} collective-permute-done((bf16[1,16,2304]{2,1,0:T(8,128)(2,1)S(1)}, bf16[1,16,2304]{2,1,0:T(8,128)(2,1)S(1)}, u32[]{:S(2)}, u32[]{:S(2)}) %collective-permute-start.10) | collective-permute-done | bytes 73760 | tf_op jit(solution)/shard_map/ppermute | solution.py:164
  54.1 2.5 %collective-permute-done.8 = bf16[1,16,2304]{2,1,0:T(8,128)(2,1)S(1)} collective-permute-done((bf16[1,16,2304]{2,1,0:T(8,128)(2,1)S(1)}, bf16[1,16,2304]{2,1,0:T(8,128)(2,1)S(1)}, u32[]{:S(2)}, u32[]{:S(2)}) %collective-permute-start.8) | collective-permute-done | bytes 73760 | tf_op jit(solution)/shard_map/ppermute | solution.py:164
  58.0 1.6 %fusion.9 = bf16[128,2048]{0,1:T(8,128)(2,1)S(1)} fusion(f32[128,2048]{0,1:T(8,128)} %collective-permute-done.5, f32[128,2048]{0,1:T(8,128)S(1)} %convolution_bitcast_fusion.3, f32[2,128,2048]{1,2,0:T(8,128)S(1)} %copy-done.2, bf16[1,16,2304]{2,1,0:T(8,128)(2,1)S(1)} %copy.25, bf16[1,128,32]{1,2,0:T(8,128)(2,1)S(1)} %copy-done.5), kind=kOutput, calls=%fused_computation.23 | convolution fusion | flops 9437184 | bytes 3739648 | tf_op jit(solution)/shard_map/bnr,brd->bnd/dot_general | solution.py:135
  59.6 1.0 %copy.16 = bf16[128,2048]{1,0:T(8,128)(2,1)} copy(bf16[128,2048]{0,1:T(8,128)(2,1)S(1)} %fusion.9) | data formatting | bytes 1048576
  (59 shorter events, 6.3 us)
Async XLA Ops:
  0.6 25.2 %copy-start = (bf16[128,2048]{1,0:T(8,128)(2,1)S(1)}, bf16[128,2048]{1,0:T(8,128)(2,1)}, u32[]{:S(2)}) copy-start(bf16[128,2048]{1,0:T(8,128)(2,1)} %param.6) | copy-start | bytes 1572868
  2.3 7.5 %collective-permute-start.1 = (bf16[1,16,2304]{2,1,0:T(8,128)(2,1)S(1)}, bf16[1,16,2304]{2,1,0:T(8,128)(2,1)S(1)}, u32[]{:S(2)}, u32[]{:S(2)}) collective-permute-start(bf16[1,16,2304]{2,1,0:T(8,128)(2,1)S(1)} %get-tuple-element.22), channel_id=1, source_target_pairs={{0,4},{4,0},{8,12},{12,8},{16,20},{20,16},{24,28},{28,24},{1,5},{5... | collective-permute-start | bytes 221192 | tf_op jit(solution)/shard_map/ppermute | solution.py:36
  5.2 1.7 %copy-start.3 = (bf16[128,256]{1,0:T(8,128)(2,1)S(1)}, bf16[128,256]{1,0:T(8,128)(2,1)}, u32[]{:S(2)}) copy-start(bf16[128,256]{1,0:T(8,128)(2,1)} %param.7) | copy-start | bytes 196612
  9.0 17.1 %collective-permute-start = (f32[2,128,2048]{1,2,0:T(8,128)}, f32[2,128,2048]{1,2,0:T(8,128)S(1)}, u32[]{:S(2)}, u32[]{:S(2)}) collective-permute-start(f32[2,128,2048]{1,2,0:T(8,128)} %convolution_bitcast_fusion), channel_id=1, source_target_pairs={{0,1},{1,0},{2,3},{3,2},{4,5},{5,4},{6,7},{7,6},{8,9},{9,8},{10,11... | collective-permute-start | bytes 6291464 | tf_op jit(solution)/shard_map/ppermute | solution.py:80
  9.8 9.1 %collective-permute-start.2 = (bf16[2,16,2304]{2,1,0:T(8,128)(2,1)S(1)}, bf16[2,16,2304]{2,1,0:T(8,128)(2,1)S(1)}, u32[]{:S(2)}, u32[]{:S(2)}) collective-permute-start(bf16[2,16,2304]{2,1,0:T(8,128)(2,1)S(1)} %pad_maximum_fusion.1), channel_id=1, source_target_pairs={{0,8},{4,12},{8,0},{12,4},{16,24},{20,28},{24,16},{28,20},{1,9},{5... | collective-permute-start | bytes 442376 | tf_op jit(solution)/shard_map/ppermute | solution.py:41
  11.4 13.9 %collective-permute-start.3 = (bf16[2,16,2304]{2,1,0:T(8,128)(2,1)S(1)}, bf16[2,16,2304]{2,1,0:T(8,128)(2,1)S(1)}, u32[]{:S(2)}, u32[]{:S(2)}) collective-permute-start(bf16[2,16,2304]{2,1,0:T(8,128)(2,1)S(1)} %pad_maximum_fusion.1), channel_id=1, source_target_pairs={{0,16},{4,20},{8,24},{12,28},{16,0},{20,4},{24,8},{28,12},{1,17},{... | collective-permute-start | bytes 442376 | tf_op jit(solution)/shard_map/ppermute | solution.py:41
  14.0 11.4 %collective-permute-start.4 = (bf16[2,16,2304]{2,1,0:T(8,128)(2,1)S(1)}, bf16[2,16,2304]{2,1,0:T(8,128)(2,1)S(1)}, u32[]{:S(2)}, u32[]{:S(2)}) collective-permute-start(bf16[2,16,2304]{2,1,0:T(8,128)(2,1)S(1)} %pad_maximum_fusion.1), channel_id=1, source_target_pairs={{0,24},{4,28},{8,16},{12,20},{16,8},{20,12},{24,0},{28,4},{1,25},{... | collective-permute-start | bytes 442376 | tf_op jit(solution)/shard_map/ppermute | solution.py:41
  26.1 9.1 %copy-start.1 = (f32[2,128,2048]{1,2,0:T(8,128)}, f32[2,128,2048]{1,2,0:T(8,128)S(1)}, u32[]{:S(2)}) copy-start(f32[2,128,2048]{1,2,0:T(8,128)S(1)} %collective-permute-done) | copy-start | bytes 6291460
  29.5 1.2 %collective-permute-start.6 = (f32[1,128,32]{1,2,0:T(8,128)S(1)}, f32[1,128,32]{1,2,0:T(8,128)S(1)}, u32[]{:S(2)}, u32[]{:S(2)}) collective-permute-start(f32[1,128,32]{1,2,0:T(8,128)S(1)} %pad_maximum_fusion.2), channel_id=1, source_target_pairs={{0,1},{1,0},{2,3},{3,2},{4,5},{5,4},{6,7},{7,6},{8,9},{9,8},{10,11... | collective-permute-start | bytes 49160 | tf_op jit(solution)/shard_map/ppermute | solution.py:55
  30.7 3.7 %collective-permute-start.7 = (f32[1,128,32]{1,2,0:T(8,128)S(1)}, f32[1,128,32]{1,2,0:T(8,128)S(1)}, u32[]{:S(2)}, u32[]{:S(2)}) collective-permute-start(f32[1,128,32]{1,2,0:T(8,128)S(1)} %add.109), channel_id=1, source_target_pairs={{0,2},{1,3},{2,0},{3,1},{4,6},{5,7},{6,4},{7,5},{8,10},{9,11},{10,... | collective-permute-start | bytes 49160 | tf_op jit(solution)/shard_map/ppermute | solution.py:55
  32.4 25.6 %collective-permute-start.5 = (f32[128,2048]{0,1:T(8,128)}, f32[128,2048]{0,1:T(8,128)}, u32[]{:S(2)}, u32[]{:S(2)}) collective-permute-start(f32[128,2048]{0,1:T(8,128)} %fusion.5), channel_id=1, source_target_pairs={{0,2},{1,3},{2,0},{3,1},{4,6},{5,7},{6,4},{7,5},{8,10},{9,11},{10,... | collective-permute-start | bytes 3145736 | tf_op jit(solution)/shard_map/ppermute | solution.py:89
  34.5 0.6 copy-start.4
  35.6 10.1 %collective-permute-start.14 = (bf16[1,16,2304]{2,1,0:T(8,128)(2,1)S(1)}, bf16[1,16,2304]{2,1,0:T(8,128)(2,1)S(1)}, u32[]{:S(2)}, u32[]{:S(2)}) collective-permute-start(bf16[1,16,2304]{2,1,0:T(8,128)(2,1)S(1)} %fusion.28), channel_id=1, source_target_pairs={{0,28},{4,24},{8,20},{12,16},{16,12},{20,8},{24,4},{28,0},{1,29},{... | collective-permute-start | bytes 221192 | tf_op jit(solution)/shard_map/ppermute | solution.py:164
  38.8 9.2 %collective-permute-start.13 = (bf16[1,16,2304]{2,1,0:T(8,128)(2,1)}, bf16[1,16,2304]{2,1,0:T(8,128)(2,1)S(1)}, u32[]{:S(2)}, u32[]{:S(2)}) collective-permute-start(bf16[1,16,2304]{2,1,0:T(8,128)(2,1)} %get-tuple-element.13), channel_id=1, source_target_pairs={{0,24},{4,28},{8,16},{12,20},{16,8},{20,12},{24,0},{28,4},{1,25},{... | collective-permute-start | bytes 221192 | tf_op jit(solution)/shard_map/ppermute | solution.py:164
  40.1 12.1 %collective-permute-start.12 = (bf16[1,16,2304]{2,1,0:T(8,128)(2,1)S(1)}, bf16[1,16,2304]{2,1,0:T(8,128)(2,1)S(1)}, u32[]{:S(2)}, u32[]{:S(2)}) collective-permute-start(bf16[1,16,2304]{2,1,0:T(8,128)(2,1)S(1)} %get-tuple-element.14), channel_id=1, source_target_pairs={{0,20},{4,16},{8,28},{12,24},{16,4},{20,0},{24,12},{28,8},{1,21},{... | collective-permute-start | bytes 221192 | tf_op jit(solution)/shard_map/ppermute | solution.py:164
  44.9 7.9 %collective-permute-start.11 = (bf16[1,16,2304]{2,1,0:T(8,128)(2,1)S(1)}, bf16[1,16,2304]{2,1,0:T(8,128)(2,1)S(1)}, u32[]{:S(2)}, u32[]{:S(2)}) collective-permute-start(bf16[1,16,2304]{2,1,0:T(8,128)(2,1)S(1)} %get-tuple-element.15), channel_id=1, source_target_pairs={{0,16},{4,20},{8,24},{12,28},{16,0},{20,4},{24,8},{28,12},{1,17},{... | collective-permute-start | bytes 221192 | tf_op jit(solution)/shard_map/ppermute | solution.py:164
  45.7 8.4 %collective-permute-start.10 = (bf16[1,16,2304]{2,1,0:T(8,128)(2,1)S(1)}, bf16[1,16,2304]{2,1,0:T(8,128)(2,1)S(1)}, u32[]{:S(2)}, u32[]{:S(2)}) collective-permute-start(bf16[1,16,2304]{2,1,0:T(8,128)(2,1)S(1)} %get-tuple-element.16), channel_id=1, source_target_pairs={{0,12},{4,8},{8,4},{12,0},{16,28},{20,24},{24,20},{28,16},{1,13},{... | collective-permute-start | bytes 221192 | tf_op jit(solution)/shard_map/ppermute | solution.py:164
  48.0 6.1 %collective-permute-start.9 = (bf16[1,16,2304]{2,1,0:T(8,128)(2,1)S(1)}, bf16[1,16,2304]{2,1,0:T(8,128)(2,1)S(1)}, u32[]{:S(2)}, u32[]{:S(2)}) collective-permute-start(bf16[1,16,2304]{2,1,0:T(8,128)(2,1)S(1)} %get-tuple-element.17), channel_id=1, source_target_pairs={{0,8},{4,12},{8,0},{12,4},{16,24},{20,28},{24,16},{28,20},{1,9},{5... | collective-permute-start | bytes 221192 | tf_op jit(solution)/shard_map/ppermute | solution.py:164
  52.3 5.7 %copy-start.2 = (f32[2,128,2048]{1,2,0:T(8,128)S(1)}, f32[2,128,2048]{1,2,0:T(8,128)}, u32[]{:S(2)}) copy-start(f32[2,128,2048]{1,2,0:T(8,128)} %copy-done.1) | copy-start | bytes 6291460
  52.3 5.7 %copy-start.5 = (bf16[1,128,32]{1,2,0:T(8,128)(2,1)S(1)}, bf16[1,128,32]{1,2,0:T(8,128)(2,1)}, u32[]{:S(2)}) copy-start(bf16[1,128,32]{1,2,0:T(8,128)(2,1)} %copy-done.4) | copy-start | bytes 24580
  52.3 4.4 %collective-permute-start.8 = (bf16[1,16,2304]{2,1,0:T(8,128)(2,1)S(1)}, bf16[1,16,2304]{2,1,0:T(8,128)(2,1)S(1)}, u32[]{:S(2)}, u32[]{:S(2)}) collective-permute-start(bf16[1,16,2304]{2,1,0:T(8,128)(2,1)S(1)} %get-tuple-element.12), channel_id=1, source_target_pairs={{0,4},{4,0},{8,12},{12,8},{16,20},{20,16},{24,28},{28,24},{1,5},{5... | collective-permute-start | bytes 221192 | tf_op jit(solution)/shard_map/ppermute | solution.py:164

commit v10 on v7

--- a/solution.py
+++ b/solution.py
@@ -102,6 +102,12 @@
 
 
     packed = jnp.concatenate([adapter_down_weight, adapter_up_weight], axis=2)
+    mirror = block_count == 1 and dp_size >= 4 and dp_size & (dp_size - 1) == 0
+    if mirror:
+        return _mirrored(
+            inputs, cotangent, frozen_key_weight, packed, tenant_per_block,
+            width_portion, adapter_rank_size, held_tenants, dp_size, tensor_size,
+        )
     stacked, order = _gather_dp(packed, "dp", dp_size)
     stacked = stacked.reshape(dp_size, held_tenants, *packed.shape[1:])
     owner = tenant_per_block // held_tenants
@@ -161,6 +167,81 @@
     return (grad_inputs, grad_down, grad_up)
 
 
+def _low_rank(inputs, cotangent, frozen_key_weight, sel_down, sel_up, tensor_size):
+    low_in = jnp.dot(inputs, sel_down.T, preferred_element_type=jnp.float32)
+    reduced_output = ADAPTER_SCALE * jnp.dot(cotangent, sel_up.T, preferred_element_type=jnp.float32)
+    lows = jnp.concatenate([low_in, reduced_output], axis=1)
+    base_grad, lows = _frozen_term(cotangent, frozen_key_weight, "tensor", tensor_size, lows)
+    lows = _psum_small(lows, "tensor", tensor_size)
+    rank = sel_down.shape[0]
+    low_in_b = lows[:, :rank].astype(jnp.bfloat16)
+    low_out_b = lows[:, rank:].astype(jnp.bfloat16)
+    adapter_grad = jnp.dot(low_out_b, sel_down, preferred_element_type=jnp.float32)
+    grad_inputs = (base_grad + adapter_grad).astype(jnp.bfloat16)
+    return grad_inputs, low_in_b, low_out_b
+
+
+def _mirrored(
+    inputs, cotangent, frozen_key_weight, packed, tenant_per_block,
+    width_portion, rank, held_tenants, dp_size, tensor_size,
+):
+    half = dp_size // 2
+    me = lax.axis_index("dp")
+    tenant = tenant_per_block[0]
+    owner = tenant // held_tenants
+    local = tenant % held_tenants
+    digits = jnp.zeros((held_tenants, rank, 128), jnp.float32)
+    digits = digits.at[:, 0, 0].set((tenant // 256).astype(jnp.float32))
+    digits = digits.at[:, 0, 1].set((tenant % 256).astype(jnp.float32))
+    payload = jnp.concatenate([packed, digits.astype(packed.dtype)], axis=2)
+    mirror_tenant = lax.ppermute(tenant_per_block, "dp", [(i, i ^ half) for i in range(dp_size)])[0]
+    within = [payload] + [
+        lax.ppermute(payload, "dp", [(i, i ^ s) for i in range(dp_size)]) for s in range(1, half)
+    ]
+    width = packed.shape[2]
+    tenants_within = [
+        (w[0, 0, width].astype(jnp.int32) * 256 + w[0, 0, width + 1].astype(jnp.int32))
+        for w in within
+    ]
+    adapters_within = jnp.stack([w[:, :, :width] for w in within], 0)
+
+    def pick(tenant_id):
+        slot = (tenant_id // held_tenants) ^ me
+        entry = lax.dynamic_index_in_dim(adapters_within, jnp.clip(slot, 0, half - 1), 0, keepdims=False)
+        return lax.dynamic_index_in_dim(entry, tenant_id % held_tenants, 0, keepdims=False)
+
+    crossed = lax.ppermute(pick(mirror_tenant), "dp", [(i, i ^ half) for i in range(dp_size)])
+    near = ((owner ^ me) < half)
+    selected = jnp.where(near, pick(tenant), crossed)
+    sel_down = selected[:, :width_portion]
+    sel_up = selected[:, width_portion:]
+
+    grad_inputs, low_in_b, low_out_b = _low_rank(
+        inputs, cotangent, frozen_key_weight, sel_down, sel_up, tensor_size
+    )
+
+    down_term = jnp.dot(low_out_b.T, inputs, preferred_element_type=jnp.float32)
+    up_term = ADAPTER_SCALE * jnp.dot(low_in_b.T, cotangent, preferred_element_type=jnp.float32)
+    term = jnp.concatenate([down_term, up_term], axis=1)
+    slots = jnp.arange(held_tenants)[:, None, None] == local
+    term = jnp.where(slots, term[None], 0.0)
+    zero = jnp.zeros_like(term)
+    own_sum = jnp.where(owner == me, term, zero)
+    cross_sum = jnp.where(owner == (me ^ half), term, zero)
+    for s in range(1, half):
+        mate = me ^ s
+        outgoing = jnp.where((owner == mate) | (owner == (mate ^ half)), term, zero)
+        arrived = lax.ppermute(outgoing, "dp", [(i, i ^ s) for i in range(dp_size)])
+        sender_owner = tenants_within[s] // held_tenants
+        own_sum = own_sum + jnp.where(sender_owner == me, arrived, zero)
+        cross_sum = cross_sum + jnp.where(sender_owner == (me ^ half), arrived, zero)
+    arrived = lax.ppermute(cross_sum.astype(jnp.bfloat16), "dp", [(i, i ^ half) for i in range(dp_size)])
+    grad_down = own_sum[:, :, :width_portion] + arrived[:, :, :width_portion].astype(jnp.float32)
+    grad_up = own_sum[:, :, width_portion:] + arrived[:, :, width_portion:].astype(jnp.float32)
+    inputs_shape = inputs.shape
+    return (grad_inputs.reshape(inputs_shape), grad_down, grad_up)
+
+
 def solution(mesh):
     in_specs = (
         P("dp", "tensor"),

time: 59.2 us -> 69.6 us (1.18)
  starting transfers between devices: 25.3 us -> 16 us
  waiting for transfers between devices: 18.3 us -> 26.5 us
  between operations: 1.54 us -> 6.06 us
  local copies, waits for them, and re-layouts: 2.99 us -> 6.95 us
  other arithmetic: 1.62 us -> 3.91 us
    ppermute x3, waiting for transfers between devices: 1.14 us -> 15.2 us  [_frozen_term(): got = [lax.ppermute(held[e], axis, pairs) for e in range(1, len(held), 2)]]
    ppermute x11 -> x9, starting transfers between devices: 22.5 us -> 12.2 us  [the longest x1 4.1 us: _mirrored(): lax.ppermute(tenant_per_block, 'dp', [(i, i ^ half) for i in range(dp_siz...]
    ppermute x11 -> x9, waiting for transfers between devices: 15.7 us -> 9.68 us  [the longest x1 4.13 us: _mirrored(): lax.ppermute(cross_sum.astype(jnp.bfloat16), 'dp', [(i, i ^ half) for i i...]
    slice x0 -> x3, local copies, waits for them, and re-layouts: none -> 3.31 us  [_mirrored(): w[0, 0, width + 1].astype(jnp.int32)]
    scatter x0 -> x2, local copies, waits for them, and re-layouts: none -> 1.43 us  [the longest x1 1.42 us: _mirrored(): digits = digits.at[:, 0, 1].set((tenant % 256).astype(jnp.float32))]
    ppermute x3, starting transfers between devices: 1.24 us -> 2.21 us  [_frozen_term(): got = [lax.ppermute(held[e], axis, pairs) for e in range(1, len(held), 2)]]
    another operation x1 -> x3, other arithmetic: 0.01 us -> 0.91 us  [the longest x2 0.9 us: _mirrored(): adapters_within = jnp.stack([w[:, :, :width] for w in within], 0)]
    concatenate x3 -> x2, other arithmetic: 0.09 us -> 0.87 us  [the longest x1 0.87 us: _mirrored(): payload = jnp.concatenate([packed, digits.astype(packed.dtype)], axis=2)]
  transfers between devices with their start and end apart: 16 -> 14, of which waited for: 8 -> 7; matrix products, arithmetic and copies ran while one was open for 11% -> 21% of each run, Pallas kernels for 0% -> 0%
where the time goes in v10:
time: 69.6 us; the launch traced here: 69 us
  waiting for transfers between devices  26.5 us (38%)
  starting transfers between devices  16 us (23%)
  matrix products  9.58 us (14%)
  local copies, waits for them, and re-layouts  6.95 us (10%)
  between operations  6.06 us (9%)
  other arithmetic  3.91 us (6%)
    ppermute x3, waiting for transfers between devices, _frozen_term(): got = [lax.ppermute(held[e], axis, pairs) for e in range(1, len(held), 2)]  15.2 us
    dot_general x4, matrix products, term(): lax.dot_general(cotangent, piece, (((1,), (1,)), ((), ())), preferred_ele...  7.69 us
    ppermute x1, waiting for transfers between devices, _mirrored(): lax.ppermute(cross_sum.astype(jnp.bfloat16), 'dp', [(i, i ^ half) for i i...  4.13 us
    ppermute x1, starting transfers between devices, _mirrored(): lax.ppermute(tenant_per_block, 'dp', [(i, i ^ half) for i in range(dp_siz...  4.1 us
    ppermute x3, starting transfers between devices, _mirrored(): lax.ppermute(payload, 'dp', [(i, i ^ s) for i in range(dp_size)])  3.49 us
    ppermute x3, starting transfers between devices, _mirrored(): arrived = lax.ppermute(outgoing, 'dp', [(i, i ^ s) for i in range(dp_size)])  3.49 us
    slice x3, local copies, waits for them, and re-layouts, _mirrored(): w[0, 0, width + 1].astype(jnp.int32)  3.31 us
    ppermute x1, waiting for transfers between devices, _mirrored(): lax.ppermute(pick(mirror_tenant), 'dp', [(i, i ^ half) for i in range(dp_...  3.17 us
  transfers between devices with their start and end apart: 14, of which 7 were waited for; matrix products, arithmetic and copies ran while one was open for 21% of the time, Pallas kernels for 0%

profile of v10, /device:TPU:0, one launch (start us, length us, event | category | flops | bytes accessed | tf_op | source)
XLA Modules:
  0.0 69.0 jit_solution(10365804439297816982)
XLA Ops:
  0.7 4.1 %collective-permute-start.5 = (s32[1]{0:T(128)}, s32[1]{0:T(128)}, u32[]{:S(2)}, u32[]{:S(2)}) collective-permute-start(s32[1]{0:T(128)} %param.15), channel_id=1, source_target_pairs={{0,16},{4,20},{8,24},{12,28},{16,0},{20,4},{24,8},{28,12},{1,17},{... | collective-permute-start | bytes 20 | tf_op jit(solution)/shard_map/ppermute | solution.py:197
  6.1 1.4 %scatter.9 = bf16[1,16,128]{2,1,0:T(8,128)(2,1)S(1)} dynamic-update-slice(bf16[1,16,128]{2,1,0:T(8,128)(2,1)S(1)} %scatter.6, bf16[1,1,1]{2,1,0:T(2,128)(2,1)} %bitcast.7, s32[]{:T(128)} %constant.170.clone.1, s32[]{:T(128)} %bitcast.8, s32[]{:T(128)} %bitcast.9) | dynamic-update-slice | bytes 8 | tf_op jit(solution)/shard_map/scatter | solution.py:195
  7.5 0.9 %pad_maximum_fusion.2 = bf16[1,16,2432]{2,1,0:T(8,128)(2,1)S(1)} fusion(bf16[1,16,128]{2,1,0:T(8,128)(2,1)S(1)} %scatter.9, bf16[1,16,256]{2,1,0:T(8,128)(2,1)} %param.14, bf16[1,16,2048]{2,1,0:T(8,128)(2,1)} %param.13), kind=kLoop, calls=%fused_computation.24 | loop fusion | flops 233472 | bytes 155648 | tf_op jit(solution)/shard_map/concatenate | solution.py:196
  8.4 2.5 %collective-permute-start.4 = (bf16[1,16,2432]{2,1,0:T(8,128)(2,1)S(1)}, bf16[1,16,2432]{2,1,0:T(8,128)(2,1)S(1)}, u32[]{:S(2)}, u32[]{:S(2)}) collective-permute-start(bf16[1,16,2432]{2,1,0:T(8,128)(2,1)S(1)} %pad_maximum_fusion.2), channel_id=1, source_target_pairs={{0,12},{4,8},{8,4},{12,0},{16,28},{20,24},{24,20},{28,16},{1,13},{... | collective-permute-start | bytes 233480 | tf_op jit(solution)/shard_map/ppermute | solution.py:199
  11.9 0.9 %maximum_bitcast_fusion = bf16[1,1,16,2304]{3,2,1,0:T(8,128)(2,1)S(1)} fusion(bf16[1,16,256]{2,1,0:T(8,128)(2,1)} %param.14, bf16[1,16,2048]{2,1,0:T(8,128)(2,1)} %param.13), kind=kLoop, calls=%fused_computation.28 | loop fusion | flops 147456 | bytes 147456 | tf_op jit(solution)/shard_map/stack | solution.py:206
  13.4 1.1 %collective-permute-done.4 = bf16[1,16,2432]{2,1,0:T(8,128)(2,1)S(1)} collective-permute-done((bf16[1,16,2432]{2,1,0:T(8,128)(2,1)S(1)}, bf16[1,16,2432]{2,1,0:T(8,128)(2,1)S(1)}, u32[]{:S(2)}, u32[]{:S(2)}) %collective-permute-start.4) | collective-permute-done | bytes 77856 | tf_op jit(solution)/shard_map/ppermute | solution.py:199
  16.7 1.6 %convolution_bitcast_fusion = f32[128,2048]{0,1:T(8,128)S(1)} fusion(bf16[128,256]{1,0:T(8,128)(2,1)} %param.11, bf16[8192,256]{1,0:T(8,128)(2,1)} %param.12, s32[]{:T(128)S(6)} %select_n.174), kind=kOutput, calls=%fused_computation | convolution fusion | flops 134217728 | bytes 2162692 | tf_op jit(solution)/shard_map/dot_general | solution.py:71
  18.5 3.2 %collective-permute-done.6 = bf16[16,2304]{1,0:T(8,128)(2,1)S(1)} collective-permute-done((bf16[16,2304]{1,0:T(8,128)(2,1)S(1)}, bf16[16,2304]{1,0:T(8,128)(2,1)S(1)}, u32[]{:S(2)}, u32[]{:S(2)}) %collective-permute-start.6) | collective-permute-done | bytes 73760 | tf_op jit(solution)/shard_map/ppermute | solution.py:213
  21.7 1.0 %fusion.6 = f32[128,16]{0,1:T(8,128)S(1)} fusion(bf16[128,256]{1,0:T(8,128)(2,1)} %param.11, bf16[16,2304]{1,0:T(8,128)(2,1)S(1)} %bitcast_select_fusion), kind=kOutput, calls=%fused_computation.13 | convolution fusion | flops 1050624 | bytes 81920 | tf_op jit(solution)/shard_map/dot_general | solution.py:172
  22.9 2.7 %fusion.3 = f32[128,2048]{0,1:T(8,128)} fusion(f32[128,2048]{0,1:T(8,128)S(1)} %collective-permute-done.1, bf16[128,256]{1,0:T(8,128)(2,1)S(1)} %copy-done.1, bf16[8192,256]{1,0:T(8,128)(2,1)} %param.12, s32[]{:T(128)S(6)} %select_n.173), kind=kOutput, calls=%fused_computation.7 | convolution fusion | flops 134479872 | bytes 3211268 | tf_op jit(solution)/shard_map/dot_general | solution.py:71
  25.6 1.6 %convolution_bitcast_fusion.2 = f32[128,2048]{0,1:T(8,128)S(1)} fusion(bf16[128,256]{1,0:T(8,128)(2,1)S(1)} %copy-done.1, bf16[8192,256]{1,0:T(8,128)(2,1)} %param.12, s32[]{:T(128)S(6)} %select_n.172), kind=kOutput, calls=%fused_computation.2 | convolution fusion | flops 134217728 | bytes 2162692 | tf_op jit(solution)/shard_map/dot_general | solution.py:71
  27.8 1.6 %collective-permute-start.9 = (f32[128,32]{0,1:T(8,128)S(1)}, f32[128,32]{0,1:T(8,128)S(1)}, u32[]{:S(2)}, u32[]{:S(2)}) collective-permute-start(f32[128,32]{0,1:T(8,128)S(1)} %add.105), channel_id=1, source_target_pairs={{0,2},{1,3},{2,0},{3,1},{4,6},{5,7},{6,4},{7,5},{8,10},{9,11},{10,... | collective-permute-start | bytes 49160 | tf_op jit(solution)/shard_map/ppermute | solution.py:55
  30.0 1.7 %collective-permute-done.9 = f32[128,32]{0,1:T(8,128)S(1)} collective-permute-done((f32[128,32]{0,1:T(8,128)S(1)}, f32[128,32]{0,1:T(8,128)S(1)}, u32[]{:S(2)}, u32[]{:S(2)}) %collective-permute-start.9) | collective-permute-done | bytes 16416 | tf_op jit(solution)/shard_map/ppermute | solution.py:55
  32.7 0.8 %collective-permute-start.10 = (f32[1,16,2304]{2,1,0:T(8,128)}, f32[1,16,2304]{2,1,0:T(8,128)S(1)}, u32[]{:S(2)}, u32[]{:S(2)}) collective-permute-start(f32[1,16,2304]{2,1,0:T(8,128)} %get-tuple-element.36), channel_id=1, source_target_pairs={{0,4},{4,0},{8,12},{12,8},{16,20},{20,16},{24,28},{28,24},{1,5},{5... | collective-permute-start | bytes 442376 | tf_op jit(solution)/shard_map/ppermute | solution.py:234
  33.5 1.3 %collective-permute-start.11 = (f32[1,16,2304]{2,1,0:T(8,128)}, f32[1,16,2304]{2,1,0:T(8,128)S(1)}, u32[]{:S(2)}, u32[]{:S(2)}) collective-permute-start(f32[1,16,2304]{2,1,0:T(8,128)} %get-tuple-element.37), channel_id=1, source_target_pairs={{0,8},{4,12},{8,0},{12,4},{16,24},{20,28},{24,16},{28,20},{1,9},{5... | collective-permute-start | bytes 442376 | tf_op jit(solution)/shard_map/ppermute | solution.py:234
  34.9 1.3 %collective-permute-start.12 = (f32[1,16,2304]{2,1,0:T(8,128)S(1)}, f32[1,16,2304]{2,1,0:T(8,128)S(1)}, u32[]{:S(2)}, u32[]{:S(2)}) collective-permute-start(f32[1,16,2304]{2,1,0:T(8,128)S(1)} %get-tuple-element.38), channel_id=1, source_target_pairs={{0,12},{4,8},{8,4},{12,0},{16,28},{20,24},{24,20},{28,16},{1,13},{... | collective-permute-start | bytes 442376 | tf_op jit(solution)/shard_map/ppermute | solution.py:234
  36.2 1.4 %fusion.23 = (bf16[1,1,1]{2,1,0:T(2,128)(2,1)}, bf16[1,1,1]{2,1,0:T(2,128)(2,1)}) fusion(bf16[1,16,2432]{2,1,0:T(8,128)(2,1)} %copy-done.3), kind=kLoop, calls=%fused_computation.49 | loop fusion | bytes 8 | tf_op jit(solution)/shard_map/slice | solution.py:203
  40.2 1.3 %fusion.22 = (bf16[1,1,1]{2,1,0:T(2,128)(2,1)}, bf16[1,1,1]{2,1,0:T(2,128)(2,1)}) fusion(bf16[1,16,2432]{2,1,0:T(8,128)(2,1)} %copy-done.2), kind=kLoop, calls=%fused_computation.48 | loop fusion | bytes 8 | tf_op jit(solution)/shard_map/slice | solution.py:203
  42.8 1.6 %collective-permute-start.7 = (f32[128,2048]{0,1:T(8,128)}, f32[128,2048]{0,1:T(8,128)S(1)}, u32[]{:S(2)}, u32[]{:S(2)}) collective-permute-start(f32[128,2048]{0,1:T(8,128)} %fusion.3), channel_id=1, source_target_pairs={{0,2},{1,3},{2,0},{3,1},{4,6},{5,7},{6,4},{7,5},{8,10},{9,11},{10,... | collective-permute-start | bytes 3145736 | tf_op jit(solution)/shard_map/ppermute | solution.py:83
  44.5 0.8 %collective-permute-start.13 = (bf16[1,16,2304]{2,1,0:T(8,128)(2,1)S(1)}, bf16[1,16,2304]{2,1,0:T(8,128)(2,1)S(1)}, u32[]{:S(2)}, u32[]{:S(2)}) collective-permute-start(bf16[1,16,2304]{2,1,0:T(8,128)(2,1)S(1)} %get-tuple-element.34), channel_id=1, source_target_pairs={{0,16},{4,20},{8,24},{12,28},{16,0},{20,4},{24,8},{28,12},{1,17},{... | collective-permute-start | bytes 221192 | tf_op jit(solution)/shard_map/ppermute | solution.py:238
  45.7 4.1 %collective-permute-done.13 = bf16[1,16,2304]{2,1,0:T(8,128)(2,1)S(1)} collective-permute-done((bf16[1,16,2304]{2,1,0:T(8,128)(2,1)S(1)}, bf16[1,16,2304]{2,1,0:T(8,128)(2,1)S(1)}, u32[]{:S(2)}, u32[]{:S(2)}) %collective-permute-start.13) | collective-permute-done | bytes 73760 | tf_op jit(solution)/shard_map/ppermute | solution.py:238
  51.1 15.2 %collective-permute-done.7 = f32[128,2048]{0,1:T(8,128)S(1)} collective-permute-done((f32[128,2048]{0,1:T(8,128)}, f32[128,2048]{0,1:T(8,128)S(1)}, u32[]{:S(2)}, u32[]{:S(2)}) %collective-permute-start.7) | collective-permute-done | bytes 1048608 | tf_op jit(solution)/shard_map/ppermute | solution.py:83
  66.3 1.7 %fusion.4 = bf16[128,2048]{0,1:T(8,128)(2,1)S(1)} fusion(f32[128,2048]{0,1:T(8,128)S(1)} %fusion.11, f32[128,2048]{0,1:T(8,128)S(1)} %collective-permute-done.7, f32[128,2048]{0,1:T(8,128)S(1)} %collective-permute-done, bf16[128,256]{1,0:T(8,128)(2,1)S(1)} %copy-done.1, bf16[8192,256]{1,0:T(8,128)(2,1)} %param.12, s32[]{:T(128)S(6)} %select_n.171), kind=kOutput, calls=%fused_computation.8 | convolution fusion | flops 135266304 | bytes 4784132 | tf_op jit(solution)/shard_map/dot_general | solution.py:71
  68.0 1.0 %copy.10 = bf16[128,2048]{1,0:T(8,128)(2,1)} copy(bf16[128,2048]{0,1:T(8,128)(2,1)S(1)} %fusion.4) | data formatting | bytes 1048576
  (44 shorter events, 8.1 us)
Async XLA Ops:
  0.6 22.0 %copy-start = (bf16[128,2048]{1,0:T(8,128)(2,1)S(1)}, bf16[128,2048]{1,0:T(8,128)(2,1)}, u32[]{:S(2)}) copy-start(bf16[128,2048]{1,0:T(8,128)(2,1)} %param.10) | copy-start | bytes 1572868
  0.6 22.3 %copy-start.1 = (bf16[128,256]{1,0:T(8,128)(2,1)S(1)}, bf16[128,256]{1,0:T(8,128)(2,1)}, u32[]{:S(2)}) copy-start(bf16[128,256]{1,0:T(8,128)(2,1)} %param.11) | copy-start | bytes 196612
  0.7 12.1 %collective-permute-start.5 = (s32[1]{0:T(128)}, s32[1]{0:T(128)}, u32[]{:S(2)}, u32[]{:S(2)}) collective-permute-start(s32[1]{0:T(128)} %param.15), channel_id=1, source_target_pairs={{0,16},{4,20},{8,24},{12,28},{16,0},{20,4},{24,8},{28,12},{1,17},{... | collective-permute-start | bytes 20 | tf_op jit(solution)/shard_map/ppermute | solution.py:197
  8.4 6.1 %collective-permute-start.4 = (bf16[1,16,2432]{2,1,0:T(8,128)(2,1)S(1)}, bf16[1,16,2432]{2,1,0:T(8,128)(2,1)S(1)}, u32[]{:S(2)}, u32[]{:S(2)}) collective-permute-start(bf16[1,16,2432]{2,1,0:T(8,128)(2,1)S(1)} %pad_maximum_fusion.2), channel_id=1, source_target_pairs={{0,12},{4,8},{8,4},{12,0},{16,28},{20,24},{24,20},{28,16},{1,13},{... | collective-permute-start | bytes 233480 | tf_op jit(solution)/shard_map/ppermute | solution.py:199
  10.9 4.4 %collective-permute-start.3 = (bf16[1,16,2432]{2,1,0:T(8,128)(2,1)S(1)}, bf16[1,16,2432]{2,1,0:T(8,128)(2,1)S(1)}, u32[]{:S(2)}, u32[]{:S(2)}) collective-permute-start(bf16[1,16,2432]{2,1,0:T(8,128)(2,1)S(1)} %pad_maximum_fusion.2), channel_id=1, source_target_pairs={{0,8},{4,12},{8,0},{12,4},{16,24},{20,28},{24,16},{28,20},{1,9},{5... | collective-permute-start | bytes 233480 | tf_op jit(solution)/shard_map/ppermute | solution.py:199
  11.4 4.4 %collective-permute-start.2 = (bf16[1,16,2432]{2,1,0:T(8,128)(2,1)S(1)}, bf16[1,16,2432]{2,1,0:T(8,128)(2,1)S(1)}, u32[]{:S(2)}, u32[]{:S(2)}) collective-permute-start(bf16[1,16,2432]{2,1,0:T(8,128)(2,1)S(1)} %pad_maximum_fusion.2), channel_id=1, source_target_pairs={{0,4},{4,0},{8,12},{12,8},{16,20},{20,16},{24,28},{28,24},{1,5},{5... | collective-permute-start | bytes 233480 | tf_op jit(solution)/shard_map/ppermute | solution.py:199
  15.3 0.6 copy-start.3
  15.8 0.6 copy-start.2
  16.4 5.3 %collective-permute-start.6 = (bf16[16,2304]{1,0:T(8,128)(2,1)S(1)}, bf16[16,2304]{1,0:T(8,128)(2,1)S(1)}, u32[]{:S(2)}, u32[]{:S(2)}) collective-permute-start(bf16[16,2304]{1,0:T(8,128)(2,1)S(1)} %dynamic-slice_bitcast_fusion), channel_id=1, source_target_pairs={{0,16},{4,20},{8,24},{12,28},{16,0},{20,4},{24,8},{28,12},{1,17},{... | collective-permute-start | bytes 221192 | tf_op jit(solution)/shard_map/ppermute | solution.py:213
  18.4 4.5 %collective-permute-start.1 = (f32[128,2048]{0,1:T(8,128)S(1)}, f32[128,2048]{0,1:T(8,128)S(1)}, u32[]{:S(2)}, u32[]{:S(2)}) collective-permute-start(f32[128,2048]{0,1:T(8,128)S(1)} %convolution_bitcast_fusion), channel_id=1, source_target_pairs={{0,1},{1,0},{2,3},{3,2},{4,5},{5,4},{6,7},{7,6},{8,9},{9,8},{10,11... | collective-permute-start | bytes 3145736 | tf_op jit(solution)/shard_map/ppermute | solution.py:83
  25.6 2.2 %collective-permute-start.8 = (f32[128,32]{0,1:T(8,128)S(1)}, f32[128,32]{0,1:T(8,128)S(1)}, u32[]{:S(2)}, u32[]{:S(2)}) collective-permute-start(f32[128,32]{0,1:T(8,128)S(1)} %pad_maximum_fusion.3), channel_id=1, source_target_pairs={{0,1},{1,0},{2,3},{3,2},{4,5},{5,4},{6,7},{7,6},{8,9},{9,8},{10,11... | collective-permute-start | bytes 49160 | tf_op jit(solution)/shard_map/ppermute | solution.py:55
  27.3 23.8 %collective-permute-start = (f32[128,2048]{0,1:T(8,128)S(1)}, f32[128,2048]{0,1:T(8,128)S(1)}, u32[]{:S(2)}, u32[]{:S(2)}) collective-permute-start(f32[128,2048]{0,1:T(8,128)S(1)} %convolution_bitcast_fusion.2), channel_id=1, source_target_pairs={{0,1},{1,0},{2,3},{3,2},{4,5},{5,4},{6,7},{7,6},{8,9},{9,8},{10,11... | collective-permute-start | bytes 3145736 | tf_op jit(solution)/shard_map/ppermute | solution.py:83
  27.8 3.8 %collective-permute-start.9 = (f32[128,32]{0,1:T(8,128)S(1)}, f32[128,32]{0,1:T(8,128)S(1)}, u32[]{:S(2)}, u32[]{:S(2)}) collective-permute-start(f32[128,32]{0,1:T(8,128)S(1)} %add.105), channel_id=1, source_target_pairs={{0,2},{1,3},{2,0},{3,1},{4,6},{5,7},{6,4},{7,5},{8,10},{9,11},{10,... | collective-permute-start | bytes 49160 | tf_op jit(solution)/shard_map/ppermute | solution.py:55
  32.7 11.7 %collective-permute-start.10 = (f32[1,16,2304]{2,1,0:T(8,128)}, f32[1,16,2304]{2,1,0:T(8,128)S(1)}, u32[]{:S(2)}, u32[]{:S(2)}) collective-permute-start(f32[1,16,2304]{2,1,0:T(8,128)} %get-tuple-element.36), channel_id=1, source_target_pairs={{0,4},{4,0},{8,12},{12,8},{16,20},{20,16},{24,28},{28,24},{1,5},{5... | collective-permute-start | bytes 442376 | tf_op jit(solution)/shard_map/ppermute | solution.py:234
  33.5 10.9 %collective-permute-start.11 = (f32[1,16,2304]{2,1,0:T(8,128)}, f32[1,16,2304]{2,1,0:T(8,128)S(1)}, u32[]{:S(2)}, u32[]{:S(2)}) collective-permute-start(f32[1,16,2304]{2,1,0:T(8,128)} %get-tuple-element.37), channel_id=1, source_target_pairs={{0,8},{4,12},{8,0},{12,4},{16,24},{20,28},{24,16},{28,20},{1,9},{5... | collective-permute-start | bytes 442376 | tf_op jit(solution)/shard_map/ppermute | solution.py:234
  34.9 9.5 %collective-permute-start.12 = (f32[1,16,2304]{2,1,0:T(8,128)S(1)}, f32[1,16,2304]{2,1,0:T(8,128)S(1)}, u32[]{:S(2)}, u32[]{:S(2)}) collective-permute-start(f32[1,16,2304]{2,1,0:T(8,128)S(1)} %get-tuple-element.38), channel_id=1, source_target_pairs={{0,12},{4,8},{8,4},{12,0},{16,28},{20,24},{24,20},{28,16},{1,13},{... | collective-permute-start | bytes 442376 | tf_op jit(solution)/shard_map/ppermute | solution.py:234
  42.8 23.4 %collective-permute-start.7 = (f32[128,2048]{0,1:T(8,128)}, f32[128,2048]{0,1:T(8,128)S(1)}, u32[]{:S(2)}, u32[]{:S(2)}) collective-permute-start(f32[128,2048]{0,1:T(8,128)} %fusion.3), channel_id=1, source_target_pairs={{0,2},{1,3},{2,0},{3,1},{4,6},{5,7},{6,4},{7,5},{8,10},{9,11},{10,... | collective-permute-start | bytes 3145736 | tf_op jit(solution)/shard_map/ppermute | solution.py:83
  44.5 5.3 %collective-permute-start.13 = (bf16[1,16,2304]{2,1,0:T(8,128)(2,1)S(1)}, bf16[1,16,2304]{2,1,0:T(8,128)(2,1)S(1)}, u32[]{:S(2)}, u32[]{:S(2)}) collective-permute-start(bf16[1,16,2304]{2,1,0:T(8,128)(2,1)S(1)} %get-tuple-element.34), channel_id=1, source_target_pairs={{0,16},{4,20},{8,24},{12,28},{16,0},{20,4},{24,8},{28,12},{1,17},{... | collective-permute-start | bytes 221192 | tf_op jit(solution)/shard_map/ppermute | solution.py:238

commit v11 on v10

--- a/solution.py
+++ b/solution.py
@@ -167,11 +167,39 @@
     return (grad_inputs, grad_down, grad_up)
 
 
-def _low_rank(inputs, cotangent, frozen_key_weight, sel_down, sel_up, tensor_size):
+def _frozen_first(cotangent, weight, axis, size):
+    me = lax.axis_index(axis)
+    rows = weight.shape[0] // size
+
+    def term(block):
+        piece = lax.dynamic_slice_in_dim(weight, block * rows, rows, axis=0)
+        return lax.dot_general(
+            cotangent, piece, (((1,), (1,)), ((), ())), preferred_element_type=jnp.float32
+        )
+
+    pieces = [lax.dynamic_slice_in_dim(weight, (me ^ e) * rows, rows, axis=0) for e in range(1, size, 2)]
+    leaving = jnp.einsum(
+        "nk,bdk->bnd", cotangent, jnp.stack(pieces, 0), preferred_element_type=jnp.float32
+    )
+    got = lax.ppermute(leaving, axis, [(i, i ^ 1) for i in range(size)])
+    return [term(me ^ e) + got[m] for m, e in enumerate(range(0, size, 2))]
+
+
+def _frozen_rest(held, axis, size):
+    step = 1
+    while len(held) > 1:
+        partner = 1 << step
+        pairs = [(i, i ^ partner) for i in range(size)]
+        got = [lax.ppermute(held[e], axis, pairs) for e in range(1, len(held), 2)]
+        held = [held[e] + g for e, g in zip(range(0, len(held), 2), got)]
+        step += 1
+    return held[0]
+
+
+def _low_rank(inputs, cotangent, base_grad, sel_down, sel_up, tensor_size):
     low_in = jnp.dot(inputs, sel_down.T, preferred_element_type=jnp.float32)
     reduced_output = ADAPTER_SCALE * jnp.dot(cotangent, sel_up.T, preferred_element_type=jnp.float32)
     lows = jnp.concatenate([low_in, reduced_output], axis=1)
-    base_grad, lows = _frozen_term(cotangent, frozen_key_weight, "tensor", tensor_size, lows)
     lows = _psum_small(lows, "tensor", tensor_size)
     rank = sel_down.shape[0]
     low_in_b = lows[:, :rank].astype(jnp.bfloat16)
@@ -210,14 +238,26 @@
         entry = lax.dynamic_index_in_dim(adapters_within, jnp.clip(slot, 0, half - 1), 0, keepdims=False)
         return lax.dynamic_index_in_dim(entry, tenant_id % held_tenants, 0, keepdims=False)
 
-    crossed = lax.ppermute(pick(mirror_tenant), "dp", [(i, i ^ half) for i in range(dp_size)])
+    for_mirror = pick(mirror_tenant)
+    halving = tensor_size > 1 and tensor_size & (tensor_size - 1) == 0
+    if halving:
+        frozen = _frozen_first(cotangent, frozen_key_weight, "tensor", tensor_size)
+        *leaving, for_mirror = lax.optimization_barrier((*frozen[1::2], for_mirror))
+        frozen[1::2] = leaving
+        base_grad = _frozen_rest(frozen, "tensor", tensor_size)
+    else:
+        partial = lax.dot_general(
+            cotangent, frozen_key_weight, (((1,), (1,)), ((), ())), preferred_element_type=jnp.float32
+        )
+        base_grad = lax.psum_scatter(partial, "tensor", scatter_dimension=1, tiled=True)
+    crossed = lax.ppermute(for_mirror, "dp", [(i, i ^ half) for i in range(dp_size)])
     near = ((owner ^ me) < half)
     selected = jnp.where(near, pick(tenant), crossed)
     sel_down = selected[:, :width_portion]
     sel_up = selected[:, width_portion:]
 
     grad_inputs, low_in_b, low_out_b = _low_rank(
-        inputs, cotangent, frozen_key_weight, sel_down, sel_up, tensor_size
+        inputs, cotangent, base_grad, sel_down, sel_up, tensor_size
     )
 
     down_term = jnp.dot(low_out_b.T, inputs, preferred_element_type=jnp.float32)

time: 69.6 us -> 69.7 us (level)
  waiting for transfers between devices: 26.5 us -> 31.1 us
  matrix products: 9.58 us -> 7.39 us
  starting transfers between devices: 16 us -> 14.1 us
    ppermute x4 -> x3, waiting for transfers between devices: 18.3 us -> 23.9 us  [the longest x1 13.5 us: _frozen_rest(): got = [lax.ppermute(held[e], axis, pairs) for e in range(1, len(held), 2)]]
    dot_general x4 -> x2, matrix products: 7.69 us -> 4.3 us  [term(): lax.dot_general(cotangent, piece, (((1,), (1,)), ((), ())), preferred_ele...]
    ppermute x3, waiting for transfers between devices: 2.37 us -> 0.01 us  [_mirrored(): lax.ppermute(payload, 'dp', [(i, i ^ s) for i in range(dp_size)])]
    dot_general x0 -> x1, matrix products: none -> 2.04 us  [_frozen_first(): jnp.einsum('nk,bdk->bnd', cotangent, jnp.stack(pieces, 0), preferred_elem...]
    another operation x2 -> x3, local copies, waits for them, and re-layouts: 0.6 us -> 2.36 us  [the longest x1 1.71 us: _frozen_first(): jnp.stack(pieces, 0)]
    slice x3, local copies, waits for them, and re-layouts: 3.31 us -> 1.81 us  [_mirrored(): w[0, 0, width + 1].astype(jnp.int32)]
    ppermute x1, starting transfers between devices: 4.1 us -> 2.91 us  [_mirrored(): lax.ppermute(tenant_per_block, 'dp', [(i, i ^ half) for i in range(dp_siz...]
    ppermute x3, starting transfers between devices: 3.49 us -> 4.61 us  [_mirrored(): lax.ppermute(payload, 'dp', [(i, i ^ s) for i in range(dp_size)])]
  transfers between devices with their start and end apart: 14 -> 13, of which waited for: 7 -> 7; matrix products, arithmetic and copies ran while one was open for 21% -> 14% of each run, Pallas kernels for 0% -> 0%
where the time goes in v11:
time: 69.7 us; the launch traced here: 69.3 us
  waiting for transfers between devices  31.1 us (45%)
  starting transfers between devices  14.1 us (20%)
  matrix products  7.39 us (11%)
  local copies, waits for them, and re-layouts  6.61 us (9%)
  between operations  6.12 us (9%)
  other arithmetic  3.96 us (6%)
    ppermute x1, waiting for transfers between devices, _frozen_rest(): got = [lax.ppermute(held[e], axis, pairs) for e in range(1, len(held), 2)]  13.5 us
    ppermute x1, waiting for transfers between devices, _mirrored(): lax.ppermute(for_mirror, 'dp', [(i, i ^ half) for i in range(dp_size)])  6.82 us
    ppermute x3, starting transfers between devices, _mirrored(): lax.ppermute(payload, 'dp', [(i, i ^ s) for i in range(dp_size)])  4.61 us
    dot_general x2, matrix products, term(): lax.dot_general(cotangent, piece, (((1,), (1,)), ((), ())), preferred_ele...  4.3 us
    ppermute x1, waiting for transfers between devices, _mirrored(): lax.ppermute(cross_sum.astype(jnp.bfloat16), 'dp', [(i, i ^ half) for i i...  4.09 us
    ppermute x1, waiting for transfers between devices, _frozen_first(): got = lax.ppermute(leaving, axis, [(i, i ^ 1) for i in range(size)])  3.54 us
    ppermute x3, starting transfers between devices, _mirrored(): arrived = lax.ppermute(outgoing, 'dp', [(i, i ^ s) for i in range(dp_size)])  3.49 us
    ppermute x1, starting transfers between devices, _mirrored(): lax.ppermute(tenant_per_block, 'dp', [(i, i ^ half) for i in range(dp_siz...  2.91 us
  transfers between devices with their start and end apart: 13, of which 7 were waited for; matrix products, arithmetic and copies ran while one was open for 14% of the time, Pallas kernels for 0%

profile of v11, /device:TPU:0, one launch (start us, length us, event | category | flops | bytes accessed | tf_op | source)
XLA Modules:
  0.0 69.3 jit_solution(6152372159866047907)
XLA Ops:
  1.4 0.6 fusion.31
  2.1 1.4 %scatter.9 = bf16[1,16,128]{2,1,0:T(8,128)(2,1)S(1)} dynamic-update-slice(bf16[1,16,128]{2,1,0:T(8,128)(2,1)S(1)} %scatter.6, bf16[1,1,1]{2,1,0:T(2,128)(2,1)} %bitcast.11, s32[]{:T(128)} %constant.170.clone.1, s32[]{:T(128)} %bitcast.12, s32[]{:T(128)} %bitcast.13) | dynamic-update-slice | bytes 8 | tf_op jit(solution)/shard_map/scatter | solution.py:223
  3.4 0.9 %pad_maximum_fusion.2 = bf16[1,16,2432]{2,1,0:T(8,128)(2,1)S(1)} fusion(bf16[1,16,128]{2,1,0:T(8,128)(2,1)S(1)} %scatter.9, bf16[1,16,256]{2,1,0:T(8,128)(2,1)} %param.14, bf16[1,16,2048]{2,1,0:T(8,128)(2,1)} %param.13), kind=kLoop, calls=%fused_computation.28 | loop fusion | flops 233472 | bytes 155648 | tf_op jit(solution)/shard_map/concatenate | solution.py:224
  4.3 4.0 %collective-permute-start.3 = (bf16[1,16,2432]{2,1,0:T(8,128)(2,1)S(1)}, bf16[1,16,2432]{2,1,0:T(8,128)(2,1)S(1)}, u32[]{:S(2)}, u32[]{:S(2)}) collective-permute-start(bf16[1,16,2432]{2,1,0:T(8,128)(2,1)S(1)} %pad_maximum_fusion.2), channel_id=1, source_target_pairs={{0,12},{4,8},{8,4},{12,0},{16,28},{20,24},{24,20},{28,16},{1,13},{... | collective-permute-start | bytes 233480 | tf_op jit(solution)/shard_map/ppermute | solution.py:227
  8.9 2.9 %collective-permute-start.4 = (s32[1]{0:T(128)}, s32[1]{0:T(128)}, u32[]{:S(2)}, u32[]{:S(2)}) collective-permute-start(s32[1]{0:T(128)} %param.15), channel_id=1, source_target_pairs={{0,16},{4,20},{8,24},{12,28},{16,0},{20,4},{24,8},{28,12},{1,17},{... | collective-permute-start | bytes 20 | tf_op jit(solution)/shard_map/ppermute | solution.py:225
  11.8 1.7 %dynamic-slice_bitcast_fusion.1 = (bf16[1,2048,256]{2,1,0:T(8,128)(2,1)S(1)}, bf16[1,2048,256]{2,1,0:T(8,128)(2,1)S(1)}) fusion(bf16[8192,256]{1,0:T(8,128)(2,1)} %param.12, s32[]{:T(128)S(6)} %select_n.172, s32[]{:T(128)S(6)} %select_n.173), kind=kLoop, calls=%fused_computation.21 | loop fusion | bytes 4194312 | tf_op jit(solution)/shard_map/stack | solution.py:182
  13.6 2.0 %convolution_bitcast_fusion = f32[2,128,2048]{1,2,0:T(8,128)} fusion(bf16[1,2048,256]{2,1,0:T(8,128)(2,1)S(1)} %get-tuple-element.35, bf16[1,2048,256]{2,1,0:T(8,128)(2,1)S(1)} %get-tuple-element.34, bf16[128,256]{1,0:T(8,128)(2,1)S(1)} %copy-done.1), kind=kOutput, calls=%fused_computation | convolution fusion | flops 269484032 | bytes 4259840 | tf_op jit(solution)/shard_map/nk,bdk->bnd/dot_general | solution.py:181
  16.4 3.5 %collective-permute-done = f32[2,128,2048]{1,2,0:T(8,128)S(1)} collective-permute-done((f32[2,128,2048]{1,2,0:T(8,128)}, f32[2,128,2048]{1,2,0:T(8,128)S(1)}, u32[]{:S(2)}, u32[]{:S(2)}) %collective-permute-start) | collective-permute-done | bytes 2097184 | tf_op jit(solution)/shard_map/ppermute | solution.py:184
  20.0 2.7 %fusion.5 = f32[128,2048]{0,1:T(8,128)} fusion(f32[2,128,2048]{1,2,0:T(8,128)S(1)} %collective-permute-done, bf16[128,256]{1,0:T(8,128)(2,1)S(1)} %copy-done.1, bf16[8192,256]{1,0:T(8,128)(2,1)} %param.12, s32[]{:T(128)S(6)} %select_n.174), kind=kOutput, calls=%fused_computation.13 | convolution fusion | flops 134479872 | bytes 3211268 | tf_op jit(solution)/shard_map/dot_general | solution.py:176
  22.6 6.8 %collective-permute-done.6 = bf16[16,2304]{1,0:T(8,128)(2,1)S(1)} collective-permute-done((bf16[16,2304]{1,0:T(8,128)(2,1)S(1)}, bf16[16,2304]{1,0:T(8,128)(2,1)S(1)}, u32[]{:S(2)}, u32[]{:S(2)}) %collective-permute-start.6) | collective-permute-done | bytes 73760 | tf_op jit(solution)/shard_map/ppermute | solution.py:253
  29.9 1.2 %collective-permute-done.7 = f32[128,32]{0,1:T(8,128)S(1)} collective-permute-done((f32[128,32]{0,1:T(8,128)S(1)}, f32[128,32]{0,1:T(8,128)S(1)}, u32[]{:S(2)}, u32[]{:S(2)}) %collective-permute-start.7) | collective-permute-done | bytes 16416 | tf_op jit(solution)/shard_map/ppermute | solution.py:55
  31.1 1.5 %collective-permute-start.8 = (f32[128,32]{0,1:T(8,128)S(1)}, f32[128,32]{0,1:T(8,128)S(1)}, u32[]{:S(2)}, u32[]{:S(2)}) collective-permute-start(f32[128,32]{0,1:T(8,128)S(1)} %fusion.27), channel_id=1, source_target_pairs={{0,2},{1,3},{2,0},{3,1},{4,6},{5,7},{6,4},{7,5},{8,10},{9,11},{10,... | collective-permute-start | bytes 49160 | tf_op jit(solution)/shard_map/ppermute | solution.py:55
  32.6 0.6 fusion.28
  33.2 1.6 %collective-permute-done.8 = f32[128,32]{0,1:T(8,128)S(1)} collective-permute-done((f32[128,32]{0,1:T(8,128)S(1)}, f32[128,32]{0,1:T(8,128)S(1)}, u32[]{:S(2)}, u32[]{:S(2)}) %collective-permute-start.8) | collective-permute-done | bytes 16416 | tf_op jit(solution)/shard_map/ppermute | solution.py:55
  35.1 0.8 %broadcast_select_fusion.1 = (f32[1,16,2304]{2,1,0:T(8,128)S(1)}, f32[1,16,2304]{2,1,0:T(8,128)}, f32[1,16,2304]{2,1,0:T(8,128)}) fusion(pred[]{:T(512)S(6)} %or.9, f32[1,16,256]{2,1,0:T(8,128)S(1)} %fusion.3, f32[1,16,2048]{2,1,0:T(8,128)S(1)} %convolution_bitcast_fusion.3, pred[]{:T(512)S(6)} %or.10, pred[]{:T(512)S(6)} %or.11), kind=kLoop, calls=%fused_computation.35 | loop fusion | flops 147456 | bytes 589827 | tf_op jit(solution)/shard_map/jit(_where)/select_n | solution.py:273
  35.9 2.9 %collective-permute-start.11 = (f32[1,16,2304]{2,1,0:T(8,128)}, f32[1,16,2304]{2,1,0:T(8,128)S(1)}, u32[]{:S(2)}, u32[]{:S(2)}) collective-permute-start(f32[1,16,2304]{2,1,0:T(8,128)} %get-tuple-element.40), channel_id=1, source_target_pairs={{0,12},{4,8},{8,4},{12,0},{16,28},{20,24},{24,20},{28,16},{1,13},{... | collective-permute-start | bytes 442376 | tf_op jit(solution)/shard_map/ppermute | solution.py:274
  44.4 1.6 %collective-permute-start.5 = (f32[128,2048]{0,1:T(8,128)}, f32[128,2048]{0,1:T(8,128)S(1)}, u32[]{:S(2)}, u32[]{:S(2)}) collective-permute-start(f32[128,2048]{0,1:T(8,128)} %fusion.5), channel_id=1, source_target_pairs={{0,2},{1,3},{2,0},{3,1},{4,6},{5,7},{6,4},{7,5},{8,10},{9,11},{10,... | collective-permute-start | bytes 3145736 | tf_op jit(solution)/shard_map/ppermute | solution.py:193
  46.3 1.0 %add_convert_fusion = (bf16[1,16,2304]{2,1,0:T(8,128)(2,1)S(1)}, f32[1,16,2304]{2,1,0:T(8,128)S(1)}) fusion(f32[1,16,2304]{2,1,0:T(8,128)S(1)} %collective-permute-done.11, f32[1,16,2304]{2,1,0:T(8,128)S(1)} %collective-permute-done.10, f32[1,16,2304]{2,1,0:T(8,128)} %collective-permute-done.9, pred[]{:T(512)S(6)} %eq.62, pred[]{:T(512)S(6)} %eq.61, ...), kind=kLoop, calls=%fused_computation.25 | loop fusion | flops 589824 | bytes 811016 | tf_op jit(solution)/shard_map/convert_element_type | solution.py:278
  47.4 1.6 %convolution_bitcast_fusion.2 = f32[128,2048]{0,1:T(8,128)S(1)} fusion(bf16[128,256]{1,0:T(8,128)(2,1)S(1)} %copy-done.1, bf16[8192,256]{1,0:T(8,128)(2,1)} %param.12, s32[]{:T(128)S(6)} %select_n.171), kind=kOutput, calls=%fused_computation.2 | convolution fusion | flops 134217728 | bytes 2162692 | tf_op jit(solution)/shard_map/dot_general | solution.py:176
  49.1 4.1 %collective-permute-done.12 = bf16[1,16,2304]{2,1,0:T(8,128)(2,1)S(1)} collective-permute-done((bf16[1,16,2304]{2,1,0:T(8,128)(2,1)S(1)}, bf16[1,16,2304]{2,1,0:T(8,128)(2,1)S(1)}, u32[]{:S(2)}, u32[]{:S(2)}) %collective-permute-start.12) | collective-permute-done | bytes 73760 | tf_op jit(solution)/shard_map/ppermute | solution.py:278
  53.2 0.6 slice_add_fusion.1
  53.8 0.7 slice_add_fusion
  54.4 13.5 %collective-permute-done.5 = f32[128,2048]{0,1:T(8,128)S(1)} collective-permute-done((f32[128,2048]{0,1:T(8,128)}, f32[128,2048]{0,1:T(8,128)S(1)}, u32[]{:S(2)}, u32[]{:S(2)}) %collective-permute-start.5) | collective-permute-done | bytes 1048608 | tf_op jit(solution)/shard_map/ppermute | solution.py:193
  68.3 1.0 %copy.10 = bf16[128,2048]{1,0:T(8,128)(2,1)} copy(bf16[128,2048]{0,1:T(8,128)(2,1)S(1)} %fusion.9) | data formatting | bytes 1048576
  (42 shorter events, 4.0 us)
Async XLA Ops:
  0.6 29.0 %copy-start = (bf16[128,2048]{1,0:T(8,128)(2,1)S(1)}, bf16[128,2048]{1,0:T(8,128)(2,1)}, u32[]{:S(2)}) copy-start(bf16[128,2048]{1,0:T(8,128)(2,1)} %param.10) | copy-start | bytes 1572868
  4.3 12.0 %collective-permute-start.3 = (bf16[1,16,2432]{2,1,0:T(8,128)(2,1)S(1)}, bf16[1,16,2432]{2,1,0:T(8,128)(2,1)S(1)}, u32[]{:S(2)}, u32[]{:S(2)}) collective-permute-start(bf16[1,16,2432]{2,1,0:T(8,128)(2,1)S(1)} %pad_maximum_fusion.2), channel_id=1, source_target_pairs={{0,12},{4,8},{8,4},{12,0},{16,28},{20,24},{24,20},{28,16},{1,13},{... | collective-permute-start | bytes 233480 | tf_op jit(solution)/shard_map/ppermute | solution.py:227
  8.3 8.0 %collective-permute-start.2 = (bf16[1,16,2432]{2,1,0:T(8,128)(2,1)S(1)}, bf16[1,16,2432]{2,1,0:T(8,128)(2,1)S(1)}, u32[]{:S(2)}, u32[]{:S(2)}) collective-permute-start(bf16[1,16,2432]{2,1,0:T(8,128)(2,1)S(1)} %pad_maximum_fusion.2), channel_id=1, source_target_pairs={{0,8},{4,12},{8,0},{12,4},{16,24},{20,28},{24,16},{28,20},{1,9},{5... | collective-permute-start | bytes 233480 | tf_op jit(solution)/shard_map/ppermute | solution.py:227
  8.7 7.6 %collective-permute-start.1 = (bf16[1,16,2432]{2,1,0:T(8,128)(2,1)S(1)}, bf16[1,16,2432]{2,1,0:T(8,128)(2,1)S(1)}, u32[]{:S(2)}, u32[]{:S(2)}) collective-permute-start(bf16[1,16,2432]{2,1,0:T(8,128)(2,1)S(1)} %pad_maximum_fusion.2), channel_id=1, source_target_pairs={{0,4},{4,0},{8,12},{12,8},{16,20},{20,16},{24,28},{28,24},{1,5},{5... | collective-permute-start | bytes 233480 | tf_op jit(solution)/shard_map/ppermute | solution.py:227
  8.9 6.7 %collective-permute-start.4 = (s32[1]{0:T(128)}, s32[1]{0:T(128)}, u32[]{:S(2)}, u32[]{:S(2)}) collective-permute-start(s32[1]{0:T(128)} %param.15), channel_id=1, source_target_pairs={{0,16},{4,20},{8,24},{12,28},{16,0},{20,4},{24,8},{28,12},{1,17},{... | collective-permute-start | bytes 20 | tf_op jit(solution)/shard_map/ppermute | solution.py:225
  11.8 1.7 %copy-start.1 = (bf16[128,256]{1,0:T(8,128)(2,1)S(1)}, bf16[128,256]{1,0:T(8,128)(2,1)}, u32[]{:S(2)}) copy-start(bf16[128,256]{1,0:T(8,128)(2,1)} %param.11) | copy-start | bytes 196612
  13.5 2.1 %copy-start.2 = (bf16[1,16,2048]{2,1,0:T(8,128)(2,1)S(1)}, bf16[1,16,2048]{2,1,0:T(8,128)(2,1)}, u32[]{:S(2)}) copy-start(bf16[1,16,2048]{2,1,0:T(8,128)(2,1)} %param.13) | copy-start | bytes 196612
  13.5 2.1 %copy-start.3 = (bf16[1,16,256]{2,1,0:T(8,128)(2,1)S(1)}, bf16[1,16,256]{2,1,0:T(8,128)(2,1)}, u32[]{:S(2)}) copy-start(bf16[1,16,256]{2,1,0:T(8,128)(2,1)} %param.14) | copy-start | bytes 24580
  15.6 4.4 %collective-permute-start = (f32[2,128,2048]{1,2,0:T(8,128)}, f32[2,128,2048]{1,2,0:T(8,128)S(1)}, u32[]{:S(2)}, u32[]{:S(2)}) collective-permute-start(f32[2,128,2048]{1,2,0:T(8,128)} %convolution_bitcast_fusion), channel_id=1, source_target_pairs={{0,1},{1,0},{2,3},{3,2},{4,5},{5,4},{6,7},{7,6},{8,9},{9,8},{10,11... | collective-permute-start | bytes 6291464 | tf_op jit(solution)/shard_map/ppermute | solution.py:184
  22.6 6.8 %collective-permute-start.6 = (bf16[16,2304]{1,0:T(8,128)(2,1)S(1)}, bf16[16,2304]{1,0:T(8,128)(2,1)S(1)}, u32[]{:S(2)}, u32[]{:S(2)}) collective-permute-start(bf16[16,2304]{1,0:T(8,128)(2,1)S(1)} %dynamic-slice_bitcast_fusion.2), channel_id=1, source_target_pairs={{0,16},{4,20},{8,24},{12,28},{16,0},{20,4},{24,8},{28,12},{1,17},{... | collective-permute-start | bytes 221192 | tf_op jit(solution)/shard_map/ppermute | solution.py:253
  29.9 1.2 %collective-permute-start.7 = (f32[128,32]{0,1:T(8,128)S(1)}, f32[128,32]{0,1:T(8,128)S(1)}, u32[]{:S(2)}, u32[]{:S(2)}) collective-permute-start(f32[128,32]{0,1:T(8,128)S(1)} %pad_maximum_fusion.3), channel_id=1, source_target_pairs={{0,1},{1,0},{2,3},{3,2},{4,5},{5,4},{6,7},{7,6},{8,9},{9,8},{10,11... | collective-permute-start | bytes 49160 | tf_op jit(solution)/shard_map/ppermute | solution.py:55
  31.1 3.7 %collective-permute-start.8 = (f32[128,32]{0,1:T(8,128)S(1)}, f32[128,32]{0,1:T(8,128)S(1)}, u32[]{:S(2)}, u32[]{:S(2)}) collective-permute-start(f32[128,32]{0,1:T(8,128)S(1)} %fusion.27), channel_id=1, source_target_pairs={{0,2},{1,3},{2,0},{3,1},{4,6},{5,7},{6,4},{7,5},{8,10},{9,11},{10,... | collective-permute-start | bytes 49160 | tf_op jit(solution)/shard_map/ppermute | solution.py:55
  35.9 10.1 %collective-permute-start.10 = (f32[1,16,2304]{2,1,0:T(8,128)}, f32[1,16,2304]{2,1,0:T(8,128)S(1)}, u32[]{:S(2)}, u32[]{:S(2)}) collective-permute-start(f32[1,16,2304]{2,1,0:T(8,128)} %get-tuple-element.39), channel_id=1, source_target_pairs={{0,8},{4,12},{8,0},{12,4},{16,24},{20,28},{24,16},{28,20},{1,9},{5... | collective-permute-start | bytes 442376 | tf_op jit(solution)/shard_map/ppermute | solution.py:274
  35.9 10.0 %collective-permute-start.11 = (f32[1,16,2304]{2,1,0:T(8,128)}, f32[1,16,2304]{2,1,0:T(8,128)S(1)}, u32[]{:S(2)}, u32[]{:S(2)}) collective-permute-start(f32[1,16,2304]{2,1,0:T(8,128)} %get-tuple-element.40), channel_id=1, source_target_pairs={{0,12},{4,8},{8,4},{12,0},{16,28},{20,24},{24,20},{28,16},{1,13},{... | collective-permute-start | bytes 442376 | tf_op jit(solution)/shard_map/ppermute | solution.py:274
  38.9 7.5 %collective-permute-start.9 = (f32[1,16,2304]{2,1,0:T(8,128)S(1)}, f32[1,16,2304]{2,1,0:T(8,128)}, u32[]{:S(2)}, u32[]{:S(2)}) collective-permute-start(f32[1,16,2304]{2,1,0:T(8,128)S(1)} %get-tuple-element.38), channel_id=1, source_target_pairs={{0,4},{4,0},{8,12},{12,8},{16,20},{20,16},{24,28},{28,24},{1,5},{5... | collective-permute-start | bytes 442376 | tf_op jit(solution)/shard_map/ppermute | solution.py:274
  44.4 23.5 %collective-permute-start.5 = (f32[128,2048]{0,1:T(8,128)}, f32[128,2048]{0,1:T(8,128)S(1)}, u32[]{:S(2)}, u32[]{:S(2)}) collective-permute-start(f32[128,2048]{0,1:T(8,128)} %fusion.5), channel_id=1, source_target_pairs={{0,2},{1,3},{2,0},{3,1},{4,6},{5,7},{6,4},{7,5},{8,10},{9,11},{10,... | collective-permute-start | bytes 3145736 | tf_op jit(solution)/shard_map/ppermute | solution.py:193
  47.3 5.8 %collective-permute-start.12 = (bf16[1,16,2304]{2,1,0:T(8,128)(2,1)S(1)}, bf16[1,16,2304]{2,1,0:T(8,128)(2,1)S(1)}, u32[]{:S(2)}, u32[]{:S(2)}) collective-permute-start(bf16[1,16,2304]{2,1,0:T(8,128)(2,1)S(1)} %get-tuple-element.36), channel_id=1, source_target_pairs={{0,16},{4,20},{8,24},{12,28},{16,0},{20,4},{24,8},{28,12},{1,17},{... | collective-permute-start | bytes 221192 | tf_op jit(solution)/shard_map/ppermute | solution.py:278

commit v12 on v11

--- a/solution.py
+++ b/solution.py
@@ -196,10 +196,20 @@
     return held[0]
 
 
-def _low_rank(inputs, cotangent, base_grad, sel_down, sel_up, tensor_size):
+def _low_rank(inputs, cotangent, frozen_key_weight, sel_down, sel_up, tensor_size):
     low_in = jnp.dot(inputs, sel_down.T, preferred_element_type=jnp.float32)
     reduced_output = ADAPTER_SCALE * jnp.dot(cotangent, sel_up.T, preferred_element_type=jnp.float32)
     lows = jnp.concatenate([low_in, reduced_output], axis=1)
+    if tensor_size > 1 and tensor_size & (tensor_size - 1) == 0:
+        frozen = _frozen_first(cotangent, frozen_key_weight, "tensor", tensor_size)
+        *leaving, lows = lax.optimization_barrier((*frozen[1::2], lows))
+        frozen[1::2] = leaving
+        base_grad = _frozen_rest(frozen, "tensor", tensor_size)
+    else:
+        partial = lax.dot_general(
+            cotangent, frozen_key_weight, (((1,), (1,)), ((), ())), preferred_element_type=jnp.float32
+        )
+        base_grad = lax.psum_scatter(partial, "tensor", scatter_dimension=1, tiled=True)
     lows = _psum_small(lows, "tensor", tensor_size)
     rank = sel_down.shape[0]
     low_in_b = lows[:, :rank].astype(jnp.bfloat16)
@@ -238,26 +248,14 @@
         entry = lax.dynamic_index_in_dim(adapters_within, jnp.clip(slot, 0, half - 1), 0, keepdims=False)
         return lax.dynamic_index_in_dim(entry, tenant_id % held_tenants, 0, keepdims=False)
 
-    for_mirror = pick(mirror_tenant)
-    halving = tensor_size > 1 and tensor_size & (tensor_size - 1) == 0
-    if halving:
-        frozen = _frozen_first(cotangent, frozen_key_weight, "tensor", tensor_size)
-        *leaving, for_mirror = lax.optimization_barrier((*frozen[1::2], for_mirror))
-        frozen[1::2] = leaving
-        base_grad = _frozen_rest(frozen, "tensor", tensor_size)
-    else:
-        partial = lax.dot_general(
-            cotangent, frozen_key_weight, (((1,), (1,)), ((), ())), preferred_element_type=jnp.float32
-        )
-        base_grad = lax.psum_scatter(partial, "tensor", scatter_dimension=1, tiled=True)
-    crossed = lax.ppermute(for_mirror, "dp", [(i, i ^ half) for i in range(dp_size)])
+    crossed = lax.ppermute(pick(mirror_tenant), "dp", [(i, i ^ half) for i in range(dp_size)])
     near = ((owner ^ me) < half)
     selected = jnp.where(near, pick(tenant), crossed)
     sel_down = selected[:, :width_portion]
     sel_up = selected[:, width_portion:]
 
     grad_inputs, low_in_b, low_out_b = _low_rank(
-        inputs, cotangent, base_grad, sel_down, sel_up, tensor_size
+        inputs, cotangent, frozen_key_weight, sel_down, sel_up, tensor_size
     )
 
     down_term = jnp.dot(low_out_b.T, inputs, preferred_element_type=jnp.float32)

time: 69.7 us -> 68.7 us (0.986)
  waiting for transfers between devices: 31.1 us -> 28 us
  local copies, waits for them, and re-layouts: 6.61 us -> 8.72 us
  other arithmetic: 3.96 us -> 3.03 us
  starting transfers between devices: 14.1 us -> 15 us
    ppermute x1, waiting for transfers between devices: 3.54 us -> 0.01 us  [_frozen_first(): got = lax.ppermute(leaving, axis, [(i, i ^ 1) for i in range(size)])]
    slice x3, local copies, waits for them, and re-layouts: 1.81 us -> 3.28 us  [_mirrored(): w[0, 0, width + 1].astype(jnp.int32)]
    ppermute x1, waiting for transfers between devices: 13.5 us -> 14.9 us  [_frozen_rest(): got = [lax.ppermute(held[e], axis, pairs) for e in range(1, len(held), 2)]]
    convert_element_type x1, other arithmetic: 0.99 us -> 0.08 us  [_mirrored(): cross_sum.astype(jnp.bfloat16)]
    ppermute x1, starting transfers between devices: 0.01 us -> 0.91 us  [_mirrored(): lax.ppermute(pick(mirror_tenant), 'dp', [(i, i ^ half) for i in range(dp_...]
    unnamed x9 -> x13, local copies, waits for them, and re-layouts: 1.03 us -> 1.66 us
  transfers between devices with their start and end apart: 13 -> 13, of which waited for: 7 -> 5; matrix products, arithmetic and copies ran while one was open for 14% -> 15% of each run, Pallas kernels for 0% -> 0%
where the time goes in v12:
time: 68.7 us; the launch traced here: 68.3 us
  waiting for transfers between devices  28 us (41%)
  starting transfers between devices  15 us (22%)
  local copies, waits for them, and re-layouts  8.72 us (13%)
  matrix products  7.43 us (11%)
  between operations  6.09 us (9%)
  other arithmetic  3.03 us (4%)
    ppermute x1, waiting for transfers between devices, _frozen_rest(): got = [lax.ppermute(held[e], axis, pairs) for e in range(1, len(held), 2)]  14.9 us
    ppermute x1, waiting for transfers between devices, _mirrored(): lax.ppermute(pick(mirror_tenant), 'dp', [(i, i ^ half) for i in range(dp_...  6.3 us
    ppermute x3, starting transfers between devices, _mirrored(): lax.ppermute(payload, 'dp', [(i, i ^ s) for i in range(dp_size)])  4.61 us
    dot_general x2, matrix products, term(): lax.dot_general(cotangent, piece, (((1,), (1,)), ((), ())), preferred_ele...  4.32 us
    ppermute x1, waiting for transfers between devices, _mirrored(): lax.ppermute(cross_sum.astype(jnp.bfloat16), 'dp', [(i, i ^ half) for i i...  3.91 us
    ppermute x3, starting transfers between devices, _mirrored(): arrived = lax.ppermute(outgoing, 'dp', [(i, i ^ s) for i in range(dp_size)])  3.49 us
    slice x3, local copies, waits for them, and re-layouts, _mirrored(): w[0, 0, width + 1].astype(jnp.int32)  3.28 us
    ppermute x1, starting transfers between devices, _mirrored(): lax.ppermute(tenant_per_block, 'dp', [(i, i ^ half) for i in range(dp_siz...  2.91 us
  transfers between devices with their start and end apart: 13, of which 5 were waited for; matrix products, arithmetic and copies ran while one was open for 15% of the time, Pallas kernels for 0%

profile of v12, /device:TPU:0, one launch (start us, length us, event | category | flops | bytes accessed | tf_op | source)
XLA Modules:
  0.0 68.3 jit_solution(4200578881468442771)
XLA Ops:
  1.4 0.7 fusion.30
  2.1 1.4 %scatter.9 = bf16[1,16,128]{2,1,0:T(8,128)(2,1)S(1)} dynamic-update-slice(bf16[1,16,128]{2,1,0:T(8,128)(2,1)S(1)} %scatter.6, bf16[1,1,1]{2,1,0:T(2,128)(2,1)} %bitcast.11, s32[]{:T(128)} %constant.170.clone.1, s32[]{:T(128)} %bitcast.12, s32[]{:T(128)} %bitcast.13) | dynamic-update-slice | bytes 8 | tf_op jit(solution)/shard_map/scatter | solution.py:233
  3.5 0.9 %pad_maximum_fusion.2 = bf16[1,16,2432]{2,1,0:T(8,128)(2,1)S(1)} fusion(bf16[1,16,128]{2,1,0:T(8,128)(2,1)S(1)} %scatter.9, bf16[1,16,256]{2,1,0:T(8,128)(2,1)} %param.14, bf16[1,16,2048]{2,1,0:T(8,128)(2,1)} %param.13), kind=kLoop, calls=%fused_computation.28 | loop fusion | flops 233472 | bytes 155648 | tf_op jit(solution)/shard_map/concatenate | solution.py:234
  4.3 4.0 %collective-permute-start.3 = (bf16[1,16,2432]{2,1,0:T(8,128)(2,1)S(1)}, bf16[1,16,2432]{2,1,0:T(8,128)(2,1)S(1)}, u32[]{:S(2)}, u32[]{:S(2)}) collective-permute-start(bf16[1,16,2432]{2,1,0:T(8,128)(2,1)S(1)} %pad_maximum_fusion.2), channel_id=1, source_target_pairs={{0,12},{4,8},{8,4},{12,0},{16,28},{20,24},{24,20},{28,16},{1,13},{... | collective-permute-start | bytes 233480 | tf_op jit(solution)/shard_map/ppermute | solution.py:237
  8.9 2.9 %collective-permute-start.4 = (s32[1]{0:T(128)}, s32[1]{0:T(128)}, u32[]{:S(2)}, u32[]{:S(2)}) collective-permute-start(s32[1]{0:T(128)} %param.15), channel_id=1, source_target_pairs={{0,16},{4,20},{8,24},{12,28},{16,0},{20,4},{24,8},{28,12},{1,17},{... | collective-permute-start | bytes 20 | tf_op jit(solution)/shard_map/ppermute | solution.py:235
  11.8 1.7 %dynamic-slice_bitcast_fusion.1 = (bf16[1,2048,256]{2,1,0:T(8,128)(2,1)S(1)}, bf16[1,2048,256]{2,1,0:T(8,128)(2,1)S(1)}) fusion(bf16[8192,256]{1,0:T(8,128)(2,1)} %param.12, s32[]{:T(128)S(6)} %select_n.172, s32[]{:T(128)S(6)} %select_n.173), kind=kLoop, calls=%fused_computation.21 | loop fusion | bytes 4194312 | tf_op jit(solution)/shard_map/stack | solution.py:182
  13.6 2.0 %convolution_bitcast_fusion = f32[2,128,2048]{1,2,0:T(8,128)} fusion(bf16[1,2048,256]{2,1,0:T(8,128)(2,1)S(1)} %get-tuple-element.35, bf16[1,2048,256]{2,1,0:T(8,128)(2,1)S(1)} %get-tuple-element.34, bf16[128,256]{1,0:T(8,128)(2,1)S(1)} %copy-done.1), kind=kOutput, calls=%fused_computation | convolution fusion | flops 269484032 | bytes 4259840 | tf_op jit(solution)/shard_map/nk,bdk->bnd/dot_general | solution.py:181
  17.1 0.9 %collective-permute-start.5 = (bf16[16,2304]{1,0:T(8,128)(2,1)S(1)}, bf16[16,2304]{1,0:T(8,128)(2,1)S(1)}, u32[]{:S(2)}, u32[]{:S(2)}) collective-permute-start(bf16[16,2304]{1,0:T(8,128)(2,1)S(1)} %dynamic-slice_bitcast_fusion.2), channel_id=1, source_target_pairs={{0,16},{4,20},{8,24},{12,28},{16,0},{20,4},{24,8},{28,12},{1,17},{... | collective-permute-start | bytes 221192 | tf_op jit(solution)/shard_map/ppermute | solution.py:251
  18.0 6.3 %collective-permute-done.5 = bf16[16,2304]{1,0:T(8,128)(2,1)S(1)} collective-permute-done((bf16[16,2304]{1,0:T(8,128)(2,1)S(1)}, bf16[16,2304]{1,0:T(8,128)(2,1)S(1)}, u32[]{:S(2)}, u32[]{:S(2)}) %collective-permute-start.5) | collective-permute-done | bytes 73760 | tf_op jit(solution)/shard_map/ppermute | solution.py:251
  24.7 2.7 %fusion.5 = f32[128,2048]{0,1:T(8,128)} fusion(f32[2,128,2048]{1,2,0:T(8,128)S(1)} %collective-permute-done, bf16[128,256]{1,0:T(8,128)(2,1)S(1)} %copy-done.1, bf16[8192,256]{1,0:T(8,128)(2,1)} %param.12, s32[]{:T(128)S(6)} %select_n.174), kind=kOutput, calls=%fused_computation.13 | convolution fusion | flops 134479872 | bytes 3211268 | tf_op jit(solution)/shard_map/dot_general | solution.py:176
  27.4 1.2 %collective-permute-done.7 = f32[128,32]{0,1:T(8,128)S(1)} collective-permute-done((f32[128,32]{0,1:T(8,128)S(1)}, f32[128,32]{0,1:T(8,128)S(1)}, u32[]{:S(2)}, u32[]{:S(2)}) %collective-permute-start.7) | collective-permute-done | bytes 16416 | tf_op jit(solution)/shard_map/ppermute | solution.py:55
  28.6 1.5 %collective-permute-start.8 = (f32[128,32]{0,1:T(8,128)S(1)}, f32[128,32]{0,1:T(8,128)S(1)}, u32[]{:S(2)}, u32[]{:S(2)}) collective-permute-start(f32[128,32]{0,1:T(8,128)S(1)} %add.105), channel_id=1, source_target_pairs={{0,2},{1,3},{2,0},{3,1},{4,6},{5,7},{6,4},{7,5},{8,10},{9,11},{10,... | collective-permute-start | bytes 49160 | tf_op jit(solution)/shard_map/ppermute | solution.py:55
  30.7 1.7 %collective-permute-done.8 = f32[128,32]{0,1:T(8,128)S(1)} collective-permute-done((f32[128,32]{0,1:T(8,128)S(1)}, f32[128,32]{0,1:T(8,128)S(1)}, u32[]{:S(2)}, u32[]{:S(2)}) %collective-permute-start.8) | collective-permute-done | bytes 16416 | tf_op jit(solution)/shard_map/ppermute | solution.py:55
  32.6 0.7 %broadcast_select_fusion.1 = (f32[1,16,2304]{2,1,0:T(8,128)S(1)}, f32[1,16,2304]{2,1,0:T(8,128)}, f32[1,16,2304]{2,1,0:T(8,128)}) fusion(pred[]{:T(512)S(6)} %or.9, f32[1,16,256]{2,1,0:T(8,128)S(1)} %fusion.3, f32[1,16,2048]{2,1,0:T(8,128)S(1)} %convolution_bitcast_fusion.3, pred[]{:T(512)S(6)} %or.10, pred[]{:T(512)S(6)} %or.11), kind=kLoop, calls=%fused_computation.35 | loop fusion | flops 147456 | bytes 589827 | tf_op jit(solution)/shard_map/jit(_where)/select_n | solution.py:271
  33.5 2.9 %collective-permute-start.11 = (f32[1,16,2304]{2,1,0:T(8,128)}, f32[1,16,2304]{2,1,0:T(8,128)S(1)}, u32[]{:S(2)}, u32[]{:S(2)}) collective-permute-start(f32[1,16,2304]{2,1,0:T(8,128)} %get-tuple-element.40), channel_id=1, source_target_pairs={{0,12},{4,8},{8,4},{12,0},{16,28},{20,24},{24,20},{28,16},{1,13},{... | collective-permute-start | bytes 442376 | tf_op jit(solution)/shard_map/ppermute | solution.py:272
  36.9 1.3 %fusion.28 = (bf16[1,1,1]{2,1,0:T(2,128)(2,1)}, bf16[1,1,1]{2,1,0:T(2,128)(2,1)}) fusion(bf16[1,16,2432]{2,1,0:T(8,128)(2,1)} %copy-done.4), kind=kLoop, calls=%fused_computation.53 | loop fusion | bytes 8 | tf_op jit(solution)/shard_map/slice | solution.py:241
  40.8 1.3 %fusion.29 = (bf16[1,1,1]{2,1,0:T(2,128)(2,1)}, bf16[1,1,1]{2,1,0:T(2,128)(2,1)}) fusion(bf16[1,16,2432]{2,1,0:T(8,128)(2,1)} %copy-done.3), kind=kLoop, calls=%fused_computation.54 | loop fusion | bytes 8 | tf_op jit(solution)/shard_map/slice | solution.py:241
  43.4 1.5 %collective-permute-start.6 = (f32[128,2048]{0,1:T(8,128)}, f32[128,2048]{0,1:T(8,128)S(1)}, u32[]{:S(2)}, u32[]{:S(2)}) collective-permute-start(f32[128,2048]{0,1:T(8,128)} %fusion.5), channel_id=1, source_target_pairs={{0,2},{1,3},{2,0},{3,1},{4,6},{5,7},{6,4},{7,5},{8,10},{9,11},{10,... | collective-permute-start | bytes 3145736 | tf_op jit(solution)/shard_map/ppermute | solution.py:193
  45.2 1.6 %convolution_bitcast_fusion.2 = f32[128,2048]{0,1:T(8,128)S(1)} fusion(bf16[128,256]{1,0:T(8,128)(2,1)S(1)} %copy-done.1, bf16[8192,256]{1,0:T(8,128)(2,1)} %param.12, s32[]{:T(128)S(6)} %select_n.171), kind=kOutput, calls=%fused_computation.2 | convolution fusion | flops 134217728 | bytes 2162692 | tf_op jit(solution)/shard_map/dot_general | solution.py:176
  46.8 3.9 %collective-permute-done.12 = bf16[1,16,2304]{2,1,0:T(8,128)(2,1)S(1)} collective-permute-done((bf16[1,16,2304]{2,1,0:T(8,128)(2,1)S(1)}, bf16[1,16,2304]{2,1,0:T(8,128)(2,1)S(1)}, u32[]{:S(2)}, u32[]{:S(2)}) %collective-permute-start.12) | collective-permute-done | bytes 73760 | tf_op jit(solution)/shard_map/ppermute | solution.py:276
  50.7 0.6 slice_add_fusion.1
  51.3 0.7 slice_add_fusion
  52.0 14.9 %collective-permute-done.6 = f32[128,2048]{0,1:T(8,128)S(1)} collective-permute-done((f32[128,2048]{0,1:T(8,128)}, f32[128,2048]{0,1:T(8,128)S(1)}, u32[]{:S(2)}, u32[]{:S(2)}) %collective-permute-start.6) | collective-permute-done | bytes 1048608 | tf_op jit(solution)/shard_map/ppermute | solution.py:193
  67.3 1.0 %copy.10 = bf16[128,2048]{1,0:T(8,128)(2,1)} copy(bf16[128,2048]{0,1:T(8,128)(2,1)S(1)} %fusion.9) | data formatting | bytes 1048576
  (46 shorter events, 3.8 us)
Async XLA Ops:
  0.6 23.8 %copy-start = (bf16[128,2048]{1,0:T(8,128)(2,1)S(1)}, bf16[128,2048]{1,0:T(8,128)(2,1)}, u32[]{:S(2)}) copy-start(bf16[128,2048]{1,0:T(8,128)(2,1)} %param.10) | copy-start | bytes 1572868
  4.3 12.0 %collective-permute-start.3 = (bf16[1,16,2432]{2,1,0:T(8,128)(2,1)S(1)}, bf16[1,16,2432]{2,1,0:T(8,128)(2,1)S(1)}, u32[]{:S(2)}, u32[]{:S(2)}) collective-permute-start(bf16[1,16,2432]{2,1,0:T(8,128)(2,1)S(1)} %pad_maximum_fusion.2), channel_id=1, source_target_pairs={{0,12},{4,8},{8,4},{12,0},{16,28},{20,24},{24,20},{28,16},{1,13},{... | collective-permute-start | bytes 233480 | tf_op jit(solution)/shard_map/ppermute | solution.py:237
  8.3 8.1 %collective-permute-start.2 = (bf16[1,16,2432]{2,1,0:T(8,128)(2,1)S(1)}, bf16[1,16,2432]{2,1,0:T(8,128)(2,1)S(1)}, u32[]{:S(2)}, u32[]{:S(2)}) collective-permute-start(bf16[1,16,2432]{2,1,0:T(8,128)(2,1)S(1)} %pad_maximum_fusion.2), channel_id=1, source_target_pairs={{0,8},{4,12},{8,0},{12,4},{16,24},{20,28},{24,16},{28,20},{1,9},{5... | collective-permute-start | bytes 233480 | tf_op jit(solution)/shard_map/ppermute | solution.py:237
  8.7 7.6 %collective-permute-start.1 = (bf16[1,16,2432]{2,1,0:T(8,128)(2,1)S(1)}, bf16[1,16,2432]{2,1,0:T(8,128)(2,1)S(1)}, u32[]{:S(2)}, u32[]{:S(2)}) collective-permute-start(bf16[1,16,2432]{2,1,0:T(8,128)(2,1)S(1)} %pad_maximum_fusion.2), channel_id=1, source_target_pairs={{0,4},{4,0},{8,12},{12,8},{16,20},{20,16},{24,28},{28,24},{1,5},{5... | collective-permute-start | bytes 233480 | tf_op jit(solution)/shard_map/ppermute | solution.py:237
  8.9 6.7 %collective-permute-start.4 = (s32[1]{0:T(128)}, s32[1]{0:T(128)}, u32[]{:S(2)}, u32[]{:S(2)}) collective-permute-start(s32[1]{0:T(128)} %param.15), channel_id=1, source_target_pairs={{0,16},{4,20},{8,24},{12,28},{16,0},{20,4},{24,8},{28,12},{1,17},{... | collective-permute-start | bytes 20 | tf_op jit(solution)/shard_map/ppermute | solution.py:235
  11.8 1.7 %copy-start.1 = (bf16[128,256]{1,0:T(8,128)(2,1)S(1)}, bf16[128,256]{1,0:T(8,128)(2,1)}, u32[]{:S(2)}) copy-start(bf16[128,256]{1,0:T(8,128)(2,1)} %param.11) | copy-start | bytes 196612
  13.6 2.1 %copy-start.2 = (bf16[1,16,2048]{2,1,0:T(8,128)(2,1)S(1)}, bf16[1,16,2048]{2,1,0:T(8,128)(2,1)}, u32[]{:S(2)}) copy-start(bf16[1,16,2048]{2,1,0:T(8,128)(2,1)} %param.13) | copy-start | bytes 196612
  13.6 2.1 %copy-start.5 = (bf16[1,16,256]{2,1,0:T(8,128)(2,1)S(1)}, bf16[1,16,256]{2,1,0:T(8,128)(2,1)}, u32[]{:S(2)}) copy-start(bf16[1,16,256]{2,1,0:T(8,128)(2,1)} %param.14) | copy-start | bytes 24580
  15.6 9.1 %collective-permute-start = (f32[2,128,2048]{1,2,0:T(8,128)}, f32[2,128,2048]{1,2,0:T(8,128)S(1)}, u32[]{:S(2)}, u32[]{:S(2)}) collective-permute-start(f32[2,128,2048]{1,2,0:T(8,128)} %convolution_bitcast_fusion), channel_id=1, source_target_pairs={{0,1},{1,0},{2,3},{3,2},{4,5},{5,4},{6,7},{7,6},{8,9},{9,8},{10,11... | collective-permute-start | bytes 6291464 | tf_op jit(solution)/shard_map/ppermute | solution.py:184
  16.3 0.6 copy-start.3
  16.4 0.6 copy-start.4
  17.1 7.2 %collective-permute-start.5 = (bf16[16,2304]{1,0:T(8,128)(2,1)S(1)}, bf16[16,2304]{1,0:T(8,128)(2,1)S(1)}, u32[]{:S(2)}, u32[]{:S(2)}) collective-permute-start(bf16[16,2304]{1,0:T(8,128)(2,1)S(1)} %dynamic-slice_bitcast_fusion.2), channel_id=1, source_target_pairs={{0,16},{4,20},{8,24},{12,28},{16,0},{20,4},{24,8},{28,12},{1,17},{... | collective-permute-start | bytes 221192 | tf_op jit(solution)/shard_map/ppermute | solution.py:251
  27.4 1.2 %collective-permute-start.7 = (f32[128,32]{0,1:T(8,128)S(1)}, f32[128,32]{0,1:T(8,128)S(1)}, u32[]{:S(2)}, u32[]{:S(2)}) collective-permute-start(f32[128,32]{0,1:T(8,128)S(1)} %pad_maximum_fusion.3), channel_id=1, source_target_pairs={{0,1},{1,0},{2,3},{3,2},{4,5},{5,4},{6,7},{7,6},{8,9},{9,8},{10,11... | collective-permute-start | bytes 49160 | tf_op jit(solution)/shard_map/ppermute | solution.py:55
  28.6 3.7 %collective-permute-start.8 = (f32[128,32]{0,1:T(8,128)S(1)}, f32[128,32]{0,1:T(8,128)S(1)}, u32[]{:S(2)}, u32[]{:S(2)}) collective-permute-start(f32[128,32]{0,1:T(8,128)S(1)} %add.105), channel_id=1, source_target_pairs={{0,2},{1,3},{2,0},{3,1},{4,6},{5,7},{6,4},{7,5},{8,10},{9,11},{10,... | collective-permute-start | bytes 49160 | tf_op jit(solution)/shard_map/ppermute | solution.py:55
  33.4 11.6 %collective-permute-start.10 = (f32[1,16,2304]{2,1,0:T(8,128)}, f32[1,16,2304]{2,1,0:T(8,128)S(1)}, u32[]{:S(2)}, u32[]{:S(2)}) collective-permute-start(f32[1,16,2304]{2,1,0:T(8,128)} %get-tuple-element.39), channel_id=1, source_target_pairs={{0,8},{4,12},{8,0},{12,4},{16,24},{20,28},{24,16},{28,20},{1,9},{5... | collective-permute-start | bytes 442376 | tf_op jit(solution)/shard_map/ppermute | solution.py:272
  33.5 11.5 %collective-permute-start.11 = (f32[1,16,2304]{2,1,0:T(8,128)}, f32[1,16,2304]{2,1,0:T(8,128)S(1)}, u32[]{:S(2)}, u32[]{:S(2)}) collective-permute-start(f32[1,16,2304]{2,1,0:T(8,128)} %get-tuple-element.40), channel_id=1, source_target_pairs={{0,12},{4,8},{8,4},{12,0},{16,28},{20,24},{24,20},{28,16},{1,13},{... | collective-permute-start | bytes 442376 | tf_op jit(solution)/shard_map/ppermute | solution.py:272
  36.4 8.6 %collective-permute-start.9 = (f32[1,16,2304]{2,1,0:T(8,128)S(1)}, f32[1,16,2304]{2,1,0:T(8,128)S(1)}, u32[]{:S(2)}, u32[]{:S(2)}) collective-permute-start(f32[1,16,2304]{2,1,0:T(8,128)S(1)} %get-tuple-element.38), channel_id=1, source_target_pairs={{0,4},{4,0},{8,12},{12,8},{16,20},{20,16},{24,28},{28,24},{1,5},{5... | collective-permute-start | bytes 442376 | tf_op jit(solution)/shard_map/ppermute | solution.py:272
  43.4 23.5 %collective-permute-start.6 = (f32[128,2048]{0,1:T(8,128)}, f32[128,2048]{0,1:T(8,128)S(1)}, u32[]{:S(2)}, u32[]{:S(2)}) collective-permute-start(f32[128,2048]{0,1:T(8,128)} %fusion.5), channel_id=1, source_target_pairs={{0,2},{1,3},{2,0},{3,1},{4,6},{5,7},{6,4},{7,5},{8,10},{9,11},{10,... | collective-permute-start | bytes 3145736 | tf_op jit(solution)/shard_map/ppermute | solution.py:193
  45.1 5.6 %collective-permute-start.12 = (bf16[1,16,2304]{2,1,0:T(8,128)(2,1)S(1)}, bf16[1,16,2304]{2,1,0:T(8,128)(2,1)S(1)}, u32[]{:S(2)}, u32[]{:S(2)}) collective-permute-start(bf16[1,16,2304]{2,1,0:T(8,128)(2,1)S(1)} %get-tuple-element.36), channel_id=1, source_target_pairs={{0,16},{4,20},{8,24},{12,28},{16,0},{20,4},{24,8},{28,12},{1,17},{... | collective-permute-start | bytes 221192 | tf_op jit(solution)/shard_map/ppermute | solution.py:276

commit v13 on v7

--- a/solution.py
+++ b/solution.py
@@ -102,8 +102,22 @@
 
 
     packed = jnp.concatenate([adapter_down_weight, adapter_up_weight], axis=2)
+    width = packed.shape[2]
+    routed = block_count == 1 and dp_size >= 4 and dp_size & (dp_size - 1) == 0
+    if routed:
+        tenant = tenant_per_block[0]
+        digits = jnp.zeros((held_tenants, adapter_rank_size, 128), jnp.float32)
+        digits = digits.at[:, 0, 0].set((tenant // 256).astype(jnp.float32))
+        digits = digits.at[:, 0, 1].set((tenant % 256).astype(jnp.float32))
+        packed = jnp.concatenate([packed, digits.astype(packed.dtype)], axis=2)
     stacked, order = _gather_dp(packed, "dp", dp_size)
     stacked = stacked.reshape(dp_size, held_tenants, *packed.shape[1:])
+    if routed:
+        tenants_seen = [
+            stacked[p, 0, 0, width].astype(jnp.int32) * 256 + stacked[p, 0, 0, width + 1].astype(jnp.int32)
+            for p in range(dp_size)
+        ]
+        stacked = stacked[..., :width]
     owner = tenant_per_block // held_tenants
     local = tenant_per_block % held_tenants
     pick = (order[None, :] == owner[:, None])
@@ -150,6 +164,24 @@
     down_contribution = down_contribution.reshape(dp_size, held_tenants, adapter_rank_size, width_portion)
     up_contribution = up_contribution.reshape(dp_size, held_tenants, adapter_rank_size, key_portion)
     combined = jnp.concatenate([down_contribution, up_contribution], axis=3)
+    if routed:
+        half = dp_size // 2
+        owner_me = tenant_per_block[0] // held_tenants
+        term = lax.dynamic_index_in_dim(combined, owner_me, 0, keepdims=False)
+        zero = jnp.zeros_like(term)
+        own_sum = jnp.where(owner_me == me_dp, term, zero)
+        cross_sum = jnp.where(owner_me == (me_dp ^ half), term, zero)
+        for s in range(1, half):
+            mate = me_dp ^ s
+            outgoing = jnp.where((owner_me == mate) | (owner_me == (mate ^ half)), term, zero)
+            arrived = lax.ppermute(outgoing, "dp", [(i, i ^ s) for i in range(dp_size)])
+            sender_owner = tenants_seen[s] // held_tenants
+            own_sum = own_sum + jnp.where(sender_owner == me_dp, arrived, zero)
+            cross_sum = cross_sum + jnp.where(sender_owner == (me_dp ^ half), arrived, zero)
+        arrived = lax.ppermute(cross_sum.astype(jnp.bfloat16), "dp", [(i, i ^ half) for i in range(dp_size)])
+        grad_down = own_sum[:, :, :width_portion] + arrived[:, :, :width_portion].astype(jnp.float32)
+        grad_up = own_sum[:, :, width_portion:] + arrived[:, :, width_portion:].astype(jnp.float32)
+        return (grad_inputs, grad_down, grad_up)
     owned = lax.dynamic_index_in_dim(combined, me_dp, 0, keepdims=False)
     grad_down = owned[:, :, :width_portion]
     grad_up = owned[:, :, width_portion:]

time: 59.2 us -> 76.5 us (1.29)
  waiting for transfers between devices: 18.3 us -> 33.9 us
  starting transfers between devices: 25.3 us -> 17.7 us
  other arithmetic: 1.62 us -> 5.68 us
  between operations: 1.54 us -> 5.47 us
  local copies, waits for them, and re-layouts: 2.99 us -> 4.07 us
    ppermute x3, waiting for transfers between devices: 1.14 us -> 14.5 us  [_frozen_term(): got = [lax.ppermute(held[e], axis, pairs) for e in range(1, len(held), 2)]]
    ppermute x7 -> x4, starting transfers between devices: 15 us -> 6.77 us  [the longest x3 3.67 us: on_device(): arrived = lax.ppermute(outgoing, 'dp', [(i, i ^ s) for i in range(dp_size)])]
    ppermute x2, waiting for transfers between devices: 1.5 us -> 3.25 us  [_psum_small(): lax.ppermute(total, axis, [(i, i ^ step) for i in range(size)])]
    select_n x0 -> x2, other arithmetic: none -> 1.43 us  [on_device(): jnp.where((owner_me == mate) | (owner_me == mate ^ half), term, zero)]
    scatter x0 -> x2, local copies, waits for them, and re-layouts: none -> 1.37 us  [the longest x1 1.36 us: on_device(): digits = digits.at[:, 0, 1].set((tenant % 256).astype(jnp.float32))]
    convert_element_type x8 -> x1, other arithmetic: 0.1 us -> 1.13 us  [on_device(): cross_sum.astype(jnp.bfloat16)]
    unnamed x9 -> x8, local copies, waits for them, and re-layouts: 1.97 us -> 1.07 us
    concatenate x1, other arithmetic: 0.02 us -> 0.87 us  [_gather_dp(): jnp.concatenate([local, lax.ppermute(local, axis, [(i, i ^ 1) for i in ra...]
  transfers between devices with their start and end apart: 16 -> 13, of which waited for: 8 -> 7; matrix products, arithmetic and copies ran while one was open for 11% -> 11% of each run, Pallas kernels for 0% -> 0%
where the time goes in v13:
time: 76.5 us; the launch traced here: 76 us
  waiting for transfers between devices  33.9 us (44%)
  starting transfers between devices  17.7 us (23%)
  matrix products  9.11 us (12%)
  other arithmetic  5.68 us (7%)
  between operations  5.47 us (7%)
  local copies, waits for them, and re-layouts  4.07 us (5%)
    ppermute x3, waiting for transfers between devices, _frozen_term(): got = [lax.ppermute(held[e], axis, pairs) for e in range(1, len(held), 2)]  14.5 us
    ppermute x3, waiting for transfers between devices, _gather_dp(): got.append(lax.ppermute(pair, axis, [(i, i ^ shift) for i in range(size)]))  11.8 us
    dot_general x4, matrix products, term(): lax.dot_general(cotangent, piece, (((1,), (1,)), ((), ())), preferred_ele...  7.64 us
    ppermute x3, starting transfers between devices, _gather_dp(): got.append(lax.ppermute(pair, axis, [(i, i ^ shift) for i in range(size)]))  4.73 us
    ppermute x1, waiting for transfers between devices, on_device(): lax.ppermute(cross_sum.astype(jnp.bfloat16), 'dp', [(i, i ^ half) for i i...  3.86 us
    ppermute x3, starting transfers between devices, on_device(): arrived = lax.ppermute(outgoing, 'dp', [(i, i ^ s) for i in range(dp_size)])  3.67 us
    ppermute x2, waiting for transfers between devices, _psum_small(): lax.ppermute(total, axis, [(i, i ^ step) for i in range(size)])  3.25 us
    ppermute x1, starting transfers between devices, on_device(): lax.ppermute(cross_sum.astype(jnp.bfloat16), 'dp', [(i, i ^ half) for i i...  3.09 us
  transfers between devices with their start and end apart: 13, of which 7 were waited for; matrix products, arithmetic and copies ran while one was open for 11% of the time, Pallas kernels for 0%

profile of v13, /device:TPU:0, one launch (start us, length us, event | category | flops | bytes accessed | tf_op | source)
XLA Modules:
  0.0 76.0 jit_solution(6986934187545823932)
XLA Ops:
  2.0 1.4 %scatter.9 = bf16[1,16,128]{2,1,0:T(8,128)(2,1)S(1)} dynamic-update-slice(bf16[1,16,128]{2,1,0:T(8,128)(2,1)S(1)} %scatter.6, bf16[1,1,1]{2,1,0:T(2,128)(2,1)} %bitcast.15, s32[]{:T(128)} %constant.161.clone.1, s32[]{:T(128)} %bitcast.16, s32[]{:T(128)} %bitcast.17) | dynamic-update-slice | bytes 8 | tf_op jit(solution)/shard_map/scatter | solution.py:111
  3.4 0.9 %pad_maximum_fusion.1 = (bf16[1,16,2432]{2,1,0:T(8,128)(2,1)S(1)}, bf16[8,16,2432]{2,1,0:T(8,128)(2,1)S(1)}) fusion(bf16[1,16,128]{2,1,0:T(8,128)(2,1)S(1)} %scatter.9, bf16[1,16,256]{2,1,0:T(8,128)(2,1)} %param.14, bf16[1,16,2048]{2,1,0:T(8,128)(2,1)} %param.13), kind=kLoop, calls=%fused_computation.42 | loop fusion | flops 233471 | bytes 233472 | tf_op jit(solution)/shard_map/concatenate | solution.py:112
  4.3 3.0 %collective-permute-start.2 = (bf16[1,16,2432]{2,1,0:T(8,128)(2,1)S(1)}, bf16[1,16,2432]{2,1,0:T(8,128)(2,1)S(1)}, u32[]{:S(2)}, u32[]{:S(2)}) collective-permute-start(bf16[1,16,2432]{2,1,0:T(8,128)(2,1)S(1)} %get-tuple-element.46), channel_id=1, source_target_pairs={{0,4},{4,0},{8,12},{12,8},{16,20},{20,16},{24,28},{28,24},{1,5},{5... | collective-permute-start | bytes 233480 | tf_op jit(solution)/shard_map/ppermute | solution.py:36
  7.3 1.6 %convolution_bitcast_fusion.1 = f32[128,2048]{0,1:T(8,128)S(1)} fusion(bf16[128,256]{1,0:T(8,128)(2,1)} %param.11, bf16[8192,256]{1,0:T(8,128)(2,1)} %param.12, s32[]{:T(128)S(6)} %select_n.164), kind=kOutput, calls=%fused_computation.1 | convolution fusion | flops 134217728 | bytes 2162692 | tf_op jit(solution)/shard_map/dot_general | solution.py:71
  9.7 0.9 %pad_maximum_fusion = bf16[2,16,2432]{2,1,0:T(8,128)(2,1)S(1)} fusion(bf16[1,16,2432]{2,1,0:T(8,128)(2,1)S(1)} %collective-permute-done.2, bf16[1,16,128]{2,1,0:T(8,128)(2,1)S(1)} %scatter.9, bf16[1,16,256]{2,1,0:T(8,128)(2,1)} %param.14, bf16[1,16,2048]{2,1,0:T(8,128)(2,1)} %param.13), kind=kLoop, calls=%fused_computation.24 | loop fusion | flops 622592 | bytes 311296 | tf_op jit(solution)/shard_map/concatenate | solution.py:36
  10.6 2.1 %collective-permute-start.3 = (bf16[2,16,2432]{2,1,0:T(8,128)(2,1)S(1)}, bf16[2,16,2432]{2,1,0:T(8,128)(2,1)S(1)}, u32[]{:S(2)}, u32[]{:S(2)}) collective-permute-start(bf16[2,16,2432]{2,1,0:T(8,128)(2,1)S(1)} %pad_maximum_fusion), channel_id=1, source_target_pairs={{0,8},{4,12},{8,0},{12,4},{16,24},{20,28},{24,16},{28,20},{1,9},{5... | collective-permute-start | bytes 466952 | tf_op jit(solution)/shard_map/ppermute | solution.py:41
  12.7 2.6 %collective-permute-start.4 = (bf16[2,16,2432]{2,1,0:T(8,128)(2,1)S(1)}, bf16[2,16,2432]{2,1,0:T(8,128)(2,1)S(1)}, u32[]{:S(2)}, u32[]{:S(2)}) collective-permute-start(bf16[2,16,2432]{2,1,0:T(8,128)(2,1)S(1)} %pad_maximum_fusion), channel_id=1, source_target_pairs={{0,16},{4,20},{8,24},{12,28},{16,0},{20,4},{24,8},{28,12},{1,17},{... | collective-permute-start | bytes 466952 | tf_op jit(solution)/shard_map/ppermute | solution.py:41
  15.3 3.2 %collective-permute-done.3 = bf16[2,16,2432]{2,1,0:T(8,128)(2,1)S(1)} collective-permute-done((bf16[2,16,2432]{2,1,0:T(8,128)(2,1)S(1)}, bf16[2,16,2432]{2,1,0:T(8,128)(2,1)S(1)}, u32[]{:S(2)}, u32[]{:S(2)}) %collective-permute-start.3) | collective-permute-done | bytes 155680 | tf_op jit(solution)/shard_map/ppermute | solution.py:41
  18.5 8.6 %collective-permute-done.4 = bf16[2,16,2432]{2,1,0:T(8,128)(2,1)S(1)} collective-permute-done((bf16[2,16,2432]{2,1,0:T(8,128)(2,1)S(1)}, bf16[2,16,2432]{2,1,0:T(8,128)(2,1)S(1)}, u32[]{:S(2)}, u32[]{:S(2)}) %collective-permute-start.4) | collective-permute-done | bytes 155680 | tf_op jit(solution)/shard_map/ppermute | solution.py:41
  27.9 2.7 %fusion.3 = f32[128,2048]{0,1:T(8,128)} fusion(f32[128,2048]{0,1:T(8,128)S(1)} %collective-permute-done.1, bf16[128,256]{1,0:T(8,128)(2,1)S(1)} %copy-done.1, bf16[8192,256]{1,0:T(8,128)(2,1)} %param.12, s32[]{:T(128)S(6)} %select_n.163), kind=kOutput, calls=%fused_computation.8 | convolution fusion | flops 134479872 | bytes 3211268 | tf_op jit(solution)/shard_map/dot_general | solution.py:71
  30.6 1.2 %collective-permute-done.7 = f32[1,128,32]{1,2,0:T(8,128)S(1)} collective-permute-done((f32[1,128,32]{1,2,0:T(8,128)S(1)}, f32[1,128,32]{1,2,0:T(8,128)S(1)}, u32[]{:S(2)}, u32[]{:S(2)}) %collective-permute-start.7) | collective-permute-done | bytes 16416 | tf_op jit(solution)/shard_map/ppermute | solution.py:55
  31.8 1.5 %collective-permute-start.8 = (f32[1,128,32]{1,2,0:T(8,128)S(1)}, f32[1,128,32]{1,2,0:T(8,128)S(1)}, u32[]{:S(2)}, u32[]{:S(2)}) collective-permute-start(f32[1,128,32]{1,2,0:T(8,128)S(1)} %add.104), channel_id=1, source_target_pairs={{0,2},{1,3},{2,0},{3,1},{4,6},{5,7},{6,4},{7,5},{8,10},{9,11},{10,... | collective-permute-start | bytes 49160 | tf_op jit(solution)/shard_map/ppermute | solution.py:55
  33.5 2.1 %collective-permute-done.8 = f32[1,128,32]{1,2,0:T(8,128)S(1)} collective-permute-done((f32[1,128,32]{1,2,0:T(8,128)S(1)}, f32[1,128,32]{1,2,0:T(8,128)S(1)}, u32[]{:S(2)}, u32[]{:S(2)}) %collective-permute-start.8) | collective-permute-done | bytes 16416 | tf_op jit(solution)/shard_map/ppermute | solution.py:55
  36.8 0.7 fusion.20
  37.5 2.2 %collective-permute-start.10 = (f32[1,16,2304]{2,1,0:T(8,128)}, f32[1,16,2304]{2,1,0:T(8,128)}, u32[]{:S(2)}, u32[]{:S(2)}) collective-permute-start(f32[1,16,2304]{2,1,0:T(8,128)} %get-tuple-element.44), channel_id=1, source_target_pairs={{0,8},{4,12},{8,0},{12,4},{16,24},{20,28},{24,16},{28,20},{1,9},{5... | collective-permute-start | bytes 442376 | tf_op jit(solution)/shard_map/ppermute | solution.py:177
  39.9 1.3 %collective-permute-start.9 = (f32[1,16,2304]{2,1,0:T(8,128)}, f32[1,16,2304]{2,1,0:T(8,128)}, u32[]{:S(2)}, u32[]{:S(2)}) collective-permute-start(f32[1,16,2304]{2,1,0:T(8,128)} %get-tuple-element.34), channel_id=1, source_target_pairs={{0,4},{4,0},{8,12},{12,8},{16,20},{20,16},{24,28},{28,24},{1,5},{5... | collective-permute-start | bytes 442376 | tf_op jit(solution)/shard_map/ppermute | solution.py:177
  41.2 1.6 %convolution_bitcast_fusion.3 = f32[128,2048]{0,1:T(8,128)S(1)} fusion(bf16[128,256]{1,0:T(8,128)(2,1)S(1)} %copy-done.1, bf16[8192,256]{1,0:T(8,128)(2,1)} %param.12, s32[]{:T(128)S(6)} %select_n.162), kind=kOutput, calls=%fused_computation.3 | convolution fusion | flops 134217728 | bytes 2162692 | tf_op jit(solution)/shard_map/dot_general | solution.py:71
  47.5 1.6 %collective-permute-start.6 = (f32[128,2048]{0,1:T(8,128)}, f32[128,2048]{0,1:T(8,128)S(1)}, u32[]{:S(2)}, u32[]{:S(2)}) collective-permute-start(f32[128,2048]{0,1:T(8,128)} %fusion.3), channel_id=1, source_target_pairs={{0,2},{1,3},{2,0},{3,1},{4,6},{5,7},{6,4},{7,5},{8,10},{9,11},{10,... | collective-permute-start | bytes 3145736 | tf_op jit(solution)/shard_map/ppermute | solution.py:83
  49.1 1.1 %fusion.16 = (bf16[1,16,2304]{2,1,0:T(8,128)(2,1)S(1)}, f32[1,16,2304]{2,1,0:T(8,128)S(1)}) fusion(f32[1,16,2304]{2,1,0:T(8,128)} %collective-permute-done.11, f32[1,16,2304]{2,1,0:T(8,128)} %collective-permute-done.10, f32[1,16,2304]{2,1,0:T(8,128)} %collective-permute-done.9, f32[1,1,16,2304]{3,2,0,1:T(8,128)S(1)} %get-tuple-element.35, pred[]{:T(512)S(6)} %eq.92, ...), kind=kLoop, calls=%fused_computation.29 | loop fusion | flops 552960 | bytes 811016 | tf_op jit(solution)/shard_map/convert_element_type | solution.py:181
  50.2 3.1 %collective-permute-start.12 = (bf16[1,16,2304]{2,1,0:T(8,128)(2,1)S(1)}, bf16[1,16,2304]{2,1,0:T(8,128)(2,1)S(1)}, u32[]{:S(2)}, u32[]{:S(2)}) collective-permute-start(bf16[1,16,2304]{2,1,0:T(8,128)(2,1)S(1)} %get-tuple-element.42), channel_id=1, source_target_pairs={{0,16},{4,20},{8,24},{12,28},{16,0},{20,4},{24,8},{28,12},{1,17},{... | collective-permute-start | bytes 221192 | tf_op jit(solution)/shard_map/ppermute | solution.py:181
  53.6 3.9 %collective-permute-done.12 = bf16[1,16,2304]{2,1,0:T(8,128)(2,1)S(1)} collective-permute-done((bf16[1,16,2304]{2,1,0:T(8,128)(2,1)S(1)}, bf16[1,16,2304]{2,1,0:T(8,128)(2,1)S(1)}, u32[]{:S(2)}, u32[]{:S(2)}) %collective-permute-start.12) | collective-permute-done | bytes 73760 | tf_op jit(solution)/shard_map/ppermute | solution.py:181
  58.8 14.5 %collective-permute-done.6 = f32[128,2048]{0,1:T(8,128)S(1)} collective-permute-done((f32[128,2048]{0,1:T(8,128)}, f32[128,2048]{0,1:T(8,128)S(1)}, u32[]{:S(2)}, u32[]{:S(2)}) %collective-permute-start.6) | collective-permute-done | bytes 1048608 | tf_op jit(solution)/shard_map/ppermute | solution.py:83
  73.3 1.7 %fusion.4 = bf16[128,2048]{0,1:T(8,128)(2,1)S(1)} fusion(f32[128,2048]{0,1:T(8,128)S(1)} %fusion.23, f32[128,2048]{0,1:T(8,128)S(1)} %collective-permute-done.6, f32[128,2048]{0,1:T(8,128)S(1)} %collective-permute-done, bf16[128,256]{1,0:T(8,128)(2,1)S(1)} %copy-done.1, bf16[8192,256]{1,0:T(8,128)(2,1)} %param.12, s32[]{:T(128)S(6)} %select_n.161), kind=kOutput, calls=%fused_computation.9 | convolution fusion | flops 135266304 | bytes 4784132 | tf_op jit(solution)/shard_map/dot_general | solution.py:71
  75.0 1.0 %copy.15 = bf16[128,2048]{1,0:T(8,128)(2,1)} copy(bf16[128,2048]{0,1:T(8,128)(2,1)S(1)} %fusion.4) | data formatting | bytes 1048576
  (44 shorter events, 6.1 us)
Async XLA Ops:
  0.6 27.0 %copy-start = (bf16[128,2048]{1,0:T(8,128)(2,1)S(1)}, bf16[128,2048]{1,0:T(8,128)(2,1)}, u32[]{:S(2)}) copy-start(bf16[128,2048]{1,0:T(8,128)(2,1)} %param.10) | copy-start | bytes 1572868
  0.6 26.9 %copy-start.1 = (bf16[128,256]{1,0:T(8,128)(2,1)S(1)}, bf16[128,256]{1,0:T(8,128)(2,1)}, u32[]{:S(2)}) copy-start(bf16[128,256]{1,0:T(8,128)(2,1)} %param.11) | copy-start | bytes 196612
  4.3 5.4 %collective-permute-start.2 = (bf16[1,16,2432]{2,1,0:T(8,128)(2,1)S(1)}, bf16[1,16,2432]{2,1,0:T(8,128)(2,1)S(1)}, u32[]{:S(2)}, u32[]{:S(2)}) collective-permute-start(bf16[1,16,2432]{2,1,0:T(8,128)(2,1)S(1)} %get-tuple-element.46), channel_id=1, source_target_pairs={{0,4},{4,0},{8,12},{12,8},{16,20},{20,16},{24,28},{28,24},{1,5},{5... | collective-permute-start | bytes 233480 | tf_op jit(solution)/shard_map/ppermute | solution.py:36
  9.0 19.0 %collective-permute-start.1 = (f32[128,2048]{0,1:T(8,128)S(1)}, f32[128,2048]{0,1:T(8,128)S(1)}, u32[]{:S(2)}, u32[]{:S(2)}) collective-permute-start(f32[128,2048]{0,1:T(8,128)S(1)} %convolution_bitcast_fusion.1), channel_id=1, source_target_pairs={{0,1},{1,0},{2,3},{3,2},{4,5},{5,4},{6,7},{7,6},{8,9},{9,8},{10,11... | collective-permute-start | bytes 3145736 | tf_op jit(solution)/shard_map/ppermute | solution.py:83
  10.6 7.9 %collective-permute-start.3 = (bf16[2,16,2432]{2,1,0:T(8,128)(2,1)S(1)}, bf16[2,16,2432]{2,1,0:T(8,128)(2,1)S(1)}, u32[]{:S(2)}, u32[]{:S(2)}) collective-permute-start(bf16[2,16,2432]{2,1,0:T(8,128)(2,1)S(1)} %pad_maximum_fusion), channel_id=1, source_target_pairs={{0,8},{4,12},{8,0},{12,4},{16,24},{20,28},{24,16},{28,20},{1,9},{5... | collective-permute-start | bytes 466952 | tf_op jit(solution)/shard_map/ppermute | solution.py:41
  12.7 14.4 %collective-permute-start.4 = (bf16[2,16,2432]{2,1,0:T(8,128)(2,1)S(1)}, bf16[2,16,2432]{2,1,0:T(8,128)(2,1)S(1)}, u32[]{:S(2)}, u32[]{:S(2)}) collective-permute-start(bf16[2,16,2432]{2,1,0:T(8,128)(2,1)S(1)} %pad_maximum_fusion), channel_id=1, source_target_pairs={{0,16},{4,20},{8,24},{12,28},{16,0},{20,4},{24,8},{28,12},{1,17},{... | collective-permute-start | bytes 466952 | tf_op jit(solution)/shard_map/ppermute | solution.py:41
  15.3 11.8 %collective-permute-start.5 = (bf16[2,16,2432]{2,1,0:T(8,128)(2,1)S(1)}, bf16[2,16,2432]{2,1,0:T(8,128)(2,1)S(1)}, u32[]{:S(2)}, u32[]{:S(2)}) collective-permute-start(bf16[2,16,2432]{2,1,0:T(8,128)(2,1)S(1)} %pad_maximum_fusion), channel_id=1, source_target_pairs={{0,24},{4,28},{8,16},{12,20},{16,8},{20,12},{24,0},{28,4},{1,25},{... | collective-permute-start | bytes 466952 | tf_op jit(solution)/shard_map/ppermute | solution.py:41
  30.6 1.2 %collective-permute-start.7 = (f32[1,128,32]{1,2,0:T(8,128)S(1)}, f32[1,128,32]{1,2,0:T(8,128)S(1)}, u32[]{:S(2)}, u32[]{:S(2)}) collective-permute-start(f32[1,128,32]{1,2,0:T(8,128)S(1)} %pad_maximum_fusion.2), channel_id=1, source_target_pairs={{0,1},{1,0},{2,3},{3,2},{4,5},{5,4},{6,7},{7,6},{8,9},{9,8},{10,11... | collective-permute-start | bytes 49160 | tf_op jit(solution)/shard_map/ppermute | solution.py:55
  31.8 3.7 %collective-permute-start.8 = (f32[1,128,32]{1,2,0:T(8,128)S(1)}, f32[1,128,32]{1,2,0:T(8,128)S(1)}, u32[]{:S(2)}, u32[]{:S(2)}) collective-permute-start(f32[1,128,32]{1,2,0:T(8,128)S(1)} %add.104), channel_id=1, source_target_pairs={{0,2},{1,3},{2,0},{3,1},{4,6},{5,7},{6,4},{7,5},{8,10},{9,11},{10,... | collective-permute-start | bytes 49160 | tf_op jit(solution)/shard_map/ppermute | solution.py:55
  37.5 11.5 %collective-permute-start.10 = (f32[1,16,2304]{2,1,0:T(8,128)}, f32[1,16,2304]{2,1,0:T(8,128)}, u32[]{:S(2)}, u32[]{:S(2)}) collective-permute-start(f32[1,16,2304]{2,1,0:T(8,128)} %get-tuple-element.44), channel_id=1, source_target_pairs={{0,8},{4,12},{8,0},{12,4},{16,24},{20,28},{24,16},{28,20},{1,9},{5... | collective-permute-start | bytes 442376 | tf_op jit(solution)/shard_map/ppermute | solution.py:177
  39.7 9.3 %collective-permute-start.11 = (f32[1,16,2304]{2,1,0:T(8,128)}, f32[1,16,2304]{2,1,0:T(8,128)}, u32[]{:S(2)}, u32[]{:S(2)}) collective-permute-start(f32[1,16,2304]{2,1,0:T(8,128)} %get-tuple-element.45), channel_id=1, source_target_pairs={{0,12},{4,8},{8,4},{12,0},{16,28},{20,24},{24,20},{28,16},{1,13},{... | collective-permute-start | bytes 442376 | tf_op jit(solution)/shard_map/ppermute | solution.py:177
  39.9 9.2 %collective-permute-start.9 = (f32[1,16,2304]{2,1,0:T(8,128)}, f32[1,16,2304]{2,1,0:T(8,128)}, u32[]{:S(2)}, u32[]{:S(2)}) collective-permute-start(f32[1,16,2304]{2,1,0:T(8,128)} %get-tuple-element.34), channel_id=1, source_target_pairs={{0,4},{4,0},{8,12},{12,8},{16,20},{20,16},{24,28},{28,24},{1,5},{5... | collective-permute-start | bytes 442376 | tf_op jit(solution)/shard_map/ppermute | solution.py:177
  42.8 16.0 %collective-permute-start = (f32[128,2048]{0,1:T(8,128)S(1)}, f32[128,2048]{0,1:T(8,128)S(1)}, u32[]{:S(2)}, u32[]{:S(2)}) collective-permute-start(f32[128,2048]{0,1:T(8,128)S(1)} %convolution_bitcast_fusion.3), channel_id=1, source_target_pairs={{0,1},{1,0},{2,3},{3,2},{4,5},{5,4},{6,7},{7,6},{8,9},{9,8},{10,11... | collective-permute-start | bytes 3145736 | tf_op jit(solution)/shard_map/ppermute | solution.py:83
  47.5 25.8 %collective-permute-start.6 = (f32[128,2048]{0,1:T(8,128)}, f32[128,2048]{0,1:T(8,128)S(1)}, u32[]{:S(2)}, u32[]{:S(2)}) collective-permute-start(f32[128,2048]{0,1:T(8,128)} %fusion.3), channel_id=1, source_target_pairs={{0,2},{1,3},{2,0},{3,1},{4,6},{5,7},{6,4},{7,5},{8,10},{9,11},{10,... | collective-permute-start | bytes 3145736 | tf_op jit(solution)/shard_map/ppermute | solution.py:83
  50.2 7.3 %collective-permute-start.12 = (bf16[1,16,2304]{2,1,0:T(8,128)(2,1)S(1)}, bf16[1,16,2304]{2,1,0:T(8,128)(2,1)S(1)}, u32[]{:S(2)}, u32[]{:S(2)}) collective-permute-start(bf16[1,16,2304]{2,1,0:T(8,128)(2,1)S(1)} %get-tuple-element.42), channel_id=1, source_target_pairs={{0,16},{4,20},{8,24},{12,28},{16,0},{20,4},{24,8},{28,12},{1,17},{... | collective-permute-start | bytes 221192 | tf_op jit(solution)/shard_map/ppermute | solution.py:181

commit v14 on v7

--- a/solution.py
+++ b/solution.py
@@ -32,7 +32,7 @@
         for shift, pairs in _partners(size):
             got.append(lax.ppermute(local, axis, pairs))
             sources.append(_source_of(me, shift, size))
-        return jnp.stack(got, 0), jnp.stack(sources)
+        return got, sources
     pair = jnp.concatenate([local, lax.ppermute(local, axis, [(i, i ^ 1) for i in range(size)])], 0)
     got = [pair]
     sources = [me, me ^ 1]
@@ -40,7 +40,11 @@
         shift = 2 * m
         got.append(lax.ppermute(pair, axis, [(i, i ^ shift) for i in range(size)]))
         sources += [me ^ shift, me ^ shift ^ 1]
-    return jnp.concatenate(got, 0), jnp.stack(sources)
+    held = local.shape[0]
+    pieces = []
+    for g in got:
+        pieces += [g[k * held:(k + 1) * held] for k in range(g.shape[0] // held)]
+    return pieces, sources
 
 
 def _psum_small(value, axis, size):
@@ -102,15 +106,14 @@
 
 
     packed = jnp.concatenate([adapter_down_weight, adapter_up_weight], axis=2)
-    stacked, order = _gather_dp(packed, "dp", dp_size)
-    stacked = stacked.reshape(dp_size, held_tenants, *packed.shape[1:])
+    pieces, sources = _gather_dp(packed, "dp", dp_size)
     owner = tenant_per_block // held_tenants
     local = tenant_per_block % held_tenants
-    pick = (order[None, :] == owner[:, None])
-    pick = pick[:, :, None] & (jnp.arange(held_tenants)[None, None, :] == local[:, None, None])
-    pick = pick.reshape(block_count, dp_size * held_tenants).astype(jnp.bfloat16)
-    flat = stacked.reshape(dp_size * held_tenants, adapter_rank_size, width_portion + key_portion)
-    selected = jnp.einsum("bk,krd->brd", pick, flat, preferred_element_type=jnp.float32).astype(jnp.bfloat16)
+    selected = jnp.zeros((block_count,) + packed.shape[1:], packed.dtype)
+    for piece, source in zip(pieces, sources):
+        for k in range(held_tenants):
+            hit = (owner == source) & (local == k)
+            selected = jnp.where(hit[:, None, None], piece[k][None], selected)
     sel_down = selected[:, :, :width_portion]
     sel_up = selected[:, :, width_portion:]
 

time: 59.2 us -> 58.7 us (level)
  waiting for transfers between devices: 18.3 us -> 17.1 us
    ppermute x3, waiting for transfers between devices: 11.3 us -> 7.98 us  [_gather_dp(): got.append(lax.ppermute(pair, axis, [(i, i ^ shift) for i in range(size)]))]
    ppermute x1, waiting for transfers between devices: 0.01 us -> 2.33 us  [_gather_dp(): lax.ppermute(local, axis, [(i, i ^ 1) for i in range(size)])]
    ppermute x3, waiting for transfers between devices: 1.14 us -> 0.22 us  [_frozen_term(): got = [lax.ppermute(held[e], axis, pairs) for e in range(1, len(held), 2)]]
    dot_general x1, matrix products: 0.13 us -> 0.97 us  [on_device(): jnp.einsum('bnk,brk->bnr', cotangent_blocks, sel_up, preferred_element_ty...]
    ppermute x7, waiting for transfers between devices: 4.32 us -> 5.1 us  [on_device(): lax.ppermute(outgoing.astype(jnp.bfloat16), 'dp', pairs).astype(jnp.float32)]
    unnamed x9 -> x6, local copies, waits for them, and re-layouts: 1.97 us -> 1.93 us
  transfers between devices with their start and end apart: 16 -> 16, of which waited for: 8 -> 9; matrix products, arithmetic and copies ran while one was open for 11% -> 12% of each run, Pallas kernels for 0% -> 0%
where the time goes in v14:
time: 58.7 us; the launch traced here: 58.4 us
  starting transfers between devices  25.6 us (44%)
  waiting for transfers between devices  17.1 us (29%)
  matrix products  9.63 us (16%)
  local copies, waits for them, and re-layouts  2.82 us (5%)
  other arithmetic  1.66 us (3%)
  between operations  1.51 us (3%)
    ppermute x7, starting transfers between devices, on_device(): lax.ppermute(outgoing.astype(jnp.bfloat16), 'dp', pairs).astype(jnp.float32)  15.1 us
    ppermute x3, waiting for transfers between devices, _gather_dp(): got.append(lax.ppermute(pair, axis, [(i, i ^ shift) for i in range(size)]))  7.98 us
    dot_general x4, matrix products, term(): lax.dot_general(cotangent, piece, (((1,), (1,)), ((), ())), preferred_ele...  7.62 us
    ppermute x7, waiting for transfers between devices, on_device(): lax.ppermute(outgoing.astype(jnp.bfloat16), 'dp', pairs).astype(jnp.float32)  5.1 us
    ppermute x3, starting transfers between devices, _gather_dp(): got.append(lax.ppermute(pair, axis, [(i, i ^ shift) for i in range(size)]))  4.74 us
    ppermute x1, starting transfers between devices, _gather_dp(): lax.ppermute(local, axis, [(i, i ^ 1) for i in range(size)])  2.97 us
    ppermute x1, waiting for transfers between devices, _gather_dp(): lax.ppermute(local, axis, [(i, i ^ 1) for i in range(size)])  2.33 us
    unnamed x6, local copies, waits for them, and re-layouts  1.93 us
  transfers between devices with their start and end apart: 16, of which 9 were waited for; matrix products, arithmetic and copies ran while one was open for 12% of the time, Pallas kernels for 0%

profile of v14, /device:TPU:0, one launch (start us, length us, event | category | flops | bytes accessed | tf_op | source)
XLA Modules:
  0.0 58.4 jit_solution(17578847600614994541)
XLA Ops:
  0.7 0.9 %constant_dynamic-update-slice_fusion.1 = bf16[1,16,2304]{2,1,0:T(8,128)(2,1)S(1)} fusion(bf16[1,16,2048]{2,1,0:T(8,128)(2,1)} %param.9), kind=kLoop, calls=%fused_computation.71 | loop fusion | bytes 131072
  2.3 3.0 %collective-permute-start.2 = (bf16[1,16,2304]{2,1,0:T(8,128)(2,1)S(1)}, bf16[1,16,2304]{2,1,0:T(8,128)(2,1)S(1)}, u32[]{:S(2)}, u32[]{:S(2)}) collective-permute-start(bf16[1,16,2304]{2,1,0:T(8,128)(2,1)S(1)} %constant_dynamic-update-slice_fusion), channel_id=1, source_target_pairs={{0,4},{4,0},{8,12},{12,8},{16,20},{20,16},{24,28},{28,24},{1,5},{5... | collective-permute-start | bytes 221192 | tf_op jit(solution)/shard_map/ppermute | solution.py:36
  5.2 2.3 %collective-permute-done.2 = bf16[1,16,2304]{2,1,0:T(8,128)(2,1)S(1)} collective-permute-done((bf16[1,16,2304]{2,1,0:T(8,128)(2,1)S(1)}, bf16[1,16,2304]{2,1,0:T(8,128)(2,1)S(1)}, u32[]{:S(2)}, u32[]{:S(2)}) %collective-permute-start.2) | collective-permute-done | bytes 73760 | tf_op jit(solution)/shard_map/ppermute | solution.py:36
  7.6 2.1 %collective-permute-start.5 = (bf16[2,16,2304]{2,1,0:T(8,128)(2,1)S(1)}, bf16[2,16,2304]{2,1,0:T(8,128)(2,1)S(1)}, u32[]{:S(2)}, u32[]{:S(2)}) collective-permute-start(bf16[2,16,2304]{2,1,0:T(8,128)(2,1)S(1)} %pad_maximum_fusion.1), channel_id=1, source_target_pairs={{0,8},{4,12},{8,0},{12,4},{16,24},{20,28},{24,16},{28,20},{1,9},{5... | collective-permute-start | bytes 442376 | tf_op jit(solution)/shard_map/ppermute | solution.py:41
  9.7 2.6 %collective-permute-start.4 = (bf16[2,16,2304]{2,1,0:T(8,128)(2,1)S(1)}, bf16[2,16,2304]{2,1,0:T(8,128)(2,1)S(1)}, u32[]{:S(2)}, u32[]{:S(2)}) collective-permute-start(bf16[2,16,2304]{2,1,0:T(8,128)(2,1)S(1)} %pad_maximum_fusion.1), channel_id=1, source_target_pairs={{0,16},{4,20},{8,24},{12,28},{16,0},{20,4},{24,8},{28,12},{1,17},{... | collective-permute-start | bytes 442376 | tf_op jit(solution)/shard_map/ppermute | solution.py:41
  12.3 1.6 %convolution_bitcast_fusion.1 = f32[128,2048]{0,1:T(8,128)S(1)} fusion(bf16[128,256]{1,0:T(8,128)(2,1)} %param.7, bf16[8192,256]{1,0:T(8,128)(2,1)} %param.8, s32[]{:T(128)S(6)} %select_n.81), kind=kOutput, calls=%fused_computation.1 | convolution fusion | flops 134217728 | bytes 2162692 | tf_op jit(solution)/shard_map/dot_general | solution.py:75
  14.7 8.0 %collective-permute-done.4 = bf16[2,16,2304]{2,1,0:T(8,128)(2,1)S(1)} collective-permute-done((bf16[2,16,2304]{2,1,0:T(8,128)(2,1)S(1)}, bf16[2,16,2304]{2,1,0:T(8,128)(2,1)S(1)}, u32[]{:S(2)}, u32[]{:S(2)}) %collective-permute-start.4) | collective-permute-done | bytes 147488 | tf_op jit(solution)/shard_map/ppermute | solution.py:41
  22.8 1.0 %fusion.6 = f32[1,128,16]{1,2,0:T(8,128)S(1)} fusion(bf16[128,256]{1,0:T(8,128)(2,1)} %param.7, bf16[1,16,2304]{2,1,0:T(8,128)(2,1)S(1)} %fusion.26), kind=kOutput, calls=%fused_computation.18 | convolution fusion | flops 1050624 | bytes 81920 | tf_op jit(solution)/shard_map/bnk,brk->bnr/dot_general | solution.py:123
  24.0 2.7 %fusion.3 = f32[128,2048]{0,1:T(8,128)} fusion(f32[128,2048]{0,1:T(8,128)S(1)} %collective-permute-done.1, bf16[128,256]{1,0:T(8,128)(2,1)} %param.7, bf16[8192,256]{1,0:T(8,128)(2,1)} %param.8, s32[]{:T(128)S(6)} %select_n.80), kind=kOutput, calls=%fused_computation.8 | convolution fusion | flops 134479872 | bytes 3211268 | tf_op jit(solution)/shard_map/dot_general | solution.py:75
  26.7 1.6 %convolution_bitcast_fusion.3 = f32[128,2048]{0,1:T(8,128)S(1)} fusion(bf16[128,256]{1,0:T(8,128)(2,1)S(1)} %copy-done.1, bf16[8192,256]{1,0:T(8,128)(2,1)} %param.8, s32[]{:T(128)S(6)} %select_n.79), kind=kOutput, calls=%fused_computation.3 | convolution fusion | flops 134217728 | bytes 2162692 | tf_op jit(solution)/shard_map/dot_general | solution.py:75
  28.9 1.5 %collective-permute-start.8 = (f32[1,128,32]{1,2,0:T(8,128)S(1)}, f32[1,128,32]{1,2,0:T(8,128)S(1)}, u32[]{:S(2)}, u32[]{:S(2)}) collective-permute-start(f32[1,128,32]{1,2,0:T(8,128)S(1)} %add.109), channel_id=1, source_target_pairs={{0,2},{1,3},{2,0},{3,1},{4,6},{5,7},{6,4},{7,5},{8,10},{9,11},{10,... | collective-permute-start | bytes 49160 | tf_op jit(solution)/shard_map/ppermute | solution.py:59
  31.2 1.5 %collective-permute-done.8 = f32[1,128,32]{1,2,0:T(8,128)S(1)} collective-permute-done((f32[1,128,32]{1,2,0:T(8,128)S(1)}, f32[1,128,32]{1,2,0:T(8,128)S(1)}, u32[]{:S(2)}, u32[]{:S(2)}) %collective-permute-start.8) | collective-permute-done | bytes 16416 | tf_op jit(solution)/shard_map/ppermute | solution.py:59
  33.4 3.5 %collective-permute-start.15 = (bf16[1,16,2304]{2,1,0:T(8,128)(2,1)S(1)}, bf16[1,16,2304]{2,1,0:T(8,128)(2,1)S(1)}, u32[]{:S(2)}, u32[]{:S(2)}) collective-permute-start(bf16[1,16,2304]{2,1,0:T(8,128)(2,1)S(1)} %fusion.27), channel_id=1, source_target_pairs={{0,28},{4,24},{8,20},{12,16},{16,12},{20,8},{24,4},{28,0},{1,29},{... | collective-permute-start | bytes 221192 | tf_op jit(solution)/shard_map/ppermute | solution.py:161
  36.9 1.4 %collective-permute-start.14 = (bf16[1,16,2304]{2,1,0:T(8,128)(2,1)S(1)}, bf16[1,16,2304]{2,1,0:T(8,128)(2,1)S(1)}, u32[]{:S(2)}, u32[]{:S(2)}) collective-permute-start(bf16[1,16,2304]{2,1,0:T(8,128)(2,1)S(1)} %get-tuple-element.11), channel_id=1, source_target_pairs={{0,24},{4,28},{8,16},{12,20},{16,8},{20,12},{24,0},{28,4},{1,25},{... | collective-permute-start | bytes 221192 | tf_op jit(solution)/shard_map/ppermute | solution.py:161
  38.3 1.3 %collective-permute-start.13 = (bf16[1,16,2304]{2,1,0:T(8,128)(2,1)S(1)}, bf16[1,16,2304]{2,1,0:T(8,128)(2,1)S(1)}, u32[]{:S(2)}, u32[]{:S(2)}) collective-permute-start(bf16[1,16,2304]{2,1,0:T(8,128)(2,1)S(1)} %get-tuple-element.12), channel_id=1, source_target_pairs={{0,20},{4,16},{8,28},{12,24},{16,4},{20,0},{24,12},{28,8},{1,21},{... | collective-permute-start | bytes 221192 | tf_op jit(solution)/shard_map/ppermute | solution.py:161
  39.6 1.6 %collective-permute-done.15 = bf16[1,16,2304]{2,1,0:T(8,128)(2,1)S(1)} collective-permute-done((bf16[1,16,2304]{2,1,0:T(8,128)(2,1)S(1)}, bf16[1,16,2304]{2,1,0:T(8,128)(2,1)S(1)}, u32[]{:S(2)}, u32[]{:S(2)}) %collective-permute-start.15) | collective-permute-done | bytes 73760 | tf_op jit(solution)/shard_map/ppermute | solution.py:161
  41.2 4.8 %collective-permute-start.12 = (bf16[1,16,2304]{2,1,0:T(8,128)(2,1)S(1)}, bf16[1,16,2304]{2,1,0:T(8,128)(2,1)S(1)}, u32[]{:S(2)}, u32[]{:S(2)}) collective-permute-start(bf16[1,16,2304]{2,1,0:T(8,128)(2,1)S(1)} %get-tuple-element.13), channel_id=1, source_target_pairs={{0,16},{4,20},{8,24},{12,28},{16,0},{20,4},{24,8},{28,12},{1,17},{... | collective-permute-start | bytes 221192 | tf_op jit(solution)/shard_map/ppermute | solution.py:161
  46.0 2.0 %collective-permute-start.11 = (bf16[1,16,2304]{2,1,0:T(8,128)(2,1)S(1)}, bf16[1,16,2304]{2,1,0:T(8,128)(2,1)S(1)}, u32[]{:S(2)}, u32[]{:S(2)}) collective-permute-start(bf16[1,16,2304]{2,1,0:T(8,128)(2,1)S(1)} %get-tuple-element.14), channel_id=1, source_target_pairs={{0,12},{4,8},{8,4},{12,0},{16,28},{20,24},{24,20},{28,16},{1,13},{... | collective-permute-start | bytes 221192 | tf_op jit(solution)/shard_map/ppermute | solution.py:161
  48.4 1.3 %collective-permute-start.10 = (bf16[1,16,2304]{2,1,0:T(8,128)(2,1)S(1)}, bf16[1,16,2304]{2,1,0:T(8,128)(2,1)S(1)}, u32[]{:S(2)}, u32[]{:S(2)}) collective-permute-start(bf16[1,16,2304]{2,1,0:T(8,128)(2,1)S(1)} %get-tuple-element.15), channel_id=1, source_target_pairs={{0,8},{4,12},{8,0},{12,4},{16,24},{20,28},{24,16},{28,20},{1,9},{5... | collective-permute-start | bytes 221192 | tf_op jit(solution)/shard_map/ppermute | solution.py:161
  49.8 0.8 %collective-permute-start.9 = (bf16[1,16,2304]{2,1,0:T(8,128)(2,1)S(1)}, bf16[1,16,2304]{2,1,0:T(8,128)(2,1)S(1)}, u32[]{:S(2)}, u32[]{:S(2)}) collective-permute-start(bf16[1,16,2304]{2,1,0:T(8,128)(2,1)S(1)} %get-tuple-element.10), channel_id=1, source_target_pairs={{0,4},{4,0},{8,12},{12,8},{16,20},{20,16},{24,28},{28,24},{1,5},{5... | collective-permute-start | bytes 221192 | tf_op jit(solution)/shard_map/ppermute | solution.py:161
  51.7 1.2 %collective-permute-done.10 = bf16[1,16,2304]{2,1,0:T(8,128)(2,1)S(1)} collective-permute-done((bf16[1,16,2304]{2,1,0:T(8,128)(2,1)S(1)}, bf16[1,16,2304]{2,1,0:T(8,128)(2,1)S(1)}, u32[]{:S(2)}, u32[]{:S(2)}) %collective-permute-start.10) | collective-permute-done | bytes 73760 | tf_op jit(solution)/shard_map/ppermute | solution.py:161
  52.9 1.2 %collective-permute-done.9 = bf16[1,16,2304]{2,1,0:T(8,128)(2,1)S(1)} collective-permute-done((bf16[1,16,2304]{2,1,0:T(8,128)(2,1)S(1)}, bf16[1,16,2304]{2,1,0:T(8,128)(2,1)S(1)}, u32[]{:S(2)}, u32[]{:S(2)}) %collective-permute-start.9) | collective-permute-done | bytes 73760 | tf_op jit(solution)/shard_map/ppermute | solution.py:161
  55.7 1.7 %fusion.4 = bf16[128,2048]{0,1:T(8,128)(2,1)S(1)} fusion(f32[128,2048]{0,1:T(8,128)S(1)} %fusion.28, f32[128,2048]{0,1:T(8,128)S(1)} %collective-permute-done.6, f32[128,2048]{0,1:T(8,128)S(1)} %collective-permute-done, bf16[128,256]{1,0:T(8,128)(2,1)S(1)} %copy-done.1, bf16[8192,256]{1,0:T(8,128)(2,1)} %param.8, s32[]{:T(128)S(6)} %select_n.78), kind=kOutput, calls=%fused_computation.9 | convolution fusion | flops 135266304 | bytes 4784132 | tf_op jit(solution)/shard_map/dot_general | solution.py:75
  57.4 1.0 %copy.16 = bf16[128,2048]{1,0:T(8,128)(2,1)} copy(bf16[128,2048]{0,1:T(8,128)(2,1)S(1)} %fusion.4) | data formatting | bytes 1048576
  (47 shorter events, 6.2 us)
Async XLA Ops:
  0.6 23.1 %copy-start = (bf16[128,2048]{1,0:T(8,128)(2,1)S(1)}, bf16[128,2048]{1,0:T(8,128)(2,1)}, u32[]{:S(2)}) copy-start(bf16[128,2048]{1,0:T(8,128)(2,1)} %param.6) | copy-start | bytes 1572868
  0.6 26.0 %copy-start.1 = (bf16[128,256]{1,0:T(8,128)(2,1)S(1)}, bf16[128,256]{1,0:T(8,128)(2,1)}, u32[]{:S(2)}) copy-start(bf16[128,256]{1,0:T(8,128)(2,1)} %param.7) | copy-start | bytes 196612
  2.3 5.3 %collective-permute-start.2 = (bf16[1,16,2304]{2,1,0:T(8,128)(2,1)S(1)}, bf16[1,16,2304]{2,1,0:T(8,128)(2,1)S(1)}, u32[]{:S(2)}, u32[]{:S(2)}) collective-permute-start(bf16[1,16,2304]{2,1,0:T(8,128)(2,1)S(1)} %constant_dynamic-update-slice_fusion), channel_id=1, source_target_pairs={{0,4},{4,0},{8,12},{12,8},{16,20},{20,16},{24,28},{28,24},{1,5},{5... | collective-permute-start | bytes 221192 | tf_op jit(solution)/shard_map/ppermute | solution.py:36
  7.6 7.2 %collective-permute-start.5 = (bf16[2,16,2304]{2,1,0:T(8,128)(2,1)S(1)}, bf16[2,16,2304]{2,1,0:T(8,128)(2,1)S(1)}, u32[]{:S(2)}, u32[]{:S(2)}) collective-permute-start(bf16[2,16,2304]{2,1,0:T(8,128)(2,1)S(1)} %pad_maximum_fusion.1), channel_id=1, source_target_pairs={{0,8},{4,12},{8,0},{12,4},{16,24},{20,28},{24,16},{28,20},{1,9},{5... | collective-permute-start | bytes 442376 | tf_op jit(solution)/shard_map/ppermute | solution.py:41
  9.7 13.0 %collective-permute-start.4 = (bf16[2,16,2304]{2,1,0:T(8,128)(2,1)S(1)}, bf16[2,16,2304]{2,1,0:T(8,128)(2,1)S(1)}, u32[]{:S(2)}, u32[]{:S(2)}) collective-permute-start(bf16[2,16,2304]{2,1,0:T(8,128)(2,1)S(1)} %pad_maximum_fusion.1), channel_id=1, source_target_pairs={{0,16},{4,20},{8,24},{12,28},{16,0},{20,4},{24,8},{28,12},{1,17},{... | collective-permute-start | bytes 442376 | tf_op jit(solution)/shard_map/ppermute | solution.py:41
  12.3 10.4 %collective-permute-start.3 = (bf16[2,16,2304]{2,1,0:T(8,128)(2,1)S(1)}, bf16[2,16,2304]{2,1,0:T(8,128)(2,1)S(1)}, u32[]{:S(2)}, u32[]{:S(2)}) collective-permute-start(bf16[2,16,2304]{2,1,0:T(8,128)(2,1)S(1)} %pad_maximum_fusion.1), channel_id=1, source_target_pairs={{0,24},{4,28},{8,16},{12,20},{16,8},{20,12},{24,0},{28,4},{1,25},{... | collective-permute-start | bytes 442376 | tf_op jit(solution)/shard_map/ppermute | solution.py:41
  14.0 10.0 %collective-permute-start.1 = (f32[128,2048]{0,1:T(8,128)S(1)}, f32[128,2048]{0,1:T(8,128)S(1)}, u32[]{:S(2)}, u32[]{:S(2)}) collective-permute-start(f32[128,2048]{0,1:T(8,128)S(1)} %convolution_bitcast_fusion.1), channel_id=1, source_target_pairs={{0,1},{1,0},{2,3},{3,2},{4,5},{5,4},{6,7},{7,6},{8,9},{9,8},{10,11... | collective-permute-start | bytes 3145736 | tf_op jit(solution)/shard_map/ppermute | solution.py:87
  26.7 2.2 %collective-permute-start.7 = (f32[1,128,32]{1,2,0:T(8,128)S(1)}, f32[1,128,32]{1,2,0:T(8,128)S(1)}, u32[]{:S(2)}, u32[]{:S(2)}) collective-permute-start(f32[1,128,32]{1,2,0:T(8,128)S(1)} %pad_maximum_fusion.2), channel_id=1, source_target_pairs={{0,1},{1,0},{2,3},{3,2},{4,5},{5,4},{6,7},{7,6},{8,9},{9,8},{10,11... | collective-permute-start | bytes 49160 | tf_op jit(solution)/shard_map/ppermute | solution.py:59
  28.3 27.1 %collective-permute-start = (f32[128,2048]{0,1:T(8,128)S(1)}, f32[128,2048]{0,1:T(8,128)S(1)}, u32[]{:S(2)}, u32[]{:S(2)}) collective-permute-start(f32[128,2048]{0,1:T(8,128)S(1)} %convolution_bitcast_fusion.3), channel_id=1, source_target_pairs={{0,1},{1,0},{2,3},{3,2},{4,5},{5,4},{6,7},{7,6},{8,9},{9,8},{10,11... | collective-permute-start | bytes 3145736 | tf_op jit(solution)/shard_map/ppermute | solution.py:87
  28.9 3.8 %collective-permute-start.8 = (f32[1,128,32]{1,2,0:T(8,128)S(1)}, f32[1,128,32]{1,2,0:T(8,128)S(1)}, u32[]{:S(2)}, u32[]{:S(2)}) collective-permute-start(f32[1,128,32]{1,2,0:T(8,128)S(1)} %add.109), channel_id=1, source_target_pairs={{0,2},{1,3},{2,0},{3,1},{4,6},{5,7},{6,4},{7,5},{8,10},{9,11},{10,... | collective-permute-start | bytes 49160 | tf_op jit(solution)/shard_map/ppermute | solution.py:59
  30.6 25.1 %collective-permute-start.6 = (f32[128,2048]{0,1:T(8,128)}, f32[128,2048]{0,1:T(8,128)S(1)}, u32[]{:S(2)}, u32[]{:S(2)}) collective-permute-start(f32[128,2048]{0,1:T(8,128)} %fusion.3), channel_id=1, source_target_pairs={{0,2},{1,3},{2,0},{3,1},{4,6},{5,7},{6,4},{7,5},{8,10},{9,11},{10,... | collective-permute-start | bytes 3145736 | tf_op jit(solution)/shard_map/ppermute | solution.py:87
  33.4 7.8 %collective-permute-start.15 = (bf16[1,16,2304]{2,1,0:T(8,128)(2,1)S(1)}, bf16[1,16,2304]{2,1,0:T(8,128)(2,1)S(1)}, u32[]{:S(2)}, u32[]{:S(2)}) collective-permute-start(bf16[1,16,2304]{2,1,0:T(8,128)(2,1)S(1)} %fusion.27), channel_id=1, source_target_pairs={{0,28},{4,24},{8,20},{12,16},{16,12},{20,8},{24,4},{28,0},{1,29},{... | collective-permute-start | bytes 221192 | tf_op jit(solution)/shard_map/ppermute | solution.py:161
  36.9 9.1 %collective-permute-start.14 = (bf16[1,16,2304]{2,1,0:T(8,128)(2,1)S(1)}, bf16[1,16,2304]{2,1,0:T(8,128)(2,1)S(1)}, u32[]{:S(2)}, u32[]{:S(2)}) collective-permute-start(bf16[1,16,2304]{2,1,0:T(8,128)(2,1)S(1)} %get-tuple-element.11), channel_id=1, source_target_pairs={{0,24},{4,28},{8,16},{12,20},{16,8},{20,12},{24,0},{28,4},{1,25},{... | collective-permute-start | bytes 221192 | tf_op jit(solution)/shard_map/ppermute | solution.py:161
  38.3 10.2 %collective-permute-start.13 = (bf16[1,16,2304]{2,1,0:T(8,128)(2,1)S(1)}, bf16[1,16,2304]{2,1,0:T(8,128)(2,1)S(1)}, u32[]{:S(2)}, u32[]{:S(2)}) collective-permute-start(bf16[1,16,2304]{2,1,0:T(8,128)(2,1)S(1)} %get-tuple-element.12), channel_id=1, source_target_pairs={{0,20},{4,16},{8,28},{12,24},{16,4},{20,0},{24,12},{28,8},{1,21},{... | collective-permute-start | bytes 221192 | tf_op jit(solution)/shard_map/ppermute | solution.py:161
  41.2 8.6 %collective-permute-start.12 = (bf16[1,16,2304]{2,1,0:T(8,128)(2,1)S(1)}, bf16[1,16,2304]{2,1,0:T(8,128)(2,1)S(1)}, u32[]{:S(2)}, u32[]{:S(2)}) collective-permute-start(bf16[1,16,2304]{2,1,0:T(8,128)(2,1)S(1)} %get-tuple-element.13), channel_id=1, source_target_pairs={{0,16},{4,20},{8,24},{12,28},{16,0},{20,4},{24,8},{28,12},{1,17},{... | collective-permute-start | bytes 221192 | tf_op jit(solution)/shard_map/ppermute | solution.py:161
  46.0 5.7 %collective-permute-start.11 = (bf16[1,16,2304]{2,1,0:T(8,128)(2,1)S(1)}, bf16[1,16,2304]{2,1,0:T(8,128)(2,1)S(1)}, u32[]{:S(2)}, u32[]{:S(2)}) collective-permute-start(bf16[1,16,2304]{2,1,0:T(8,128)(2,1)S(1)} %get-tuple-element.14), channel_id=1, source_target_pairs={{0,12},{4,8},{8,4},{12,0},{16,28},{20,24},{24,20},{28,16},{1,13},{... | collective-permute-start | bytes 221192 | tf_op jit(solution)/shard_map/ppermute | solution.py:161
  48.4 4.4 %collective-permute-start.10 = (bf16[1,16,2304]{2,1,0:T(8,128)(2,1)S(1)}, bf16[1,16,2304]{2,1,0:T(8,128)(2,1)S(1)}, u32[]{:S(2)}, u32[]{:S(2)}) collective-permute-start(bf16[1,16,2304]{2,1,0:T(8,128)(2,1)S(1)} %get-tuple-element.15), channel_id=1, source_target_pairs={{0,8},{4,12},{8,0},{12,4},{16,24},{20,28},{24,16},{28,20},{1,9},{5... | collective-permute-start | bytes 221192 | tf_op jit(solution)/shard_map/ppermute | solution.py:161
  49.8 4.4 %collective-permute-start.9 = (bf16[1,16,2304]{2,1,0:T(8,128)(2,1)S(1)}, bf16[1,16,2304]{2,1,0:T(8,128)(2,1)S(1)}, u32[]{:S(2)}, u32[]{:S(2)}) collective-permute-start(bf16[1,16,2304]{2,1,0:T(8,128)(2,1)S(1)} %get-tuple-element.10), channel_id=1, source_target_pairs={{0,4},{4,0},{8,12},{12,8},{16,20},{20,16},{24,28},{28,24},{1,5},{5... | collective-permute-start | bytes 221192 | tf_op jit(solution)/shard_map/ppermute | solution.py:161

commit v15 on v14

--- a/solution.py
+++ b/solution.py
@@ -114,6 +114,7 @@
         for k in range(held_tenants):
             hit = (owner == source) & (local == k)
             selected = jnp.where(hit[:, None, None], piece[k][None], selected)
+    base_grad, selected = _frozen_term(cotangent, frozen_key_weight, "tensor", tensor_size, selected)
     sel_down = selected[:, :, :width_portion]
     sel_up = selected[:, :, width_portion:]
 
@@ -124,7 +125,6 @@
         "bnk,brk->bnr", cotangent_blocks, sel_up, preferred_element_type=jnp.float32
     )
     lows = jnp.concatenate([low_in, reduced_output], axis=2)
-    base_grad, lows = _frozen_term(cotangent, frozen_key_weight, "tensor", tensor_size, lows)
     lows = _psum_small(lows, "tensor", tensor_size)
     reduced_input_batch = lows[:, :, :adapter_rank_size].astype(jnp.bfloat16)
     low_out_b = lows[:, :, adapter_rank_size:].astype(jnp.bfloat16)

time: 58.7 us -> 58.6 us (level)
  waiting for transfers between devices: 17.1 us -> 18.9 us
  starting transfers between devices: 25.6 us -> 24.7 us
  matrix products: 9.63 us -> 8.79 us
    ppermute x3, waiting for transfers between devices: 7.98 us -> 10.4 us  [_gather_dp(): got.append(lax.ppermute(pair, axis, [(i, i ^ shift) for i in range(size)]))]
    ppermute x1, waiting for transfers between devices: 2.33 us -> 0.6 us  [_gather_dp(): lax.ppermute(local, axis, [(i, i ^ 1) for i in range(size)])]
    ppermute x3, waiting for transfers between devices: 0.22 us -> 1.39 us  [_frozen_term(): got = [lax.ppermute(held[e], axis, pairs) for e in range(1, len(held), 2)]]
    ppermute x7, starting transfers between devices: 15.1 us -> 14.2 us  [on_device(): lax.ppermute(outgoing.astype(jnp.bfloat16), 'dp', pairs).astype(jnp.float32)]
    dot_general x1, matrix products: 0.97 us -> 0.13 us  [on_device(): jnp.einsum('bnk,brk->bnr', cotangent_blocks, sel_up, preferred_element_ty...]
  transfers between devices with their start and end apart: 16 -> 16, of which waited for: 9 -> 11; matrix products, arithmetic and copies ran while one was open for 12% -> 10% of each run, Pallas kernels for 0% -> 0%
where the time goes in v15:
time: 58.6 us; the launch traced here: 58.3 us
  starting transfers between devices  24.7 us (42%)
  waiting for transfers between devices  18.9 us (32%)
  matrix products  8.79 us (15%)
  local copies, waits for them, and re-layouts  2.84 us (5%)
  other arithmetic  1.65 us (3%)
  between operations  1.5 us (3%)
    ppermute x7, starting transfers between devices, on_device(): lax.ppermute(outgoing.astype(jnp.bfloat16), 'dp', pairs).astype(jnp.float32)  14.2 us
    ppermute x3, waiting for transfers between devices, _gather_dp(): got.append(lax.ppermute(pair, axis, [(i, i ^ shift) for i in range(size)]))  10.4 us
    dot_general x4, matrix products, term(): lax.dot_general(cotangent, piece, (((1,), (1,)), ((), ())), preferred_ele...  7.62 us
    ppermute x7, waiting for transfers between devices, on_device(): lax.ppermute(outgoing.astype(jnp.bfloat16), 'dp', pairs).astype(jnp.float32)  4.92 us
    ppermute x3, starting transfers between devices, _gather_dp(): got.append(lax.ppermute(pair, axis, [(i, i ^ shift) for i in range(size)]))  4.74 us
    ppermute x1, starting transfers between devices, _gather_dp(): lax.ppermute(local, axis, [(i, i ^ 1) for i in range(size)])  2.97 us
    unnamed x6, local copies, waits for them, and re-layouts  1.94 us
    ppermute x2, waiting for transfers between devices, _psum_small(): lax.ppermute(total, axis, [(i, i ^ step) for i in range(size)])  1.5 us
  transfers between devices with their start and end apart: 16, of which 11 were waited for; matrix products, arithmetic and copies ran while one was open for 10% of the time, Pallas kernels for 0%

profile of v15, /device:TPU:0, one launch (start us, length us, event | category | flops | bytes accessed | tf_op | source)
XLA Modules:
  0.0 58.3 jit_solution(10289653849645360603)
XLA Ops:
  0.7 0.9 %constant_dynamic-update-slice_fusion.1 = bf16[1,16,2304]{2,1,0:T(8,128)(2,1)S(1)} fusion(bf16[1,16,2048]{2,1,0:T(8,128)(2,1)} %param.9), kind=kLoop, calls=%fused_computation.75 | loop fusion | bytes 131072
  2.3 3.0 %collective-permute-start.2 = (bf16[1,16,2304]{2,1,0:T(8,128)(2,1)S(1)}, bf16[1,16,2304]{2,1,0:T(8,128)(2,1)S(1)}, u32[]{:S(2)}, u32[]{:S(2)}) collective-permute-start(bf16[1,16,2304]{2,1,0:T(8,128)(2,1)S(1)} %constant_dynamic-update-slice_fusion), channel_id=1, source_target_pairs={{0,4},{4,0},{8,12},{12,8},{16,20},{20,16},{24,28},{28,24},{1,5},{5... | collective-permute-start | bytes 221192 | tf_op jit(solution)/shard_map/ppermute | solution.py:36
  5.2 1.6 %convolution_bitcast_fusion.1 = f32[128,2048]{0,1:T(8,128)S(1)} fusion(bf16[128,256]{1,0:T(8,128)(2,1)} %param.7, bf16[8192,256]{1,0:T(8,128)(2,1)} %param.8, s32[]{:T(128)S(6)} %select_n.81), kind=kOutput, calls=%fused_computation.1 | convolution fusion | flops 134217728 | bytes 2162692 | tf_op jit(solution)/shard_map/dot_general | solution.py:75
  7.6 2.1 %collective-permute-start.5 = (bf16[2,16,2304]{2,1,0:T(8,128)(2,1)S(1)}, bf16[2,16,2304]{2,1,0:T(8,128)(2,1)S(1)}, u32[]{:S(2)}, u32[]{:S(2)}) collective-permute-start(bf16[2,16,2304]{2,1,0:T(8,128)(2,1)S(1)} %pad_maximum_fusion.1), channel_id=1, source_target_pairs={{0,8},{4,12},{8,0},{12,4},{16,24},{20,28},{24,16},{28,20},{1,9},{5... | collective-permute-start | bytes 442376 | tf_op jit(solution)/shard_map/ppermute | solution.py:41
  9.7 2.6 %collective-permute-start.4 = (bf16[2,16,2304]{2,1,0:T(8,128)(2,1)S(1)}, bf16[2,16,2304]{2,1,0:T(8,128)(2,1)S(1)}, u32[]{:S(2)}, u32[]{:S(2)}) collective-permute-start(bf16[2,16,2304]{2,1,0:T(8,128)(2,1)S(1)} %pad_maximum_fusion.1), channel_id=1, source_target_pairs={{0,16},{4,20},{8,24},{12,28},{16,0},{20,4},{24,8},{28,12},{1,17},{... | collective-permute-start | bytes 442376 | tf_op jit(solution)/shard_map/ppermute | solution.py:41
  13.0 2.1 %collective-permute-done.5 = bf16[2,16,2304]{2,1,0:T(8,128)(2,1)S(1)} collective-permute-done((bf16[2,16,2304]{2,1,0:T(8,128)(2,1)S(1)}, bf16[2,16,2304]{2,1,0:T(8,128)(2,1)S(1)}, u32[]{:S(2)}, u32[]{:S(2)}) %collective-permute-start.5) | collective-permute-done | bytes 147488 | tf_op jit(solution)/shard_map/ppermute | solution.py:41
  15.1 8.4 %collective-permute-done.4 = bf16[2,16,2304]{2,1,0:T(8,128)(2,1)S(1)} collective-permute-done((bf16[2,16,2304]{2,1,0:T(8,128)(2,1)S(1)}, bf16[2,16,2304]{2,1,0:T(8,128)(2,1)S(1)}, u32[]{:S(2)}, u32[]{:S(2)}) %collective-permute-start.4) | collective-permute-done | bytes 147488 | tf_op jit(solution)/shard_map/ppermute | solution.py:41
  23.5 2.7 %fusion.3 = f32[128,2048]{0,1:T(8,128)} fusion(f32[128,2048]{0,1:T(8,128)S(1)} %collective-permute-done.1, bf16[128,256]{1,0:T(8,128)(2,1)} %param.7, bf16[8192,256]{1,0:T(8,128)(2,1)} %param.8, s32[]{:T(128)S(6)} %select_n.80), kind=kOutput, calls=%fused_computation.8 | convolution fusion | flops 134479872 | bytes 3211268 | tf_op jit(solution)/shard_map/dot_general | solution.py:75
  26.6 1.7 %convolution_bitcast_fusion.3 = f32[128,2048]{0,1:T(8,128)S(1)} fusion(bf16[128,256]{1,0:T(8,128)(2,1)S(1)} %copy-done.1, bf16[8192,256]{1,0:T(8,128)(2,1)} %param.8, s32[]{:T(128)S(6)} %select_n.79), kind=kOutput, calls=%fused_computation.3 | convolution fusion | flops 134217728 | bytes 2162692 | tf_op jit(solution)/shard_map/dot_general | solution.py:75
  28.8 1.5 %collective-permute-start.8 = (f32[1,128,32]{1,2,0:T(8,128)S(1)}, f32[1,128,32]{1,2,0:T(8,128)S(1)}, u32[]{:S(2)}, u32[]{:S(2)}) collective-permute-start(f32[1,128,32]{1,2,0:T(8,128)S(1)} %fusion.39), channel_id=1, source_target_pairs={{0,2},{1,3},{2,0},{3,1},{4,6},{5,7},{6,4},{7,5},{8,10},{9,11},{10,... | collective-permute-start | bytes 49160 | tf_op jit(solution)/shard_map/ppermute | solution.py:59
  31.1 1.5 %collective-permute-done.8 = f32[1,128,32]{1,2,0:T(8,128)S(1)} collective-permute-done((f32[1,128,32]{1,2,0:T(8,128)S(1)}, f32[1,128,32]{1,2,0:T(8,128)S(1)}, u32[]{:S(2)}, u32[]{:S(2)}) %collective-permute-start.8) | collective-permute-done | bytes 16416 | tf_op jit(solution)/shard_map/ppermute | solution.py:59
  33.2 2.8 %collective-permute-start.15 = (bf16[1,16,2304]{2,1,0:T(8,128)(2,1)S(1)}, bf16[1,16,2304]{2,1,0:T(8,128)(2,1)S(1)}, u32[]{:S(2)}, u32[]{:S(2)}) collective-permute-start(bf16[1,16,2304]{2,1,0:T(8,128)(2,1)S(1)} %fusion.27), channel_id=1, source_target_pairs={{0,28},{4,24},{8,20},{12,16},{16,12},{20,8},{24,4},{28,0},{1,29},{... | collective-permute-start | bytes 221192 | tf_op jit(solution)/shard_map/ppermute | solution.py:161
  36.0 1.4 %collective-permute-start.14 = (bf16[1,16,2304]{2,1,0:T(8,128)(2,1)S(1)}, bf16[1,16,2304]{2,1,0:T(8,128)(2,1)S(1)}, u32[]{:S(2)}, u32[]{:S(2)}) collective-permute-start(bf16[1,16,2304]{2,1,0:T(8,128)(2,1)S(1)} %get-tuple-element.11), channel_id=1, source_target_pairs={{0,24},{4,28},{8,16},{12,20},{16,8},{20,12},{24,0},{28,4},{1,25},{... | collective-permute-start | bytes 221192 | tf_op jit(solution)/shard_map/ppermute | solution.py:161
  37.4 2.1 %collective-permute-start.13 = (bf16[1,16,2304]{2,1,0:T(8,128)(2,1)S(1)}, bf16[1,16,2304]{2,1,0:T(8,128)(2,1)S(1)}, u32[]{:S(2)}, u32[]{:S(2)}) collective-permute-start(bf16[1,16,2304]{2,1,0:T(8,128)(2,1)S(1)} %get-tuple-element.12), channel_id=1, source_target_pairs={{0,20},{4,16},{8,28},{12,24},{16,4},{20,0},{24,12},{28,8},{1,21},{... | collective-permute-start | bytes 221192 | tf_op jit(solution)/shard_map/ppermute | solution.py:161
  39.4 1.6 %collective-permute-done.15 = bf16[1,16,2304]{2,1,0:T(8,128)(2,1)S(1)} collective-permute-done((bf16[1,16,2304]{2,1,0:T(8,128)(2,1)S(1)}, bf16[1,16,2304]{2,1,0:T(8,128)(2,1)S(1)}, u32[]{:S(2)}, u32[]{:S(2)}) %collective-permute-start.15) | collective-permute-done | bytes 73760 | tf_op jit(solution)/shard_map/ppermute | solution.py:161
  41.1 4.8 %collective-permute-start.12 = (bf16[1,16,2304]{2,1,0:T(8,128)(2,1)S(1)}, bf16[1,16,2304]{2,1,0:T(8,128)(2,1)S(1)}, u32[]{:S(2)}, u32[]{:S(2)}) collective-permute-start(bf16[1,16,2304]{2,1,0:T(8,128)(2,1)S(1)} %get-tuple-element.13), channel_id=1, source_target_pairs={{0,16},{4,20},{8,24},{12,28},{16,0},{20,4},{24,8},{28,12},{1,17},{... | collective-permute-start | bytes 221192 | tf_op jit(solution)/shard_map/ppermute | solution.py:161
  45.9 2.0 %collective-permute-start.11 = (bf16[1,16,2304]{2,1,0:T(8,128)(2,1)S(1)}, bf16[1,16,2304]{2,1,0:T(8,128)(2,1)S(1)}, u32[]{:S(2)}, u32[]{:S(2)}) collective-permute-start(bf16[1,16,2304]{2,1,0:T(8,128)(2,1)S(1)} %get-tuple-element.14), channel_id=1, source_target_pairs={{0,12},{4,8},{8,4},{12,0},{16,28},{20,24},{24,20},{28,16},{1,13},{... | collective-permute-start | bytes 221192 | tf_op jit(solution)/shard_map/ppermute | solution.py:161
  48.5 1.3 %collective-permute-start.9 = (bf16[1,16,2304]{2,1,0:T(8,128)(2,1)S(1)}, bf16[1,16,2304]{2,1,0:T(8,128)(2,1)S(1)}, u32[]{:S(2)}, u32[]{:S(2)}) collective-permute-start(bf16[1,16,2304]{2,1,0:T(8,128)(2,1)S(1)} %get-tuple-element.10), channel_id=1, source_target_pairs={{0,4},{4,0},{8,12},{12,8},{16,20},{20,16},{24,28},{28,24},{1,5},{5... | collective-permute-start | bytes 221192 | tf_op jit(solution)/shard_map/ppermute | solution.py:161
  50.2 1.2 %collective-permute-done.11 = bf16[1,16,2304]{2,1,0:T(8,128)(2,1)S(1)} collective-permute-done((bf16[1,16,2304]{2,1,0:T(8,128)(2,1)S(1)}, bf16[1,16,2304]{2,1,0:T(8,128)(2,1)S(1)}, u32[]{:S(2)}, u32[]{:S(2)}) %collective-permute-start.11) | collective-permute-done | bytes 73760 | tf_op jit(solution)/shard_map/ppermute | solution.py:161
  51.5 1.3 %collective-permute-done.10 = bf16[1,16,2304]{2,1,0:T(8,128)(2,1)S(1)} collective-permute-done((bf16[1,16,2304]{2,1,0:T(8,128)(2,1)S(1)}, bf16[1,16,2304]{2,1,0:T(8,128)(2,1)S(1)}, u32[]{:S(2)}, u32[]{:S(2)}) %collective-permute-start.10) | collective-permute-done | bytes 73760 | tf_op jit(solution)/shard_map/ppermute | solution.py:161
  53.5 0.7 %slice_add_fusion = f32[1,16,2048]{2,1,0:T(8,128)} fusion(f32[1,16,2304]{2,1,0:T(8,128)S(1)} %convert_element_type.155, f32[1,16,2304]{2,1,0:T(8,128)S(1)} %convert_element_type.152, f32[1,16,2304]{2,1,0:T(8,128)S(1)} %convert_element_type.149, f32[1,16,2304]{2,1,0:T(8,128)S(1)} %convert_element_type.146, f32[1,16,2304]{2,1,0:T(8,128)S(1)} %convert_element_type.143, ...), kind=kLoop, calls=%fused_computation.36 | loop fusion | flops 229376 | bytes 1179648 | tf_op jit(solution)/shard_map/add | solution.py:162
  54.2 1.4 %collective-permute-done.6 = f32[128,2048]{0,1:T(8,128)S(1)} collective-permute-done((f32[128,2048]{0,1:T(8,128)}, f32[128,2048]{0,1:T(8,128)S(1)}, u32[]{:S(2)}, u32[]{:S(2)}) %collective-permute-start.6) | collective-permute-done | bytes 1048608 | tf_op jit(solution)/shard_map/ppermute | solution.py:87
  55.6 1.7 %fusion.4 = bf16[128,2048]{0,1:T(8,128)(2,1)S(1)} fusion(f32[128,2048]{0,1:T(8,128)S(1)} %fusion.28, f32[128,2048]{0,1:T(8,128)S(1)} %collective-permute-done.6, f32[128,2048]{0,1:T(8,128)S(1)} %collective-permute-done, bf16[128,256]{1,0:T(8,128)(2,1)S(1)} %copy-done.1, bf16[8192,256]{1,0:T(8,128)(2,1)} %param.8, s32[]{:T(128)S(6)} %select_n.78), kind=kOutput, calls=%fused_computation.9 | convolution fusion | flops 135266304 | bytes 4784132 | tf_op jit(solution)/shard_map/dot_general | solution.py:75
  57.3 1.0 %copy.16 = bf16[128,2048]{1,0:T(8,128)(2,1)} copy(bf16[128,2048]{0,1:T(8,128)(2,1)S(1)} %fusion.4) | data formatting | bytes 1048576
  (47 shorter events, 5.6 us)
Async XLA Ops:
  0.6 25.7 %copy-start = (bf16[128,2048]{1,0:T(8,128)(2,1)S(1)}, bf16[128,2048]{1,0:T(8,128)(2,1)}, u32[]{:S(2)}) copy-start(bf16[128,2048]{1,0:T(8,128)(2,1)} %param.6) | copy-start | bytes 1572868
  0.6 25.5 %copy-start.1 = (bf16[128,256]{1,0:T(8,128)(2,1)S(1)}, bf16[128,256]{1,0:T(8,128)(2,1)}, u32[]{:S(2)}) copy-start(bf16[128,256]{1,0:T(8,128)(2,1)} %param.7) | copy-start | bytes 196612
  2.3 5.3 %collective-permute-start.2 = (bf16[1,16,2304]{2,1,0:T(8,128)(2,1)S(1)}, bf16[1,16,2304]{2,1,0:T(8,128)(2,1)S(1)}, u32[]{:S(2)}, u32[]{:S(2)}) collective-permute-start(bf16[1,16,2304]{2,1,0:T(8,128)(2,1)S(1)} %constant_dynamic-update-slice_fusion), channel_id=1, source_target_pairs={{0,4},{4,0},{8,12},{12,8},{16,20},{20,16},{24,28},{28,24},{1,5},{5... | collective-permute-start | bytes 221192 | tf_op jit(solution)/shard_map/ppermute | solution.py:36
  6.9 16.6 %collective-permute-start.1 = (f32[128,2048]{0,1:T(8,128)S(1)}, f32[128,2048]{0,1:T(8,128)S(1)}, u32[]{:S(2)}, u32[]{:S(2)}) collective-permute-start(f32[128,2048]{0,1:T(8,128)S(1)} %convolution_bitcast_fusion.1), channel_id=1, source_target_pairs={{0,1},{1,0},{2,3},{3,2},{4,5},{5,4},{6,7},{7,6},{8,9},{9,8},{10,11... | collective-permute-start | bytes 3145736 | tf_op jit(solution)/shard_map/ppermute | solution.py:87
  7.6 7.5 %collective-permute-start.5 = (bf16[2,16,2304]{2,1,0:T(8,128)(2,1)S(1)}, bf16[2,16,2304]{2,1,0:T(8,128)(2,1)S(1)}, u32[]{:S(2)}, u32[]{:S(2)}) collective-permute-start(bf16[2,16,2304]{2,1,0:T(8,128)(2,1)S(1)} %pad_maximum_fusion.1), channel_id=1, source_target_pairs={{0,8},{4,12},{8,0},{12,4},{16,24},{20,28},{24,16},{28,20},{1,9},{5... | collective-permute-start | bytes 442376 | tf_op jit(solution)/shard_map/ppermute | solution.py:41
  9.7 13.7 %collective-permute-start.4 = (bf16[2,16,2304]{2,1,0:T(8,128)(2,1)S(1)}, bf16[2,16,2304]{2,1,0:T(8,128)(2,1)S(1)}, u32[]{:S(2)}, u32[]{:S(2)}) collective-permute-start(bf16[2,16,2304]{2,1,0:T(8,128)(2,1)S(1)} %pad_maximum_fusion.1), channel_id=1, source_target_pairs={{0,16},{4,20},{8,24},{12,28},{16,0},{20,4},{24,8},{28,12},{1,17},{... | collective-permute-start | bytes 442376 | tf_op jit(solution)/shard_map/ppermute | solution.py:41
  12.3 11.1 %collective-permute-start.3 = (bf16[2,16,2304]{2,1,0:T(8,128)(2,1)S(1)}, bf16[2,16,2304]{2,1,0:T(8,128)(2,1)S(1)}, u32[]{:S(2)}, u32[]{:S(2)}) collective-permute-start(bf16[2,16,2304]{2,1,0:T(8,128)(2,1)S(1)} %pad_maximum_fusion.1), channel_id=1, source_target_pairs={{0,24},{4,28},{8,16},{12,20},{16,8},{20,12},{24,0},{28,4},{1,25},{... | collective-permute-start | bytes 442376 | tf_op jit(solution)/shard_map/ppermute | solution.py:41
  26.6 2.2 %collective-permute-start.7 = (f32[1,128,32]{1,2,0:T(8,128)S(1)}, f32[1,128,32]{1,2,0:T(8,128)S(1)}, u32[]{:S(2)}, u32[]{:S(2)}) collective-permute-start(f32[1,128,32]{1,2,0:T(8,128)S(1)} %pad_maximum_fusion.2), channel_id=1, source_target_pairs={{0,1},{1,0},{2,3},{3,2},{4,5},{5,4},{6,7},{7,6},{8,9},{9,8},{10,11... | collective-permute-start | bytes 49160 | tf_op jit(solution)/shard_map/ppermute | solution.py:59
  28.2 26.0 %collective-permute-start = (f32[128,2048]{0,1:T(8,128)S(1)}, f32[128,2048]{0,1:T(8,128)S(1)}, u32[]{:S(2)}, u32[]{:S(2)}) collective-permute-start(f32[128,2048]{0,1:T(8,128)S(1)} %convolution_bitcast_fusion.3), channel_id=1, source_target_pairs={{0,1},{1,0},{2,3},{3,2},{4,5},{5,4},{6,7},{7,6},{8,9},{9,8},{10,11... | collective-permute-start | bytes 3145736 | tf_op jit(solution)/shard_map/ppermute | solution.py:87
  28.8 3.7 %collective-permute-start.8 = (f32[1,128,32]{1,2,0:T(8,128)S(1)}, f32[1,128,32]{1,2,0:T(8,128)S(1)}, u32[]{:S(2)}, u32[]{:S(2)}) collective-permute-start(f32[1,128,32]{1,2,0:T(8,128)S(1)} %fusion.39), channel_id=1, source_target_pairs={{0,2},{1,3},{2,0},{3,1},{4,6},{5,7},{6,4},{7,5},{8,10},{9,11},{10,... | collective-permute-start | bytes 49160 | tf_op jit(solution)/shard_map/ppermute | solution.py:59
  30.5 25.1 %collective-permute-start.6 = (f32[128,2048]{0,1:T(8,128)}, f32[128,2048]{0,1:T(8,128)S(1)}, u32[]{:S(2)}, u32[]{:S(2)}) collective-permute-start(f32[128,2048]{0,1:T(8,128)} %fusion.3), channel_id=1, source_target_pairs={{0,2},{1,3},{2,0},{3,1},{4,6},{5,7},{6,4},{7,5},{8,10},{9,11},{10,... | collective-permute-start | bytes 3145736 | tf_op jit(solution)/shard_map/ppermute | solution.py:87
  33.2 7.9 %collective-permute-start.15 = (bf16[1,16,2304]{2,1,0:T(8,128)(2,1)S(1)}, bf16[1,16,2304]{2,1,0:T(8,128)(2,1)S(1)}, u32[]{:S(2)}, u32[]{:S(2)}) collective-permute-start(bf16[1,16,2304]{2,1,0:T(8,128)(2,1)S(1)} %fusion.27), channel_id=1, source_target_pairs={{0,28},{4,24},{8,20},{12,16},{16,12},{20,8},{24,4},{28,0},{1,29},{... | collective-permute-start | bytes 221192 | tf_op jit(solution)/shard_map/ppermute | solution.py:161
  36.0 9.8 %collective-permute-start.14 = (bf16[1,16,2304]{2,1,0:T(8,128)(2,1)S(1)}, bf16[1,16,2304]{2,1,0:T(8,128)(2,1)S(1)}, u32[]{:S(2)}, u32[]{:S(2)}) collective-permute-start(bf16[1,16,2304]{2,1,0:T(8,128)(2,1)S(1)} %get-tuple-element.11), channel_id=1, source_target_pairs={{0,24},{4,28},{8,16},{12,20},{16,8},{20,12},{24,0},{28,4},{1,25},{... | collective-permute-start | bytes 221192 | tf_op jit(solution)/shard_map/ppermute | solution.py:161
  37.4 11.1 %collective-permute-start.13 = (bf16[1,16,2304]{2,1,0:T(8,128)(2,1)S(1)}, bf16[1,16,2304]{2,1,0:T(8,128)(2,1)S(1)}, u32[]{:S(2)}, u32[]{:S(2)}) collective-permute-start(bf16[1,16,2304]{2,1,0:T(8,128)(2,1)S(1)} %get-tuple-element.12), channel_id=1, source_target_pairs={{0,20},{4,16},{8,28},{12,24},{16,4},{20,0},{24,12},{28,8},{1,21},{... | collective-permute-start | bytes 221192 | tf_op jit(solution)/shard_map/ppermute | solution.py:161
  41.1 7.5 %collective-permute-start.12 = (bf16[1,16,2304]{2,1,0:T(8,128)(2,1)S(1)}, bf16[1,16,2304]{2,1,0:T(8,128)(2,1)S(1)}, u32[]{:S(2)}, u32[]{:S(2)}) collective-permute-start(bf16[1,16,2304]{2,1,0:T(8,128)(2,1)S(1)} %get-tuple-element.13), channel_id=1, source_target_pairs={{0,16},{4,20},{8,24},{12,28},{16,0},{20,4},{24,8},{28,12},{1,17},{... | collective-permute-start | bytes 221192 | tf_op jit(solution)/shard_map/ppermute | solution.py:161
  45.9 5.6 %collective-permute-start.11 = (bf16[1,16,2304]{2,1,0:T(8,128)(2,1)S(1)}, bf16[1,16,2304]{2,1,0:T(8,128)(2,1)S(1)}, u32[]{:S(2)}, u32[]{:S(2)}) collective-permute-start(bf16[1,16,2304]{2,1,0:T(8,128)(2,1)S(1)} %get-tuple-element.14), channel_id=1, source_target_pairs={{0,12},{4,8},{8,4},{12,0},{16,28},{20,24},{24,20},{28,16},{1,13},{... | collective-permute-start | bytes 221192 | tf_op jit(solution)/shard_map/ppermute | solution.py:161
  48.4 4.4 %collective-permute-start.10 = (bf16[1,16,2304]{2,1,0:T(8,128)(2,1)S(1)}, bf16[1,16,2304]{2,1,0:T(8,128)(2,1)S(1)}, u32[]{:S(2)}, u32[]{:S(2)}) collective-permute-start(bf16[1,16,2304]{2,1,0:T(8,128)(2,1)S(1)} %get-tuple-element.15), channel_id=1, source_target_pairs={{0,8},{4,12},{8,0},{12,4},{16,24},{20,28},{24,16},{28,20},{1,9},{5... | collective-permute-start | bytes 221192 | tf_op jit(solution)/shard_map/ppermute | solution.py:161
  48.5 4.4 %collective-permute-start.9 = (bf16[1,16,2304]{2,1,0:T(8,128)(2,1)S(1)}, bf16[1,16,2304]{2,1,0:T(8,128)(2,1)S(1)}, u32[]{:S(2)}, u32[]{:S(2)}) collective-permute-start(bf16[1,16,2304]{2,1,0:T(8,128)(2,1)S(1)} %get-tuple-element.10), channel_id=1, source_target_pairs={{0,4},{4,0},{8,12},{12,8},{16,20},{20,16},{24,28},{28,24},{1,5},{5... | collective-permute-start | bytes 221192 | tf_op jit(solution)/shard_map/ppermute | solution.py:161

commit v16 on v14

--- a/solution.py
+++ b/solution.py
@@ -33,13 +33,13 @@
             got.append(lax.ppermute(local, axis, pairs))
             sources.append(_source_of(me, shift, size))
         return got, sources
-    pair = jnp.concatenate([local, lax.ppermute(local, axis, [(i, i ^ 1) for i in range(size)])], 0)
+    half = size // 2
+    pair = jnp.concatenate([local, lax.ppermute(local, axis, [(i, i ^ half) for i in range(size)])], 0)
     got = [pair]
-    sources = [me, me ^ 1]
-    for m in range(1, size // 2):
-        shift = 2 * m
+    sources = [me, me ^ half]
+    for shift in range(1, half):
         got.append(lax.ppermute(pair, axis, [(i, i ^ shift) for i in range(size)]))
-        sources += [me ^ shift, me ^ shift ^ 1]
+        sources += [me ^ shift, me ^ shift ^ half]
     held = local.shape[0]
     pieces = []
     for g in got:

time: 58.7 us -> 56.7 us (0.966)
  waiting for transfers between devices: 17.1 us -> 14.2 us
  starting transfers between devices: 25.6 us -> 26.5 us
    ppermute x3, waiting for transfers between devices: 7.98 us -> 3.71 us  [_gather_dp(): got.append(lax.ppermute(pair, axis, [(i, i ^ shift) for i in range(size)]))]
    ppermute x1, waiting for transfers between devices: 2.33 us -> 3.91 us  [_gather_dp(): lax.ppermute(local, axis, [(i, i ^ half) for i in range(size)])]
    ppermute x3, starting transfers between devices: 4.74 us -> 3.55 us  [_gather_dp(): got.append(lax.ppermute(pair, axis, [(i, i ^ shift) for i in range(size)]))]
    ppermute x1, starting transfers between devices: 2.97 us -> 4.04 us  [_gather_dp(): lax.ppermute(local, axis, [(i, i ^ half) for i in range(size)])]
    ppermute x7, starting transfers between devices: 15.1 us -> 16.1 us  [on_device(): lax.ppermute(outgoing.astype(jnp.bfloat16), 'dp', pairs).astype(jnp.float32)]
  transfers between devices with their start and end apart: 16 -> 16, of which waited for: 9 -> 10; matrix products, arithmetic and copies ran while one was open for 12% -> 13% of each run, Pallas kernels for 0% -> 0%
where the time goes in v16:
time: 56.7 us; the launch traced here: 56.3 us
  starting transfers between devices  26.5 us (47%)
  waiting for transfers between devices  14.2 us (25%)
  matrix products  9.65 us (17%)
  local copies, waits for them, and re-layouts  2.82 us (5%)
  other arithmetic  1.66 us (3%)
  between operations  1.52 us (3%)
    ppermute x7, starting transfers between devices, on_device(): lax.ppermute(outgoing.astype(jnp.bfloat16), 'dp', pairs).astype(jnp.float32)  16.1 us
    dot_general x4, matrix products, term(): lax.dot_general(cotangent, piece, (((1,), (1,)), ((), ())), preferred_ele...  7.64 us
    ppermute x7, waiting for transfers between devices, on_device(): lax.ppermute(outgoing.astype(jnp.bfloat16), 'dp', pairs).astype(jnp.float32)  5.03 us
    ppermute x1, starting transfers between devices, _gather_dp(): lax.ppermute(local, axis, [(i, i ^ half) for i in range(size)])  4.04 us
    ppermute x1, waiting for transfers between devices, _gather_dp(): lax.ppermute(local, axis, [(i, i ^ half) for i in range(size)])  3.91 us
    ppermute x3, waiting for transfers between devices, _gather_dp(): got.append(lax.ppermute(pair, axis, [(i, i ^ shift) for i in range(size)]))  3.71 us
    ppermute x3, starting transfers between devices, _gather_dp(): got.append(lax.ppermute(pair, axis, [(i, i ^ shift) for i in range(size)]))  3.55 us
    unnamed x6, local copies, waits for them, and re-layouts  1.93 us
  transfers between devices with their start and end apart: 16, of which 10 were waited for; matrix products, arithmetic and copies ran while one was open for 13% of the time, Pallas kernels for 0%

profile of v16, /device:TPU:0, one launch (start us, length us, event | category | flops | bytes accessed | tf_op | source)
XLA Modules:
  0.0 56.3 jit_solution(3106689794022618240)
XLA Ops:
  0.7 0.9 %constant_dynamic-update-slice_fusion.1 = bf16[1,16,2304]{2,1,0:T(8,128)(2,1)S(1)} fusion(bf16[1,16,2048]{2,1,0:T(8,128)(2,1)} %param.9), kind=kLoop, calls=%fused_computation.71 | loop fusion | bytes 131072
  2.3 4.0 %collective-permute-start.2 = (bf16[1,16,2304]{2,1,0:T(8,128)(2,1)S(1)}, bf16[1,16,2304]{2,1,0:T(8,128)(2,1)S(1)}, u32[]{:S(2)}, u32[]{:S(2)}) collective-permute-start(bf16[1,16,2304]{2,1,0:T(8,128)(2,1)S(1)} %constant_dynamic-update-slice_fusion), channel_id=1, source_target_pairs={{0,16},{4,20},{8,24},{12,28},{16,0},{20,4},{24,8},{28,12},{1,17},{... | collective-permute-start | bytes 221192 | tf_op jit(solution)/shard_map/ppermute | solution.py:37
  6.3 3.9 %collective-permute-done.2 = bf16[1,16,2304]{2,1,0:T(8,128)(2,1)S(1)} collective-permute-done((bf16[1,16,2304]{2,1,0:T(8,128)(2,1)S(1)}, bf16[1,16,2304]{2,1,0:T(8,128)(2,1)S(1)}, u32[]{:S(2)}, u32[]{:S(2)}) %collective-permute-start.2) | collective-permute-done | bytes 73760 | tf_op jit(solution)/shard_map/ppermute | solution.py:37
  10.2 1.8 %collective-permute-start.5 = (bf16[2,16,2304]{2,1,0:T(8,128)(2,1)S(1)}, bf16[2,16,2304]{2,1,0:T(8,128)(2,1)S(1)}, u32[]{:S(2)}, u32[]{:S(2)}) collective-permute-start(bf16[2,16,2304]{2,1,0:T(8,128)(2,1)S(1)} %pad_maximum_fusion.1), channel_id=1, source_target_pairs={{0,4},{4,0},{8,12},{12,8},{16,20},{20,16},{24,28},{28,24},{1,5},{5... | collective-permute-start | bytes 442376 | tf_op jit(solution)/shard_map/ppermute | solution.py:41
  12.5 1.3 %collective-permute-start.3 = (bf16[2,16,2304]{2,1,0:T(8,128)(2,1)S(1)}, bf16[2,16,2304]{2,1,0:T(8,128)(2,1)S(1)}, u32[]{:S(2)}, u32[]{:S(2)}) collective-permute-start(bf16[2,16,2304]{2,1,0:T(8,128)(2,1)S(1)} %pad_maximum_fusion.1), channel_id=1, source_target_pairs={{0,12},{4,8},{8,4},{12,0},{16,28},{20,24},{24,20},{28,16},{1,13},{... | collective-permute-start | bytes 442376 | tf_op jit(solution)/shard_map/ppermute | solution.py:41
  13.8 1.6 %convolution_bitcast_fusion.1 = f32[128,2048]{0,1:T(8,128)S(1)} fusion(bf16[128,256]{1,0:T(8,128)(2,1)} %param.7, bf16[8192,256]{1,0:T(8,128)(2,1)} %param.8, s32[]{:T(128)S(6)} %select_n.81), kind=kOutput, calls=%fused_computation.1 | convolution fusion | flops 134217728 | bytes 2162692 | tf_op jit(solution)/shard_map/dot_general | solution.py:75
  16.3 1.3 %collective-permute-done.4 = bf16[2,16,2304]{2,1,0:T(8,128)(2,1)S(1)} collective-permute-done((bf16[2,16,2304]{2,1,0:T(8,128)(2,1)S(1)}, bf16[2,16,2304]{2,1,0:T(8,128)(2,1)S(1)}, u32[]{:S(2)}, u32[]{:S(2)}) %collective-permute-start.4) | collective-permute-done | bytes 147488 | tf_op jit(solution)/shard_map/ppermute | solution.py:41
  17.6 2.3 %collective-permute-done.3 = bf16[2,16,2304]{2,1,0:T(8,128)(2,1)S(1)} collective-permute-done((bf16[2,16,2304]{2,1,0:T(8,128)(2,1)S(1)}, bf16[2,16,2304]{2,1,0:T(8,128)(2,1)S(1)}, u32[]{:S(2)}, u32[]{:S(2)}) %collective-permute-start.3) | collective-permute-done | bytes 147488 | tf_op jit(solution)/shard_map/ppermute | solution.py:41
  20.0 1.0 %fusion.6 = f32[1,128,16]{1,2,0:T(8,128)S(1)} fusion(bf16[128,256]{1,0:T(8,128)(2,1)} %param.7, bf16[1,16,2304]{2,1,0:T(8,128)(2,1)S(1)} %fusion.26), kind=kOutput, calls=%fused_computation.18 | convolution fusion | flops 1050624 | bytes 81920 | tf_op jit(solution)/shard_map/bnk,brk->bnr/dot_general | solution.py:123
  21.2 2.7 %fusion.3 = f32[128,2048]{0,1:T(8,128)} fusion(f32[128,2048]{0,1:T(8,128)S(1)} %collective-permute-done.1, bf16[128,256]{1,0:T(8,128)(2,1)} %param.7, bf16[8192,256]{1,0:T(8,128)(2,1)} %param.8, s32[]{:T(128)S(6)} %select_n.80), kind=kOutput, calls=%fused_computation.8 | convolution fusion | flops 134479872 | bytes 3211268 | tf_op jit(solution)/shard_map/dot_general | solution.py:75
  23.9 1.6 %convolution_bitcast_fusion.3 = f32[128,2048]{0,1:T(8,128)S(1)} fusion(bf16[128,256]{1,0:T(8,128)(2,1)S(1)} %copy-done.1, bf16[8192,256]{1,0:T(8,128)(2,1)} %param.8, s32[]{:T(128)S(6)} %select_n.79), kind=kOutput, calls=%fused_computation.3 | convolution fusion | flops 134217728 | bytes 2162692 | tf_op jit(solution)/shard_map/dot_general | solution.py:75
  26.1 1.6 %collective-permute-start.8 = (f32[1,128,32]{1,2,0:T(8,128)S(1)}, f32[1,128,32]{1,2,0:T(8,128)S(1)}, u32[]{:S(2)}, u32[]{:S(2)}) collective-permute-start(f32[1,128,32]{1,2,0:T(8,128)S(1)} %add.109), channel_id=1, source_target_pairs={{0,2},{1,3},{2,0},{3,1},{4,6},{5,7},{6,4},{7,5},{8,10},{9,11},{10,... | collective-permute-start | bytes 49160 | tf_op jit(solution)/shard_map/ppermute | solution.py:59
  28.4 1.5 %collective-permute-done.8 = f32[1,128,32]{1,2,0:T(8,128)S(1)} collective-permute-done((f32[1,128,32]{1,2,0:T(8,128)S(1)}, f32[1,128,32]{1,2,0:T(8,128)S(1)}, u32[]{:S(2)}, u32[]{:S(2)}) %collective-permute-start.8) | collective-permute-done | bytes 16416 | tf_op jit(solution)/shard_map/ppermute | solution.py:59
  30.5 4.7 %collective-permute-start.15 = (bf16[1,16,2304]{2,1,0:T(8,128)(2,1)S(1)}, bf16[1,16,2304]{2,1,0:T(8,128)(2,1)S(1)}, u32[]{:S(2)}, u32[]{:S(2)}) collective-permute-start(bf16[1,16,2304]{2,1,0:T(8,128)(2,1)S(1)} %fusion.27), channel_id=1, source_target_pairs={{0,28},{4,24},{8,20},{12,16},{16,12},{20,8},{24,4},{28,0},{1,29},{... | collective-permute-start | bytes 221192 | tf_op jit(solution)/shard_map/ppermute | solution.py:161
  35.4 0.8 %collective-permute-start.13 = (bf16[1,16,2304]{2,1,0:T(8,128)(2,1)S(1)}, bf16[1,16,2304]{2,1,0:T(8,128)(2,1)S(1)}, u32[]{:S(2)}, u32[]{:S(2)}) collective-permute-start(bf16[1,16,2304]{2,1,0:T(8,128)(2,1)S(1)} %get-tuple-element.12), channel_id=1, source_target_pairs={{0,20},{4,16},{8,28},{12,24},{16,4},{20,0},{24,12},{28,8},{1,21},{... | collective-permute-start | bytes 221192 | tf_op jit(solution)/shard_map/ppermute | solution.py:161
  36.2 1.8 %collective-permute-done.15 = bf16[1,16,2304]{2,1,0:T(8,128)(2,1)S(1)} collective-permute-done((bf16[1,16,2304]{2,1,0:T(8,128)(2,1)S(1)}, bf16[1,16,2304]{2,1,0:T(8,128)(2,1)S(1)}, u32[]{:S(2)}, u32[]{:S(2)}) %collective-permute-start.15) | collective-permute-done | bytes 73760 | tf_op jit(solution)/shard_map/ppermute | solution.py:161
  38.0 6.9 %collective-permute-start.12 = (bf16[1,16,2304]{2,1,0:T(8,128)(2,1)S(1)}, bf16[1,16,2304]{2,1,0:T(8,128)(2,1)S(1)}, u32[]{:S(2)}, u32[]{:S(2)}) collective-permute-start(bf16[1,16,2304]{2,1,0:T(8,128)(2,1)S(1)} %get-tuple-element.13), channel_id=1, source_target_pairs={{0,16},{4,20},{8,24},{12,28},{16,0},{20,4},{24,8},{28,12},{1,17},{... | collective-permute-start | bytes 221192 | tf_op jit(solution)/shard_map/ppermute | solution.py:161
  45.1 2.7 %collective-permute-start.10 = (bf16[1,16,2304]{2,1,0:T(8,128)(2,1)S(1)}, bf16[1,16,2304]{2,1,0:T(8,128)(2,1)S(1)}, u32[]{:S(2)}, u32[]{:S(2)}) collective-permute-start(bf16[1,16,2304]{2,1,0:T(8,128)(2,1)S(1)} %get-tuple-element.15), channel_id=1, source_target_pairs={{0,8},{4,12},{8,0},{12,4},{16,24},{20,28},{24,16},{28,20},{1,9},{5... | collective-permute-start | bytes 221192 | tf_op jit(solution)/shard_map/ppermute | solution.py:161
  47.9 0.8 %collective-permute-start.9 = (bf16[1,16,2304]{2,1,0:T(8,128)(2,1)S(1)}, bf16[1,16,2304]{2,1,0:T(8,128)(2,1)S(1)}, u32[]{:S(2)}, u32[]{:S(2)}) collective-permute-start(bf16[1,16,2304]{2,1,0:T(8,128)(2,1)S(1)} %get-tuple-element.10), channel_id=1, source_target_pairs={{0,4},{4,0},{8,12},{12,8},{16,20},{20,16},{24,28},{28,24},{1,5},{5... | collective-permute-start | bytes 221192 | tf_op jit(solution)/shard_map/ppermute | solution.py:161
  49.2 1.1 %collective-permute-done.11 = bf16[1,16,2304]{2,1,0:T(8,128)(2,1)S(1)} collective-permute-done((bf16[1,16,2304]{2,1,0:T(8,128)(2,1)S(1)}, bf16[1,16,2304]{2,1,0:T(8,128)(2,1)S(1)}, u32[]{:S(2)}, u32[]{:S(2)}) %collective-permute-start.11) | collective-permute-done | bytes 73760 | tf_op jit(solution)/shard_map/ppermute | solution.py:161
  50.9 1.3 %collective-permute-done.9 = bf16[1,16,2304]{2,1,0:T(8,128)(2,1)S(1)} collective-permute-done((bf16[1,16,2304]{2,1,0:T(8,128)(2,1)S(1)}, bf16[1,16,2304]{2,1,0:T(8,128)(2,1)S(1)}, u32[]{:S(2)}, u32[]{:S(2)}) %collective-permute-start.9) | collective-permute-done | bytes 73760 | tf_op jit(solution)/shard_map/ppermute | solution.py:161
  52.9 0.7 %slice_add_fusion = f32[1,16,2048]{2,1,0:T(8,128)} fusion(f32[1,16,2304]{2,1,0:T(8,128)S(1)} %convert_element_type.155, f32[1,16,2304]{2,1,0:T(8,128)S(1)} %convert_element_type.152, f32[1,16,2304]{2,1,0:T(8,128)S(1)} %convert_element_type.149, f32[1,16,2304]{2,1,0:T(8,128)S(1)} %convert_element_type.146, f32[1,16,2304]{2,1,0:T(8,128)S(1)} %convert_element_type.143, ...), kind=kLoop, calls=%fused_computation.36 | loop fusion | flops 229376 | bytes 1179648 | tf_op jit(solution)/shard_map/add | solution.py:162
  53.6 1.7 %fusion.4 = bf16[128,2048]{0,1:T(8,128)(2,1)S(1)} fusion(f32[128,2048]{0,1:T(8,128)S(1)} %fusion.28, f32[128,2048]{0,1:T(8,128)S(1)} %collective-permute-done.6, f32[128,2048]{0,1:T(8,128)S(1)} %collective-permute-done, bf16[128,256]{1,0:T(8,128)(2,1)S(1)} %copy-done.1, bf16[8192,256]{1,0:T(8,128)(2,1)} %param.8, s32[]{:T(128)S(6)} %select_n.78), kind=kOutput, calls=%fused_computation.9 | convolution fusion | flops 135266304 | bytes 4784132 | tf_op jit(solution)/shard_map/dot_general | solution.py:75
  55.3 1.0 %copy.16 = bf16[128,2048]{1,0:T(8,128)(2,1)} copy(bf16[128,2048]{0,1:T(8,128)(2,1)S(1)} %fusion.4) | data formatting | bytes 1048576
  (47 shorter events, 5.5 us)
Async XLA Ops:
  0.6 20.3 %copy-start = (bf16[128,2048]{1,0:T(8,128)(2,1)S(1)}, bf16[128,2048]{1,0:T(8,128)(2,1)}, u32[]{:S(2)}) copy-start(bf16[128,2048]{1,0:T(8,128)(2,1)} %param.6) | copy-start | bytes 1572868
  0.6 23.2 %copy-start.1 = (bf16[128,256]{1,0:T(8,128)(2,1)S(1)}, bf16[128,256]{1,0:T(8,128)(2,1)}, u32[]{:S(2)}) copy-start(bf16[128,256]{1,0:T(8,128)(2,1)} %param.7) | copy-start | bytes 196612
  2.3 7.9 %collective-permute-start.2 = (bf16[1,16,2304]{2,1,0:T(8,128)(2,1)S(1)}, bf16[1,16,2304]{2,1,0:T(8,128)(2,1)S(1)}, u32[]{:S(2)}, u32[]{:S(2)}) collective-permute-start(bf16[1,16,2304]{2,1,0:T(8,128)(2,1)S(1)} %constant_dynamic-update-slice_fusion), channel_id=1, source_target_pairs={{0,16},{4,20},{8,24},{12,28},{16,0},{20,4},{24,8},{28,12},{1,17},{... | collective-permute-start | bytes 221192 | tf_op jit(solution)/shard_map/ppermute | solution.py:37
  10.2 6.0 %collective-permute-start.5 = (bf16[2,16,2304]{2,1,0:T(8,128)(2,1)S(1)}, bf16[2,16,2304]{2,1,0:T(8,128)(2,1)S(1)}, u32[]{:S(2)}, u32[]{:S(2)}) collective-permute-start(bf16[2,16,2304]{2,1,0:T(8,128)(2,1)S(1)} %pad_maximum_fusion.1), channel_id=1, source_target_pairs={{0,4},{4,0},{8,12},{12,8},{16,20},{20,16},{24,28},{28,24},{1,5},{5... | collective-permute-start | bytes 442376 | tf_op jit(solution)/shard_map/ppermute | solution.py:41
  12.0 5.6 %collective-permute-start.4 = (bf16[2,16,2304]{2,1,0:T(8,128)(2,1)S(1)}, bf16[2,16,2304]{2,1,0:T(8,128)(2,1)S(1)}, u32[]{:S(2)}, u32[]{:S(2)}) collective-permute-start(bf16[2,16,2304]{2,1,0:T(8,128)(2,1)S(1)} %pad_maximum_fusion.1), channel_id=1, source_target_pairs={{0,8},{4,12},{8,0},{12,4},{16,24},{20,28},{24,16},{28,20},{1,9},{5... | collective-permute-start | bytes 442376 | tf_op jit(solution)/shard_map/ppermute | solution.py:41
  12.5 7.4 %collective-permute-start.3 = (bf16[2,16,2304]{2,1,0:T(8,128)(2,1)S(1)}, bf16[2,16,2304]{2,1,0:T(8,128)(2,1)S(1)}, u32[]{:S(2)}, u32[]{:S(2)}) collective-permute-start(bf16[2,16,2304]{2,1,0:T(8,128)(2,1)S(1)} %pad_maximum_fusion.1), channel_id=1, source_target_pairs={{0,12},{4,8},{8,4},{12,0},{16,28},{20,24},{24,20},{28,16},{1,13},{... | collective-permute-start | bytes 442376 | tf_op jit(solution)/shard_map/ppermute | solution.py:41
  15.4 5.8 %collective-permute-start.1 = (f32[128,2048]{0,1:T(8,128)S(1)}, f32[128,2048]{0,1:T(8,128)S(1)}, u32[]{:S(2)}, u32[]{:S(2)}) collective-permute-start(f32[128,2048]{0,1:T(8,128)S(1)} %convolution_bitcast_fusion.1), channel_id=1, source_target_pairs={{0,1},{1,0},{2,3},{3,2},{4,5},{5,4},{6,7},{7,6},{8,9},{9,8},{10,11... | collective-permute-start | bytes 3145736 | tf_op jit(solution)/shard_map/ppermute | solution.py:87
  23.9 2.2 %collective-permute-start.7 = (f32[1,128,32]{1,2,0:T(8,128)S(1)}, f32[1,128,32]{1,2,0:T(8,128)S(1)}, u32[]{:S(2)}, u32[]{:S(2)}) collective-permute-start(f32[1,128,32]{1,2,0:T(8,128)S(1)} %pad_maximum_fusion.2), channel_id=1, source_target_pairs={{0,1},{1,0},{2,3},{3,2},{4,5},{5,4},{6,7},{7,6},{8,9},{9,8},{10,11... | collective-permute-start | bytes 49160 | tf_op jit(solution)/shard_map/ppermute | solution.py:59
  25.5 28.1 %collective-permute-start = (f32[128,2048]{0,1:T(8,128)S(1)}, f32[128,2048]{0,1:T(8,128)S(1)}, u32[]{:S(2)}, u32[]{:S(2)}) collective-permute-start(f32[128,2048]{0,1:T(8,128)S(1)} %convolution_bitcast_fusion.3), channel_id=1, source_target_pairs={{0,1},{1,0},{2,3},{3,2},{4,5},{5,4},{6,7},{7,6},{8,9},{9,8},{10,11... | collective-permute-start | bytes 3145736 | tf_op jit(solution)/shard_map/ppermute | solution.py:87
  26.1 3.8 %collective-permute-start.8 = (f32[1,128,32]{1,2,0:T(8,128)S(1)}, f32[1,128,32]{1,2,0:T(8,128)S(1)}, u32[]{:S(2)}, u32[]{:S(2)}) collective-permute-start(f32[1,128,32]{1,2,0:T(8,128)S(1)} %add.109), channel_id=1, source_target_pairs={{0,2},{1,3},{2,0},{3,1},{4,6},{5,7},{6,4},{7,5},{8,10},{9,11},{10,... | collective-permute-start | bytes 49160 | tf_op jit(solution)/shard_map/ppermute | solution.py:59
  27.8 25.8 %collective-permute-start.6 = (f32[128,2048]{0,1:T(8,128)}, f32[128,2048]{0,1:T(8,128)S(1)}, u32[]{:S(2)}, u32[]{:S(2)}) collective-permute-start(f32[128,2048]{0,1:T(8,128)} %fusion.3), channel_id=1, source_target_pairs={{0,2},{1,3},{2,0},{3,1},{4,6},{5,7},{6,4},{7,5},{8,10},{9,11},{10,... | collective-permute-start | bytes 3145736 | tf_op jit(solution)/shard_map/ppermute | solution.py:87
  30.5 7.5 %collective-permute-start.15 = (bf16[1,16,2304]{2,1,0:T(8,128)(2,1)S(1)}, bf16[1,16,2304]{2,1,0:T(8,128)(2,1)S(1)}, u32[]{:S(2)}, u32[]{:S(2)}) collective-permute-start(bf16[1,16,2304]{2,1,0:T(8,128)(2,1)S(1)} %fusion.27), channel_id=1, source_target_pairs={{0,28},{4,24},{8,20},{12,16},{16,12},{20,8},{24,4},{28,0},{1,29},{... | collective-permute-start | bytes 221192 | tf_op jit(solution)/shard_map/ppermute | solution.py:161
  35.3 9.6 %collective-permute-start.14 = (bf16[1,16,2304]{2,1,0:T(8,128)(2,1)S(1)}, bf16[1,16,2304]{2,1,0:T(8,128)(2,1)S(1)}, u32[]{:S(2)}, u32[]{:S(2)}) collective-permute-start(bf16[1,16,2304]{2,1,0:T(8,128)(2,1)S(1)} %get-tuple-element.11), channel_id=1, source_target_pairs={{0,24},{4,28},{8,16},{12,20},{16,8},{20,12},{24,0},{28,4},{1,25},{... | collective-permute-start | bytes 221192 | tf_op jit(solution)/shard_map/ppermute | solution.py:161
  35.4 9.7 %collective-permute-start.13 = (bf16[1,16,2304]{2,1,0:T(8,128)(2,1)S(1)}, bf16[1,16,2304]{2,1,0:T(8,128)(2,1)S(1)}, u32[]{:S(2)}, u32[]{:S(2)}) collective-permute-start(bf16[1,16,2304]{2,1,0:T(8,128)(2,1)S(1)} %get-tuple-element.12), channel_id=1, source_target_pairs={{0,20},{4,16},{8,28},{12,24},{16,4},{20,0},{24,12},{28,8},{1,21},{... | collective-permute-start | bytes 221192 | tf_op jit(solution)/shard_map/ppermute | solution.py:161
  38.0 9.9 %collective-permute-start.12 = (bf16[1,16,2304]{2,1,0:T(8,128)(2,1)S(1)}, bf16[1,16,2304]{2,1,0:T(8,128)(2,1)S(1)}, u32[]{:S(2)}, u32[]{:S(2)}) collective-permute-start(bf16[1,16,2304]{2,1,0:T(8,128)(2,1)S(1)} %get-tuple-element.13), channel_id=1, source_target_pairs={{0,16},{4,20},{8,24},{12,28},{16,0},{20,4},{24,8},{28,12},{1,17},{... | collective-permute-start | bytes 221192 | tf_op jit(solution)/shard_map/ppermute | solution.py:161
  45.0 5.3 %collective-permute-start.11 = (bf16[1,16,2304]{2,1,0:T(8,128)(2,1)S(1)}, bf16[1,16,2304]{2,1,0:T(8,128)(2,1)S(1)}, u32[]{:S(2)}, u32[]{:S(2)}) collective-permute-start(bf16[1,16,2304]{2,1,0:T(8,128)(2,1)S(1)} %get-tuple-element.14), channel_id=1, source_target_pairs={{0,12},{4,8},{8,4},{12,0},{16,28},{20,24},{24,20},{28,16},{1,13},{... | collective-permute-start | bytes 221192 | tf_op jit(solution)/shard_map/ppermute | solution.py:161
  45.1 5.8 %collective-permute-start.10 = (bf16[1,16,2304]{2,1,0:T(8,128)(2,1)S(1)}, bf16[1,16,2304]{2,1,0:T(8,128)(2,1)S(1)}, u32[]{:S(2)}, u32[]{:S(2)}) collective-permute-start(bf16[1,16,2304]{2,1,0:T(8,128)(2,1)S(1)} %get-tuple-element.15), channel_id=1, source_target_pairs={{0,8},{4,12},{8,0},{12,4},{16,24},{20,28},{24,16},{28,20},{1,9},{5... | collective-permute-start | bytes 221192 | tf_op jit(solution)/shard_map/ppermute | solution.py:161
  47.9 4.4 %collective-permute-start.9 = (bf16[1,16,2304]{2,1,0:T(8,128)(2,1)S(1)}, bf16[1,16,2304]{2,1,0:T(8,128)(2,1)S(1)}, u32[]{:S(2)}, u32[]{:S(2)}) collective-permute-start(bf16[1,16,2304]{2,1,0:T(8,128)(2,1)S(1)} %get-tuple-element.10), channel_id=1, source_target_pairs={{0,4},{4,0},{8,12},{12,8},{16,20},{20,16},{24,28},{28,24},{1,5},{5... | collective-permute-start | bytes 221192 | tf_op jit(solution)/shard_map/ppermute | solution.py:161

commit v17 on v16

--- a/solution.py
+++ b/solution.py
@@ -106,7 +106,22 @@
 
 
     packed = jnp.concatenate([adapter_down_weight, adapter_up_weight], axis=2)
+    width = packed.shape[2]
+    routed = block_count == 1 and dp_size >= 4 and dp_size & (dp_size - 1) == 0
+    if routed:
+        tenant = tenant_per_block[0]
+        digits = jnp.zeros((held_tenants, adapter_rank_size, 128), jnp.float32)
+        digits = digits.at[:, 0, 0].set((tenant // 256).astype(jnp.float32))
+        digits = digits.at[:, 0, 1].set((tenant % 256).astype(jnp.float32))
+        packed = jnp.concatenate([packed, digits.astype(packed.dtype)], axis=2)
     pieces, sources = _gather_dp(packed, "dp", dp_size)
+    if routed:
+        mates_tenant = [
+            pieces[2 * m][0, 0, width].astype(jnp.int32) * 256 + pieces[2 * m][0, 0, width + 1].astype(jnp.int32)
+            for m in range(dp_size // 2)
+        ]
+        pieces = [q[..., :width] for q in pieces]
+        packed = packed[..., :width]
     owner = tenant_per_block // held_tenants
     local = tenant_per_block % held_tenants
     selected = jnp.zeros((block_count,) + packed.shape[1:], packed.dtype)
@@ -153,6 +168,24 @@
     down_contribution = down_contribution.reshape(dp_size, held_tenants, adapter_rank_size, width_portion)
     up_contribution = up_contribution.reshape(dp_size, held_tenants, adapter_rank_size, key_portion)
     combined = jnp.concatenate([down_contribution, up_contribution], axis=3)
+    if routed:
+        half = dp_size // 2
+        owner_me = tenant_per_block[0] // held_tenants
+        term = lax.dynamic_index_in_dim(combined, owner_me, 0, keepdims=False)
+        zero = jnp.zeros_like(term)
+        own_sum = jnp.where(owner_me == me_dp, term, zero)
+        cross_sum = jnp.where(owner_me == (me_dp ^ half), term, zero)
+        for m in range(1, half):
+            mate = me_dp ^ m
+            outgoing = jnp.where((owner_me == mate) | (owner_me == (mate ^ half)), term, zero)
+            arrived = lax.ppermute(outgoing, "dp", [(i, i ^ m) for i in range(dp_size)])
+            sender_owner = mates_tenant[m] // held_tenants
+            own_sum = own_sum + jnp.where(sender_owner == me_dp, arrived, zero)
+            cross_sum = cross_sum + jnp.where(sender_owner == (me_dp ^ half), arrived, zero)
+        arrived = lax.ppermute(cross_sum.astype(jnp.bfloat16), "dp", [(i, i ^ half) for i in range(dp_size)])
+        grad_down = own_sum[:, :, :width_portion] + arrived[:, :, :width_portion].astype(jnp.float32)
+        grad_up = own_sum[:, :, width_portion:] + arrived[:, :, width_portion:].astype(jnp.float32)
+        return (grad_inputs, grad_down, grad_up)
     owned = lax.dynamic_index_in_dim(combined, me_dp, 0, keepdims=False)
     grad_down = owned[:, :, :width_portion]
     grad_up = owned[:, :, width_portion:]

time: 56.7 us -> 69.2 us (1.22)
  waiting for transfers between devices: 14.2 us -> 24.4 us
  starting transfers between devices: 26.5 us -> 17.3 us
  between operations: 1.52 us -> 5.42 us
  local copies, waits for them, and re-layouts: 2.82 us -> 6.6 us
  other arithmetic: 1.66 us -> 4.93 us
    ppermute x3, waiting for transfers between devices: 0.01 us -> 14.2 us  [_frozen_term(): got = [lax.ppermute(held[e], axis, pairs) for e in range(1, len(held), 2)]]
    ppermute x7 -> x4, starting transfers between devices: 16.1 us -> 6.61 us  [the longest x3 3.49 us: on_device(): arrived = lax.ppermute(outgoing, 'dp', [(i, i ^ m) for i in range(dp_size)])]
    slice x0 -> x3, local copies, waits for them, and re-layouts: none -> 3.26 us  [on_device(): pieces[2 * m][0, 0, width + 1].astype(jnp.int32)]
    ppermute x7 -> x4, waiting for transfers between devices: 5.03 us -> 1.99 us  [the longest x1 1.98 us: on_device(): lax.ppermute(cross_sum.astype(jnp.bfloat16), 'dp', [(i, i ^ half) for i i...]
    ppermute x1, waiting for transfers between devices: 3.91 us -> 1.43 us  [_gather_dp(): lax.ppermute(local, axis, [(i, i ^ half) for i in range(size)])]
    scatter x0 -> x2, local copies, waits for them, and re-layouts: none -> 1.48 us  [the longest x1 1.47 us: on_device(): digits = digits.at[:, 0, 1].set((tenant % 256).astype(jnp.float32))]
    dot_general x4, matrix products: 7.64 us -> 8.86 us  [term(): lax.dot_general(cotangent, piece, (((1,), (1,)), ((), ())), preferred_ele...]
    ppermute x2, waiting for transfers between devices: 1.5 us -> 2.68 us  [_psum_small(): lax.ppermute(total, axis, [(i, i ^ step) for i in range(size)])]
  transfers between devices with their start and end apart: 16 -> 13, of which waited for: 10 -> 7; matrix products, arithmetic and copies ran while one was open for 13% -> 23% of each run, Pallas kernels for 0% -> 0%
where the time goes in v17:
time: 69.2 us; the launch traced here: 68.7 us
  waiting for transfers between devices  24.4 us (35%)
  starting transfers between devices  17.3 us (25%)
  matrix products  10 us (14%)
  local copies, waits for them, and re-layouts  6.6 us (10%)
  between operations  5.42 us (8%)
  other arithmetic  4.93 us (7%)
    ppermute x3, waiting for transfers between devices, _frozen_term(): got = [lax.ppermute(held[e], axis, pairs) for e in range(1, len(held), 2)]  14.2 us
    dot_general x4, matrix products, term(): lax.dot_general(cotangent, piece, (((1,), (1,)), ((), ())), preferred_ele...  8.86 us
    ppermute x3, waiting for transfers between devices, _gather_dp(): got.append(lax.ppermute(pair, axis, [(i, i ^ shift) for i in range(size)]))  4.04 us
    ppermute x1, starting transfers between devices, _gather_dp(): lax.ppermute(local, axis, [(i, i ^ half) for i in range(size)])  4.04 us
    ppermute x3, starting transfers between devices, _gather_dp(): got.append(lax.ppermute(pair, axis, [(i, i ^ shift) for i in range(size)]))  3.55 us
    ppermute x3, starting transfers between devices, on_device(): arrived = lax.ppermute(outgoing, 'dp', [(i, i ^ m) for i in range(dp_size)])  3.49 us
    slice x3, local copies, waits for them, and re-layouts, on_device(): pieces[2 * m][0, 0, width + 1].astype(jnp.int32)  3.26 us
    ppermute x1, starting transfers between devices, on_device(): lax.ppermute(cross_sum.astype(jnp.bfloat16), 'dp', [(i, i ^ half) for i i...  3.13 us
  transfers between devices with their start and end apart: 13, of which 7 were waited for; matrix products, arithmetic and copies ran while one was open for 23% of the time, Pallas kernels for 0%

profile of v17, /device:TPU:0, one launch (start us, length us, event | category | flops | bytes accessed | tf_op | source)
XLA Modules:
  0.0 68.7 jit_solution(16400069925679297896)
XLA Ops:
  2.1 1.5 %scatter.9 = bf16[1,16,128]{2,1,0:T(8,128)(2,1)S(1)} dynamic-update-slice(bf16[1,16,128]{2,1,0:T(8,128)(2,1)S(1)} %scatter.6, bf16[1,1,1]{2,1,0:T(2,128)(2,1)} %bitcast.8, s32[]{:T(128)} %constant.160.clone.1, s32[]{:T(128)} %bitcast.9, s32[]{:T(128)} %bitcast.10) | dynamic-update-slice | bytes 8 | tf_op jit(solution)/shard_map/scatter | solution.py:115
  4.4 4.0 %collective-permute-start.2 = (bf16[1,16,2432]{2,1,0:T(8,128)(2,1)S(1)}, bf16[1,16,2432]{2,1,0:T(8,128)(2,1)S(1)}, u32[]{:S(2)}, u32[]{:S(2)}) collective-permute-start(bf16[1,16,2432]{2,1,0:T(8,128)(2,1)S(1)} %pad_maximum_fusion.1), channel_id=1, source_target_pairs={{0,16},{4,20},{8,24},{12,28},{16,0},{20,4},{24,8},{28,12},{1,17},{... | collective-permute-start | bytes 233480 | tf_op jit(solution)/shard_map/ppermute | solution.py:37
  8.5 2.6 %convolution_bitcast_fusion.1 = f32[128,2048]{0,1:T(8,128)} fusion(bf16[128,256]{1,0:T(8,128)(2,1)} %param.11, bf16[8192,256]{1,0:T(8,128)(2,1)} %param.12, s32[]{:T(128)S(6)} %select_n.197), kind=kOutput, calls=%fused_computation.1 | convolution fusion | flops 134217728 | bytes 2162692 | tf_op jit(solution)/shard_map/dot_general | solution.py:75
  11.1 1.4 %collective-permute-done.2 = bf16[1,16,2432]{2,1,0:T(8,128)(2,1)S(1)} collective-permute-done((bf16[1,16,2432]{2,1,0:T(8,128)(2,1)S(1)}, bf16[1,16,2432]{2,1,0:T(8,128)(2,1)S(1)}, u32[]{:S(2)}, u32[]{:S(2)}) %collective-permute-start.2) | collective-permute-done | bytes 77856 | tf_op jit(solution)/shard_map/ppermute | solution.py:37
  13.4 1.7 %collective-permute-start.3 = (bf16[2,16,2432]{2,1,0:T(8,128)(2,1)S(1)}, bf16[2,16,2432]{2,1,0:T(8,128)(2,1)S(1)}, u32[]{:S(2)}, u32[]{:S(2)}) collective-permute-start(bf16[2,16,2432]{2,1,0:T(8,128)(2,1)S(1)} %pad_maximum_fusion), channel_id=1, source_target_pairs={{0,12},{4,8},{8,4},{12,0},{16,28},{20,24},{24,20},{28,16},{1,13},{... | collective-permute-start | bytes 466952 | tf_op jit(solution)/shard_map/ppermute | solution.py:41
  15.1 1.5 %collective-permute-start.4 = (bf16[2,16,2432]{2,1,0:T(8,128)(2,1)S(1)}, bf16[2,16,2432]{2,1,0:T(8,128)(2,1)S(1)}, u32[]{:S(2)}, u32[]{:S(2)}) collective-permute-start(bf16[2,16,2432]{2,1,0:T(8,128)(2,1)S(1)} %pad_maximum_fusion), channel_id=1, source_target_pairs={{0,8},{4,12},{8,0},{12,4},{16,24},{20,28},{24,16},{28,20},{1,9},{5... | collective-permute-start | bytes 466952 | tf_op jit(solution)/shard_map/ppermute | solution.py:41
  16.9 1.6 %convolution_bitcast_fusion.3 = f32[128,2048]{0,1:T(8,128)S(1)} fusion(bf16[128,256]{1,0:T(8,128)(2,1)} %param.11, bf16[8192,256]{1,0:T(8,128)(2,1)} %param.12, s32[]{:T(128)S(6)} %select_n.195), kind=kOutput, calls=%fused_computation.3 | convolution fusion | flops 134217728 | bytes 2162692 | tf_op jit(solution)/shard_map/dot_general | solution.py:75
  18.7 2.3 %collective-permute-done.3 = bf16[2,16,2432]{2,1,0:T(8,128)(2,1)S(1)} collective-permute-done((bf16[2,16,2432]{2,1,0:T(8,128)(2,1)S(1)}, bf16[2,16,2432]{2,1,0:T(8,128)(2,1)S(1)}, u32[]{:S(2)}, u32[]{:S(2)}) %collective-permute-start.3) | collective-permute-done | bytes 155680 | tf_op jit(solution)/shard_map/ppermute | solution.py:41
  21.1 1.7 %collective-permute-done.4 = bf16[2,16,2432]{2,1,0:T(8,128)(2,1)S(1)} collective-permute-done((bf16[2,16,2432]{2,1,0:T(8,128)(2,1)S(1)}, bf16[2,16,2432]{2,1,0:T(8,128)(2,1)S(1)}, u32[]{:S(2)}, u32[]{:S(2)}) %collective-permute-start.4) | collective-permute-done | bytes 155680 | tf_op jit(solution)/shard_map/ppermute | solution.py:41
  23.3 2.9 %fusion.3 = f32[128,2048]{0,1:T(8,128)} fusion(f32[128,2048]{0,1:T(8,128)} %collective-permute-done.1, bf16[128,256]{1,0:T(8,128)(2,1)S(1)} %copy-done.1, bf16[8192,256]{1,0:T(8,128)(2,1)} %param.12, s32[]{:T(128)S(6)} %select_n.196), kind=kOutput, calls=%fused_computation.8 | convolution fusion | flops 134479872 | bytes 3211268 | tf_op jit(solution)/shard_map/dot_general | solution.py:75
  26.4 1.0 %collective-permute-done.7 = f32[1,128,32]{1,2,0:T(8,128)S(1)} collective-permute-done((f32[1,128,32]{1,2,0:T(8,128)S(1)}, f32[1,128,32]{1,2,0:T(8,128)S(1)}, u32[]{:S(2)}, u32[]{:S(2)}) %collective-permute-start.7) | collective-permute-done | bytes 16416 | tf_op jit(solution)/shard_map/ppermute | solution.py:59
  27.4 1.5 %collective-permute-start.8 = (f32[1,128,32]{1,2,0:T(8,128)S(1)}, f32[1,128,32]{1,2,0:T(8,128)S(1)}, u32[]{:S(2)}, u32[]{:S(2)}) collective-permute-start(f32[1,128,32]{1,2,0:T(8,128)S(1)} %add.104), channel_id=1, source_target_pairs={{0,2},{1,3},{2,0},{3,1},{4,6},{5,7},{6,4},{7,5},{8,10},{9,11},{10,... | collective-permute-start | bytes 49160 | tf_op jit(solution)/shard_map/ppermute | solution.py:59
  29.5 1.7 %collective-permute-done.8 = f32[1,128,32]{1,2,0:T(8,128)S(1)} collective-permute-done((f32[1,128,32]{1,2,0:T(8,128)S(1)}, f32[1,128,32]{1,2,0:T(8,128)S(1)}, u32[]{:S(2)}, u32[]{:S(2)}) %collective-permute-start.8) | collective-permute-done | bytes 16416 | tf_op jit(solution)/shard_map/ppermute | solution.py:59
  32.4 1.6 %collective-permute-start.10 = (f32[1,16,2304]{2,1,0:T(8,128)}, f32[1,16,2304]{2,1,0:T(8,128)S(1)}, u32[]{:S(2)}, u32[]{:S(2)}) collective-permute-start(f32[1,16,2304]{2,1,0:T(8,128)} %get-tuple-element.44), channel_id=1, source_target_pairs={{0,8},{4,12},{8,0},{12,4},{16,24},{20,28},{24,16},{28,20},{1,9},{5... | collective-permute-start | bytes 442376 | tf_op jit(solution)/shard_map/ppermute | solution.py:181
  34.1 1.3 %collective-permute-start.11 = (f32[1,16,2304]{2,1,0:T(8,128)S(1)}, f32[1,16,2304]{2,1,0:T(8,128)S(1)}, u32[]{:S(2)}, u32[]{:S(2)}) collective-permute-start(f32[1,16,2304]{2,1,0:T(8,128)S(1)} %get-tuple-element.45), channel_id=1, source_target_pairs={{0,12},{4,8},{8,4},{12,0},{16,28},{20,24},{24,20},{28,16},{1,13},{... | collective-permute-start | bytes 442376 | tf_op jit(solution)/shard_map/ppermute | solution.py:181
  35.9 1.3 %fusion.33 = (bf16[1,1,1]{2,1,0:T(2,128)(2,1)}, bf16[1,1,1]{2,1,0:T(2,128)(2,1)}) fusion(bf16[2,16,2432]{2,1,0:T(8,128)(2,1)} %copy-done.4), kind=kLoop, calls=%fused_computation.63 | loop fusion | bytes 8 | tf_op jit(solution)/shard_map/slice | solution.py:120
  39.8 1.3 %fusion.34 = (bf16[1,1,1]{2,1,0:T(2,128)(2,1)}, bf16[1,1,1]{2,1,0:T(2,128)(2,1)}) fusion(bf16[2,16,2432]{2,1,0:T(8,128)(2,1)} %copy-done.3), kind=kLoop, calls=%fused_computation.64 | loop fusion | bytes 8 | tf_op jit(solution)/shard_map/slice | solution.py:120
  42.5 1.6 %collective-permute-start.6 = (f32[128,2048]{0,1:T(8,128)}, f32[128,2048]{0,1:T(8,128)S(1)}, u32[]{:S(2)}, u32[]{:S(2)}) collective-permute-start(f32[128,2048]{0,1:T(8,128)} %fusion.3), channel_id=1, source_target_pairs={{0,2},{1,3},{2,0},{3,1},{4,6},{5,7},{6,4},{7,5},{8,10},{9,11},{10,... | collective-permute-start | bytes 3145736 | tf_op jit(solution)/shard_map/ppermute | solution.py:87
  44.0 1.0 %fusion.14 = (bf16[1,16,2304]{2,1,0:T(8,128)(2,1)S(1)}, f32[1,16,2304]{2,1,0:T(8,128)S(1)}) fusion(f32[1,16,2304]{2,1,0:T(8,128)S(1)} %collective-permute-done.11, f32[1,16,2304]{2,1,0:T(8,128)S(1)} %collective-permute-done.10, f32[1,16,2304]{2,1,0:T(8,128)} %collective-permute-done.9, f32[1,1,16,2304]{3,2,0,1:T(8,128)S(1)} %get-tuple-element.35, ...), kind=kLoop, calls=%fused_computation.26 | loop fusion | flops 552960 | bytes 811016 | tf_op jit(solution)/shard_map/convert_element_type | solution.py:185
  45.0 3.1 %collective-permute-start.12 = (bf16[1,16,2304]{2,1,0:T(8,128)(2,1)S(1)}, bf16[1,16,2304]{2,1,0:T(8,128)(2,1)S(1)}, u32[]{:S(2)}, u32[]{:S(2)}) collective-permute-start(bf16[1,16,2304]{2,1,0:T(8,128)(2,1)S(1)} %get-tuple-element.36), channel_id=1, source_target_pairs={{0,16},{4,20},{8,24},{12,28},{16,0},{20,4},{24,8},{28,12},{1,17},{... | collective-permute-start | bytes 221192 | tf_op jit(solution)/shard_map/ppermute | solution.py:185
  48.5 2.0 %collective-permute-done.12 = bf16[1,16,2304]{2,1,0:T(8,128)(2,1)S(1)} collective-permute-done((bf16[1,16,2304]{2,1,0:T(8,128)(2,1)S(1)}, bf16[1,16,2304]{2,1,0:T(8,128)(2,1)S(1)}, u32[]{:S(2)}, u32[]{:S(2)}) %collective-permute-start.12) | collective-permute-done | bytes 73760 | tf_op jit(solution)/shard_map/ppermute | solution.py:185
  51.8 14.2 %collective-permute-done.6 = f32[128,2048]{0,1:T(8,128)S(1)} collective-permute-done((f32[128,2048]{0,1:T(8,128)}, f32[128,2048]{0,1:T(8,128)S(1)}, u32[]{:S(2)}, u32[]{:S(2)}) %collective-permute-start.6) | collective-permute-done | bytes 1048608 | tf_op jit(solution)/shard_map/ppermute | solution.py:87
  66.0 1.7 %fusion.4 = bf16[128,2048]{0,1:T(8,128)(2,1)S(1)} fusion(f32[128,2048]{0,1:T(8,128)S(1)} %fusion.26, f32[128,2048]{0,1:T(8,128)S(1)} %collective-permute-done.6, f32[128,2048]{0,1:T(8,128)S(1)} %collective-permute-done, bf16[128,256]{1,0:T(8,128)(2,1)S(1)} %copy-done.1, bf16[8192,256]{1,0:T(8,128)(2,1)} %param.12, s32[]{:T(128)S(6)} %select_n.194), kind=kOutput, calls=%fused_computation.9 | convolution fusion | flops 135266304 | bytes 4784132 | tf_op jit(solution)/shard_map/dot_general | solution.py:75
  67.7 1.0 %copy.15 = bf16[128,2048]{1,0:T(8,128)(2,1)} copy(bf16[128,2048]{0,1:T(8,128)(2,1)S(1)} %fusion.4) | data formatting | bytes 1048576
  (47 shorter events, 7.5 us)
Async XLA Ops:
  0.6 22.4 %copy-start = (bf16[128,2048]{1,0:T(8,128)(2,1)S(1)}, bf16[128,2048]{1,0:T(8,128)(2,1)}, u32[]{:S(2)}) copy-start(bf16[128,2048]{1,0:T(8,128)(2,1)} %param.10) | copy-start | bytes 1572868
  0.6 22.1 %copy-start.2 = (bf16[1,16,2048]{2,1,0:T(8,128)(2,1)S(1)}, bf16[1,16,2048]{2,1,0:T(8,128)(2,1)}, u32[]{:S(2)}) copy-start(bf16[1,16,2048]{2,1,0:T(8,128)(2,1)} %param.13) | copy-start | bytes 196612
  0.7 22.1 %copy-start.5 = (bf16[1,16,256]{2,1,0:T(8,128)(2,1)S(1)}, bf16[1,16,256]{2,1,0:T(8,128)(2,1)}, u32[]{:S(2)}) copy-start(bf16[1,16,256]{2,1,0:T(8,128)(2,1)} %param.14) | copy-start | bytes 24580
  0.7 22.2 %copy-start.1 = (bf16[128,256]{1,0:T(8,128)(2,1)S(1)}, bf16[128,256]{1,0:T(8,128)(2,1)}, u32[]{:S(2)}) copy-start(bf16[128,256]{1,0:T(8,128)(2,1)} %param.11) | copy-start | bytes 196612
  4.4 8.1 %collective-permute-start.2 = (bf16[1,16,2432]{2,1,0:T(8,128)(2,1)S(1)}, bf16[1,16,2432]{2,1,0:T(8,128)(2,1)S(1)}, u32[]{:S(2)}, u32[]{:S(2)}) collective-permute-start(bf16[1,16,2432]{2,1,0:T(8,128)(2,1)S(1)} %pad_maximum_fusion.1), channel_id=1, source_target_pairs={{0,16},{4,20},{8,24},{12,28},{16,0},{20,4},{24,8},{28,12},{1,17},{... | collective-permute-start | bytes 233480 | tf_op jit(solution)/shard_map/ppermute | solution.py:37
  11.1 12.2 %collective-permute-start.1 = (f32[128,2048]{0,1:T(8,128)}, f32[128,2048]{0,1:T(8,128)}, u32[]{:S(2)}, u32[]{:S(2)}) collective-permute-start(f32[128,2048]{0,1:T(8,128)} %convolution_bitcast_fusion.1), channel_id=1, source_target_pairs={{0,1},{1,0},{2,3},{3,2},{4,5},{5,4},{6,7},{7,6},{8,9},{9,8},{10,11... | collective-permute-start | bytes 3145736 | tf_op jit(solution)/shard_map/ppermute | solution.py:87
  13.4 7.7 %collective-permute-start.3 = (bf16[2,16,2432]{2,1,0:T(8,128)(2,1)S(1)}, bf16[2,16,2432]{2,1,0:T(8,128)(2,1)S(1)}, u32[]{:S(2)}, u32[]{:S(2)}) collective-permute-start(bf16[2,16,2432]{2,1,0:T(8,128)(2,1)S(1)} %pad_maximum_fusion), channel_id=1, source_target_pairs={{0,12},{4,8},{8,4},{12,0},{16,28},{20,24},{24,20},{28,16},{1,13},{... | collective-permute-start | bytes 466952 | tf_op jit(solution)/shard_map/ppermute | solution.py:41
  15.1 7.6 %collective-permute-start.4 = (bf16[2,16,2432]{2,1,0:T(8,128)(2,1)S(1)}, bf16[2,16,2432]{2,1,0:T(8,128)(2,1)S(1)}, u32[]{:S(2)}, u32[]{:S(2)}) collective-permute-start(bf16[2,16,2432]{2,1,0:T(8,128)(2,1)S(1)} %pad_maximum_fusion), channel_id=1, source_target_pairs={{0,8},{4,12},{8,0},{12,4},{16,24},{20,28},{24,16},{28,20},{1,9},{5... | collective-permute-start | bytes 466952 | tf_op jit(solution)/shard_map/ppermute | solution.py:41
  16.6 6.1 %collective-permute-start.5 = (bf16[2,16,2432]{2,1,0:T(8,128)(2,1)S(1)}, bf16[2,16,2432]{2,1,0:T(8,128)(2,1)S(1)}, u32[]{:S(2)}, u32[]{:S(2)}) collective-permute-start(bf16[2,16,2432]{2,1,0:T(8,128)(2,1)S(1)} %pad_maximum_fusion), channel_id=1, source_target_pairs={{0,4},{4,0},{8,12},{12,8},{16,20},{20,16},{24,28},{28,24},{1,5},{5... | collective-permute-start | bytes 466952 | tf_op jit(solution)/shard_map/ppermute | solution.py:41
  18.6 33.2 %collective-permute-start = (f32[128,2048]{0,1:T(8,128)S(1)}, f32[128,2048]{0,1:T(8,128)S(1)}, u32[]{:S(2)}, u32[]{:S(2)}) collective-permute-start(f32[128,2048]{0,1:T(8,128)S(1)} %convolution_bitcast_fusion.3), channel_id=1, source_target_pairs={{0,1},{1,0},{2,3},{3,2},{4,5},{5,4},{6,7},{7,6},{8,9},{9,8},{10,11... | collective-permute-start | bytes 3145736 | tf_op jit(solution)/shard_map/ppermute | solution.py:87
  21.1 10.6 %copy-start.3 = (bf16[2,16,2432]{2,1,0:T(8,128)(2,1)}, bf16[2,16,2432]{2,1,0:T(8,128)(2,1)S(1)}, u32[]{:S(2)}) copy-start(bf16[2,16,2432]{2,1,0:T(8,128)(2,1)S(1)} %collective-permute-done.3) | copy-start | bytes 466948
  22.8 9.7 %copy-start.4 = (bf16[2,16,2432]{2,1,0:T(8,128)(2,1)}, bf16[2,16,2432]{2,1,0:T(8,128)(2,1)S(1)}, u32[]{:S(2)}) copy-start(bf16[2,16,2432]{2,1,0:T(8,128)(2,1)S(1)} %collective-permute-done.4) | copy-start | bytes 466948
  26.2 1.2 %collective-permute-start.7 = (f32[1,128,32]{1,2,0:T(8,128)S(1)}, f32[1,128,32]{1,2,0:T(8,128)S(1)}, u32[]{:S(2)}, u32[]{:S(2)}) collective-permute-start(f32[1,128,32]{1,2,0:T(8,128)S(1)} %pad_maximum_fusion.2), channel_id=1, source_target_pairs={{0,1},{1,0},{2,3},{3,2},{4,5},{5,4},{6,7},{7,6},{8,9},{9,8},{10,11... | collective-permute-start | bytes 49160 | tf_op jit(solution)/shard_map/ppermute | solution.py:59
  27.4 3.7 %collective-permute-start.8 = (f32[1,128,32]{1,2,0:T(8,128)S(1)}, f32[1,128,32]{1,2,0:T(8,128)S(1)}, u32[]{:S(2)}, u32[]{:S(2)}) collective-permute-start(f32[1,128,32]{1,2,0:T(8,128)S(1)} %add.104), channel_id=1, source_target_pairs={{0,2},{1,3},{2,0},{3,1},{4,6},{5,7},{6,4},{7,5},{8,10},{9,11},{10,... | collective-permute-start | bytes 49160 | tf_op jit(solution)/shard_map/ppermute | solution.py:59
  32.4 11.6 %collective-permute-start.10 = (f32[1,16,2304]{2,1,0:T(8,128)}, f32[1,16,2304]{2,1,0:T(8,128)S(1)}, u32[]{:S(2)}, u32[]{:S(2)}) collective-permute-start(f32[1,16,2304]{2,1,0:T(8,128)} %get-tuple-element.44), channel_id=1, source_target_pairs={{0,8},{4,12},{8,0},{12,4},{16,24},{20,28},{24,16},{28,20},{1,9},{5... | collective-permute-start | bytes 442376 | tf_op jit(solution)/shard_map/ppermute | solution.py:181
  34.1 10.0 %collective-permute-start.11 = (f32[1,16,2304]{2,1,0:T(8,128)S(1)}, f32[1,16,2304]{2,1,0:T(8,128)S(1)}, u32[]{:S(2)}, u32[]{:S(2)}) collective-permute-start(f32[1,16,2304]{2,1,0:T(8,128)S(1)} %get-tuple-element.45), channel_id=1, source_target_pairs={{0,12},{4,8},{8,4},{12,0},{16,28},{20,24},{24,20},{28,16},{1,13},{... | collective-permute-start | bytes 442376 | tf_op jit(solution)/shard_map/ppermute | solution.py:181
  35.3 8.7 %collective-permute-start.9 = (f32[1,16,2304]{2,1,0:T(8,128)S(1)}, f32[1,16,2304]{2,1,0:T(8,128)}, u32[]{:S(2)}, u32[]{:S(2)}) collective-permute-start(f32[1,16,2304]{2,1,0:T(8,128)S(1)} %get-tuple-element.34), channel_id=1, source_target_pairs={{0,4},{4,0},{8,12},{12,8},{16,20},{20,16},{24,28},{28,24},{1,5},{5... | collective-permute-start | bytes 442376 | tf_op jit(solution)/shard_map/ppermute | solution.py:181
  42.5 23.5 %collective-permute-start.6 = (f32[128,2048]{0,1:T(8,128)}, f32[128,2048]{0,1:T(8,128)S(1)}, u32[]{:S(2)}, u32[]{:S(2)}) collective-permute-start(f32[128,2048]{0,1:T(8,128)} %fusion.3), channel_id=1, source_target_pairs={{0,2},{1,3},{2,0},{3,1},{4,6},{5,7},{6,4},{7,5},{8,10},{9,11},{10,... | collective-permute-start | bytes 3145736 | tf_op jit(solution)/shard_map/ppermute | solution.py:87
  45.0 5.5 %collective-permute-start.12 = (bf16[1,16,2304]{2,1,0:T(8,128)(2,1)S(1)}, bf16[1,16,2304]{2,1,0:T(8,128)(2,1)S(1)}, u32[]{:S(2)}, u32[]{:S(2)}) collective-permute-start(bf16[1,16,2304]{2,1,0:T(8,128)(2,1)S(1)} %get-tuple-element.36), channel_id=1, source_target_pairs={{0,16},{4,20},{8,24},{12,28},{16,0},{20,4},{24,8},{28,12},{1,17},{... | collective-permute-start | bytes 221192 | tf_op jit(solution)/shard_map/ppermute | solution.py:185

commit v18 on v16

--- a/solution.py
+++ b/solution.py
@@ -66,7 +66,7 @@
         partial = lax.dot_general(
             cotangent, weight, (((1,), (1,)), ((), ())), preferred_element_type=jnp.float32
         )
-        return lax.psum_scatter(partial, axis, scatter_dimension=1, tiled=True), ready
+        return (lax.psum_scatter(partial, axis, scatter_dimension=1, tiled=True), None), ready
     me = lax.axis_index(axis)
     rows = weight.shape[0] // size
 
@@ -85,9 +85,11 @@
         partner = 1 << step
         pairs = [(i, i ^ partner) for i in range(size)]
         got = [lax.ppermute(held[e], axis, pairs) for e in range(1, len(held), 2)]
+        if len(held) == 2:
+            return (held[0], got[0]), ready
         held = [held[e] + g for e, g in zip(range(0, len(held), 2), got)]
         step += 1
-    return held[0], ready
+    return (held[0], None), ready
 
 
 def on_device(
@@ -124,10 +126,15 @@
         "bnk,brk->bnr", cotangent_blocks, sel_up, preferred_element_type=jnp.float32
     )
     lows = jnp.concatenate([low_in, reduced_output], axis=2)
-    base_grad, lows = _frozen_term(cotangent, frozen_key_weight, "tensor", tensor_size, lows)
+    (own_grad, far_grad), lows = _frozen_term(cotangent, frozen_key_weight, "tensor", tensor_size, lows)
     lows = _psum_small(lows, "tensor", tensor_size)
     reduced_input_batch = lows[:, :, :adapter_rank_size].astype(jnp.bfloat16)
     low_out_b = lows[:, :, adapter_rank_size:].astype(jnp.bfloat16)
+    if far_grad is None:
+        base_grad = own_grad
+    else:
+        own_grad, low_out_b = lax.optimization_barrier((own_grad, low_out_b))
+        base_grad = own_grad + far_grad
 
     adapter_grad = jnp.einsum(
         "bnr,brd->bnd", low_out_b, sel_down, preferred_element_type=jnp.float32

time: 56.7 us -> 62.7 us (1.11)
  waiting for transfers between devices: 14.2 us -> 20 us
  starting transfers between devices: 26.5 us -> 24.6 us
  matrix products: 9.65 us -> 10.6 us
  local copies, waits for them, and re-layouts: 2.82 us -> 3.47 us
    ppermute x3, waiting for transfers between devices: 0.01 us -> 9.68 us  [_frozen_term(): got = [lax.ppermute(held[e], axis, pairs) for e in range(1, len(held), 2)]]
    ppermute x7, starting transfers between devices: 16.1 us -> 13.9 us  [on_device(): lax.ppermute(outgoing.astype(jnp.bfloat16), 'dp', pairs).astype(jnp.float32)]
    ppermute x7, waiting for transfers between devices: 5.03 us -> 3.19 us  [on_device(): lax.ppermute(outgoing.astype(jnp.bfloat16), 'dp', pairs).astype(jnp.float32)]
    ppermute x1, waiting for transfers between devices: 3.91 us -> 2.17 us  [_gather_dp(): lax.ppermute(local, axis, [(i, i ^ half) for i in range(size)])]
    dot_general x1, matrix products: 0.35 us -> 1.57 us  [on_device(): jnp.einsum('bnr,brd->bnd', low_out_b, sel_down, preferred_element_type=jn...]
    dot_general x1, matrix products: 0.97 us -> 0.13 us  [on_device(): jnp.einsum('bnk,brk->bnr', cotangent_blocks, sel_up, preferred_element_ty...]
    convert_element_type x1, local copies, waits for them, and re-layouts: 0.03 us -> 0.66 us  [on_device(): outgoing.astype(jnp.bfloat16)]
  transfers between devices with their start and end apart: 16 -> 16, of which waited for: 10 -> 12; matrix products, arithmetic and copies ran while one was open for 13% -> 18% of each run, Pallas kernels for 0% -> 0%
where the time goes in v18:
time: 62.7 us; the launch traced here: 61.9 us
  starting transfers between devices  24.6 us (39%)
  waiting for transfers between devices  20 us (32%)
  matrix products  10.6 us (17%)
  local copies, waits for them, and re-layouts  3.47 us (6%)
  other arithmetic  1.66 us (3%)
  between operations  1.54 us (2%)
    ppermute x7, starting transfers between devices, on_device(): lax.ppermute(outgoing.astype(jnp.bfloat16), 'dp', pairs).astype(jnp.float32)  13.9 us
    ppermute x3, waiting for transfers between devices, _frozen_term(): got = [lax.ppermute(held[e], axis, pairs) for e in range(1, len(held), 2)]  9.68 us
    dot_general x4, matrix products, term(): lax.dot_general(cotangent, piece, (((1,), (1,)), ((), ())), preferred_ele...  8.22 us
    ppermute x1, starting transfers between devices, _gather_dp(): lax.ppermute(local, axis, [(i, i ^ half) for i in range(size)])  4.04 us
    ppermute x3, waiting for transfers between devices, _gather_dp(): got.append(lax.ppermute(pair, axis, [(i, i ^ shift) for i in range(size)]))  3.7 us
    ppermute x3, starting transfers between devices, _gather_dp(): got.append(lax.ppermute(pair, axis, [(i, i ^ shift) for i in range(size)]))  3.55 us
    ppermute x7, waiting for transfers between devices, on_device(): lax.ppermute(outgoing.astype(jnp.bfloat16), 'dp', pairs).astype(jnp.float32)  3.19 us
    ppermute x1, waiting for transfers between devices, _gather_dp(): lax.ppermute(local, axis, [(i, i ^ half) for i in range(size)])  2.17 us
  transfers between devices with their start and end apart: 16, of which 12 were waited for; matrix products, arithmetic and copies ran while one was open for 18% of the time, Pallas kernels for 0%

profile of v18, /device:TPU:0, one launch (start us, length us, event | category | flops | bytes accessed | tf_op | source)
XLA Modules:
  0.0 61.9 jit_solution(6504218509167925468)
XLA Ops:
  0.7 0.9 %constant_dynamic-update-slice_fusion.1 = bf16[1,16,2304]{2,1,0:T(8,128)(2,1)S(1)} fusion(bf16[1,16,2048]{2,1,0:T(8,128)(2,1)} %param.9), kind=kLoop, calls=%fused_computation.69 | loop fusion | bytes 131072
  2.3 4.0 %collective-permute-start.2 = (bf16[1,16,2304]{2,1,0:T(8,128)(2,1)S(1)}, bf16[1,16,2304]{2,1,0:T(8,128)(2,1)S(1)}, u32[]{:S(2)}, u32[]{:S(2)}) collective-permute-start(bf16[1,16,2304]{2,1,0:T(8,128)(2,1)S(1)} %constant_dynamic-update-slice_fusion), channel_id=1, source_target_pairs={{0,16},{4,20},{8,24},{12,28},{16,0},{20,4},{24,8},{28,12},{1,17},{... | collective-permute-start | bytes 221192 | tf_op jit(solution)/shard_map/ppermute | solution.py:37
  6.3 1.6 %convolution_bitcast_fusion.3 = f32[128,2048]{0,1:T(8,128)S(1)} fusion(bf16[128,256]{1,0:T(8,128)(2,1)} %param.7, bf16[8192,256]{1,0:T(8,128)(2,1)} %param.8, s32[]{:T(128)S(6)} %select_n.79), kind=kOutput, calls=%fused_computation.3 | convolution fusion | flops 134217728 | bytes 2162692 | tf_op jit(solution)/shard_map/dot_general | solution.py:75
  8.0 2.2 %collective-permute-done.2 = bf16[1,16,2304]{2,1,0:T(8,128)(2,1)S(1)} collective-permute-done((bf16[1,16,2304]{2,1,0:T(8,128)(2,1)S(1)}, bf16[1,16,2304]{2,1,0:T(8,128)(2,1)S(1)}, u32[]{:S(2)}, u32[]{:S(2)}) %collective-permute-start.2) | collective-permute-done | bytes 73760 | tf_op jit(solution)/shard_map/ppermute | solution.py:37
  10.2 1.8 %collective-permute-start.5 = (bf16[2,16,2304]{2,1,0:T(8,128)(2,1)S(1)}, bf16[2,16,2304]{2,1,0:T(8,128)(2,1)S(1)}, u32[]{:S(2)}, u32[]{:S(2)}) collective-permute-start(bf16[2,16,2304]{2,1,0:T(8,128)(2,1)S(1)} %pad_maximum_fusion.1), channel_id=1, source_target_pairs={{0,4},{4,0},{8,12},{12,8},{16,20},{20,16},{24,28},{28,24},{1,5},{5... | collective-permute-start | bytes 442376 | tf_op jit(solution)/shard_map/ppermute | solution.py:41
  12.5 1.3 %collective-permute-start.3 = (bf16[2,16,2304]{2,1,0:T(8,128)(2,1)S(1)}, bf16[2,16,2304]{2,1,0:T(8,128)(2,1)S(1)}, u32[]{:S(2)}, u32[]{:S(2)}) collective-permute-start(bf16[2,16,2304]{2,1,0:T(8,128)(2,1)S(1)} %pad_maximum_fusion.1), channel_id=1, source_target_pairs={{0,12},{4,8},{8,4},{12,0},{16,28},{20,24},{24,20},{28,16},{1,13},{... | collective-permute-start | bytes 442376 | tf_op jit(solution)/shard_map/ppermute | solution.py:41
  13.8 1.6 %convolution_bitcast_fusion.1 = f32[128,2048]{0,1:T(8,128)S(1)} fusion(bf16[128,256]{1,0:T(8,128)(2,1)} %param.7, bf16[8192,256]{1,0:T(8,128)(2,1)} %param.8, s32[]{:T(128)S(6)} %select_n.81), kind=kOutput, calls=%fused_computation.1 | convolution fusion | flops 134217728 | bytes 2162692 | tf_op jit(solution)/shard_map/dot_general | solution.py:75
  16.3 1.3 %collective-permute-done.4 = bf16[2,16,2304]{2,1,0:T(8,128)(2,1)S(1)} collective-permute-done((bf16[2,16,2304]{2,1,0:T(8,128)(2,1)S(1)}, bf16[2,16,2304]{2,1,0:T(8,128)(2,1)S(1)}, u32[]{:S(2)}, u32[]{:S(2)}) %collective-permute-start.4) | collective-permute-done | bytes 147488 | tf_op jit(solution)/shard_map/ppermute | solution.py:41
  17.6 2.3 %collective-permute-done.3 = bf16[2,16,2304]{2,1,0:T(8,128)(2,1)S(1)} collective-permute-done((bf16[2,16,2304]{2,1,0:T(8,128)(2,1)S(1)}, bf16[2,16,2304]{2,1,0:T(8,128)(2,1)S(1)}, u32[]{:S(2)}, u32[]{:S(2)}) %collective-permute-start.3) | collective-permute-done | bytes 147488 | tf_op jit(solution)/shard_map/ppermute | solution.py:41
  20.4 3.0 %fusion.1 = f32[128,2048]{0,1:T(8,128)} fusion(f32[128,2048]{0,1:T(8,128)} %collective-permute-done.1, bf16[128,256]{1,0:T(8,128)(2,1)S(1)} %copy-done.1, bf16[8192,256]{1,0:T(8,128)(2,1)} %param.8, s32[]{:T(128)S(6)} %select_n.80), kind=kOutput, calls=%fused_computation.6 | convolution fusion | flops 134479872 | bytes 3211268 | tf_op jit(solution)/shard_map/dot_general | solution.py:75
  23.6 1.0 %collective-permute-done.6 = f32[1,128,32]{1,2,0:T(8,128)S(1)} collective-permute-done((f32[1,128,32]{1,2,0:T(8,128)S(1)}, f32[1,128,32]{1,2,0:T(8,128)S(1)}, u32[]{:S(2)}, u32[]{:S(2)}) %collective-permute-start.6) | collective-permute-done | bytes 16416 | tf_op jit(solution)/shard_map/ppermute | solution.py:59
  24.5 1.5 %collective-permute-start.7 = (f32[1,128,32]{1,2,0:T(8,128)S(1)}, f32[1,128,32]{1,2,0:T(8,128)S(1)}, u32[]{:S(2)}, u32[]{:S(2)}) collective-permute-start(f32[1,128,32]{1,2,0:T(8,128)S(1)} %add.108), channel_id=1, source_target_pairs={{0,2},{1,3},{2,0},{3,1},{4,6},{5,7},{6,4},{7,5},{8,10},{9,11},{10,... | collective-permute-start | bytes 49160 | tf_op jit(solution)/shard_map/ppermute | solution.py:59
  26.0 2.0 %fusion = f32[128,2048]{0,1:T(8,128)S(1)} fusion(f32[128,2048]{0,1:T(8,128)} %collective-permute-done, bf16[128,256]{1,0:T(8,128)(2,1)S(1)} %copy-done.1, bf16[8192,256]{1,0:T(8,128)(2,1)} %param.8, s32[]{:T(128)S(6)} %select_n.78), kind=kOutput, calls=%fused_computation.5 | convolution fusion | flops 134479872 | bytes 3211268 | tf_op jit(solution)/shard_map/dot_general | solution.py:75
  28.9 4.7 %collective-permute-start.15 = (bf16[1,16,2304]{2,1,0:T(8,128)(2,1)S(1)}, bf16[1,16,2304]{2,1,0:T(8,128)(2,1)S(1)}, u32[]{:S(2)}, u32[]{:S(2)}) collective-permute-start(bf16[1,16,2304]{2,1,0:T(8,128)(2,1)S(1)} %fusion.24), channel_id=1, source_target_pairs={{0,28},{4,24},{8,20},{12,16},{16,12},{20,8},{24,4},{28,0},{1,29},{... | collective-permute-start | bytes 221192 | tf_op jit(solution)/shard_map/ppermute | solution.py:168
  34.3 0.8 %collective-permute-start.13 = (bf16[1,16,2304]{2,1,0:T(8,128)(2,1)S(1)}, bf16[1,16,2304]{2,1,0:T(8,128)(2,1)S(1)}, u32[]{:S(2)}, u32[]{:S(2)}) collective-permute-start(bf16[1,16,2304]{2,1,0:T(8,128)(2,1)S(1)} %get-tuple-element.16), channel_id=1, source_target_pairs={{0,20},{4,16},{8,28},{12,24},{16,4},{20,0},{24,12},{28,8},{1,21},{... | collective-permute-start | bytes 221192 | tf_op jit(solution)/shard_map/ppermute | solution.py:168
  35.1 1.5 %collective-permute-start.8 = (f32[128,2048]{0,1:T(8,128)}, f32[128,2048]{0,1:T(8,128)}, u32[]{:S(2)}, u32[]{:S(2)}) collective-permute-start(f32[128,2048]{0,1:T(8,128)} %fusion.1), channel_id=1, source_target_pairs={{0,2},{1,3},{2,0},{3,1},{4,6},{5,7},{6,4},{7,5},{8,10},{9,11},{10,... | collective-permute-start | bytes 3145736 | tf_op jit(solution)/shard_map/ppermute | solution.py:87
  36.6 2.2 %collective-permute-start.12 = (bf16[1,16,2304]{2,1,0:T(8,128)(2,1)S(1)}, bf16[1,16,2304]{2,1,0:T(8,128)(2,1)S(1)}, u32[]{:S(2)}, u32[]{:S(2)}) collective-permute-start(bf16[1,16,2304]{2,1,0:T(8,128)(2,1)S(1)} %get-tuple-element.17), channel_id=1, source_target_pairs={{0,16},{4,20},{8,24},{12,28},{16,0},{20,4},{24,8},{28,12},{1,17},{... | collective-permute-start | bytes 221192 | tf_op jit(solution)/shard_map/ppermute | solution.py:168
  38.8 2.3 %collective-permute-start.11 = (bf16[1,16,2304]{2,1,0:T(8,128)(2,1)S(1)}, bf16[1,16,2304]{2,1,0:T(8,128)(2,1)S(1)}, u32[]{:S(2)}, u32[]{:S(2)}) collective-permute-start(bf16[1,16,2304]{2,1,0:T(8,128)(2,1)S(1)} %get-tuple-element.18), channel_id=1, source_target_pairs={{0,12},{4,8},{8,4},{12,0},{16,28},{20,24},{24,20},{28,16},{1,13},{... | collective-permute-start | bytes 221192 | tf_op jit(solution)/shard_map/ppermute | solution.py:168
  41.1 2.2 %collective-permute-start.10 = (bf16[1,16,2304]{2,1,0:T(8,128)(2,1)S(1)}, bf16[1,16,2304]{2,1,0:T(8,128)(2,1)S(1)}, u32[]{:S(2)}, u32[]{:S(2)}) collective-permute-start(bf16[1,16,2304]{2,1,0:T(8,128)(2,1)S(1)} %get-tuple-element.19), channel_id=1, source_target_pairs={{0,8},{4,12},{8,0},{12,4},{16,24},{20,28},{24,16},{28,20},{1,9},{5... | collective-permute-start | bytes 221192 | tf_op jit(solution)/shard_map/ppermute | solution.py:168
  43.9 1.6 %collective-permute-start.9 = (bf16[1,16,2304]{2,1,0:T(8,128)(2,1)S(1)}, bf16[1,16,2304]{2,1,0:T(8,128)(2,1)S(1)}, u32[]{:S(2)}, u32[]{:S(2)}) collective-permute-start(bf16[1,16,2304]{2,1,0:T(8,128)(2,1)S(1)} %get-tuple-element.14), channel_id=1, source_target_pairs={{0,4},{4,0},{8,12},{12,8},{16,20},{20,16},{24,28},{28,24},{1,5},{5... | collective-permute-start | bytes 221192 | tf_op jit(solution)/shard_map/ppermute | solution.py:168
  46.5 1.8 %collective-permute-done.9 = bf16[1,16,2304]{2,1,0:T(8,128)(2,1)S(1)} collective-permute-done((bf16[1,16,2304]{2,1,0:T(8,128)(2,1)S(1)}, bf16[1,16,2304]{2,1,0:T(8,128)(2,1)S(1)}, u32[]{:S(2)}, u32[]{:S(2)}) %collective-permute-start.9) | collective-permute-done | bytes 73760 | tf_op jit(solution)/shard_map/ppermute | solution.py:168
  49.6 9.7 %collective-permute-done.8 = f32[128,2048]{0,1:T(8,128)} collective-permute-done((f32[128,2048]{0,1:T(8,128)}, f32[128,2048]{0,1:T(8,128)}, u32[]{:S(2)}, u32[]{:S(2)}) %collective-permute-start.8) | collective-permute-done | bytes 1048608 | tf_op jit(solution)/shard_map/ppermute | solution.py:87
  59.3 1.6 %add_convert_fusion = bf16[128,2048]{0,1:T(8,128)(2,1)S(1)} fusion(f32[128,2048]{0,1:T(8,128)S(1)} %fusion, f32[128,2048]{0,1:T(8,128)} %collective-permute-done.8, bf16[1,16,2304]{2,1,0:T(8,128)(2,1)S(1)} %fusion.23, bf16[1,128,16]{1,2,0:T(8,128)(2,1)S(1)} %get-tuple-element.10), kind=kOutput, calls=%fused_computation.17 | convolution fusion | flops 9175040 | bytes 2691072 | tf_op jit(solution)/shard_map/bnr,brd->bnd/dot_general | solution.py:139
  60.9 1.0 %copy.16 = bf16[128,2048]{1,0:T(8,128)(2,1)} copy(bf16[128,2048]{0,1:T(8,128)(2,1)S(1)} %add_convert_fusion) | data formatting | bytes 1048576
  (47 shorter events, 6.3 us)
Async XLA Ops:
  0.6 19.5 %copy-start = (bf16[128,2048]{1,0:T(8,128)(2,1)S(1)}, bf16[128,2048]{1,0:T(8,128)(2,1)}, u32[]{:S(2)}) copy-start(bf16[128,2048]{1,0:T(8,128)(2,1)} %param.6) | copy-start | bytes 1572868
  0.6 19.3 %copy-start.1 = (bf16[128,256]{1,0:T(8,128)(2,1)S(1)}, bf16[128,256]{1,0:T(8,128)(2,1)}, u32[]{:S(2)}) copy-start(bf16[128,256]{1,0:T(8,128)(2,1)} %param.7) | copy-start | bytes 196612
  2.3 7.9 %collective-permute-start.2 = (bf16[1,16,2304]{2,1,0:T(8,128)(2,1)S(1)}, bf16[1,16,2304]{2,1,0:T(8,128)(2,1)S(1)}, u32[]{:S(2)}, u32[]{:S(2)}) collective-permute-start(bf16[1,16,2304]{2,1,0:T(8,128)(2,1)S(1)} %constant_dynamic-update-slice_fusion), channel_id=1, source_target_pairs={{0,16},{4,20},{8,24},{12,28},{16,0},{20,4},{24,8},{28,12},{1,17},{... | collective-permute-start | bytes 221192 | tf_op jit(solution)/shard_map/ppermute | solution.py:37
  8.0 18.1 %collective-permute-start = (f32[128,2048]{0,1:T(8,128)S(1)}, f32[128,2048]{0,1:T(8,128)}, u32[]{:S(2)}, u32[]{:S(2)}) collective-permute-start(f32[128,2048]{0,1:T(8,128)S(1)} %convolution_bitcast_fusion.3), channel_id=1, source_target_pairs={{0,1},{1,0},{2,3},{3,2},{4,5},{5,4},{6,7},{7,6},{8,9},{9,8},{10,11... | collective-permute-start | bytes 3145736 | tf_op jit(solution)/shard_map/ppermute | solution.py:87
  10.2 6.0 %collective-permute-start.5 = (bf16[2,16,2304]{2,1,0:T(8,128)(2,1)S(1)}, bf16[2,16,2304]{2,1,0:T(8,128)(2,1)S(1)}, u32[]{:S(2)}, u32[]{:S(2)}) collective-permute-start(bf16[2,16,2304]{2,1,0:T(8,128)(2,1)S(1)} %pad_maximum_fusion.1), channel_id=1, source_target_pairs={{0,4},{4,0},{8,12},{12,8},{16,20},{20,16},{24,28},{28,24},{1,5},{5... | collective-permute-start | bytes 442376 | tf_op jit(solution)/shard_map/ppermute | solution.py:41
  12.0 5.6 %collective-permute-start.4 = (bf16[2,16,2304]{2,1,0:T(8,128)(2,1)S(1)}, bf16[2,16,2304]{2,1,0:T(8,128)(2,1)S(1)}, u32[]{:S(2)}, u32[]{:S(2)}) collective-permute-start(bf16[2,16,2304]{2,1,0:T(8,128)(2,1)S(1)} %pad_maximum_fusion.1), channel_id=1, source_target_pairs={{0,8},{4,12},{8,0},{12,4},{16,24},{20,28},{24,16},{28,20},{1,9},{5... | collective-permute-start | bytes 442376 | tf_op jit(solution)/shard_map/ppermute | solution.py:41
  12.5 7.4 %collective-permute-start.3 = (bf16[2,16,2304]{2,1,0:T(8,128)(2,1)S(1)}, bf16[2,16,2304]{2,1,0:T(8,128)(2,1)S(1)}, u32[]{:S(2)}, u32[]{:S(2)}) collective-permute-start(bf16[2,16,2304]{2,1,0:T(8,128)(2,1)S(1)} %pad_maximum_fusion.1), channel_id=1, source_target_pairs={{0,12},{4,8},{8,4},{12,0},{16,28},{20,24},{24,20},{28,16},{1,13},{... | collective-permute-start | bytes 442376 | tf_op jit(solution)/shard_map/ppermute | solution.py:41
  15.5 4.9 %collective-permute-start.1 = (f32[128,2048]{0,1:T(8,128)S(1)}, f32[128,2048]{0,1:T(8,128)}, u32[]{:S(2)}, u32[]{:S(2)}) collective-permute-start(f32[128,2048]{0,1:T(8,128)S(1)} %convolution_bitcast_fusion.1), channel_id=1, source_target_pairs={{0,1},{1,0},{2,3},{3,2},{4,5},{5,4},{6,7},{7,6},{8,9},{9,8},{10,11... | collective-permute-start | bytes 3145736 | tf_op jit(solution)/shard_map/ppermute | solution.py:87
  23.4 1.2 %collective-permute-start.6 = (f32[1,128,32]{1,2,0:T(8,128)S(1)}, f32[1,128,32]{1,2,0:T(8,128)S(1)}, u32[]{:S(2)}, u32[]{:S(2)}) collective-permute-start(f32[1,128,32]{1,2,0:T(8,128)S(1)} %pad_maximum_fusion.2), channel_id=1, source_target_pairs={{0,1},{1,0},{2,3},{3,2},{4,5},{5,4},{6,7},{7,6},{8,9},{9,8},{10,11... | collective-permute-start | bytes 49160 | tf_op jit(solution)/shard_map/ppermute | solution.py:59
  24.5 3.7 %collective-permute-start.7 = (f32[1,128,32]{1,2,0:T(8,128)S(1)}, f32[1,128,32]{1,2,0:T(8,128)S(1)}, u32[]{:S(2)}, u32[]{:S(2)}) collective-permute-start(f32[1,128,32]{1,2,0:T(8,128)S(1)} %add.108), channel_id=1, source_target_pairs={{0,2},{1,3},{2,0},{3,1},{4,6},{5,7},{6,4},{7,5},{8,10},{9,11},{10,... | collective-permute-start | bytes 49160 | tf_op jit(solution)/shard_map/ppermute | solution.py:59
  28.9 9.9 %collective-permute-start.15 = (bf16[1,16,2304]{2,1,0:T(8,128)(2,1)S(1)}, bf16[1,16,2304]{2,1,0:T(8,128)(2,1)S(1)}, u32[]{:S(2)}, u32[]{:S(2)}) collective-permute-start(bf16[1,16,2304]{2,1,0:T(8,128)(2,1)S(1)} %fusion.24), channel_id=1, source_target_pairs={{0,28},{4,24},{8,20},{12,16},{16,12},{20,8},{24,4},{28,0},{1,29},{... | collective-permute-start | bytes 221192 | tf_op jit(solution)/shard_map/ppermute | solution.py:168
  34.3 6.8 %collective-permute-start.14 = (bf16[1,16,2304]{2,1,0:T(8,128)(2,1)}, bf16[1,16,2304]{2,1,0:T(8,128)(2,1)S(1)}, u32[]{:S(2)}, u32[]{:S(2)}) collective-permute-start(bf16[1,16,2304]{2,1,0:T(8,128)(2,1)} %get-tuple-element.15), channel_id=1, source_target_pairs={{0,24},{4,28},{8,16},{12,20},{16,8},{20,12},{24,0},{28,4},{1,25},{... | collective-permute-start | bytes 221192 | tf_op jit(solution)/shard_map/ppermute | solution.py:168
  34.3 9.6 %collective-permute-start.13 = (bf16[1,16,2304]{2,1,0:T(8,128)(2,1)S(1)}, bf16[1,16,2304]{2,1,0:T(8,128)(2,1)S(1)}, u32[]{:S(2)}, u32[]{:S(2)}) collective-permute-start(bf16[1,16,2304]{2,1,0:T(8,128)(2,1)S(1)} %get-tuple-element.16), channel_id=1, source_target_pairs={{0,20},{4,16},{8,28},{12,24},{16,4},{20,0},{24,12},{28,8},{1,21},{... | collective-permute-start | bytes 221192 | tf_op jit(solution)/shard_map/ppermute | solution.py:168
  35.1 24.2 %collective-permute-start.8 = (f32[128,2048]{0,1:T(8,128)}, f32[128,2048]{0,1:T(8,128)}, u32[]{:S(2)}, u32[]{:S(2)}) collective-permute-start(f32[128,2048]{0,1:T(8,128)} %fusion.1), channel_id=1, source_target_pairs={{0,2},{1,3},{2,0},{3,1},{4,6},{5,7},{6,4},{7,5},{8,10},{9,11},{10,... | collective-permute-start | bytes 3145736 | tf_op jit(solution)/shard_map/ppermute | solution.py:87
  36.6 9.1 %collective-permute-start.12 = (bf16[1,16,2304]{2,1,0:T(8,128)(2,1)S(1)}, bf16[1,16,2304]{2,1,0:T(8,128)(2,1)S(1)}, u32[]{:S(2)}, u32[]{:S(2)}) collective-permute-start(bf16[1,16,2304]{2,1,0:T(8,128)(2,1)S(1)} %get-tuple-element.17), channel_id=1, source_target_pairs={{0,16},{4,20},{8,24},{12,28},{16,0},{20,4},{24,8},{28,12},{1,17},{... | collective-permute-start | bytes 221192 | tf_op jit(solution)/shard_map/ppermute | solution.py:168
  38.8 7.2 %collective-permute-start.11 = (bf16[1,16,2304]{2,1,0:T(8,128)(2,1)S(1)}, bf16[1,16,2304]{2,1,0:T(8,128)(2,1)S(1)}, u32[]{:S(2)}, u32[]{:S(2)}) collective-permute-start(bf16[1,16,2304]{2,1,0:T(8,128)(2,1)S(1)} %get-tuple-element.18), channel_id=1, source_target_pairs={{0,12},{4,8},{8,4},{12,0},{16,28},{20,24},{24,20},{28,16},{1,13},{... | collective-permute-start | bytes 221192 | tf_op jit(solution)/shard_map/ppermute | solution.py:168
  41.1 5.3 %collective-permute-start.10 = (bf16[1,16,2304]{2,1,0:T(8,128)(2,1)S(1)}, bf16[1,16,2304]{2,1,0:T(8,128)(2,1)S(1)}, u32[]{:S(2)}, u32[]{:S(2)}) collective-permute-start(bf16[1,16,2304]{2,1,0:T(8,128)(2,1)S(1)} %get-tuple-element.19), channel_id=1, source_target_pairs={{0,8},{4,12},{8,0},{12,4},{16,24},{20,28},{24,16},{28,20},{1,9},{5... | collective-permute-start | bytes 221192 | tf_op jit(solution)/shard_map/ppermute | solution.py:168
  43.9 4.4 %collective-permute-start.9 = (bf16[1,16,2304]{2,1,0:T(8,128)(2,1)S(1)}, bf16[1,16,2304]{2,1,0:T(8,128)(2,1)S(1)}, u32[]{:S(2)}, u32[]{:S(2)}) collective-permute-start(bf16[1,16,2304]{2,1,0:T(8,128)(2,1)S(1)} %get-tuple-element.14), channel_id=1, source_target_pairs={{0,4},{4,0},{8,12},{12,8},{16,20},{20,16},{24,28},{28,24},{1,5},{5... | collective-permute-start | bytes 221192 | tf_op jit(solution)/shard_map/ppermute | solution.py:168

commit v19 on v16

--- a/solution.py
+++ b/solution.py
@@ -33,13 +33,16 @@
             got.append(lax.ppermute(local, axis, pairs))
             sources.append(_source_of(me, shift, size))
         return got, sources
-    half = size // 2
-    pair = jnp.concatenate([local, lax.ppermute(local, axis, [(i, i ^ half) for i in range(size)])], 0)
-    got = [pair]
-    sources = [me, me ^ half]
-    for shift in range(1, half):
-        got.append(lax.ppermute(pair, axis, [(i, i ^ shift) for i in range(size)]))
-        sources += [me ^ shift, me ^ shift ^ half]
+    held_now = local
+    sources = [me]
+    shift = size // 2
+    while shift >= 1:
+        held_now = jnp.concatenate(
+            [held_now, lax.ppermute(held_now, axis, [(i, i ^ shift) for i in range(size)])], 0
+        )
+        sources = sources + [src ^ shift for src in sources]
+        shift //= 2
+    got = [held_now]
     held = local.shape[0]
     pieces = []
     for g in got:

time: 56.7 us -> 61.4 us (1.083)
  waiting for transfers between devices: 14.2 us -> 17.3 us
  other arithmetic: 1.66 us -> 2.7 us
    ppermute x4 -> x3, waiting for transfers between devices: 7.62 us -> 11.1 us  [_gather_dp(): lax.ppermute(held_now, axis, [(i, i ^ shift) for i in range(size)])]
    ppermute x7, starting transfers between devices: 16.1 us -> 17.6 us  [on_device(): lax.ppermute(outgoing.astype(jnp.bfloat16), 'dp', pairs).astype(jnp.float32)]
    ppermute x4 -> x3, starting transfers between devices: 7.59 us -> 6.56 us  [_gather_dp(): lax.ppermute(held_now, axis, [(i, i ^ shift) for i in range(size)])]
    select_n x1, other arithmetic: 0.04 us -> 1.04 us  [on_device(): selected = jnp.where(hit[:, None, None], piece[k][None], selected)]
  transfers between devices with their start and end apart: 16 -> 15, of which waited for: 10 -> 10; matrix products, arithmetic and copies ran while one was open for 13% -> 13% of each run, Pallas kernels for 0% -> 0%
where the time goes in v19:
time: 61.4 us; the launch traced here: 61 us
  starting transfers between devices  27 us (44%)
  waiting for transfers between devices  17.3 us (28%)
  matrix products  9.65 us (16%)
  local copies, waits for them, and re-layouts  2.83 us (5%)
  other arithmetic  2.7 us (4%)
  between operations  1.52 us (2%)
    ppermute x7, starting transfers between devices, on_device(): lax.ppermute(outgoing.astype(jnp.bfloat16), 'dp', pairs).astype(jnp.float32)  17.6 us
    ppermute x3, waiting for transfers between devices, _gather_dp(): lax.ppermute(held_now, axis, [(i, i ^ shift) for i in range(size)])  11.1 us
    dot_general x4, matrix products, term(): lax.dot_general(cotangent, piece, (((1,), (1,)), ((), ())), preferred_ele...  7.63 us
    ppermute x3, starting transfers between devices, _gather_dp(): lax.ppermute(held_now, axis, [(i, i ^ shift) for i in range(size)])  6.56 us
    ppermute x7, waiting for transfers between devices, on_device(): lax.ppermute(outgoing.astype(jnp.bfloat16), 'dp', pairs).astype(jnp.float32)  4.72 us
    unnamed x6, local copies, waits for them, and re-layouts  1.93 us
    ppermute x2, starting transfers between devices, _psum_small(): lax.ppermute(total, axis, [(i, i ^ step) for i in range(size)])  1.77 us
    ppermute x2, waiting for transfers between devices, _psum_small(): lax.ppermute(total, axis, [(i, i ^ step) for i in range(size)])  1.5 us
  transfers between devices with their start and end apart: 15, of which 10 were waited for; matrix products, arithmetic and copies ran while one was open for 13% of the time, Pallas kernels for 0%

profile of v19, /device:TPU:0, one launch (start us, length us, event | category | flops | bytes accessed | tf_op | source)
XLA Modules:
  0.0 61.0 jit_solution(14338856164400045031)
XLA Ops:
  0.7 0.9 %constant_dynamic-update-slice_fusion.1 = bf16[1,16,2304]{2,1,0:T(8,128)(2,1)S(1)} fusion(bf16[1,16,2048]{2,1,0:T(8,128)(2,1)} %param.9), kind=kLoop, calls=%fused_computation.72 | loop fusion | bytes 131072
  2.3 4.0 %collective-permute-start.2 = (bf16[1,16,2304]{2,1,0:T(8,128)(2,1)S(1)}, bf16[1,16,2304]{2,1,0:T(8,128)(2,1)S(1)}, u32[]{:S(2)}, u32[]{:S(2)}) collective-permute-start(bf16[1,16,2304]{2,1,0:T(8,128)(2,1)S(1)} %constant_dynamic-update-slice_fusion), channel_id=1, source_target_pairs={{0,16},{4,20},{8,24},{12,28},{16,0},{20,4},{24,8},{28,12},{1,17},{... | collective-permute-start | bytes 221192 | tf_op jit(solution)/shard_map/ppermute | solution.py:41
  6.3 3.9 %collective-permute-done.2 = bf16[1,16,2304]{2,1,0:T(8,128)(2,1)S(1)} collective-permute-done((bf16[1,16,2304]{2,1,0:T(8,128)(2,1)S(1)}, bf16[1,16,2304]{2,1,0:T(8,128)(2,1)S(1)}, u32[]{:S(2)}, u32[]{:S(2)}) %collective-permute-start.2) | collective-permute-done | bytes 73760 | tf_op jit(solution)/shard_map/ppermute | solution.py:41
  10.2 0.7 %collective-permute-start.3 = (bf16[2,16,2304]{2,1,0:T(8,128)(2,1)S(1)}, bf16[2,16,2304]{2,1,0:T(8,128)(2,1)S(1)}, u32[]{:S(2)}, u32[]{:S(2)}) collective-permute-start(bf16[2,16,2304]{2,1,0:T(8,128)(2,1)S(1)} %pad_maximum_fusion.2), channel_id=1, source_target_pairs={{0,8},{4,12},{8,0},{12,4},{16,24},{20,28},{24,16},{28,20},{1,9},{5... | collective-permute-start | bytes 442376 | tf_op jit(solution)/shard_map/ppermute | solution.py:41
  10.9 4.5 %collective-permute-done.3 = bf16[2,16,2304]{2,1,0:T(8,128)(2,1)S(1)} collective-permute-done((bf16[2,16,2304]{2,1,0:T(8,128)(2,1)S(1)}, bf16[2,16,2304]{2,1,0:T(8,128)(2,1)S(1)}, u32[]{:S(2)}, u32[]{:S(2)}) %collective-permute-start.3) | collective-permute-done | bytes 147488 | tf_op jit(solution)/shard_map/ppermute | solution.py:41
  15.5 1.8 %collective-permute-start.4 = (bf16[4,16,2304]{2,1,0:T(8,128)(2,1)S(1)}, bf16[4,16,2304]{2,1,0:T(8,128)(2,1)}, u32[]{:S(2)}, u32[]{:S(2)}) collective-permute-start(bf16[4,16,2304]{2,1,0:T(8,128)(2,1)S(1)} %pad_maximum_fusion.1), channel_id=1, source_target_pairs={{0,4},{4,0},{8,12},{12,8},{16,20},{20,16},{24,28},{28,24},{1,5},{5... | collective-permute-start | bytes 884744 | tf_op jit(solution)/shard_map/ppermute | solution.py:41
  17.3 1.6 %convolution_bitcast_fusion.1 = f32[128,2048]{0,1:T(8,128)S(1)} fusion(bf16[128,256]{1,0:T(8,128)(2,1)} %param.7, bf16[8192,256]{1,0:T(8,128)(2,1)} %param.8, s32[]{:T(128)S(6)} %select_n.81), kind=kOutput, calls=%fused_computation.1 | convolution fusion | flops 134217728 | bytes 2162692 | tf_op jit(solution)/shard_map/dot_general | solution.py:78
  19.7 2.7 %collective-permute-done.4 = bf16[4,16,2304]{2,1,0:T(8,128)(2,1)} collective-permute-done((bf16[4,16,2304]{2,1,0:T(8,128)(2,1)S(1)}, bf16[4,16,2304]{2,1,0:T(8,128)(2,1)}, u32[]{:S(2)}, u32[]{:S(2)}) %collective-permute-start.4) | collective-permute-done | bytes 294944 | tf_op jit(solution)/shard_map/ppermute | solution.py:41
  22.4 1.0 %fusion.26 = bf16[1,16,2304]{2,1,0:T(8,128)(2,1)S(1)} fusion(bf16[2,16,2304]{2,1,0:T(8,128)(2,1)S(1)} %collective-permute-done.3, bf16[4,16,2304]{2,1,0:T(8,128)(2,1)} %collective-permute-done.4, bf16[1,16,2304]{2,1,0:T(8,128)(2,1)S(1)} %collective-permute-done.2, bf16[1,16,2304]{2,1,0:T(8,128)(2,1)S(1)} %constant_dynamic-update-slice_fusion, pred[]{:T(512)} %bitcast.19, ...), kind=kLoop, calls=%fused_computation.55 | loop fusion | flops 294912 | bytes 663560 | tf_op jit(solution)/shard_map/jit(_where)/select_n | solution.py:119
  23.4 1.0 %fusion.6 = f32[1,128,16]{1,2,0:T(8,128)S(1)} fusion(bf16[128,256]{1,0:T(8,128)(2,1)} %param.7, bf16[1,16,2304]{2,1,0:T(8,128)(2,1)S(1)} %fusion.26), kind=kOutput, calls=%fused_computation.18 | convolution fusion | flops 1050624 | bytes 81920 | tf_op jit(solution)/shard_map/bnk,brk->bnr/dot_general | solution.py:126
  24.7 2.7 %fusion.3 = f32[128,2048]{0,1:T(8,128)} fusion(f32[128,2048]{0,1:T(8,128)S(1)} %collective-permute-done.1, bf16[128,256]{1,0:T(8,128)(2,1)S(1)} %copy-done.1, bf16[8192,256]{1,0:T(8,128)(2,1)} %param.8, s32[]{:T(128)S(6)} %select_n.80), kind=kOutput, calls=%fused_computation.8 | convolution fusion | flops 134479872 | bytes 3211268 | tf_op jit(solution)/shard_map/dot_general | solution.py:78
  27.3 1.6 %convolution_bitcast_fusion.3 = f32[128,2048]{0,1:T(8,128)S(1)} fusion(bf16[128,256]{1,0:T(8,128)(2,1)S(1)} %copy-done.1, bf16[8192,256]{1,0:T(8,128)(2,1)} %param.8, s32[]{:T(128)S(6)} %select_n.79), kind=kOutput, calls=%fused_computation.3 | convolution fusion | flops 134217728 | bytes 2162692 | tf_op jit(solution)/shard_map/dot_general | solution.py:78
  29.6 1.8 %collective-permute-start.7 = (f32[1,128,32]{1,2,0:T(8,128)S(1)}, f32[1,128,32]{1,2,0:T(8,128)S(1)}, u32[]{:S(2)}, u32[]{:S(2)}) collective-permute-start(f32[1,128,32]{1,2,0:T(8,128)S(1)} %add.109), channel_id=1, source_target_pairs={{0,2},{1,3},{2,0},{3,1},{4,6},{5,7},{6,4},{7,5},{8,10},{9,11},{10,... | collective-permute-start | bytes 49160 | tf_op jit(solution)/shard_map/ppermute | solution.py:62
  31.9 1.5 %collective-permute-done.7 = f32[1,128,32]{1,2,0:T(8,128)S(1)} collective-permute-done((f32[1,128,32]{1,2,0:T(8,128)S(1)}, f32[1,128,32]{1,2,0:T(8,128)S(1)}, u32[]{:S(2)}, u32[]{:S(2)}) %collective-permute-start.7) | collective-permute-done | bytes 16416 | tf_op jit(solution)/shard_map/ppermute | solution.py:62
  34.0 6.0 %collective-permute-start.14 = (bf16[1,16,2304]{2,1,0:T(8,128)(2,1)S(1)}, bf16[1,16,2304]{2,1,0:T(8,128)(2,1)S(1)}, u32[]{:S(2)}, u32[]{:S(2)}) collective-permute-start(bf16[1,16,2304]{2,1,0:T(8,128)(2,1)S(1)} %fusion.27), channel_id=1, source_target_pairs={{0,28},{4,24},{8,20},{12,16},{16,12},{20,8},{24,4},{28,0},{1,29},{... | collective-permute-start | bytes 221192 | tf_op jit(solution)/shard_map/ppermute | solution.py:164
  40.1 1.1 %collective-permute-start.12 = (bf16[1,16,2304]{2,1,0:T(8,128)(2,1)S(1)}, bf16[1,16,2304]{2,1,0:T(8,128)(2,1)S(1)}, u32[]{:S(2)}, u32[]{:S(2)}) collective-permute-start(bf16[1,16,2304]{2,1,0:T(8,128)(2,1)S(1)} %get-tuple-element.12), channel_id=1, source_target_pairs={{0,20},{4,16},{8,28},{12,24},{16,4},{20,0},{24,12},{28,8},{1,21},{... | collective-permute-start | bytes 221192 | tf_op jit(solution)/shard_map/ppermute | solution.py:164
  41.2 1.5 %collective-permute-done.14 = bf16[1,16,2304]{2,1,0:T(8,128)(2,1)S(1)} collective-permute-done((bf16[1,16,2304]{2,1,0:T(8,128)(2,1)S(1)}, bf16[1,16,2304]{2,1,0:T(8,128)(2,1)S(1)}, u32[]{:S(2)}, u32[]{:S(2)}) %collective-permute-start.14) | collective-permute-done | bytes 73760 | tf_op jit(solution)/shard_map/ppermute | solution.py:164
  42.7 6.9 %collective-permute-start.11 = (bf16[1,16,2304]{2,1,0:T(8,128)(2,1)S(1)}, bf16[1,16,2304]{2,1,0:T(8,128)(2,1)S(1)}, u32[]{:S(2)}, u32[]{:S(2)}) collective-permute-start(bf16[1,16,2304]{2,1,0:T(8,128)(2,1)S(1)} %get-tuple-element.13), channel_id=1, source_target_pairs={{0,16},{4,20},{8,24},{12,28},{16,0},{20,4},{24,8},{28,12},{1,17},{... | collective-permute-start | bytes 221192 | tf_op jit(solution)/shard_map/ppermute | solution.py:164
  49.8 2.7 %collective-permute-start.9 = (bf16[1,16,2304]{2,1,0:T(8,128)(2,1)S(1)}, bf16[1,16,2304]{2,1,0:T(8,128)(2,1)S(1)}, u32[]{:S(2)}, u32[]{:S(2)}) collective-permute-start(bf16[1,16,2304]{2,1,0:T(8,128)(2,1)S(1)} %get-tuple-element.15), channel_id=1, source_target_pairs={{0,8},{4,12},{8,0},{12,4},{16,24},{20,28},{24,16},{28,20},{1,9},{5... | collective-permute-start | bytes 221192 | tf_op jit(solution)/shard_map/ppermute | solution.py:164
  52.6 0.9 %collective-permute-start.8 = (bf16[1,16,2304]{2,1,0:T(8,128)(2,1)S(1)}, bf16[1,16,2304]{2,1,0:T(8,128)(2,1)S(1)}, u32[]{:S(2)}, u32[]{:S(2)}) collective-permute-start(bf16[1,16,2304]{2,1,0:T(8,128)(2,1)S(1)} %get-tuple-element.10), channel_id=1, source_target_pairs={{0,4},{4,0},{8,12},{12,8},{16,20},{20,16},{24,28},{28,24},{1,5},{5... | collective-permute-start | bytes 221192 | tf_op jit(solution)/shard_map/ppermute | solution.py:164
  53.8 1.1 %collective-permute-done.10 = bf16[1,16,2304]{2,1,0:T(8,128)(2,1)S(1)} collective-permute-done((bf16[1,16,2304]{2,1,0:T(8,128)(2,1)S(1)}, bf16[1,16,2304]{2,1,0:T(8,128)(2,1)S(1)}, u32[]{:S(2)}, u32[]{:S(2)}) %collective-permute-start.10) | collective-permute-done | bytes 73760 | tf_op jit(solution)/shard_map/ppermute | solution.py:164
  55.6 1.3 %collective-permute-done.8 = bf16[1,16,2304]{2,1,0:T(8,128)(2,1)S(1)} collective-permute-done((bf16[1,16,2304]{2,1,0:T(8,128)(2,1)S(1)}, bf16[1,16,2304]{2,1,0:T(8,128)(2,1)S(1)}, u32[]{:S(2)}, u32[]{:S(2)}) %collective-permute-start.8) | collective-permute-done | bytes 73760 | tf_op jit(solution)/shard_map/ppermute | solution.py:164
  58.3 1.7 %fusion.4 = bf16[128,2048]{0,1:T(8,128)(2,1)S(1)} fusion(f32[128,2048]{0,1:T(8,128)S(1)} %fusion.28, f32[128,2048]{0,1:T(8,128)S(1)} %collective-permute-done.5, f32[128,2048]{0,1:T(8,128)S(1)} %collective-permute-done, bf16[128,256]{1,0:T(8,128)(2,1)S(1)} %copy-done.1, bf16[8192,256]{1,0:T(8,128)(2,1)} %param.8, s32[]{:T(128)S(6)} %select_n.78), kind=kOutput, calls=%fused_computation.9 | convolution fusion | flops 135266304 | bytes 4784132 | tf_op jit(solution)/shard_map/dot_general | solution.py:78
  59.9 1.0 %copy.16 = bf16[128,2048]{1,0:T(8,128)(2,1)} copy(bf16[128,2048]{0,1:T(8,128)(2,1)S(1)} %fusion.4) | data formatting | bytes 1048576
  (46 shorter events, 5.5 us)
Async XLA Ops:
  0.6 23.7 %copy-start = (bf16[128,2048]{1,0:T(8,128)(2,1)S(1)}, bf16[128,2048]{1,0:T(8,128)(2,1)}, u32[]{:S(2)}) copy-start(bf16[128,2048]{1,0:T(8,128)(2,1)} %param.6) | copy-start | bytes 1572868
  0.6 24.0 %copy-start.1 = (bf16[128,256]{1,0:T(8,128)(2,1)S(1)}, bf16[128,256]{1,0:T(8,128)(2,1)}, u32[]{:S(2)}) copy-start(bf16[128,256]{1,0:T(8,128)(2,1)} %param.7) | copy-start | bytes 196612
  2.3 7.9 %collective-permute-start.2 = (bf16[1,16,2304]{2,1,0:T(8,128)(2,1)S(1)}, bf16[1,16,2304]{2,1,0:T(8,128)(2,1)S(1)}, u32[]{:S(2)}, u32[]{:S(2)}) collective-permute-start(bf16[1,16,2304]{2,1,0:T(8,128)(2,1)S(1)} %constant_dynamic-update-slice_fusion), channel_id=1, source_target_pairs={{0,16},{4,20},{8,24},{12,28},{16,0},{20,4},{24,8},{28,12},{1,17},{... | collective-permute-start | bytes 221192 | tf_op jit(solution)/shard_map/ppermute | solution.py:41
  10.2 5.2 %collective-permute-start.3 = (bf16[2,16,2304]{2,1,0:T(8,128)(2,1)S(1)}, bf16[2,16,2304]{2,1,0:T(8,128)(2,1)S(1)}, u32[]{:S(2)}, u32[]{:S(2)}) collective-permute-start(bf16[2,16,2304]{2,1,0:T(8,128)(2,1)S(1)} %pad_maximum_fusion.2), channel_id=1, source_target_pairs={{0,8},{4,12},{8,0},{12,4},{16,24},{20,28},{24,16},{28,20},{1,9},{5... | collective-permute-start | bytes 442376 | tf_op jit(solution)/shard_map/ppermute | solution.py:41
  15.5 6.9 %collective-permute-start.4 = (bf16[4,16,2304]{2,1,0:T(8,128)(2,1)S(1)}, bf16[4,16,2304]{2,1,0:T(8,128)(2,1)}, u32[]{:S(2)}, u32[]{:S(2)}) collective-permute-start(bf16[4,16,2304]{2,1,0:T(8,128)(2,1)S(1)} %pad_maximum_fusion.1), channel_id=1, source_target_pairs={{0,4},{4,0},{8,12},{12,8},{16,20},{20,16},{24,28},{28,24},{1,5},{5... | collective-permute-start | bytes 884744 | tf_op jit(solution)/shard_map/ppermute | solution.py:41
  18.9 5.7 %collective-permute-start.1 = (f32[128,2048]{0,1:T(8,128)S(1)}, f32[128,2048]{0,1:T(8,128)S(1)}, u32[]{:S(2)}, u32[]{:S(2)}) collective-permute-start(f32[128,2048]{0,1:T(8,128)S(1)} %convolution_bitcast_fusion.1), channel_id=1, source_target_pairs={{0,1},{1,0},{2,3},{3,2},{4,5},{5,4},{6,7},{7,6},{8,9},{9,8},{10,11... | collective-permute-start | bytes 3145736 | tf_op jit(solution)/shard_map/ppermute | solution.py:90
  27.3 2.2 %collective-permute-start.6 = (f32[1,128,32]{1,2,0:T(8,128)S(1)}, f32[1,128,32]{1,2,0:T(8,128)S(1)}, u32[]{:S(2)}, u32[]{:S(2)}) collective-permute-start(f32[1,128,32]{1,2,0:T(8,128)S(1)} %pad_maximum_fusion.3), channel_id=1, source_target_pairs={{0,1},{1,0},{2,3},{3,2},{4,5},{5,4},{6,7},{7,6},{8,9},{9,8},{10,11... | collective-permute-start | bytes 49160 | tf_op jit(solution)/shard_map/ppermute | solution.py:62
  29.0 29.3 %collective-permute-start = (f32[128,2048]{0,1:T(8,128)S(1)}, f32[128,2048]{0,1:T(8,128)S(1)}, u32[]{:S(2)}, u32[]{:S(2)}) collective-permute-start(f32[128,2048]{0,1:T(8,128)S(1)} %convolution_bitcast_fusion.3), channel_id=1, source_target_pairs={{0,1},{1,0},{2,3},{3,2},{4,5},{5,4},{6,7},{7,6},{8,9},{9,8},{10,11... | collective-permute-start | bytes 3145736 | tf_op jit(solution)/shard_map/ppermute | solution.py:90
  29.6 3.8 %collective-permute-start.7 = (f32[1,128,32]{1,2,0:T(8,128)S(1)}, f32[1,128,32]{1,2,0:T(8,128)S(1)}, u32[]{:S(2)}, u32[]{:S(2)}) collective-permute-start(f32[1,128,32]{1,2,0:T(8,128)S(1)} %add.109), channel_id=1, source_target_pairs={{0,2},{1,3},{2,0},{3,1},{4,6},{5,7},{6,4},{7,5},{8,10},{9,11},{10,... | collective-permute-start | bytes 49160 | tf_op jit(solution)/shard_map/ppermute | solution.py:62
  31.5 26.8 %collective-permute-start.5 = (f32[128,2048]{0,1:T(8,128)}, f32[128,2048]{0,1:T(8,128)S(1)}, u32[]{:S(2)}, u32[]{:S(2)}) collective-permute-start(f32[128,2048]{0,1:T(8,128)} %fusion.3), channel_id=1, source_target_pairs={{0,2},{1,3},{2,0},{3,1},{4,6},{5,7},{6,4},{7,5},{8,10},{9,11},{10,... | collective-permute-start | bytes 3145736 | tf_op jit(solution)/shard_map/ppermute | solution.py:90
  34.0 8.7 %collective-permute-start.14 = (bf16[1,16,2304]{2,1,0:T(8,128)(2,1)S(1)}, bf16[1,16,2304]{2,1,0:T(8,128)(2,1)S(1)}, u32[]{:S(2)}, u32[]{:S(2)}) collective-permute-start(bf16[1,16,2304]{2,1,0:T(8,128)(2,1)S(1)} %fusion.27), channel_id=1, source_target_pairs={{0,28},{4,24},{8,20},{12,16},{16,12},{20,8},{24,4},{28,0},{1,29},{... | collective-permute-start | bytes 221192 | tf_op jit(solution)/shard_map/ppermute | solution.py:164
  40.0 9.6 %collective-permute-start.13 = (bf16[1,16,2304]{2,1,0:T(8,128)(2,1)S(1)}, bf16[1,16,2304]{2,1,0:T(8,128)(2,1)S(1)}, u32[]{:S(2)}, u32[]{:S(2)}) collective-permute-start(bf16[1,16,2304]{2,1,0:T(8,128)(2,1)S(1)} %get-tuple-element.11), channel_id=1, source_target_pairs={{0,24},{4,28},{8,16},{12,20},{16,8},{20,12},{24,0},{28,4},{1,25},{... | collective-permute-start | bytes 221192 | tf_op jit(solution)/shard_map/ppermute | solution.py:164
  40.1 9.7 %collective-permute-start.12 = (bf16[1,16,2304]{2,1,0:T(8,128)(2,1)S(1)}, bf16[1,16,2304]{2,1,0:T(8,128)(2,1)S(1)}, u32[]{:S(2)}, u32[]{:S(2)}) collective-permute-start(bf16[1,16,2304]{2,1,0:T(8,128)(2,1)S(1)} %get-tuple-element.12), channel_id=1, source_target_pairs={{0,20},{4,16},{8,28},{12,24},{16,4},{20,0},{24,12},{28,8},{1,21},{... | collective-permute-start | bytes 221192 | tf_op jit(solution)/shard_map/ppermute | solution.py:164
  42.7 9.9 %collective-permute-start.11 = (bf16[1,16,2304]{2,1,0:T(8,128)(2,1)S(1)}, bf16[1,16,2304]{2,1,0:T(8,128)(2,1)S(1)}, u32[]{:S(2)}, u32[]{:S(2)}) collective-permute-start(bf16[1,16,2304]{2,1,0:T(8,128)(2,1)S(1)} %get-tuple-element.13), channel_id=1, source_target_pairs={{0,16},{4,20},{8,24},{12,28},{16,0},{20,4},{24,8},{28,12},{1,17},{... | collective-permute-start | bytes 221192 | tf_op jit(solution)/shard_map/ppermute | solution.py:164
  49.6 5.3 %collective-permute-start.10 = (bf16[1,16,2304]{2,1,0:T(8,128)(2,1)S(1)}, bf16[1,16,2304]{2,1,0:T(8,128)(2,1)S(1)}, u32[]{:S(2)}, u32[]{:S(2)}) collective-permute-start(bf16[1,16,2304]{2,1,0:T(8,128)(2,1)S(1)} %get-tuple-element.14), channel_id=1, source_target_pairs={{0,12},{4,8},{8,4},{12,0},{16,28},{20,24},{24,20},{28,16},{1,13},{... | collective-permute-start | bytes 221192 | tf_op jit(solution)/shard_map/ppermute | solution.py:164
  49.8 5.8 %collective-permute-start.9 = (bf16[1,16,2304]{2,1,0:T(8,128)(2,1)S(1)}, bf16[1,16,2304]{2,1,0:T(8,128)(2,1)S(1)}, u32[]{:S(2)}, u32[]{:S(2)}) collective-permute-start(bf16[1,16,2304]{2,1,0:T(8,128)(2,1)S(1)} %get-tuple-element.15), channel_id=1, source_target_pairs={{0,8},{4,12},{8,0},{12,4},{16,24},{20,28},{24,16},{28,20},{1,9},{5... | collective-permute-start | bytes 221192 | tf_op jit(solution)/shard_map/ppermute | solution.py:164
  52.6 4.4 %collective-permute-start.8 = (bf16[1,16,2304]{2,1,0:T(8,128)(2,1)S(1)}, bf16[1,16,2304]{2,1,0:T(8,128)(2,1)S(1)}, u32[]{:S(2)}, u32[]{:S(2)}) collective-permute-start(bf16[1,16,2304]{2,1,0:T(8,128)(2,1)S(1)} %get-tuple-element.10), channel_id=1, source_target_pairs={{0,4},{4,0},{8,12},{12,8},{16,20},{20,16},{24,28},{28,24},{1,5},{5... | collective-permute-start | bytes 221192 | tf_op jit(solution)/shard_map/ppermute | solution.py:164

commit v20 on v16

--- a/solution.py
+++ b/solution.py
@@ -62,7 +62,7 @@
 
 
 def _frozen_term(cotangent, weight, axis, size, ready=None):
-    if size & (size - 1) != 0:
+    if size & (size - 1) != 0 or size == 1:
         partial = lax.dot_general(
             cotangent, weight, (((1,), (1,)), ((), ())), preferred_element_type=jnp.float32
         )
@@ -76,8 +76,13 @@
             cotangent, piece, (((1,), (1,)), ((), ())), preferred_element_type=jnp.float32
         )
 
-    held = [term(me ^ e) for e in range(size)]
-    step = 0
+    pieces = [lax.dynamic_slice_in_dim(weight, (me ^ e) * rows, rows, axis=0) for e in range(1, size, 2)]
+    leaving = jnp.einsum(
+        "nk,bdk->bnd", cotangent, jnp.stack(pieces, 0), preferred_element_type=jnp.float32
+    )
+    got = lax.ppermute(leaving, axis, [(i, i ^ 1) for i in range(size)])
+    held = [term(me ^ e) + got[m] for m, e in enumerate(range(0, size, 2))]
+    step = 1
     while len(held) > 1:
         if step == 1 and ready is not None:
             *leaving, ready = lax.optimization_barrier((*held[1::2], ready))

time: 56.7 us -> 58 us (1.023)
  waiting for transfers between devices: 14.2 us -> 17.6 us
  starting transfers between devices: 26.5 us -> 23.3 us
  local copies, waits for them, and re-layouts: 2.82 us -> 4.13 us
    dot_general x4 -> x2, matrix products: 7.64 us -> 5.05 us  [term(): lax.dot_general(cotangent, piece, (((1,), (1,)), ((), ())), preferred_ele...]
    ppermute x7, starting transfers between devices: 16.1 us -> 13.6 us  [on_device(): lax.ppermute(outgoing.astype(jnp.bfloat16), 'dp', pairs).astype(jnp.float32)]
    ppermute x3, waiting for transfers between devices: 3.71 us -> 5.85 us  [_gather_dp(): got.append(lax.ppermute(pair, axis, [(i, i ^ shift) for i in range(size)]))]
    dot_general x0 -> x1, matrix products: none -> 2.04 us  [_frozen_term(): jnp.einsum('nk,bdk->bnd', cotangent, jnp.stack(pieces, 0), preferred_elem...]
    ppermute x7, waiting for transfers between devices: 5.03 us -> 3.04 us  [on_device(): lax.ppermute(outgoing.astype(jnp.bfloat16), 'dp', pairs).astype(jnp.float32)]
    another operation x1 -> x2, local copies, waits for them, and re-layouts: 0.01 us -> 1.75 us  [the longest x1 1.75 us: _frozen_term(): jnp.stack(pieces, 0)]
    ppermute x3 -> x1, waiting for transfers between devices: 0.01 us -> 1.45 us  [_frozen_term(): got = [lax.ppermute(held[e], axis, pairs) for e in range(1, len(held), 2)]]
    dot_general x1, matrix products: 0.35 us -> 1.58 us  [on_device(): jnp.einsum('bnr,brd->bnd', low_out_b, sel_down, preferred_element_type=jn...]
  transfers between devices with their start and end apart: 16 -> 15, of which waited for: 10 -> 11; matrix products, arithmetic and copies ran while one was open for 13% -> 9% of each run, Pallas kernels for 0% -> 0%
where the time goes in v20:
time: 58 us; the launch traced here: 57.7 us
  starting transfers between devices  23.3 us (40%)
  waiting for transfers between devices  17.6 us (30%)
  matrix products  9.49 us (16%)
  local copies, waits for them, and re-layouts  4.13 us (7%)
  other arithmetic  1.67 us (3%)
  between operations  1.56 us (3%)
    ppermute x7, starting transfers between devices, on_device(): lax.ppermute(outgoing.astype(jnp.bfloat16), 'dp', pairs).astype(jnp.float32)  13.6 us
    ppermute x3, waiting for transfers between devices, _gather_dp(): got.append(lax.ppermute(pair, axis, [(i, i ^ shift) for i in range(size)]))  5.85 us
    dot_general x2, matrix products, term(): lax.dot_general(cotangent, piece, (((1,), (1,)), ((), ())), preferred_ele...  5.05 us
    ppermute x1, waiting for transfers between devices, _gather_dp(): lax.ppermute(local, axis, [(i, i ^ half) for i in range(size)])  4.52 us
    ppermute x1, starting transfers between devices, _gather_dp(): lax.ppermute(local, axis, [(i, i ^ half) for i in range(size)])  3.65 us
    ppermute x3, starting transfers between devices, _gather_dp(): got.append(lax.ppermute(pair, axis, [(i, i ^ shift) for i in range(size)]))  3.55 us
    ppermute x7, waiting for transfers between devices, on_device(): lax.ppermute(outgoing.astype(jnp.bfloat16), 'dp', pairs).astype(jnp.float32)  3.04 us
    ppermute x2, waiting for transfers between devices, _psum_small(): lax.ppermute(total, axis, [(i, i ^ step) for i in range(size)])  2.68 us
  transfers between devices with their start and end apart: 15, of which 11 were waited for; matrix products, arithmetic and copies ran while one was open for 9% of the time, Pallas kernels for 0%

profile of v20, /device:TPU:0, one launch (start us, length us, event | category | flops | bytes accessed | tf_op | source)
XLA Modules:
  0.0 57.7 jit_solution(11597919134699333566)
XLA Ops:
  0.7 1.8 %dynamic-slice_bitcast_fusion.1 = (bf16[1,2048,256]{2,1,0:T(8,128)(2,1)S(1)}, bf16[1,2048,256]{2,1,0:T(8,128)(2,1)S(1)}) fusion(bf16[8192,256]{1,0:T(8,128)(2,1)} %param.8, s32[]{:T(128)S(6)} %select_n.79, s32[]{:T(128)S(6)} %select_n.80), kind=kLoop, calls=%fused_computation.26 | loop fusion | bytes 4194312 | tf_op jit(solution)/shard_map/stack | solution.py:81
  2.5 2.0 %convolution_bitcast_fusion = f32[2,128,2048]{1,2,0:T(8,128)} fusion(bf16[1,2048,256]{2,1,0:T(8,128)(2,1)S(1)} %get-tuple-element.11, bf16[1,2048,256]{2,1,0:T(8,128)(2,1)S(1)} %get-tuple-element.10, bf16[128,256]{1,0:T(8,128)(2,1)S(1)} %copy-done.3), kind=kOutput, calls=%fused_computation | convolution fusion | flops 269484032 | bytes 4259840 | tf_op jit(solution)/shard_map/nk,bdk->bnd/dot_general | solution.py:80
  5.0 3.6 %collective-permute-start.1 = (bf16[1,16,2304]{2,1,0:T(8,128)(2,1)S(1)}, bf16[1,16,2304]{2,1,0:T(8,128)(2,1)S(1)}, u32[]{:S(2)}, u32[]{:S(2)}) collective-permute-start(bf16[1,16,2304]{2,1,0:T(8,128)(2,1)S(1)} %constant_dynamic-update-slice_fusion), channel_id=1, source_target_pairs={{0,16},{4,20},{8,24},{12,28},{16,0},{20,4},{24,8},{28,12},{1,17},{... | collective-permute-start | bytes 221192 | tf_op jit(solution)/shard_map/ppermute | solution.py:37
  8.6 4.5 %collective-permute-done.1 = bf16[1,16,2304]{2,1,0:T(8,128)(2,1)S(1)} collective-permute-done((bf16[1,16,2304]{2,1,0:T(8,128)(2,1)S(1)}, bf16[1,16,2304]{2,1,0:T(8,128)(2,1)S(1)}, u32[]{:S(2)}, u32[]{:S(2)}) %collective-permute-start.1) | collective-permute-done | bytes 73760 | tf_op jit(solution)/shard_map/ppermute | solution.py:37
  13.2 1.6 %collective-permute-start.4 = (bf16[2,16,2304]{2,1,0:T(8,128)(2,1)S(1)}, bf16[2,16,2304]{2,1,0:T(8,128)(2,1)S(1)}, u32[]{:S(2)}, u32[]{:S(2)}) collective-permute-start(bf16[2,16,2304]{2,1,0:T(8,128)(2,1)S(1)} %pad_maximum_fusion.1), channel_id=1, source_target_pairs={{0,4},{4,0},{8,12},{12,8},{16,20},{20,16},{24,28},{28,24},{1,5},{5... | collective-permute-start | bytes 442376 | tf_op jit(solution)/shard_map/ppermute | solution.py:41
  15.5 1.2 %collective-permute-start.2 = (bf16[2,16,2304]{2,1,0:T(8,128)(2,1)S(1)}, bf16[2,16,2304]{2,1,0:T(8,128)(2,1)S(1)}, u32[]{:S(2)}, u32[]{:S(2)}) collective-permute-start(bf16[2,16,2304]{2,1,0:T(8,128)(2,1)S(1)} %pad_maximum_fusion.1), channel_id=1, source_target_pairs={{0,12},{4,8},{8,4},{12,0},{16,28},{20,24},{24,20},{28,16},{1,13},{... | collective-permute-start | bytes 442376 | tf_op jit(solution)/shard_map/ppermute | solution.py:41
  17.4 1.7 %collective-permute-done.4 = bf16[2,16,2304]{2,1,0:T(8,128)(2,1)S(1)} collective-permute-done((bf16[2,16,2304]{2,1,0:T(8,128)(2,1)S(1)}, bf16[2,16,2304]{2,1,0:T(8,128)(2,1)S(1)}, u32[]{:S(2)}, u32[]{:S(2)}) %collective-permute-start.4) | collective-permute-done | bytes 147488 | tf_op jit(solution)/shard_map/ppermute | solution.py:41
  19.1 2.5 %collective-permute-done.3 = bf16[2,16,2304]{2,1,0:T(8,128)(2,1)S(1)} collective-permute-done((bf16[2,16,2304]{2,1,0:T(8,128)(2,1)S(1)}, bf16[2,16,2304]{2,1,0:T(8,128)(2,1)S(1)}, u32[]{:S(2)}, u32[]{:S(2)}) %collective-permute-start.3) | collective-permute-done | bytes 147488 | tf_op jit(solution)/shard_map/ppermute | solution.py:41
  21.6 1.7 %collective-permute-done.2 = bf16[2,16,2304]{2,1,0:T(8,128)(2,1)S(1)} collective-permute-done((bf16[2,16,2304]{2,1,0:T(8,128)(2,1)S(1)}, bf16[2,16,2304]{2,1,0:T(8,128)(2,1)S(1)}, u32[]{:S(2)}, u32[]{:S(2)}) %collective-permute-start.2) | collective-permute-done | bytes 147488 | tf_op jit(solution)/shard_map/ppermute | solution.py:41
  23.7 3.4 %fusion.5 = f32[128,2048]{0,1:T(8,128)} fusion(f32[2,128,2048]{1,2,0:T(8,128)S(1)} %collective-permute-done, bf16[128,256]{1,0:T(8,128)(2,1)S(1)} %copy-done.3, bf16[8192,256]{1,0:T(8,128)(2,1)} %param.8, s32[]{:T(128)S(6)} %select_n.81), kind=kOutput, calls=%fused_computation.18 | convolution fusion | flops 134479872 | bytes 3211268 | tf_op jit(solution)/shard_map/dot_general | solution.py:75
  27.1 1.2 %collective-permute-done.6 = f32[1,128,32]{1,2,0:T(8,128)S(1)} collective-permute-done((f32[1,128,32]{1,2,0:T(8,128)S(1)}, f32[1,128,32]{1,2,0:T(8,128)S(1)}, u32[]{:S(2)}, u32[]{:S(2)}) %collective-permute-start.6) | collective-permute-done | bytes 16416 | tf_op jit(solution)/shard_map/ppermute | solution.py:59
  28.3 1.3 %collective-permute-start.7 = (f32[1,128,32]{1,2,0:T(8,128)S(1)}, f32[1,128,32]{1,2,0:T(8,128)S(1)}, u32[]{:S(2)}, u32[]{:S(2)}) collective-permute-start(f32[1,128,32]{1,2,0:T(8,128)S(1)} %add.109), channel_id=1, source_target_pairs={{0,2},{1,3},{2,0},{3,1},{4,6},{5,7},{6,4},{7,5},{8,10},{9,11},{10,... | collective-permute-start | bytes 49160 | tf_op jit(solution)/shard_map/ppermute | solution.py:59
  30.6 1.5 %collective-permute-done.7 = f32[1,128,32]{1,2,0:T(8,128)S(1)} collective-permute-done((f32[1,128,32]{1,2,0:T(8,128)S(1)}, f32[1,128,32]{1,2,0:T(8,128)S(1)}, u32[]{:S(2)}, u32[]{:S(2)}) %collective-permute-start.7) | collective-permute-done | bytes 16416 | tf_op jit(solution)/shard_map/ppermute | solution.py:59
  33.2 4.7 %collective-permute-start.14 = (bf16[1,16,2304]{2,1,0:T(8,128)(2,1)S(1)}, bf16[1,16,2304]{2,1,0:T(8,128)(2,1)S(1)}, u32[]{:S(2)}, u32[]{:S(2)}) collective-permute-start(bf16[1,16,2304]{2,1,0:T(8,128)(2,1)S(1)} %fusion.30), channel_id=1, source_target_pairs={{0,28},{4,24},{8,20},{12,16},{16,12},{20,8},{24,4},{28,0},{1,29},{... | collective-permute-start | bytes 221192 | tf_op jit(solution)/shard_map/ppermute | solution.py:166
  38.6 0.8 %collective-permute-start.12 = (bf16[1,16,2304]{2,1,0:T(8,128)(2,1)S(1)}, bf16[1,16,2304]{2,1,0:T(8,128)(2,1)S(1)}, u32[]{:S(2)}, u32[]{:S(2)}) collective-permute-start(bf16[1,16,2304]{2,1,0:T(8,128)(2,1)S(1)} %get-tuple-element.14), channel_id=1, source_target_pairs={{0,20},{4,16},{8,28},{12,24},{16,4},{20,0},{24,12},{28,8},{1,21},{... | collective-permute-start | bytes 221192 | tf_op jit(solution)/shard_map/ppermute | solution.py:166
  39.4 1.6 %convolution_bitcast_fusion.3 = f32[128,2048]{0,1:T(8,128)S(1)} fusion(bf16[128,256]{1,0:T(8,128)(2,1)S(1)} %copy-done.3, bf16[8192,256]{1,0:T(8,128)(2,1)} %param.8, s32[]{:T(128)S(6)} %select_n.78), kind=kOutput, calls=%fused_computation.3 | convolution fusion | flops 134217728 | bytes 2162692 | tf_op jit(solution)/shard_map/dot_general | solution.py:75
  41.0 2.3 %collective-permute-start.11 = (bf16[1,16,2304]{2,1,0:T(8,128)(2,1)S(1)}, bf16[1,16,2304]{2,1,0:T(8,128)(2,1)S(1)}, u32[]{:S(2)}, u32[]{:S(2)}) collective-permute-start(bf16[1,16,2304]{2,1,0:T(8,128)(2,1)S(1)} %get-tuple-element.15), channel_id=1, source_target_pairs={{0,16},{4,20},{8,24},{12,28},{16,0},{20,4},{24,8},{28,12},{1,17},{... | collective-permute-start | bytes 221192 | tf_op jit(solution)/shard_map/ppermute | solution.py:166
  43.3 2.4 %collective-permute-start.10 = (bf16[1,16,2304]{2,1,0:T(8,128)(2,1)S(1)}, bf16[1,16,2304]{2,1,0:T(8,128)(2,1)S(1)}, u32[]{:S(2)}, u32[]{:S(2)}) collective-permute-start(bf16[1,16,2304]{2,1,0:T(8,128)(2,1)S(1)} %get-tuple-element.16), channel_id=1, source_target_pairs={{0,12},{4,8},{8,4},{12,0},{16,28},{20,24},{24,20},{28,16},{1,13},{... | collective-permute-start | bytes 221192 | tf_op jit(solution)/shard_map/ppermute | solution.py:166
  45.7 1.8 %collective-permute-start.9 = (bf16[1,16,2304]{2,1,0:T(8,128)(2,1)S(1)}, bf16[1,16,2304]{2,1,0:T(8,128)(2,1)S(1)}, u32[]{:S(2)}, u32[]{:S(2)}) collective-permute-start(bf16[1,16,2304]{2,1,0:T(8,128)(2,1)S(1)} %get-tuple-element.17), channel_id=1, source_target_pairs={{0,8},{4,12},{8,0},{12,4},{16,24},{20,28},{24,16},{28,20},{1,9},{5... | collective-permute-start | bytes 221192 | tf_op jit(solution)/shard_map/ppermute | solution.py:166
  48.0 1.6 %collective-permute-start.8 = (bf16[1,16,2304]{2,1,0:T(8,128)(2,1)S(1)}, bf16[1,16,2304]{2,1,0:T(8,128)(2,1)S(1)}, u32[]{:S(2)}, u32[]{:S(2)}) collective-permute-start(bf16[1,16,2304]{2,1,0:T(8,128)(2,1)S(1)} %get-tuple-element.12), channel_id=1, source_target_pairs={{0,4},{4,0},{8,12},{12,8},{16,20},{20,16},{24,28},{28,24},{1,5},{5... | collective-permute-start | bytes 221192 | tf_op jit(solution)/shard_map/ppermute | solution.py:166
  50.6 1.7 %collective-permute-done.8 = bf16[1,16,2304]{2,1,0:T(8,128)(2,1)S(1)} collective-permute-done((bf16[1,16,2304]{2,1,0:T(8,128)(2,1)S(1)}, bf16[1,16,2304]{2,1,0:T(8,128)(2,1)S(1)}, u32[]{:S(2)}, u32[]{:S(2)}) %collective-permute-start.8) | collective-permute-done | bytes 73760 | tf_op jit(solution)/shard_map/ppermute | solution.py:166
  53.7 1.4 %collective-permute-done.5 = f32[128,2048]{0,1:T(8,128)} collective-permute-done((f32[128,2048]{0,1:T(8,128)}, f32[128,2048]{0,1:T(8,128)}, u32[]{:S(2)}, u32[]{:S(2)}) %collective-permute-start.5) | collective-permute-done | bytes 1048608 | tf_op jit(solution)/shard_map/ppermute | solution.py:92
  55.1 1.6 %fusion.9 = bf16[128,2048]{0,1:T(8,128)(2,1)S(1)} fusion(f32[128,2048]{0,1:T(8,128)} %collective-permute-done.5, f32[128,2048]{0,1:T(8,128)S(1)} %convolution_bitcast_fusion.3, f32[2,128,2048]{1,2,0:T(8,128)S(1)} %copy-done.2, bf16[1,16,2304]{2,1,0:T(8,128)(2,1)S(1)} %fusion.29, bf16[1,128,32]{1,2,0:T(8,128)(2,1)S(1)} %copy-done.6), kind=kOutput, calls=%fused_computation.23 | convolution fusion | flops 9437184 | bytes 3739648 | tf_op jit(solution)/shard_map/bnr,brd->bnd/dot_general | solution.py:137
  56.7 1.0 %copy.16 = bf16[128,2048]{1,0:T(8,128)(2,1)} copy(bf16[128,2048]{0,1:T(8,128)(2,1)S(1)} %fusion.9) | data formatting | bytes 1048576
  (57 shorter events, 7.1 us)
Async XLA Ops:
  0.6 22.8 %copy-start = (bf16[128,2048]{1,0:T(8,128)(2,1)S(1)}, bf16[128,2048]{1,0:T(8,128)(2,1)}, u32[]{:S(2)}) copy-start(bf16[128,2048]{1,0:T(8,128)(2,1)} %param.6) | copy-start | bytes 1572868
  0.7 1.8 %copy-start.3 = (bf16[128,256]{1,0:T(8,128)(2,1)S(1)}, bf16[128,256]{1,0:T(8,128)(2,1)}, u32[]{:S(2)}) copy-start(bf16[128,256]{1,0:T(8,128)(2,1)} %param.7) | copy-start | bytes 196612
  2.4 2.5 %copy-start.4 = (bf16[1,16,2048]{2,1,0:T(8,128)(2,1)S(1)}, bf16[1,16,2048]{2,1,0:T(8,128)(2,1)}, u32[]{:S(2)}) copy-start(bf16[1,16,2048]{2,1,0:T(8,128)(2,1)} %param.9) | copy-start | bytes 196612
  2.4 2.5 %copy-start.7 = (bf16[1,16,256]{2,1,0:T(8,128)(2,1)S(1)}, bf16[1,16,256]{2,1,0:T(8,128)(2,1)}, u32[]{:S(2)}) copy-start(bf16[1,16,256]{2,1,0:T(8,128)(2,1)} %param.10) | copy-start | bytes 24580
  4.5 19.2 %collective-permute-start = (f32[2,128,2048]{1,2,0:T(8,128)}, f32[2,128,2048]{1,2,0:T(8,128)S(1)}, u32[]{:S(2)}, u32[]{:S(2)}) collective-permute-start(f32[2,128,2048]{1,2,0:T(8,128)} %convolution_bitcast_fusion), channel_id=1, source_target_pairs={{0,1},{1,0},{2,3},{3,2},{4,5},{5,4},{6,7},{7,6},{8,9},{9,8},{10,11... | collective-permute-start | bytes 6291464 | tf_op jit(solution)/shard_map/ppermute | solution.py:83
  5.0 8.2 %collective-permute-start.1 = (bf16[1,16,2304]{2,1,0:T(8,128)(2,1)S(1)}, bf16[1,16,2304]{2,1,0:T(8,128)(2,1)S(1)}, u32[]{:S(2)}, u32[]{:S(2)}) collective-permute-start(bf16[1,16,2304]{2,1,0:T(8,128)(2,1)S(1)} %constant_dynamic-update-slice_fusion), channel_id=1, source_target_pairs={{0,16},{4,20},{8,24},{12,28},{16,0},{20,4},{24,8},{28,12},{1,17},{... | collective-permute-start | bytes 221192 | tf_op jit(solution)/shard_map/ppermute | solution.py:37
  13.2 5.9 %collective-permute-start.4 = (bf16[2,16,2304]{2,1,0:T(8,128)(2,1)S(1)}, bf16[2,16,2304]{2,1,0:T(8,128)(2,1)S(1)}, u32[]{:S(2)}, u32[]{:S(2)}) collective-permute-start(bf16[2,16,2304]{2,1,0:T(8,128)(2,1)S(1)} %pad_maximum_fusion.1), channel_id=1, source_target_pairs={{0,4},{4,0},{8,12},{12,8},{16,20},{20,16},{24,28},{28,24},{1,5},{5... | collective-permute-start | bytes 442376 | tf_op jit(solution)/shard_map/ppermute | solution.py:41
  14.8 6.8 %collective-permute-start.3 = (bf16[2,16,2304]{2,1,0:T(8,128)(2,1)S(1)}, bf16[2,16,2304]{2,1,0:T(8,128)(2,1)S(1)}, u32[]{:S(2)}, u32[]{:S(2)}) collective-permute-start(bf16[2,16,2304]{2,1,0:T(8,128)(2,1)S(1)} %pad_maximum_fusion.1), channel_id=1, source_target_pairs={{0,8},{4,12},{8,0},{12,4},{16,24},{20,28},{24,16},{28,20},{1,9},{5... | collective-permute-start | bytes 442376 | tf_op jit(solution)/shard_map/ppermute | solution.py:41
  15.5 7.8 %collective-permute-start.2 = (bf16[2,16,2304]{2,1,0:T(8,128)(2,1)S(1)}, bf16[2,16,2304]{2,1,0:T(8,128)(2,1)S(1)}, u32[]{:S(2)}, u32[]{:S(2)}) collective-permute-start(bf16[2,16,2304]{2,1,0:T(8,128)(2,1)S(1)} %pad_maximum_fusion.1), channel_id=1, source_target_pairs={{0,12},{4,8},{8,4},{12,0},{16,28},{20,24},{24,20},{28,16},{1,13},{... | collective-permute-start | bytes 442376 | tf_op jit(solution)/shard_map/ppermute | solution.py:41
  23.7 9.1 %copy-start.1 = (f32[2,128,2048]{1,2,0:T(8,128)}, f32[2,128,2048]{1,2,0:T(8,128)S(1)}, u32[]{:S(2)}) copy-start(f32[2,128,2048]{1,2,0:T(8,128)S(1)} %collective-permute-done) | copy-start | bytes 6291460
  27.1 1.2 %collective-permute-start.6 = (f32[1,128,32]{1,2,0:T(8,128)S(1)}, f32[1,128,32]{1,2,0:T(8,128)S(1)}, u32[]{:S(2)}, u32[]{:S(2)}) collective-permute-start(f32[1,128,32]{1,2,0:T(8,128)S(1)} %pad_maximum_fusion.2), channel_id=1, source_target_pairs={{0,1},{1,0},{2,3},{3,2},{4,5},{5,4},{6,7},{7,6},{8,9},{9,8},{10,11... | collective-permute-start | bytes 49160 | tf_op jit(solution)/shard_map/ppermute | solution.py:59
  28.3 3.7 %collective-permute-start.7 = (f32[1,128,32]{1,2,0:T(8,128)S(1)}, f32[1,128,32]{1,2,0:T(8,128)S(1)}, u32[]{:S(2)}, u32[]{:S(2)}) collective-permute-start(f32[1,128,32]{1,2,0:T(8,128)S(1)} %add.109), channel_id=1, source_target_pairs={{0,2},{1,3},{2,0},{3,1},{4,6},{5,7},{6,4},{7,5},{8,10},{9,11},{10,... | collective-permute-start | bytes 49160 | tf_op jit(solution)/shard_map/ppermute | solution.py:59
  29.8 25.3 %collective-permute-start.5 = (f32[128,2048]{0,1:T(8,128)}, f32[128,2048]{0,1:T(8,128)}, u32[]{:S(2)}, u32[]{:S(2)}) collective-permute-start(f32[128,2048]{0,1:T(8,128)} %fusion.5), channel_id=1, source_target_pairs={{0,2},{1,3},{2,0},{3,1},{4,6},{5,7},{6,4},{7,5},{8,10},{9,11},{10,... | collective-permute-start | bytes 3145736 | tf_op jit(solution)/shard_map/ppermute | solution.py:92
  32.1 0.6 %copy-start.5 = (bf16[1,128,32]{1,2,0:T(8,128)(2,1)}, bf16[1,128,32]{1,2,0:T(8,128)(2,1)S(1)}, u32[]{:S(2)}) copy-start(bf16[1,128,32]{1,2,0:T(8,128)(2,1)S(1)} %add_convert_fusion) | copy-start | bytes 24580
  33.2 10.1 %collective-permute-start.14 = (bf16[1,16,2304]{2,1,0:T(8,128)(2,1)S(1)}, bf16[1,16,2304]{2,1,0:T(8,128)(2,1)S(1)}, u32[]{:S(2)}, u32[]{:S(2)}) collective-permute-start(bf16[1,16,2304]{2,1,0:T(8,128)(2,1)S(1)} %fusion.30), channel_id=1, source_target_pairs={{0,28},{4,24},{8,20},{12,16},{16,12},{20,8},{24,4},{28,0},{1,29},{... | collective-permute-start | bytes 221192 | tf_op jit(solution)/shard_map/ppermute | solution.py:166
  38.6 7.1 %collective-permute-start.13 = (bf16[1,16,2304]{2,1,0:T(8,128)(2,1)}, bf16[1,16,2304]{2,1,0:T(8,128)(2,1)S(1)}, u32[]{:S(2)}, u32[]{:S(2)}) collective-permute-start(bf16[1,16,2304]{2,1,0:T(8,128)(2,1)} %get-tuple-element.13), channel_id=1, source_target_pairs={{0,24},{4,28},{8,16},{12,20},{16,8},{20,12},{24,0},{28,4},{1,25},{... | collective-permute-start | bytes 221192 | tf_op jit(solution)/shard_map/ppermute | solution.py:166
  38.6 9.4 %collective-permute-start.12 = (bf16[1,16,2304]{2,1,0:T(8,128)(2,1)S(1)}, bf16[1,16,2304]{2,1,0:T(8,128)(2,1)S(1)}, u32[]{:S(2)}, u32[]{:S(2)}) collective-permute-start(bf16[1,16,2304]{2,1,0:T(8,128)(2,1)S(1)} %get-tuple-element.14), channel_id=1, source_target_pairs={{0,20},{4,16},{8,28},{12,24},{16,4},{20,0},{24,12},{28,8},{1,21},{... | collective-permute-start | bytes 221192 | tf_op jit(solution)/shard_map/ppermute | solution.py:166
  41.0 8.7 %collective-permute-start.11 = (bf16[1,16,2304]{2,1,0:T(8,128)(2,1)S(1)}, bf16[1,16,2304]{2,1,0:T(8,128)(2,1)S(1)}, u32[]{:S(2)}, u32[]{:S(2)}) collective-permute-start(bf16[1,16,2304]{2,1,0:T(8,128)(2,1)S(1)} %get-tuple-element.15), channel_id=1, source_target_pairs={{0,16},{4,20},{8,24},{12,28},{16,0},{20,4},{24,8},{28,12},{1,17},{... | collective-permute-start | bytes 221192 | tf_op jit(solution)/shard_map/ppermute | solution.py:166
  43.3 6.6 %collective-permute-start.10 = (bf16[1,16,2304]{2,1,0:T(8,128)(2,1)S(1)}, bf16[1,16,2304]{2,1,0:T(8,128)(2,1)S(1)}, u32[]{:S(2)}, u32[]{:S(2)}) collective-permute-start(bf16[1,16,2304]{2,1,0:T(8,128)(2,1)S(1)} %get-tuple-element.16), channel_id=1, source_target_pairs={{0,12},{4,8},{8,4},{12,0},{16,28},{20,24},{24,20},{28,16},{1,13},{... | collective-permute-start | bytes 221192 | tf_op jit(solution)/shard_map/ppermute | solution.py:166
  45.7 4.9 %collective-permute-start.9 = (bf16[1,16,2304]{2,1,0:T(8,128)(2,1)S(1)}, bf16[1,16,2304]{2,1,0:T(8,128)(2,1)S(1)}, u32[]{:S(2)}, u32[]{:S(2)}) collective-permute-start(bf16[1,16,2304]{2,1,0:T(8,128)(2,1)S(1)} %get-tuple-element.17), channel_id=1, source_target_pairs={{0,8},{4,12},{8,0},{12,4},{16,24},{20,28},{24,16},{28,20},{1,9},{5... | collective-permute-start | bytes 221192 | tf_op jit(solution)/shard_map/ppermute | solution.py:166
  48.0 7.2 %copy-start.2 = (f32[2,128,2048]{1,2,0:T(8,128)S(1)}, f32[2,128,2048]{1,2,0:T(8,128)}, u32[]{:S(2)}) copy-start(f32[2,128,2048]{1,2,0:T(8,128)} %copy-done.1) | copy-start | bytes 6291460
  48.0 7.2 %copy-start.6 = (bf16[1,128,32]{1,2,0:T(8,128)(2,1)S(1)}, bf16[1,128,32]{1,2,0:T(8,128)(2,1)}, u32[]{:S(2)}) copy-start(bf16[1,128,32]{1,2,0:T(8,128)(2,1)} %copy-done.5) | copy-start | bytes 24580
  48.0 4.4 %collective-permute-start.8 = (bf16[1,16,2304]{2,1,0:T(8,128)(2,1)S(1)}, bf16[1,16,2304]{2,1,0:T(8,128)(2,1)S(1)}, u32[]{:S(2)}, u32[]{:S(2)}) collective-permute-start(bf16[1,16,2304]{2,1,0:T(8,128)(2,1)S(1)} %get-tuple-element.12), channel_id=1, source_target_pairs={{0,4},{4,0},{8,12},{12,8},{16,20},{20,16},{24,28},{28,24},{1,5},{5... | collective-permute-start | bytes 221192 | tf_op jit(solution)/shard_map/ppermute | solution.py:166

commit v21 on v16

--- a/solution.py
+++ b/solution.py
@@ -48,7 +48,7 @@
 
 
 def _psum_small(value, axis, size):
-    if size & (size - 1) != 0:
+    if True:
         total = value
         for _, pairs in _partners(size):
             total = total + lax.ppermute(value, axis, pairs)

time: 56.7 us -> 54.2 us (0.956)
  starting transfers between devices: 26.5 us -> 21.3 us
  waiting for transfers between devices: 14.2 us -> 16.5 us
    ppermute x7, starting transfers between devices: 16.1 us -> 9.99 us  [on_device(): lax.ppermute(outgoing.astype(jnp.bfloat16), 'dp', pairs).astype(jnp.float32)]
    ppermute x7, waiting for transfers between devices: 5.03 us -> 11.2 us  [on_device(): lax.ppermute(outgoing.astype(jnp.bfloat16), 'dp', pairs).astype(jnp.float32)]
    ppermute x1, waiting for transfers between devices: 3.91 us -> 1.28 us  [_gather_dp(): lax.ppermute(local, axis, [(i, i ^ half) for i in range(size)])]
    ppermute x2 -> x3, waiting for transfers between devices: 1.5 us -> 0.01 us  [_psum_small(): total = total + lax.ppermute(value, axis, pairs)]
    dot_general x4, matrix products: 7.64 us -> 8.91 us  [term(): lax.dot_general(cotangent, piece, (((1,), (1,)), ((), ())), preferred_ele...]
    dot_general x1, matrix products: 0.97 us -> 0.13 us  [on_device(): jnp.einsum('bnk,brk->bnr', cotangent_blocks, sel_up, preferred_element_ty...]
    ppermute x3, starting transfers between devices: 1.21 us -> 1.81 us  [_frozen_term(): got = [lax.ppermute(held[e], axis, pairs) for e in range(1, len(held), 2)]]
    ppermute x2 -> x3, starting transfers between devices: 1.56 us -> 1.88 us  [_psum_small(): total = total + lax.ppermute(value, axis, pairs)]
  transfers between devices with their start and end apart: 16 -> 17, of which waited for: 10 -> 10; matrix products, arithmetic and copies ran while one was open for 13% -> 19% of each run, Pallas kernels for 0% -> 0%
where the time goes in v21:
time: 54.2 us; the launch traced here: 53.9 us
  starting transfers between devices  21.3 us (39%)
  waiting for transfers between devices  16.5 us (30%)
  matrix products  10.1 us (19%)
  local copies, waits for them, and re-layouts  2.84 us (5%)
  other arithmetic  1.66 us (3%)
  between operations  1.54 us (3%)
    ppermute x7, waiting for transfers between devices, on_device(): lax.ppermute(outgoing.astype(jnp.bfloat16), 'dp', pairs).astype(jnp.float32)  11.2 us
    ppermute x7, starting transfers between devices, on_device(): lax.ppermute(outgoing.astype(jnp.bfloat16), 'dp', pairs).astype(jnp.float32)  9.99 us
    dot_general x4, matrix products, term(): lax.dot_general(cotangent, piece, (((1,), (1,)), ((), ())), preferred_ele...  8.91 us
    ppermute x1, starting transfers between devices, _gather_dp(): lax.ppermute(local, axis, [(i, i ^ half) for i in range(size)])  4.04 us
    ppermute x3, waiting for transfers between devices, _gather_dp(): got.append(lax.ppermute(pair, axis, [(i, i ^ shift) for i in range(size)]))  3.84 us
    ppermute x3, starting transfers between devices, _gather_dp(): got.append(lax.ppermute(pair, axis, [(i, i ^ shift) for i in range(size)]))  3.55 us
    unnamed x6, local copies, waits for them, and re-layouts  1.94 us
    ppermute x3, starting transfers between devices, _psum_small(): total = total + lax.ppermute(value, axis, pairs)  1.88 us
  transfers between devices with their start and end apart: 17, of which 10 were waited for; matrix products, arithmetic and copies ran while one was open for 19% of the time, Pallas kernels for 0%

profile of v21, /device:TPU:0, one launch (start us, length us, event | category | flops | bytes accessed | tf_op | source)
XLA Modules:
  0.0 53.9 jit_solution(6989866887748307751)
XLA Ops:
  0.7 0.9 %constant_dynamic-update-slice_fusion.1 = bf16[1,16,2304]{2,1,0:T(8,128)(2,1)S(1)} fusion(bf16[1,16,2048]{2,1,0:T(8,128)(2,1)} %param.9), kind=kLoop, calls=%fused_computation.71 | loop fusion | bytes 131072
  2.3 4.0 %collective-permute-start.2 = (bf16[1,16,2304]{2,1,0:T(8,128)(2,1)S(1)}, bf16[1,16,2304]{2,1,0:T(8,128)(2,1)S(1)}, u32[]{:S(2)}, u32[]{:S(2)}) collective-permute-start(bf16[1,16,2304]{2,1,0:T(8,128)(2,1)S(1)} %constant_dynamic-update-slice_fusion), channel_id=1, source_target_pairs={{0,16},{4,20},{8,24},{12,28},{16,0},{20,4},{24,8},{28,12},{1,17},{... | collective-permute-start | bytes 221192 | tf_op jit(solution)/shard_map/ppermute | solution.py:37
  6.3 2.6 %convolution_bitcast_fusion.1 = f32[128,2048]{0,1:T(8,128)} fusion(bf16[128,256]{1,0:T(8,128)(2,1)} %param.7, bf16[8192,256]{1,0:T(8,128)(2,1)} %param.8, s32[]{:T(128)S(6)} %select_n.81), kind=kOutput, calls=%fused_computation.1 | convolution fusion | flops 134217728 | bytes 2162692 | tf_op jit(solution)/shard_map/dot_general | solution.py:75
  8.9 1.3 %collective-permute-done.2 = bf16[1,16,2304]{2,1,0:T(8,128)(2,1)S(1)} collective-permute-done((bf16[1,16,2304]{2,1,0:T(8,128)(2,1)S(1)}, bf16[1,16,2304]{2,1,0:T(8,128)(2,1)S(1)}, u32[]{:S(2)}, u32[]{:S(2)}) %collective-permute-start.2) | collective-permute-done | bytes 73760 | tf_op jit(solution)/shard_map/ppermute | solution.py:37
  10.2 1.8 %collective-permute-start.5 = (bf16[2,16,2304]{2,1,0:T(8,128)(2,1)S(1)}, bf16[2,16,2304]{2,1,0:T(8,128)(2,1)S(1)}, u32[]{:S(2)}, u32[]{:S(2)}) collective-permute-start(bf16[2,16,2304]{2,1,0:T(8,128)(2,1)S(1)} %pad_maximum_fusion.1), channel_id=1, source_target_pairs={{0,4},{4,0},{8,12},{12,8},{16,20},{20,16},{24,28},{28,24},{1,5},{5... | collective-permute-start | bytes 442376 | tf_op jit(solution)/shard_map/ppermute | solution.py:41
  12.5 1.3 %collective-permute-start.3 = (bf16[2,16,2304]{2,1,0:T(8,128)(2,1)S(1)}, bf16[2,16,2304]{2,1,0:T(8,128)(2,1)S(1)}, u32[]{:S(2)}, u32[]{:S(2)}) collective-permute-start(bf16[2,16,2304]{2,1,0:T(8,128)(2,1)S(1)} %pad_maximum_fusion.1), channel_id=1, source_target_pairs={{0,12},{4,8},{8,4},{12,0},{16,28},{20,24},{24,20},{28,16},{1,13},{... | collective-permute-start | bytes 442376 | tf_op jit(solution)/shard_map/ppermute | solution.py:41
  13.8 1.6 %convolution_bitcast_fusion.3 = f32[128,2048]{0,1:T(8,128)S(1)} fusion(bf16[128,256]{1,0:T(8,128)(2,1)} %param.7, bf16[8192,256]{1,0:T(8,128)(2,1)} %param.8, s32[]{:T(128)S(6)} %select_n.79), kind=kOutput, calls=%fused_computation.3 | convolution fusion | flops 134217728 | bytes 2162692 | tf_op jit(solution)/shard_map/dot_general | solution.py:75
  16.2 1.9 %collective-permute-done.4 = bf16[2,16,2304]{2,1,0:T(8,128)(2,1)S(1)} collective-permute-done((bf16[2,16,2304]{2,1,0:T(8,128)(2,1)S(1)}, bf16[2,16,2304]{2,1,0:T(8,128)(2,1)S(1)}, u32[]{:S(2)}, u32[]{:S(2)}) %collective-permute-start.4) | collective-permute-done | bytes 147488 | tf_op jit(solution)/shard_map/ppermute | solution.py:41
  18.1 2.0 %collective-permute-done.3 = bf16[2,16,2304]{2,1,0:T(8,128)(2,1)S(1)} collective-permute-done((bf16[2,16,2304]{2,1,0:T(8,128)(2,1)S(1)}, bf16[2,16,2304]{2,1,0:T(8,128)(2,1)S(1)}, u32[]{:S(2)}, u32[]{:S(2)}) %collective-permute-start.3) | collective-permute-done | bytes 147488 | tf_op jit(solution)/shard_map/ppermute | solution.py:41
  20.5 3.0 %fusion.3 = f32[128,2048]{0,1:T(8,128)} fusion(f32[128,2048]{0,1:T(8,128)} %collective-permute-done.1, bf16[128,256]{1,0:T(8,128)(2,1)S(1)} %copy-done.1, bf16[8192,256]{1,0:T(8,128)(2,1)} %param.8, s32[]{:T(128)S(6)} %select_n.80), kind=kOutput, calls=%fused_computation.8 | convolution fusion | flops 134479872 | bytes 3211268 | tf_op jit(solution)/shard_map/dot_general | solution.py:75
  23.5 1.7 %collective-permute-start.8 = (f32[1,128,32]{1,2,0:T(8,128)S(1)}, f32[1,128,32]{1,2,0:T(8,128)S(1)}, u32[]{:S(2)}, u32[]{:S(2)}) collective-permute-start(f32[1,128,32]{1,2,0:T(8,128)S(1)} %pad_maximum_fusion.2), channel_id=1, source_target_pairs={{0,2},{1,3},{2,0},{3,1},{4,6},{5,7},{6,4},{7,5},{8,10},{9,11},{10,... | collective-permute-start | bytes 49160 | tf_op jit(solution)/shard_map/ppermute | solution.py:54
  25.5 1.7 %collective-permute-start.6 = (f32[128,2048]{0,1:T(8,128)}, f32[128,2048]{0,1:T(8,128)S(1)}, u32[]{:S(2)}, u32[]{:S(2)}) collective-permute-start(f32[128,2048]{0,1:T(8,128)} %fusion.3), channel_id=1, source_target_pairs={{0,2},{1,3},{2,0},{3,1},{4,6},{5,7},{6,4},{7,5},{8,10},{9,11},{10,... | collective-permute-start | bytes 3145736 | tf_op jit(solution)/shard_map/ppermute | solution.py:87
  27.9 4.6 %collective-permute-start.16 = (bf16[1,16,2304]{2,1,0:T(8,128)(2,1)S(1)}, bf16[1,16,2304]{2,1,0:T(8,128)(2,1)S(1)}, u32[]{:S(2)}, u32[]{:S(2)}) collective-permute-start(bf16[1,16,2304]{2,1,0:T(8,128)(2,1)S(1)} %fusion.27), channel_id=1, source_target_pairs={{0,28},{4,24},{8,20},{12,16},{16,12},{20,8},{24,4},{28,0},{1,29},{... | collective-permute-start | bytes 221192 | tf_op jit(solution)/shard_map/ppermute | solution.py:161
  32.6 0.9 %collective-permute-start.14 = (bf16[1,16,2304]{2,1,0:T(8,128)(2,1)S(1)}, bf16[1,16,2304]{2,1,0:T(8,128)(2,1)S(1)}, u32[]{:S(2)}, u32[]{:S(2)}) collective-permute-start(bf16[1,16,2304]{2,1,0:T(8,128)(2,1)S(1)} %get-tuple-element.12), channel_id=1, source_target_pairs={{0,20},{4,16},{8,28},{12,24},{16,4},{20,0},{24,12},{28,8},{1,21},{... | collective-permute-start | bytes 221192 | tf_op jit(solution)/shard_map/ppermute | solution.py:161
  33.5 2.1 %collective-permute-done.16 = bf16[1,16,2304]{2,1,0:T(8,128)(2,1)S(1)} collective-permute-done((bf16[1,16,2304]{2,1,0:T(8,128)(2,1)S(1)}, bf16[1,16,2304]{2,1,0:T(8,128)(2,1)S(1)}, u32[]{:S(2)}, u32[]{:S(2)}) %collective-permute-start.16) | collective-permute-done | bytes 73760 | tf_op jit(solution)/shard_map/ppermute | solution.py:161
  35.6 0.9 %collective-permute-start.13 = (bf16[1,16,2304]{2,1,0:T(8,128)(2,1)S(1)}, bf16[1,16,2304]{2,1,0:T(8,128)(2,1)S(1)}, u32[]{:S(2)}, u32[]{:S(2)}) collective-permute-start(bf16[1,16,2304]{2,1,0:T(8,128)(2,1)S(1)} %get-tuple-element.13), channel_id=1, source_target_pairs={{0,16},{4,20},{8,24},{12,28},{16,0},{20,4},{24,8},{28,12},{1,17},{... | collective-permute-start | bytes 221192 | tf_op jit(solution)/shard_map/ppermute | solution.py:161
  36.5 3.1 %collective-permute-done.15 = bf16[1,16,2304]{2,1,0:T(8,128)(2,1)S(1)} collective-permute-done((bf16[1,16,2304]{2,1,0:T(8,128)(2,1)S(1)}, bf16[1,16,2304]{2,1,0:T(8,128)(2,1)S(1)}, u32[]{:S(2)}, u32[]{:S(2)}) %collective-permute-start.15) | collective-permute-done | bytes 73760 | tf_op jit(solution)/shard_map/ppermute | solution.py:161
  39.6 2.8 %collective-permute-start.12 = (bf16[1,16,2304]{2,1,0:T(8,128)(2,1)S(1)}, bf16[1,16,2304]{2,1,0:T(8,128)(2,1)S(1)}, u32[]{:S(2)}, u32[]{:S(2)}) collective-permute-start(bf16[1,16,2304]{2,1,0:T(8,128)(2,1)S(1)} %get-tuple-element.14), channel_id=1, source_target_pairs={{0,12},{4,8},{8,4},{12,0},{16,28},{20,24},{24,20},{28,16},{1,13},{... | collective-permute-start | bytes 221192 | tf_op jit(solution)/shard_map/ppermute | solution.py:161
  42.4 1.4 %collective-permute-done.14 = bf16[1,16,2304]{2,1,0:T(8,128)(2,1)S(1)} collective-permute-done((bf16[1,16,2304]{2,1,0:T(8,128)(2,1)S(1)}, bf16[1,16,2304]{2,1,0:T(8,128)(2,1)S(1)}, u32[]{:S(2)}, u32[]{:S(2)}) %collective-permute-start.14) | collective-permute-done | bytes 73760 | tf_op jit(solution)/shard_map/ppermute | solution.py:161
  44.0 1.3 %collective-permute-done.13 = bf16[1,16,2304]{2,1,0:T(8,128)(2,1)S(1)} collective-permute-done((bf16[1,16,2304]{2,1,0:T(8,128)(2,1)S(1)}, bf16[1,16,2304]{2,1,0:T(8,128)(2,1)S(1)}, u32[]{:S(2)}, u32[]{:S(2)}) %collective-permute-start.13) | collective-permute-done | bytes 73760 | tf_op jit(solution)/shard_map/ppermute | solution.py:161
  46.4 1.8 %collective-permute-done.11 = bf16[1,16,2304]{2,1,0:T(8,128)(2,1)S(1)} collective-permute-done((bf16[1,16,2304]{2,1,0:T(8,128)(2,1)S(1)}, bf16[1,16,2304]{2,1,0:T(8,128)(2,1)S(1)}, u32[]{:S(2)}, u32[]{:S(2)}) %collective-permute-start.11) | collective-permute-done | bytes 73760 | tf_op jit(solution)/shard_map/ppermute | solution.py:161
  48.2 1.4 %collective-permute-done.10 = bf16[1,16,2304]{2,1,0:T(8,128)(2,1)S(1)} collective-permute-done((bf16[1,16,2304]{2,1,0:T(8,128)(2,1)S(1)}, bf16[1,16,2304]{2,1,0:T(8,128)(2,1)S(1)}, u32[]{:S(2)}, u32[]{:S(2)}) %collective-permute-start.10) | collective-permute-done | bytes 73760 | tf_op jit(solution)/shard_map/ppermute | solution.py:161
  51.2 1.7 %fusion.4 = bf16[128,2048]{0,1:T(8,128)(2,1)S(1)} fusion(f32[128,2048]{0,1:T(8,128)S(1)} %fusion.28, f32[128,2048]{0,1:T(8,128)S(1)} %collective-permute-done.6, f32[128,2048]{0,1:T(8,128)S(1)} %collective-permute-done, bf16[128,256]{1,0:T(8,128)(2,1)S(1)} %copy-done.1, bf16[8192,256]{1,0:T(8,128)(2,1)} %param.8, s32[]{:T(128)S(6)} %select_n.78), kind=kOutput, calls=%fused_computation.9 | convolution fusion | flops 135266304 | bytes 4784132 | tf_op jit(solution)/shard_map/dot_general | solution.py:75
  52.9 1.0 %copy.16 = bf16[128,2048]{1,0:T(8,128)(2,1)} copy(bf16[128,2048]{0,1:T(8,128)(2,1)S(1)} %fusion.4) | data formatting | bytes 1048576
  (48 shorter events, 5.5 us)
Async XLA Ops:
  0.6 19.6 %copy-start = (bf16[128,2048]{1,0:T(8,128)(2,1)S(1)}, bf16[128,2048]{1,0:T(8,128)(2,1)}, u32[]{:S(2)}) copy-start(bf16[128,2048]{1,0:T(8,128)(2,1)} %param.6) | copy-start | bytes 1572868
  0.6 19.5 %copy-start.1 = (bf16[128,256]{1,0:T(8,128)(2,1)S(1)}, bf16[128,256]{1,0:T(8,128)(2,1)}, u32[]{:S(2)}) copy-start(bf16[128,256]{1,0:T(8,128)(2,1)} %param.7) | copy-start | bytes 196612
  2.3 7.9 %collective-permute-start.2 = (bf16[1,16,2304]{2,1,0:T(8,128)(2,1)S(1)}, bf16[1,16,2304]{2,1,0:T(8,128)(2,1)S(1)}, u32[]{:S(2)}, u32[]{:S(2)}) collective-permute-start(bf16[1,16,2304]{2,1,0:T(8,128)(2,1)S(1)} %constant_dynamic-update-slice_fusion), channel_id=1, source_target_pairs={{0,16},{4,20},{8,24},{12,28},{16,0},{20,4},{24,8},{28,12},{1,17},{... | collective-permute-start | bytes 221192 | tf_op jit(solution)/shard_map/ppermute | solution.py:37
  8.9 11.6 %collective-permute-start.1 = (f32[128,2048]{0,1:T(8,128)}, f32[128,2048]{0,1:T(8,128)}, u32[]{:S(2)}, u32[]{:S(2)}) collective-permute-start(f32[128,2048]{0,1:T(8,128)} %convolution_bitcast_fusion.1), channel_id=1, source_target_pairs={{0,1},{1,0},{2,3},{3,2},{4,5},{5,4},{6,7},{7,6},{8,9},{9,8},{10,11... | collective-permute-start | bytes 3145736 | tf_op jit(solution)/shard_map/ppermute | solution.py:87
  10.2 6.0 %collective-permute-start.5 = (bf16[2,16,2304]{2,1,0:T(8,128)(2,1)S(1)}, bf16[2,16,2304]{2,1,0:T(8,128)(2,1)S(1)}, u32[]{:S(2)}, u32[]{:S(2)}) collective-permute-start(bf16[2,16,2304]{2,1,0:T(8,128)(2,1)S(1)} %pad_maximum_fusion.1), channel_id=1, source_target_pairs={{0,4},{4,0},{8,12},{12,8},{16,20},{20,16},{24,28},{28,24},{1,5},{5... | collective-permute-start | bytes 442376 | tf_op jit(solution)/shard_map/ppermute | solution.py:41
  12.0 6.1 %collective-permute-start.4 = (bf16[2,16,2304]{2,1,0:T(8,128)(2,1)S(1)}, bf16[2,16,2304]{2,1,0:T(8,128)(2,1)S(1)}, u32[]{:S(2)}, u32[]{:S(2)}) collective-permute-start(bf16[2,16,2304]{2,1,0:T(8,128)(2,1)S(1)} %pad_maximum_fusion.1), channel_id=1, source_target_pairs={{0,8},{4,12},{8,0},{12,4},{16,24},{20,28},{24,16},{28,20},{1,9},{5... | collective-permute-start | bytes 442376 | tf_op jit(solution)/shard_map/ppermute | solution.py:41
  12.5 7.6 %collective-permute-start.3 = (bf16[2,16,2304]{2,1,0:T(8,128)(2,1)S(1)}, bf16[2,16,2304]{2,1,0:T(8,128)(2,1)S(1)}, u32[]{:S(2)}, u32[]{:S(2)}) collective-permute-start(bf16[2,16,2304]{2,1,0:T(8,128)(2,1)S(1)} %pad_maximum_fusion.1), channel_id=1, source_target_pairs={{0,12},{4,8},{8,4},{12,0},{16,28},{20,24},{24,20},{28,16},{1,13},{... | collective-permute-start | bytes 442376 | tf_op jit(solution)/shard_map/ppermute | solution.py:41
  15.5 35.5 %collective-permute-start = (f32[128,2048]{0,1:T(8,128)S(1)}, f32[128,2048]{0,1:T(8,128)S(1)}, u32[]{:S(2)}, u32[]{:S(2)}) collective-permute-start(f32[128,2048]{0,1:T(8,128)S(1)} %convolution_bitcast_fusion.3), channel_id=1, source_target_pairs={{0,1},{1,0},{2,3},{3,2},{4,5},{5,4},{6,7},{7,6},{8,9},{9,8},{10,11... | collective-permute-start | bytes 3145736 | tf_op jit(solution)/shard_map/ppermute | solution.py:87
  23.5 3.8 %collective-permute-start.9 = (f32[1,128,32]{1,2,0:T(8,128)S(1)}, f32[1,128,32]{1,2,0:T(8,128)S(1)}, u32[]{:S(2)}, u32[]{:S(2)}) collective-permute-start(f32[1,128,32]{1,2,0:T(8,128)S(1)} %pad_maximum_fusion.2), channel_id=1, source_target_pairs={{0,3},{1,2},{2,1},{3,0},{4,7},{5,6},{6,5},{7,4},{8,11},{9,10},{10,... | collective-permute-start | bytes 49160 | tf_op jit(solution)/shard_map/ppermute | solution.py:54
  23.5 3.8 %collective-permute-start.8 = (f32[1,128,32]{1,2,0:T(8,128)S(1)}, f32[1,128,32]{1,2,0:T(8,128)S(1)}, u32[]{:S(2)}, u32[]{:S(2)}) collective-permute-start(f32[1,128,32]{1,2,0:T(8,128)S(1)} %pad_maximum_fusion.2), channel_id=1, source_target_pairs={{0,2},{1,3},{2,0},{3,1},{4,6},{5,7},{6,4},{7,5},{8,10},{9,11},{10,... | collective-permute-start | bytes 49160 | tf_op jit(solution)/shard_map/ppermute | solution.py:54
  25.2 2.0 %collective-permute-start.7 = (f32[1,128,32]{1,2,0:T(8,128)S(1)}, f32[1,128,32]{1,2,0:T(8,128)S(1)}, u32[]{:S(2)}, u32[]{:S(2)}) collective-permute-start(f32[1,128,32]{1,2,0:T(8,128)S(1)} %pad_maximum_fusion.2), channel_id=1, source_target_pairs={{0,1},{1,0},{2,3},{3,2},{4,5},{5,4},{6,7},{7,6},{8,9},{9,8},{10,11... | collective-permute-start | bytes 49160 | tf_op jit(solution)/shard_map/ppermute | solution.py:54
  25.5 25.7 %collective-permute-start.6 = (f32[128,2048]{0,1:T(8,128)}, f32[128,2048]{0,1:T(8,128)S(1)}, u32[]{:S(2)}, u32[]{:S(2)}) collective-permute-start(f32[128,2048]{0,1:T(8,128)} %fusion.3), channel_id=1, source_target_pairs={{0,2},{1,3},{2,0},{3,1},{4,6},{5,7},{6,4},{7,5},{8,10},{9,11},{10,... | collective-permute-start | bytes 3145736 | tf_op jit(solution)/shard_map/ppermute | solution.py:87
  27.9 7.7 %collective-permute-start.16 = (bf16[1,16,2304]{2,1,0:T(8,128)(2,1)S(1)}, bf16[1,16,2304]{2,1,0:T(8,128)(2,1)S(1)}, u32[]{:S(2)}, u32[]{:S(2)}) collective-permute-start(bf16[1,16,2304]{2,1,0:T(8,128)(2,1)S(1)} %fusion.27), channel_id=1, source_target_pairs={{0,28},{4,24},{8,20},{12,16},{16,12},{20,8},{24,4},{28,0},{1,29},{... | collective-permute-start | bytes 221192 | tf_op jit(solution)/shard_map/ppermute | solution.py:161
  32.5 7.1 %collective-permute-start.15 = (bf16[1,16,2304]{2,1,0:T(8,128)(2,1)S(1)}, bf16[1,16,2304]{2,1,0:T(8,128)(2,1)S(1)}, u32[]{:S(2)}, u32[]{:S(2)}) collective-permute-start(bf16[1,16,2304]{2,1,0:T(8,128)(2,1)S(1)} %get-tuple-element.11), channel_id=1, source_target_pairs={{0,24},{4,28},{8,16},{12,20},{16,8},{20,12},{24,0},{28,4},{1,25},{... | collective-permute-start | bytes 221192 | tf_op jit(solution)/shard_map/ppermute | solution.py:161
  32.6 11.2 %collective-permute-start.14 = (bf16[1,16,2304]{2,1,0:T(8,128)(2,1)S(1)}, bf16[1,16,2304]{2,1,0:T(8,128)(2,1)S(1)}, u32[]{:S(2)}, u32[]{:S(2)}) collective-permute-start(bf16[1,16,2304]{2,1,0:T(8,128)(2,1)S(1)} %get-tuple-element.12), channel_id=1, source_target_pairs={{0,20},{4,16},{8,28},{12,24},{16,4},{20,0},{24,12},{28,8},{1,21},{... | collective-permute-start | bytes 221192 | tf_op jit(solution)/shard_map/ppermute | solution.py:161
  35.6 9.7 %collective-permute-start.13 = (bf16[1,16,2304]{2,1,0:T(8,128)(2,1)S(1)}, bf16[1,16,2304]{2,1,0:T(8,128)(2,1)S(1)}, u32[]{:S(2)}, u32[]{:S(2)}) collective-permute-start(bf16[1,16,2304]{2,1,0:T(8,128)(2,1)S(1)} %get-tuple-element.13), channel_id=1, source_target_pairs={{0,16},{4,20},{8,24},{12,28},{16,0},{20,4},{24,8},{28,12},{1,17},{... | collective-permute-start | bytes 221192 | tf_op jit(solution)/shard_map/ppermute | solution.py:161
  39.6 6.7 %collective-permute-start.12 = (bf16[1,16,2304]{2,1,0:T(8,128)(2,1)S(1)}, bf16[1,16,2304]{2,1,0:T(8,128)(2,1)S(1)}, u32[]{:S(2)}, u32[]{:S(2)}) collective-permute-start(bf16[1,16,2304]{2,1,0:T(8,128)(2,1)S(1)} %get-tuple-element.14), channel_id=1, source_target_pairs={{0,12},{4,8},{8,4},{12,0},{16,28},{20,24},{24,20},{28,16},{1,13},{... | collective-permute-start | bytes 221192 | tf_op jit(solution)/shard_map/ppermute | solution.py:161
  43.8 4.4 %collective-permute-start.11 = (bf16[1,16,2304]{2,1,0:T(8,128)(2,1)S(1)}, bf16[1,16,2304]{2,1,0:T(8,128)(2,1)S(1)}, u32[]{:S(2)}, u32[]{:S(2)}) collective-permute-start(bf16[1,16,2304]{2,1,0:T(8,128)(2,1)S(1)} %get-tuple-element.15), channel_id=1, source_target_pairs={{0,8},{4,12},{8,0},{12,4},{16,24},{20,28},{24,16},{28,20},{1,9},{5... | collective-permute-start | bytes 221192 | tf_op jit(solution)/shard_map/ppermute | solution.py:161
  45.3 4.4 %collective-permute-start.10 = (bf16[1,16,2304]{2,1,0:T(8,128)(2,1)S(1)}, bf16[1,16,2304]{2,1,0:T(8,128)(2,1)S(1)}, u32[]{:S(2)}, u32[]{:S(2)}) collective-permute-start(bf16[1,16,2304]{2,1,0:T(8,128)(2,1)S(1)} %get-tuple-element.10), channel_id=1, source_target_pairs={{0,4},{4,0},{8,12},{12,8},{16,20},{20,16},{24,28},{28,24},{1,5},{5... | collective-permute-start | bytes 221192 | tf_op jit(solution)/shard_map/ppermute | solution.py:161

commit v22 on v21

--- a/solution.py
+++ b/solution.py
@@ -156,7 +156,7 @@
     owned = lax.dynamic_index_in_dim(combined, me_dp, 0, keepdims=False)
     grad_down = owned[:, :, :width_portion]
     grad_up = owned[:, :, width_portion:]
-    for shift, pairs in _partners(dp_size):
+    for shift, pairs in sorted(_partners(dp_size), key=lambda sp: -sp[0]):
         outgoing = lax.dynamic_index_in_dim(combined, _dest_of(me_dp, shift, dp_size), 0, keepdims=False)
         arrived = lax.ppermute(outgoing.astype(jnp.bfloat16), "dp", pairs).astype(jnp.float32)
         grad_down = grad_down + arrived[:, :, :width_portion]

time: 54.2 us -> 54.2 us (level)
  waiting for transfers between devices: 16.5 us -> 9.25 us
  starting transfers between devices: 21.3 us -> 28.5 us
    ppermute x7, waiting for transfers between devices: 11.2 us -> 3.15 us  [on_device(): lax.ppermute(outgoing.astype(jnp.bfloat16), 'dp', pairs).astype(jnp.float32)]
    ppermute x7, starting transfers between devices: 9.99 us -> 17.3 us  [on_device(): lax.ppermute(outgoing.astype(jnp.bfloat16), 'dp', pairs).astype(jnp.float32)]
    ppermute x3, waiting for transfers between devices: 0.25 us -> 0.97 us  [_frozen_term(): got = [lax.ppermute(held[e], axis, pairs) for e in range(1, len(held), 2)]]
  transfers between devices with their start and end apart: 17 -> 17, of which waited for: 10 -> 6; matrix products, arithmetic and copies ran while one was open for 19% -> 19% of each run, Pallas kernels for 0% -> 0%
where the time goes in v22:
time: 54.2 us; the launch traced here: 53.9 us
  starting transfers between devices  28.5 us (53%)
  matrix products  10.1 us (19%)
  waiting for transfers between devices  9.25 us (17%)
  local copies, waits for them, and re-layouts  2.84 us (5%)
  other arithmetic  1.66 us (3%)
  between operations  1.55 us (3%)
    ppermute x7, starting transfers between devices, on_device(): lax.ppermute(outgoing.astype(jnp.bfloat16), 'dp', pairs).astype(jnp.float32)  17.3 us
    dot_general x4, matrix products, term(): lax.dot_general(cotangent, piece, (((1,), (1,)), ((), ())), preferred_ele...  8.91 us
    ppermute x1, starting transfers between devices, _gather_dp(): lax.ppermute(local, axis, [(i, i ^ half) for i in range(size)])  4.04 us
    ppermute x3, waiting for transfers between devices, _gather_dp(): got.append(lax.ppermute(pair, axis, [(i, i ^ shift) for i in range(size)]))  3.84 us
    ppermute x3, starting transfers between devices, _gather_dp(): got.append(lax.ppermute(pair, axis, [(i, i ^ shift) for i in range(size)]))  3.55 us
    ppermute x7, waiting for transfers between devices, on_device(): lax.ppermute(outgoing.astype(jnp.bfloat16), 'dp', pairs).astype(jnp.float32)  3.15 us
    unnamed x6, local copies, waits for them, and re-layouts  1.94 us
    ppermute x3, starting transfers between devices, _psum_small(): total = total + lax.ppermute(value, axis, pairs)  1.88 us
  transfers between devices with their start and end apart: 17, of which 6 were waited for; matrix products, arithmetic and copies ran while one was open for 19% of the time, Pallas kernels for 0%

profile of v22, /device:TPU:0, one launch (start us, length us, event | category | flops | bytes accessed | tf_op | source)
XLA Modules:
  0.0 53.9 jit_solution(9207561085504258293)
XLA Ops:
  0.7 0.9 %constant_dynamic-update-slice_fusion.1 = bf16[1,16,2304]{2,1,0:T(8,128)(2,1)S(1)} fusion(bf16[1,16,2048]{2,1,0:T(8,128)(2,1)} %param.9), kind=kLoop, calls=%fused_computation.71 | loop fusion | bytes 131072
  2.3 4.0 %collective-permute-start.2 = (bf16[1,16,2304]{2,1,0:T(8,128)(2,1)S(1)}, bf16[1,16,2304]{2,1,0:T(8,128)(2,1)S(1)}, u32[]{:S(2)}, u32[]{:S(2)}) collective-permute-start(bf16[1,16,2304]{2,1,0:T(8,128)(2,1)S(1)} %constant_dynamic-update-slice_fusion), channel_id=1, source_target_pairs={{0,16},{4,20},{8,24},{12,28},{16,0},{20,4},{24,8},{28,12},{1,17},{... | collective-permute-start | bytes 221192 | tf_op jit(solution)/shard_map/ppermute | solution.py:37
  6.3 2.6 %convolution_bitcast_fusion.1 = f32[128,2048]{0,1:T(8,128)} fusion(bf16[128,256]{1,0:T(8,128)(2,1)} %param.7, bf16[8192,256]{1,0:T(8,128)(2,1)} %param.8, s32[]{:T(128)S(6)} %select_n.81), kind=kOutput, calls=%fused_computation.1 | convolution fusion | flops 134217728 | bytes 2162692 | tf_op jit(solution)/shard_map/dot_general | solution.py:75
  8.9 1.3 %collective-permute-done.2 = bf16[1,16,2304]{2,1,0:T(8,128)(2,1)S(1)} collective-permute-done((bf16[1,16,2304]{2,1,0:T(8,128)(2,1)S(1)}, bf16[1,16,2304]{2,1,0:T(8,128)(2,1)S(1)}, u32[]{:S(2)}, u32[]{:S(2)}) %collective-permute-start.2) | collective-permute-done | bytes 73760 | tf_op jit(solution)/shard_map/ppermute | solution.py:37
  10.2 1.8 %collective-permute-start.5 = (bf16[2,16,2304]{2,1,0:T(8,128)(2,1)S(1)}, bf16[2,16,2304]{2,1,0:T(8,128)(2,1)S(1)}, u32[]{:S(2)}, u32[]{:S(2)}) collective-permute-start(bf16[2,16,2304]{2,1,0:T(8,128)(2,1)S(1)} %pad_maximum_fusion.1), channel_id=1, source_target_pairs={{0,4},{4,0},{8,12},{12,8},{16,20},{20,16},{24,28},{28,24},{1,5},{5... | collective-permute-start | bytes 442376 | tf_op jit(solution)/shard_map/ppermute | solution.py:41
  12.5 1.3 %collective-permute-start.3 = (bf16[2,16,2304]{2,1,0:T(8,128)(2,1)S(1)}, bf16[2,16,2304]{2,1,0:T(8,128)(2,1)S(1)}, u32[]{:S(2)}, u32[]{:S(2)}) collective-permute-start(bf16[2,16,2304]{2,1,0:T(8,128)(2,1)S(1)} %pad_maximum_fusion.1), channel_id=1, source_target_pairs={{0,12},{4,8},{8,4},{12,0},{16,28},{20,24},{24,20},{28,16},{1,13},{... | collective-permute-start | bytes 442376 | tf_op jit(solution)/shard_map/ppermute | solution.py:41
  13.8 1.6 %convolution_bitcast_fusion.3 = f32[128,2048]{0,1:T(8,128)S(1)} fusion(bf16[128,256]{1,0:T(8,128)(2,1)} %param.7, bf16[8192,256]{1,0:T(8,128)(2,1)} %param.8, s32[]{:T(128)S(6)} %select_n.79), kind=kOutput, calls=%fused_computation.3 | convolution fusion | flops 134217728 | bytes 2162692 | tf_op jit(solution)/shard_map/dot_general | solution.py:75
  16.2 1.9 %collective-permute-done.4 = bf16[2,16,2304]{2,1,0:T(8,128)(2,1)S(1)} collective-permute-done((bf16[2,16,2304]{2,1,0:T(8,128)(2,1)S(1)}, bf16[2,16,2304]{2,1,0:T(8,128)(2,1)S(1)}, u32[]{:S(2)}, u32[]{:S(2)}) %collective-permute-start.4) | collective-permute-done | bytes 147488 | tf_op jit(solution)/shard_map/ppermute | solution.py:41
  18.1 2.0 %collective-permute-done.3 = bf16[2,16,2304]{2,1,0:T(8,128)(2,1)S(1)} collective-permute-done((bf16[2,16,2304]{2,1,0:T(8,128)(2,1)S(1)}, bf16[2,16,2304]{2,1,0:T(8,128)(2,1)S(1)}, u32[]{:S(2)}, u32[]{:S(2)}) %collective-permute-start.3) | collective-permute-done | bytes 147488 | tf_op jit(solution)/shard_map/ppermute | solution.py:41
  20.5 3.0 %fusion.3 = f32[128,2048]{0,1:T(8,128)} fusion(f32[128,2048]{0,1:T(8,128)} %collective-permute-done.1, bf16[128,256]{1,0:T(8,128)(2,1)S(1)} %copy-done.1, bf16[8192,256]{1,0:T(8,128)(2,1)} %param.8, s32[]{:T(128)S(6)} %select_n.80), kind=kOutput, calls=%fused_computation.8 | convolution fusion | flops 134479872 | bytes 3211268 | tf_op jit(solution)/shard_map/dot_general | solution.py:75
  23.5 1.7 %collective-permute-start.8 = (f32[1,128,32]{1,2,0:T(8,128)S(1)}, f32[1,128,32]{1,2,0:T(8,128)S(1)}, u32[]{:S(2)}, u32[]{:S(2)}) collective-permute-start(f32[1,128,32]{1,2,0:T(8,128)S(1)} %pad_maximum_fusion.2), channel_id=1, source_target_pairs={{0,2},{1,3},{2,0},{3,1},{4,6},{5,7},{6,4},{7,5},{8,10},{9,11},{10,... | collective-permute-start | bytes 49160 | tf_op jit(solution)/shard_map/ppermute | solution.py:54
  25.5 1.7 %collective-permute-start.6 = (f32[128,2048]{0,1:T(8,128)}, f32[128,2048]{0,1:T(8,128)S(1)}, u32[]{:S(2)}, u32[]{:S(2)}) collective-permute-start(f32[128,2048]{0,1:T(8,128)} %fusion.3), channel_id=1, source_target_pairs={{0,2},{1,3},{2,0},{3,1},{4,6},{5,7},{6,4},{7,5},{8,10},{9,11},{10,... | collective-permute-start | bytes 3145736 | tf_op jit(solution)/shard_map/ppermute | solution.py:87
  27.9 1.1 %collective-permute-start.16 = (bf16[1,16,2304]{2,1,0:T(8,128)(2,1)S(1)}, bf16[1,16,2304]{2,1,0:T(8,128)(2,1)S(1)}, u32[]{:S(2)}, u32[]{:S(2)}) collective-permute-start(bf16[1,16,2304]{2,1,0:T(8,128)(2,1)S(1)} %fusion.27), channel_id=1, source_target_pairs={{0,4},{4,0},{8,12},{12,8},{16,20},{20,16},{24,28},{28,24},{1,5},{5... | collective-permute-start | bytes 221192 | tf_op jit(solution)/shard_map/ppermute | solution.py:161
  29.1 1.7 %collective-permute-start.15 = (bf16[1,16,2304]{2,1,0:T(8,128)(2,1)S(1)}, bf16[1,16,2304]{2,1,0:T(8,128)(2,1)S(1)}, u32[]{:S(2)}, u32[]{:S(2)}) collective-permute-start(bf16[1,16,2304]{2,1,0:T(8,128)(2,1)S(1)} %get-tuple-element.11), channel_id=1, source_target_pairs={{0,8},{4,12},{8,0},{12,4},{16,24},{20,28},{24,16},{28,20},{1,9},{5... | collective-permute-start | bytes 221192 | tf_op jit(solution)/shard_map/ppermute | solution.py:161
  30.8 0.8 %collective-permute-start.14 = (bf16[1,16,2304]{2,1,0:T(8,128)(2,1)S(1)}, bf16[1,16,2304]{2,1,0:T(8,128)(2,1)S(1)}, u32[]{:S(2)}, u32[]{:S(2)}) collective-permute-start(bf16[1,16,2304]{2,1,0:T(8,128)(2,1)S(1)} %get-tuple-element.12), channel_id=1, source_target_pairs={{0,12},{4,8},{8,4},{12,0},{16,28},{20,24},{24,20},{28,16},{1,13},{... | collective-permute-start | bytes 221192 | tf_op jit(solution)/shard_map/ppermute | solution.py:161
  31.6 1.2 %collective-permute-done.16 = bf16[1,16,2304]{2,1,0:T(8,128)(2,1)S(1)} collective-permute-done((bf16[1,16,2304]{2,1,0:T(8,128)(2,1)S(1)}, bf16[1,16,2304]{2,1,0:T(8,128)(2,1)S(1)}, u32[]{:S(2)}, u32[]{:S(2)}) %collective-permute-start.16) | collective-permute-done | bytes 73760 | tf_op jit(solution)/shard_map/ppermute | solution.py:161
  32.8 2.2 %collective-permute-start.13 = (bf16[1,16,2304]{2,1,0:T(8,128)(2,1)S(1)}, bf16[1,16,2304]{2,1,0:T(8,128)(2,1)S(1)}, u32[]{:S(2)}, u32[]{:S(2)}) collective-permute-start(bf16[1,16,2304]{2,1,0:T(8,128)(2,1)S(1)} %get-tuple-element.13), channel_id=1, source_target_pairs={{0,16},{4,20},{8,24},{12,28},{16,0},{20,4},{24,8},{28,12},{1,17},{... | collective-permute-start | bytes 221192 | tf_op jit(solution)/shard_map/ppermute | solution.py:161
  35.0 1.4 %collective-permute-start.12 = (bf16[1,16,2304]{2,1,0:T(8,128)(2,1)S(1)}, bf16[1,16,2304]{2,1,0:T(8,128)(2,1)S(1)}, u32[]{:S(2)}, u32[]{:S(2)}) collective-permute-start(bf16[1,16,2304]{2,1,0:T(8,128)(2,1)S(1)} %get-tuple-element.14), channel_id=1, source_target_pairs={{0,20},{4,16},{8,28},{12,24},{16,4},{20,0},{24,12},{28,8},{1,21},{... | collective-permute-start | bytes 221192 | tf_op jit(solution)/shard_map/ppermute | solution.py:161
  36.4 3.8 %collective-permute-start.11 = (bf16[1,16,2304]{2,1,0:T(8,128)(2,1)S(1)}, bf16[1,16,2304]{2,1,0:T(8,128)(2,1)S(1)}, u32[]{:S(2)}, u32[]{:S(2)}) collective-permute-start(bf16[1,16,2304]{2,1,0:T(8,128)(2,1)S(1)} %get-tuple-element.15), channel_id=1, source_target_pairs={{0,24},{4,28},{8,16},{12,20},{16,8},{20,12},{24,0},{28,4},{1,25},{... | collective-permute-start | bytes 221192 | tf_op jit(solution)/shard_map/ppermute | solution.py:161
  40.1 6.3 %collective-permute-start.10 = (bf16[1,16,2304]{2,1,0:T(8,128)(2,1)S(1)}, bf16[1,16,2304]{2,1,0:T(8,128)(2,1)S(1)}, u32[]{:S(2)}, u32[]{:S(2)}) collective-permute-start(bf16[1,16,2304]{2,1,0:T(8,128)(2,1)S(1)} %get-tuple-element.10), channel_id=1, source_target_pairs={{0,28},{4,24},{8,20},{12,16},{16,12},{20,8},{24,4},{28,0},{1,29},{... | collective-permute-start | bytes 221192 | tf_op jit(solution)/shard_map/ppermute | solution.py:161
  47.0 1.9 %collective-permute-done.10 = bf16[1,16,2304]{2,1,0:T(8,128)(2,1)S(1)} collective-permute-done((bf16[1,16,2304]{2,1,0:T(8,128)(2,1)S(1)}, bf16[1,16,2304]{2,1,0:T(8,128)(2,1)S(1)}, u32[]{:S(2)}, u32[]{:S(2)}) %collective-permute-start.10) | collective-permute-done | bytes 73760 | tf_op jit(solution)/shard_map/ppermute | solution.py:161
  50.3 1.0 %collective-permute-done.6 = f32[128,2048]{0,1:T(8,128)S(1)} collective-permute-done((f32[128,2048]{0,1:T(8,128)}, f32[128,2048]{0,1:T(8,128)S(1)}, u32[]{:S(2)}, u32[]{:S(2)}) %collective-permute-start.6) | collective-permute-done | bytes 1048608 | tf_op jit(solution)/shard_map/ppermute | solution.py:87
  51.2 1.7 %fusion.4 = bf16[128,2048]{0,1:T(8,128)(2,1)S(1)} fusion(f32[128,2048]{0,1:T(8,128)S(1)} %fusion.28, f32[128,2048]{0,1:T(8,128)S(1)} %collective-permute-done.6, f32[128,2048]{0,1:T(8,128)S(1)} %collective-permute-done, bf16[128,256]{1,0:T(8,128)(2,1)S(1)} %copy-done.1, bf16[8192,256]{1,0:T(8,128)(2,1)} %param.8, s32[]{:T(128)S(6)} %select_n.78), kind=kOutput, calls=%fused_computation.9 | convolution fusion | flops 135266304 | bytes 4784132 | tf_op jit(solution)/shard_map/dot_general | solution.py:75
  52.9 1.0 %copy.16 = bf16[128,2048]{1,0:T(8,128)(2,1)} copy(bf16[128,2048]{0,1:T(8,128)(2,1)S(1)} %fusion.4) | data formatting | bytes 1048576
  (48 shorter events, 4.4 us)
Async XLA Ops:
  0.6 19.6 %copy-start = (bf16[128,2048]{1,0:T(8,128)(2,1)S(1)}, bf16[128,2048]{1,0:T(8,128)(2,1)}, u32[]{:S(2)}) copy-start(bf16[128,2048]{1,0:T(8,128)(2,1)} %param.6) | copy-start | bytes 1572868
  0.6 19.5 %copy-start.1 = (bf16[128,256]{1,0:T(8,128)(2,1)S(1)}, bf16[128,256]{1,0:T(8,128)(2,1)}, u32[]{:S(2)}) copy-start(bf16[128,256]{1,0:T(8,128)(2,1)} %param.7) | copy-start | bytes 196612
  2.3 7.9 %collective-permute-start.2 = (bf16[1,16,2304]{2,1,0:T(8,128)(2,1)S(1)}, bf16[1,16,2304]{2,1,0:T(8,128)(2,1)S(1)}, u32[]{:S(2)}, u32[]{:S(2)}) collective-permute-start(bf16[1,16,2304]{2,1,0:T(8,128)(2,1)S(1)} %constant_dynamic-update-slice_fusion), channel_id=1, source_target_pairs={{0,16},{4,20},{8,24},{12,28},{16,0},{20,4},{24,8},{28,12},{1,17},{... | collective-permute-start | bytes 221192 | tf_op jit(solution)/shard_map/ppermute | solution.py:37
  8.9 11.6 %collective-permute-start.1 = (f32[128,2048]{0,1:T(8,128)}, f32[128,2048]{0,1:T(8,128)}, u32[]{:S(2)}, u32[]{:S(2)}) collective-permute-start(f32[128,2048]{0,1:T(8,128)} %convolution_bitcast_fusion.1), channel_id=1, source_target_pairs={{0,1},{1,0},{2,3},{3,2},{4,5},{5,4},{6,7},{7,6},{8,9},{9,8},{10,11... | collective-permute-start | bytes 3145736 | tf_op jit(solution)/shard_map/ppermute | solution.py:87
  10.2 6.0 %collective-permute-start.5 = (bf16[2,16,2304]{2,1,0:T(8,128)(2,1)S(1)}, bf16[2,16,2304]{2,1,0:T(8,128)(2,1)S(1)}, u32[]{:S(2)}, u32[]{:S(2)}) collective-permute-start(bf16[2,16,2304]{2,1,0:T(8,128)(2,1)S(1)} %pad_maximum_fusion.1), channel_id=1, source_target_pairs={{0,4},{4,0},{8,12},{12,8},{16,20},{20,16},{24,28},{28,24},{1,5},{5... | collective-permute-start | bytes 442376 | tf_op jit(solution)/shard_map/ppermute | solution.py:41
  12.0 6.1 %collective-permute-start.4 = (bf16[2,16,2304]{2,1,0:T(8,128)(2,1)S(1)}, bf16[2,16,2304]{2,1,0:T(8,128)(2,1)S(1)}, u32[]{:S(2)}, u32[]{:S(2)}) collective-permute-start(bf16[2,16,2304]{2,1,0:T(8,128)(2,1)S(1)} %pad_maximum_fusion.1), channel_id=1, source_target_pairs={{0,8},{4,12},{8,0},{12,4},{16,24},{20,28},{24,16},{28,20},{1,9},{5... | collective-permute-start | bytes 442376 | tf_op jit(solution)/shard_map/ppermute | solution.py:41
  12.5 7.6 %collective-permute-start.3 = (bf16[2,16,2304]{2,1,0:T(8,128)(2,1)S(1)}, bf16[2,16,2304]{2,1,0:T(8,128)(2,1)S(1)}, u32[]{:S(2)}, u32[]{:S(2)}) collective-permute-start(bf16[2,16,2304]{2,1,0:T(8,128)(2,1)S(1)} %pad_maximum_fusion.1), channel_id=1, source_target_pairs={{0,12},{4,8},{8,4},{12,0},{16,28},{20,24},{24,20},{28,16},{1,13},{... | collective-permute-start | bytes 442376 | tf_op jit(solution)/shard_map/ppermute | solution.py:41
  15.5 34.8 %collective-permute-start = (f32[128,2048]{0,1:T(8,128)S(1)}, f32[128,2048]{0,1:T(8,128)S(1)}, u32[]{:S(2)}, u32[]{:S(2)}) collective-permute-start(f32[128,2048]{0,1:T(8,128)S(1)} %convolution_bitcast_fusion.3), channel_id=1, source_target_pairs={{0,1},{1,0},{2,3},{3,2},{4,5},{5,4},{6,7},{7,6},{8,9},{9,8},{10,11... | collective-permute-start | bytes 3145736 | tf_op jit(solution)/shard_map/ppermute | solution.py:87
  23.5 3.8 %collective-permute-start.9 = (f32[1,128,32]{1,2,0:T(8,128)S(1)}, f32[1,128,32]{1,2,0:T(8,128)S(1)}, u32[]{:S(2)}, u32[]{:S(2)}) collective-permute-start(f32[1,128,32]{1,2,0:T(8,128)S(1)} %pad_maximum_fusion.2), channel_id=1, source_target_pairs={{0,3},{1,2},{2,1},{3,0},{4,7},{5,6},{6,5},{7,4},{8,11},{9,10},{10,... | collective-permute-start | bytes 49160 | tf_op jit(solution)/shard_map/ppermute | solution.py:54
  23.5 3.8 %collective-permute-start.8 = (f32[1,128,32]{1,2,0:T(8,128)S(1)}, f32[1,128,32]{1,2,0:T(8,128)S(1)}, u32[]{:S(2)}, u32[]{:S(2)}) collective-permute-start(f32[1,128,32]{1,2,0:T(8,128)S(1)} %pad_maximum_fusion.2), channel_id=1, source_target_pairs={{0,2},{1,3},{2,0},{3,1},{4,6},{5,7},{6,4},{7,5},{8,10},{9,11},{10,... | collective-permute-start | bytes 49160 | tf_op jit(solution)/shard_map/ppermute | solution.py:54
  25.2 2.0 %collective-permute-start.7 = (f32[1,128,32]{1,2,0:T(8,128)S(1)}, f32[1,128,32]{1,2,0:T(8,128)S(1)}, u32[]{:S(2)}, u32[]{:S(2)}) collective-permute-start(f32[1,128,32]{1,2,0:T(8,128)S(1)} %pad_maximum_fusion.2), channel_id=1, source_target_pairs={{0,1},{1,0},{2,3},{3,2},{4,5},{5,4},{6,7},{7,6},{8,9},{9,8},{10,11... | collective-permute-start | bytes 49160 | tf_op jit(solution)/shard_map/ppermute | solution.py:54
  25.5 25.7 %collective-permute-start.6 = (f32[128,2048]{0,1:T(8,128)}, f32[128,2048]{0,1:T(8,128)S(1)}, u32[]{:S(2)}, u32[]{:S(2)}) collective-permute-start(f32[128,2048]{0,1:T(8,128)} %fusion.3), channel_id=1, source_target_pairs={{0,2},{1,3},{2,0},{3,1},{4,6},{5,7},{6,4},{7,5},{8,10},{9,11},{10,... | collective-permute-start | bytes 3145736 | tf_op jit(solution)/shard_map/ppermute | solution.py:87
  27.9 4.9 %collective-permute-start.16 = (bf16[1,16,2304]{2,1,0:T(8,128)(2,1)S(1)}, bf16[1,16,2304]{2,1,0:T(8,128)(2,1)S(1)}, u32[]{:S(2)}, u32[]{:S(2)}) collective-permute-start(bf16[1,16,2304]{2,1,0:T(8,128)(2,1)S(1)} %fusion.27), channel_id=1, source_target_pairs={{0,4},{4,0},{8,12},{12,8},{16,20},{20,16},{24,28},{28,24},{1,5},{5... | collective-permute-start | bytes 221192 | tf_op jit(solution)/shard_map/ppermute | solution.py:161
  29.1 5.9 %collective-permute-start.15 = (bf16[1,16,2304]{2,1,0:T(8,128)(2,1)S(1)}, bf16[1,16,2304]{2,1,0:T(8,128)(2,1)S(1)}, u32[]{:S(2)}, u32[]{:S(2)}) collective-permute-start(bf16[1,16,2304]{2,1,0:T(8,128)(2,1)S(1)} %get-tuple-element.11), channel_id=1, source_target_pairs={{0,8},{4,12},{8,0},{12,4},{16,24},{20,28},{24,16},{28,20},{1,9},{5... | collective-permute-start | bytes 221192 | tf_op jit(solution)/shard_map/ppermute | solution.py:161
  30.8 5.6 %collective-permute-start.14 = (bf16[1,16,2304]{2,1,0:T(8,128)(2,1)S(1)}, bf16[1,16,2304]{2,1,0:T(8,128)(2,1)S(1)}, u32[]{:S(2)}, u32[]{:S(2)}) collective-permute-start(bf16[1,16,2304]{2,1,0:T(8,128)(2,1)S(1)} %get-tuple-element.12), channel_id=1, source_target_pairs={{0,12},{4,8},{8,4},{12,0},{16,28},{20,24},{24,20},{28,16},{1,13},{... | collective-permute-start | bytes 221192 | tf_op jit(solution)/shard_map/ppermute | solution.py:161
  32.8 7.4 %collective-permute-start.13 = (bf16[1,16,2304]{2,1,0:T(8,128)(2,1)S(1)}, bf16[1,16,2304]{2,1,0:T(8,128)(2,1)S(1)}, u32[]{:S(2)}, u32[]{:S(2)}) collective-permute-start(bf16[1,16,2304]{2,1,0:T(8,128)(2,1)S(1)} %get-tuple-element.13), channel_id=1, source_target_pairs={{0,16},{4,20},{8,24},{12,28},{16,0},{20,4},{24,8},{28,12},{1,17},{... | collective-permute-start | bytes 221192 | tf_op jit(solution)/shard_map/ppermute | solution.py:161
  35.0 11.9 %collective-permute-start.12 = (bf16[1,16,2304]{2,1,0:T(8,128)(2,1)S(1)}, bf16[1,16,2304]{2,1,0:T(8,128)(2,1)S(1)}, u32[]{:S(2)}, u32[]{:S(2)}) collective-permute-start(bf16[1,16,2304]{2,1,0:T(8,128)(2,1)S(1)} %get-tuple-element.14), channel_id=1, source_target_pairs={{0,20},{4,16},{8,28},{12,24},{16,4},{20,0},{24,12},{28,8},{1,21},{... | collective-permute-start | bytes 221192 | tf_op jit(solution)/shard_map/ppermute | solution.py:161
  36.4 10.6 %collective-permute-start.11 = (bf16[1,16,2304]{2,1,0:T(8,128)(2,1)S(1)}, bf16[1,16,2304]{2,1,0:T(8,128)(2,1)S(1)}, u32[]{:S(2)}, u32[]{:S(2)}) collective-permute-start(bf16[1,16,2304]{2,1,0:T(8,128)(2,1)S(1)} %get-tuple-element.15), channel_id=1, source_target_pairs={{0,24},{4,28},{8,16},{12,20},{16,8},{20,12},{24,0},{28,4},{1,25},{... | collective-permute-start | bytes 221192 | tf_op jit(solution)/shard_map/ppermute | solution.py:161
  40.1 8.8 %collective-permute-start.10 = (bf16[1,16,2304]{2,1,0:T(8,128)(2,1)S(1)}, bf16[1,16,2304]{2,1,0:T(8,128)(2,1)S(1)}, u32[]{:S(2)}, u32[]{:S(2)}) collective-permute-start(bf16[1,16,2304]{2,1,0:T(8,128)(2,1)S(1)} %get-tuple-element.10), channel_id=1, source_target_pairs={{0,28},{4,24},{8,20},{12,16},{16,12},{20,8},{24,4},{28,0},{1,29},{... | collective-permute-start | bytes 221192 | tf_op jit(solution)/shard_map/ppermute | solution.py:161
